TPU v7x, 128 devices: a whole 4x4x4 slice. The times are simulated.
128 devices in a mesh: blk: 32 (over y, z, core), lvl: 4 (over x).
Axes of the slice: x: 4, y: 4, z: 4, core: 2. Of those that a mesh axis runs over, the one named last changes fastest.
Arguments:
- rhs: bfloat16 [4, 32, 768, 384], P('lvl', 'blk'), may hold values from -6 to 6
- inverse: bfloat16 [4, 32, 768, 768], P('lvl', 'blk'), may hold values from -1 to 3
- left_factors: bfloat16 [4, 32, 4, 768, 128], P('lvl', 'blk'), may hold values from -0.1875 to 0.1875
- right_factors: bfloat16 [4, 32, 4, 768, 128], P('lvl', 'blk'), may hold values from -0.21875 to 0.21875
- sources: int32 [4, 32, 4], replicated, may hold values from 0 to 31, as said below
- ranks: int32 [4, 32, 4], replicated, may hold values from 32 to 128
- owner: int32 [4, 32], replicated, may hold values from 0 to 31, as said below
Outputs:
- forward: bfloat16 [4, 32, 768, 384], P('lvl', 'blk')
- backward: bfloat16 [4, 32, 768, 384], P('lvl', 'blk')
Inputs may be any that keep to these rules, and one draw needn't show every extreme that they name: Every row owner[l] is a permutation of the positions; position p is stored on blk index p. sources[l] names blocks of level l - 1 (the row of level 0 names blocks of the last level and is unused); for each level and each k, column k names every block once; between consecutive levels the tiles from the blocks of one blk index to those of another number 0 or exactly 1.
All inputs are finite; a program needn't handle non-finite values.
Results may differ from a plain program's by a relative error of at most 0.02.
Values may be sent and summed in bfloat16 or wider, within the bound.
No kernel may reach another device: no remote copies, remote signals or barrier semaphores. Data moves between devices by JAX's collectives and lax.ppermute only.
A program may use at most 64 MiB of HBM per device.

v0:
```python
import jax
import jax.numpy as jnp
from jax import lax
from jax.sharding import PartitionSpec as P


def passed_along(array, axis, by):
    peers = lax.axis_size(axis)
    pairs = [(i, i + by) for i in range(peers) if 0 <= i + by < peers]
    return lax.ppermute(array, axis, pairs)


def level_maps(sources, owner, ranks, section_at):
    block_count = owner.shape[1]
    position = jnp.arange(block_count, dtype=jnp.int32)
    holder = jnp.zeros((block_count,), jnp.int32).at[owner[section_at]].set(position)
    src_block = sources[section_at][holder]
    src_pos = owner[section_at - 1][src_block]
    rank_pos = ranks[section_at][holder]
    columns = jnp.broadcast_to(
        jnp.arange(src_pos.shape[1], dtype=jnp.int32)[None, :], src_pos.shape
    )
    targets = jnp.broadcast_to(position[:, None], src_pos.shape)
    target_of = jnp.zeros(src_pos.shape, jnp.int32).at[src_pos, columns].set(targets)
    return (src_pos, rank_pos, columns, target_of)


def slot_numbers(src_pos, per_dev, device_count):
    block_count, lane_count = src_pos.shape
    target_dev = jnp.arange(block_count, dtype=jnp.int32)[:, None] // per_dev
    pair_ids = (src_pos // per_dev * device_count + target_dev).reshape(-1)
    ordinal = jnp.arange(block_count * lane_count, dtype=jnp.int32)
    earlier = (pair_ids[None, :] == pair_ids[:, None]) & (ordinal[None, :] < ordinal[:, None])
    return jnp.sum(earlier.astype(jnp.int32), axis=1).reshape(block_count, lane_count)


def route_plan(sources, owner, ranks, section_at, per_dev, device_count, spread):
    src_pos, rank_pos, columns, target_of = level_maps(sources, owner, ranks, section_at)
    slot_ids = slot_numbers(src_pos, per_dev, device_count)
    first_row = lax.axis_index("blk") * per_dev
    mine_src = lax.dynamic_slice_in_dim(src_pos, first_row, per_dev, 0)
    mine_slots = lax.dynamic_slice_in_dim(slot_ids, first_row, per_dev, 0)
    mine_rank = lax.dynamic_slice_in_dim(rank_pos, first_row, per_dev, 0)
    mine_target = lax.dynamic_slice_in_dim(target_of, first_row, per_dev, 0)
    lane_ids = columns[:per_dev]
    to_target = (mine_target // per_dev * spread + slot_ids[mine_target, lane_ids]).reshape(-1)
    from_source = (mine_src // per_dev * spread + mine_slots).reshape(-1)
    return (to_target, from_source, mine_rank)


def rank_mask(rank_pos, width):
    return (jnp.arange(width, dtype=jnp.int32)[None, None, :] < rank_pos[:, :, None]).astype(
        jnp.float32
    )


def route_lanes(values, send_at, take_at, total_slots):
    holder = jnp.zeros((total_slots,) + values.shape[1:], values.dtype).at[send_at].set(values)
    arrived = lax.all_to_all(holder, "blk", split_axis=0, concat_axis=0, tiled=True)
    return arrived[take_at]


def local(rhs, inverse, left_factors, right_factors, sources, ranks, owner):
    per_dev = rhs.shape[1]
    tile_count = left_factors.shape[2]
    rank_width = left_factors.shape[4]
    rhs_width = rhs.shape[3]
    level_count = sources.shape[0]
    device_count = lax.axis_size("blk")
    spread = max(1, tile_count * per_dev // device_count)
    total_slots = device_count * spread
    rhs_here = rhs[0]
    inverse_here = inverse[0]
    left_here = left_factors[0]
    right_here = right_factors[0]
    my_level = lax.axis_index("lvl")
    plans = [None]
    for section_at in range(1, level_count):
        plans.append(route_plan(sources, owner, ranks, section_at, per_dev, device_count, spread))
    lane_shape = (per_dev * tile_count, rank_width, rhs_width)
    full_shape = (per_dev, tile_count, rank_width, rhs_width)
    incoming = jnp.zeros(lane_shape, jnp.bfloat16)
    solved = jnp.zeros(rhs_here.shape, jnp.bfloat16)
    for section_at in range(level_count):
        if section_at > 0:
            rank_keep = rank_mask(plans[section_at][2], rank_width).astype(jnp.bfloat16)
        else:
            rank_keep = jnp.ones((per_dev, tile_count, rank_width), jnp.bfloat16)
        need_coef = section_at + 1 < level_count

        def advance(operands):
            previous, arriving = operands
            masked = arriving.reshape(full_shape) * rank_keep[..., None]
            update = jnp.einsum(
                "jkbr,jkrn->jbn", left_here, masked, preferred_element_type=jnp.float32
            )
            reduced = (rhs_here.astype(jnp.float32) - update).astype(jnp.bfloat16)
            result = jnp.einsum(
                "jab,jbn->jan", inverse_here, reduced, preferred_element_type=jnp.float32
            ).astype(jnp.bfloat16)
            if need_coef:
                outgoing = jnp.einsum(
                    "qkbr,qbn->qkrn", right_here, result, preferred_element_type=jnp.float32
                )
                outgoing = outgoing.astype(jnp.bfloat16).reshape(lane_shape)
            else:
                outgoing = jnp.zeros(lane_shape, jnp.bfloat16)
            return (result, outgoing)

        def unchanged(operands):
            return (operands[0], jnp.zeros(lane_shape, jnp.bfloat16))

        solved, coefficients = lax.cond(
            my_level == section_at, advance, unchanged, (solved, incoming)
        )
        if need_coef:
            send_at, take_at, rank_next = plans[section_at + 1]
            routed = route_lanes(coefficients, send_at, take_at, total_slots)
            incoming = passed_along(routed, "lvl", 1)
    answer = jnp.zeros(rhs_here.shape, jnp.bfloat16)
    returning = jnp.zeros(lane_shape, jnp.bfloat16)
    for section_at in reversed(range(level_count)):
        need_send = section_at > 0
        if need_send:
            keep_float = rank_mask(plans[section_at][2], rank_width)
        else:
            keep_float = jnp.ones((per_dev, tile_count, rank_width), jnp.float32)

        def retreat(operands):
            previous, arriving = operands
            carried = jnp.einsum(
                "qkbr,qkrn->qbn",
                right_here,
                arriving.reshape(full_shape),
                preferred_element_type=jnp.float32,
            )
            reduced = (solved.astype(jnp.float32) - carried).astype(jnp.bfloat16)
            result = jnp.einsum(
                "jba,jbn->jan", inverse_here, reduced, preferred_element_type=jnp.float32
            ).astype(jnp.bfloat16)
            if need_send:
                projected = jnp.einsum(
                    "jkbr,jbn->jkrn", left_here, result, preferred_element_type=jnp.float32
                )
                outgoing = (
                    (projected * keep_float[..., None]).astype(jnp.bfloat16).reshape(lane_shape)
                )
            else:
                outgoing = jnp.zeros(lane_shape, jnp.bfloat16)
            return (result, outgoing)

        def remain(operands):
            return (operands[0], jnp.zeros(lane_shape, jnp.bfloat16))

        answer, sending = lax.cond(my_level == section_at, retreat, remain, (answer, returning))
        if need_send:
            send_at, take_at, rank_here = plans[section_at]
            routed = route_lanes(sending, take_at, send_at, total_slots)
            returning = passed_along(routed, "lvl", -1)
    return (solved[None], answer[None])


def solution(mesh):
    return jax.shard_map(
        local,
        mesh=mesh,
        in_specs=(
            P("lvl", "blk", None, None),
            P("lvl", "blk", None, None),
            P("lvl", "blk", None, None, None),
            P("lvl", "blk", None, None, None),
            P(),
            P(),
            P(),
        ),
        out_specs=(P("lvl", "blk", None, None), P("lvl", "blk", None, None)),
        check_vma=False,
    )
```

profile of v0, /device:TPU:1, one launch (start us, length us, event | category | flops | bytes accessed | tf_op | source)
XLA Modules:
  0.0 456.3 jit_solution(13668373669344162529)
XLA Ops:
  13.5 6.5 %scatter_fusion.4 = s32[32,4]{0,1:T(4,128)S(1)} fusion(s32[32,4]{0,1:T(4,128)S(1)} %broadcast.615.clone, s32[128]{0:T(128)S(1)} %reshape.1099, s32[128]{0:T(128)S(1)} %reshape.1057), kind=kCustom, calls=%fused_computation.25 | custom fusion | bytes 2560 | tf_op jit(solution)/shard_map/scatter | solution.py:24
  20.2 6.5 %scatter_fusion.2 = s32[32,4]{0,1:T(4,128)S(1)} fusion(s32[32,4]{0,1:T(4,128)S(1)} %broadcast.615.clone.1, s32[128]{0:T(128)S(1)} %reshape.1077, s32[128]{0:T(128)S(1)} %reshape.1057), kind=kCustom, calls=%fused_computation.22 | custom fusion | bytes 2560 | tf_op jit(solution)/shard_map/scatter | solution.py:24
  27.2 6.5 %scatter_fusion = s32[32,4]{0,1:T(4,128)S(1)} fusion(s32[32,4]{0,1:T(4,128)S(1)} %broadcast.615.clone.2, s32[128]{0:T(128)S(1)} %reshape.1055, s32[128]{0:T(128)S(1)} %reshape.1057), kind=kCustom, calls=%fused_computation.19 | custom fusion | bytes 2560 | tf_op jit(solution)/shard_map/scatter | solution.py:24
  43.1 9.7 %all-to-all-start = ((bf16[32,128,384]{2,1,0:T(8,128)(2,1)}), bf16[32,128,384]{2,1,0:T(8,128)(2,1)S(1)}, u32[]{:S(2)}, u32[]{:S(2)}) async-start(bf16[32,128,384]{2,1,0:T(8,128)(2,1)} %scatter_fusion.1), calls=%async_computation | async-start | bytes 6291456 | tf_op jit(solution)/shard_map/all_to_all | solution.py:59
  55.7 36.9 %all-to-all-done = bf16[32,128,384]{2,1,0:T(8,128)(2,1)S(1)} async-done(((bf16[32,128,384]{2,1,0:T(8,128)(2,1)}), bf16[32,128,384]{2,1,0:T(8,128)(2,1)S(1)}, u32[]{:S(2)}, u32[]{:S(2)}) %all-to-all-start) | async-done | bytes 3145760 | tf_op jit(solution)/shard_map/all_to_all | solution.py:59
  96.0 8.0 %collective-permute-done = bf16[4,128,384]{2,1,0:T(8,128)(2,1)S(1)} collective-permute-done((bf16[4,128,384]{2,1,0:T(8,128)(2,1)}, bf16[4,128,384]{2,1,0:T(8,128)(2,1)S(1)}, u32[]{:S(2)}, u32[]{:S(2)}) %collective-permute-start) | collective-permute-done | bytes 393248 | tf_op jit(solution)/shard_map/ppermute | solution.py:10
  108.5 5.0 %all-to-all-start.1 = ((bf16[32,128,384]{2,1,0:T(8,128)(2,1)}), bf16[32,128,384]{2,1,0:T(8,128)(2,1)S(1)}, u32[]{:S(2)}, u32[]{:S(2)}) async-start(bf16[32,128,384]{2,1,0:T(8,128)(2,1)} %scatter_fusion.3), calls=%async_computation.1 | async-start | bytes 6291456 | tf_op jit(solution)/shard_map/all_to_all | solution.py:59
  115.0 38.3 %all-to-all-done.1 = bf16[32,128,384]{2,1,0:T(8,128)(2,1)S(1)} async-done(((bf16[32,128,384]{2,1,0:T(8,128)(2,1)}), bf16[32,128,384]{2,1,0:T(8,128)(2,1)S(1)}, u32[]{:S(2)}, u32[]{:S(2)}) %all-to-all-start.1) | async-done | bytes 3145760 | tf_op jit(solution)/shard_map/all_to_all | solution.py:59
  154.6 9.6 %collective-permute-start.1 = (bf16[4,128,384]{2,1,0:T(8,128)(2,1)}, bf16[4,128,384]{2,1,0:T(8,128)(2,1)S(1)}, u32[]{:S(2)}, u32[]{:S(2)}) collective-permute-start(bf16[4,128,384]{2,1,0:T(8,128)(2,1)} %gather_fusion.9), channel_id=1, source_target_pairs={{0,1},{1,2},{2,3},{4,5},{5,6},{6,7},{8,9},{9,10},{10,11},{12,13},{... | collective-permute-start | bytes 1179656 | tf_op jit(solution)/shard_map/ppermute | solution.py:10
  164.9 7.7 %collective-permute-done.1 = bf16[4,128,384]{2,1,0:T(8,128)(2,1)S(1)} collective-permute-done((bf16[4,128,384]{2,1,0:T(8,128)(2,1)}, bf16[4,128,384]{2,1,0:T(8,128)(2,1)S(1)}, u32[]{:S(2)}, u32[]{:S(2)}) %collective-permute-start.1) | collective-permute-done | bytes 393248 | tf_op jit(solution)/shard_map/ppermute | solution.py:10
  177.3 5.4 %all-to-all-start.2 = ((bf16[32,128,384]{2,1,0:T(8,128)(2,1)}), bf16[32,128,384]{2,1,0:T(8,128)(2,1)S(1)}, u32[]{:S(2)}, u32[]{:S(2)}) async-start(bf16[32,128,384]{2,1,0:T(8,128)(2,1)} %scatter_fusion.5), calls=%async_computation.2 | async-start | bytes 6291456 | tf_op jit(solution)/shard_map/all_to_all | solution.py:59
  182.7 39.7 %all-to-all-done.2 = bf16[32,128,384]{2,1,0:T(8,128)(2,1)S(1)} async-done(((bf16[32,128,384]{2,1,0:T(8,128)(2,1)}), bf16[32,128,384]{2,1,0:T(8,128)(2,1)S(1)}, u32[]{:S(2)}, u32[]{:S(2)}) %all-to-all-start.2) | async-done | bytes 3145760 | tf_op jit(solution)/shard_map/all_to_all | solution.py:59
  223.8 4.0 collective-permute-start.2
  228.5 7.6 %collective-permute-done.2 = bf16[4,128,384]{2,1,0:T(8,128)(2,1)S(1)} collective-permute-done((bf16[4,128,384]{2,1,0:T(8,128)(2,1)}, bf16[4,128,384]{2,1,0:T(8,128)(2,1)S(1)}, u32[]{:S(2)}, u32[]{:S(2)}) %collective-permute-start.2) | collective-permute-done | bytes 393248 | tf_op jit(solution)/shard_map/ppermute | solution.py:10
  243.8 5.4 %all-to-all-start.3 = ((bf16[32,128,384]{2,1,0:T(8,128)(2,1)}), bf16[32,128,384]{2,1,0:T(8,128)(2,1)S(1)}, u32[]{:S(2)}, u32[]{:S(2)}) async-start(bf16[32,128,384]{2,1,0:T(8,128)(2,1)} %scatter_fusion.6), calls=%async_computation.3 | async-start | bytes 6291456 | tf_op jit(solution)/shard_map/all_to_all | solution.py:59
  249.2 39.7 %all-to-all-done.3 = bf16[32,128,384]{2,1,0:T(8,128)(2,1)S(1)} async-done(((bf16[32,128,384]{2,1,0:T(8,128)(2,1)}), bf16[32,128,384]{2,1,0:T(8,128)(2,1)S(1)}, u32[]{:S(2)}, u32[]{:S(2)}) %all-to-all-start.3) | async-done | bytes 3145760 | tf_op jit(solution)/shard_map/all_to_all | solution.py:59
  290.8 15.1 %collective-permute-done.3 = bf16[4,128,384]{2,1,0:T(8,128)(2,1)S(1)} collective-permute-done((bf16[4,128,384]{2,1,0:T(8,128)(2,1)S(1)}, bf16[4,128,384]{2,1,0:T(8,128)(2,1)S(1)}, u32[]{:S(2)}, u32[]{:S(2)}) %collective-permute-start.3) | collective-permute-done | bytes 393248 | tf_op jit(solution)/shard_map/ppermute | solution.py:10
  310.5 5.2 %all-to-all-start.4 = ((bf16[32,128,384]{2,1,0:T(8,128)(2,1)}), bf16[32,128,384]{2,1,0:T(8,128)(2,1)S(1)}, u32[]{:S(2)}, u32[]{:S(2)}) async-start(bf16[32,128,384]{2,1,0:T(8,128)(2,1)} %scatter_fusion.7), calls=%async_computation.4 | async-start | bytes 6291456 | tf_op jit(solution)/shard_map/all_to_all | solution.py:59
  315.7 39.7 %all-to-all-done.4 = bf16[32,128,384]{2,1,0:T(8,128)(2,1)S(1)} async-done(((bf16[32,128,384]{2,1,0:T(8,128)(2,1)}), bf16[32,128,384]{2,1,0:T(8,128)(2,1)S(1)}, u32[]{:S(2)}, u32[]{:S(2)}) %all-to-all-start.4) | async-done | bytes 3145760 | tf_op jit(solution)/shard_map/all_to_all | solution.py:59
  357.4 11.8 %collective-permute-done.4 = bf16[4,128,384]{2,1,0:T(8,128)(2,1)S(1)} collective-permute-done((bf16[4,128,384]{2,1,0:T(8,128)(2,1)S(1)}, bf16[4,128,384]{2,1,0:T(8,128)(2,1)S(1)}, u32[]{:S(2)}, u32[]{:S(2)}) %collective-permute-start.4) | collective-permute-done | bytes 393248 | tf_op jit(solution)/shard_map/ppermute | solution.py:10
  373.7 5.0 %all-to-all-start.5 = ((bf16[32,128,384]{2,1,0:T(8,128)(2,1)}), bf16[32,128,384]{2,1,0:T(8,128)(2,1)S(1)}, u32[]{:S(2)}, u32[]{:S(2)}) async-start(bf16[32,128,384]{2,1,0:T(8,128)(2,1)} %scatter_fusion.8), calls=%async_computation.5 | async-start | bytes 6291456 | tf_op jit(solution)/shard_map/all_to_all | solution.py:59
  378.8 39.7 %all-to-all-done.5 = bf16[32,128,384]{2,1,0:T(8,128)(2,1)S(1)} async-done(((bf16[32,128,384]{2,1,0:T(8,128)(2,1)}), bf16[32,128,384]{2,1,0:T(8,128)(2,1)S(1)}, u32[]{:S(2)}, u32[]{:S(2)}) %all-to-all-start.5) | async-done | bytes 3145760 | tf_op jit(solution)/shard_map/all_to_all | solution.py:59
  420.5 30.8 %collective-permute-done.5 = bf16[4,128,384]{2,1,0:T(8,128)(2,1)S(1)} collective-permute-done((bf16[4,128,384]{2,1,0:T(8,128)(2,1)S(1)}, bf16[4,128,384]{2,1,0:T(8,128)(2,1)S(1)}, u32[]{:S(2)}, u32[]{:S(2)}) %collective-permute-start.5) | collective-permute-done | bytes 393248 | tf_op jit(solution)/shard_map/ppermute | solution.py:10
  451.3 4.2 conditional.15
  (179 shorter events, 77.3 us)
Async XLA Ops:
  4.6 1.5 copy-start
  6.4 28.4 %copy-start.1 = (bf16[1,1,768,384]{2,3,1,0:T(8,128)(2,1)}, bf16[1,1,768,384]{2,3,1,0:T(8,128)(2,1)S(1)}, u32[]{:S(2)}) copy-start(bf16[1,1,768,384]{2,3,1,0:T(8,128)(2,1)S(1)} %copy.84) | copy-start | bytes 1769476
  27.1 7.6 %copy-start.9 = (bf16[1,1,768,768]{3,2,1,0:T(8,128)(2,1)S(1)}, bf16[1,1,768,768]{3,2,1,0:T(8,128)(2,1)}, u32[]{:S(2)}) copy-start(bf16[1,1,768,768]{3,2,1,0:T(8,128)(2,1)} %param.24) | copy-start | bytes 3538948
  27.2 7.6 %copy-start.13 = (bf16[1,1,4,768,128]{4,3,2,1,0:T(8,128)(2,1)S(1)}, bf16[1,1,4,768,128]{4,3,2,1,0:T(8,128)(2,1)}, u32[]{:S(2)}) copy-start(bf16[1,1,4,768,128]{4,3,2,1,0:T(8,128)(2,1)} %param.25) | copy-start | bytes 2359300
  43.1 9.9 %copy-start.4 = (s32[4,32,4]{1,2,0:T(4,128)S(1)}, s32[4,32,4]{1,2,0:T(4,128)}, u32[]{:S(2)}) copy-start(s32[4,32,4]{1,2,0:T(4,128)} %param.28) | copy-start | bytes 6148
  43.1 49.5 %all-to-all-start = ((bf16[32,128,384]{2,1,0:T(8,128)(2,1)}), bf16[32,128,384]{2,1,0:T(8,128)(2,1)S(1)}, u32[]{:S(2)}, u32[]{:S(2)}) async-start(bf16[32,128,384]{2,1,0:T(8,128)(2,1)} %scatter_fusion.1), calls=%async_computation | async-start | bytes 6291456 | tf_op jit(solution)/shard_map/all_to_all | solution.py:59
  94.0 10.0 %collective-permute-start = (bf16[4,128,384]{2,1,0:T(8,128)(2,1)}, bf16[4,128,384]{2,1,0:T(8,128)(2,1)S(1)}, u32[]{:S(2)}, u32[]{:S(2)}) collective-permute-start(bf16[4,128,384]{2,1,0:T(8,128)(2,1)} %gather_fusion.4), channel_id=1, source_target_pairs={{0,1},{1,2},{2,3},{4,5},{5,6},{6,7},{8,9},{9,10},{10,11},{12,13},{... | collective-permute-start | bytes 1179656 | tf_op jit(solution)/shard_map/ppermute | solution.py:10
  95.3 10.8 %copy-start.5 = (s32[4]{0:T(128)}, s32[4]{0:T(128)S(1)}, u32[]{:S(2)}) copy-start(s32[4]{0:T(128)S(1)} %fusion.117) | copy-start | bytes 52
  108.5 44.8 %all-to-all-start.1 = ((bf16[32,128,384]{2,1,0:T(8,128)(2,1)}), bf16[32,128,384]{2,1,0:T(8,128)(2,1)S(1)}, u32[]{:S(2)}, u32[]{:S(2)}) async-start(bf16[32,128,384]{2,1,0:T(8,128)(2,1)} %scatter_fusion.3), calls=%async_computation.1 | async-start | bytes 6291456 | tf_op jit(solution)/shard_map/all_to_all | solution.py:59
  154.6 17.9 %collective-permute-start.1 = (bf16[4,128,384]{2,1,0:T(8,128)(2,1)}, bf16[4,128,384]{2,1,0:T(8,128)(2,1)S(1)}, u32[]{:S(2)}, u32[]{:S(2)}) collective-permute-start(bf16[4,128,384]{2,1,0:T(8,128)(2,1)} %gather_fusion.9), channel_id=1, source_target_pairs={{0,1},{1,2},{2,3},{4,5},{5,6},{6,7},{8,9},{9,10},{10,11},{12,13},{... | collective-permute-start | bytes 1179656 | tf_op jit(solution)/shard_map/ppermute | solution.py:10
  177.3 45.2 %all-to-all-start.2 = ((bf16[32,128,384]{2,1,0:T(8,128)(2,1)}), bf16[32,128,384]{2,1,0:T(8,128)(2,1)S(1)}, u32[]{:S(2)}, u32[]{:S(2)}) async-start(bf16[32,128,384]{2,1,0:T(8,128)(2,1)} %scatter_fusion.5), calls=%async_computation.2 | async-start | bytes 6291456 | tf_op jit(solution)/shard_map/all_to_all | solution.py:59
  223.8 12.4 %collective-permute-start.2 = (bf16[4,128,384]{2,1,0:T(8,128)(2,1)}, bf16[4,128,384]{2,1,0:T(8,128)(2,1)S(1)}, u32[]{:S(2)}, u32[]{:S(2)}) collective-permute-start(bf16[4,128,384]{2,1,0:T(8,128)(2,1)} %gather_fusion.14), channel_id=1, source_target_pairs={{0,1},{1,2},{2,3},{4,5},{5,6},{6,7},{8,9},{9,10},{10,11},{12,13},{... | collective-permute-start | bytes 1179656 | tf_op jit(solution)/shard_map/ppermute | solution.py:10
  236.1 1.5 copy-start.17
  237.6 0.8 copy-start.2
  243.8 45.1 %all-to-all-start.3 = ((bf16[32,128,384]{2,1,0:T(8,128)(2,1)}), bf16[32,128,384]{2,1,0:T(8,128)(2,1)S(1)}, u32[]{:S(2)}, u32[]{:S(2)}) async-start(bf16[32,128,384]{2,1,0:T(8,128)(2,1)} %scatter_fusion.6), calls=%async_computation.3 | async-start | bytes 6291456 | tf_op jit(solution)/shard_map/all_to_all | solution.py:59
  289.5 16.4 %collective-permute-start.3 = (bf16[4,128,384]{2,1,0:T(8,128)(2,1)S(1)}, bf16[4,128,384]{2,1,0:T(8,128)(2,1)S(1)}, u32[]{:S(2)}, u32[]{:S(2)}) collective-permute-start(bf16[4,128,384]{2,1,0:T(8,128)(2,1)S(1)} %gather_fusion.15), channel_id=1, source_target_pairs={{1,0},{2,1},{3,2},{5,4},{6,5},{7,6},{9,8},{10,9},{11,10},{13,12},{... | collective-permute-start | bytes 1179656 | tf_op jit(solution)/shard_map/ppermute | solution.py:10
  310.5 5.2 %copy-start.6 = (s32[4]{0:T(128)S(1)}, s32[4]{0:T(128)}, u32[]{:S(2)}) copy-start(s32[4]{0:T(128)} %copy-done.5) | copy-start | bytes 52
  310.5 44.9 %all-to-all-start.4 = ((bf16[32,128,384]{2,1,0:T(8,128)(2,1)}), bf16[32,128,384]{2,1,0:T(8,128)(2,1)S(1)}, u32[]{:S(2)}, u32[]{:S(2)}) async-start(bf16[32,128,384]{2,1,0:T(8,128)(2,1)} %scatter_fusion.7), calls=%async_computation.4 | async-start | bytes 6291456 | tf_op jit(solution)/shard_map/all_to_all | solution.py:59
  356.1 13.1 %collective-permute-start.4 = (bf16[4,128,384]{2,1,0:T(8,128)(2,1)S(1)}, bf16[4,128,384]{2,1,0:T(8,128)(2,1)S(1)}, u32[]{:S(2)}, u32[]{:S(2)}) collective-permute-start(bf16[4,128,384]{2,1,0:T(8,128)(2,1)S(1)} %gather_fusion.16), channel_id=1, source_target_pairs={{1,0},{2,1},{3,2},{5,4},{6,5},{7,6},{9,8},{10,9},{11,10},{13,12},{... | collective-permute-start | bytes 1179656 | tf_op jit(solution)/shard_map/ppermute | solution.py:10
  373.7 44.8 %all-to-all-start.5 = ((bf16[32,128,384]{2,1,0:T(8,128)(2,1)}), bf16[32,128,384]{2,1,0:T(8,128)(2,1)S(1)}, u32[]{:S(2)}, u32[]{:S(2)}) async-start(bf16[32,128,384]{2,1,0:T(8,128)(2,1)} %scatter_fusion.8), calls=%async_computation.5 | async-start | bytes 6291456 | tf_op jit(solution)/shard_map/all_to_all | solution.py:59
  419.2 32.1 %collective-permute-start.5 = (bf16[4,128,384]{2,1,0:T(8,128)(2,1)S(1)}, bf16[4,128,384]{2,1,0:T(8,128)(2,1)S(1)}, u32[]{:S(2)}, u32[]{:S(2)}) collective-permute-start(bf16[4,128,384]{2,1,0:T(8,128)(2,1)S(1)} %gather_fusion.17), channel_id=1, source_target_pairs={{1,0},{2,1},{3,2},{5,4},{6,5},{7,6},{9,8},{10,9},{11,10},{13,12},{... | collective-permute-start | bytes 1179656 | tf_op jit(solution)/shard_map/ppermute | solution.py:10
  451.3 1.5 copy-start.12
  455.5 0.8 copy-start.3
where the time goes:
time: 458 us; the launch traced here: 456 us
  waiting for transfers between devices  315 us (69%)
  local copies, waits for them, and re-layouts  74.9 us (16%)
  starting transfers between devices  54.5 us (12%)
  matrix products  6 us (1%)
    all_to_all x6, waiting for transfers between devices, route_lanes(): lax.all_to_all(holder, 'blk', split_axis=0, concat_axis=0, tiled=True)  234 us
    ppermute x6, waiting for transfers between devices, passed_along(): return lax.ppermute(array, axis, pairs)  81 us
    all_to_all x6, starting transfers between devices, route_lanes(): lax.all_to_all(holder, 'blk', split_axis=0, concat_axis=0, tiled=True)  35.7 us
    scatter x3, local copies, waits for them, and re-layouts, level_maps(): jnp.zeros(src_pos.shape, jnp.int32).at[src_pos, columns].set(targets)  19.4 us
    ppermute x6, starting transfers between devices, passed_along(): return lax.ppermute(array, axis, pairs)  18.8 us
    another operation x16, local copies, waits for them, and re-layouts  15.1 us
    scatter x6, local copies, waits for them, and re-layouts, route_lanes(): jnp.zeros((total_slots,) + values.shape[1:], values.dtype).at[send_at]  14.2 us
  transfers between devices with their start and end apart: 12, of which 12 were waited for; matrix products, arithmetic and copies ran while one was open for 1% of the time, Pallas kernels for 0%

commit v1 on v0

v1 whole, which is shorter than its diff:
```python
import jax
import jax.numpy as jnp
from jax import lax
from jax.sharding import PartitionSpec as P


def routing_tables(sources, owner, ranks):
    level_count, block_count = owner.shape
    position = jnp.arange(block_count, dtype=jnp.int32)
    tables = [None]
    for t in range(1, level_count):
        at_pos = (owner[t][None, :] == position[:, None]).astype(jnp.int32)
        src_block = jnp.sum(at_pos[:, :, None] * sources[t][None, :, :], axis=1)
        rank_pos = jnp.sum(at_pos[:, :, None] * ranks[t][None, :, :], axis=1)
        pick = (src_block[:, :, None] == position[None, None, :]).astype(jnp.int32)
        src_pos = jnp.sum(pick * owner[t - 1][None, None, :], axis=2)
        hit = (src_pos[:, None, :] == position[None, :, None]).astype(jnp.int32)
        target_of = jnp.sum(hit * position[:, None, None], axis=0)
        tables.append((src_pos, rank_pos, target_of))
    return tables


def mine(table, me):
    block_count = table.shape[0]
    row = (jnp.arange(block_count, dtype=jnp.int32) == me).astype(jnp.int32)
    return jnp.sum(row[:, None] * table, axis=0)


def one_hot(index, count, dtype):
    return (index[:, None] == jnp.arange(count, dtype=jnp.int32)[None, :]).astype(dtype)


def spread(out, src_row, row_count, my_row):
    width = out.shape[-1] // row_count
    piece = None
    for r in range(row_count):
        part = out[..., r * width:(r + 1) * width]
        if r == src_row:
            got = jnp.where(my_row == r, part, jnp.zeros_like(part))
        else:
            got = lax.ppermute(part, "lvl", [(src_row, r)])
        piece = got if piece is None else piece + got
    return piece


def collect(routed, dst_row, row_count):
    parts = []
    for r in range(row_count):
        if r == dst_row:
            parts.append(routed)
        else:
            parts.append(lax.ppermute(routed, "lvl", [(r, dst_row)]))
    return jnp.concatenate(parts, axis=-1)


def route(piece, send_to, take_from, block_count):
    send = one_hot(send_to, block_count, piece.dtype)
    holder = jnp.einsum("kj,krn->jrn", send, piece, preferred_element_type=jnp.float32)
    holder = holder.astype(piece.dtype)
    arrived = lax.all_to_all(holder, "blk", split_axis=0, concat_axis=0, tiled=True)
    take = one_hot(take_from, block_count, piece.dtype)
    routed = jnp.einsum("kj,jrn->krn", take, arrived, preferred_element_type=jnp.float32)
    return routed.astype(piece.dtype)


def local(rhs, inverse, left_factors, right_factors, sources, ranks, owner):
    assert rhs.shape[1] == 1
    level_count = sources.shape[0]
    block_count = owner.shape[1]
    row_count = lax.axis_size("lvl")
    rank_width = left_factors.shape[4]
    rhs_here = rhs[0, 0]
    inverse_here = inverse[0, 0]
    left_here = left_factors[0, 0]
    right_here = right_factors[0, 0]
    my_row = lax.axis_index("lvl")
    me = lax.axis_index("blk")
    tables = routing_tables(sources, owner, ranks)
    mine_src = [None] + [mine(tables[t][0], me) for t in range(1, level_count)]
    mine_rank = [None] + [mine(tables[t][1], me) for t in range(1, level_count)]
    mine_target = [None] + [mine(tables[t][2], me) for t in range(1, level_count)]
    lanes = jnp.arange(rank_width, dtype=jnp.int32)

    def keep_of(t):
        return (lanes[None, :] < mine_rank[t][:, None]).astype(jnp.float32)

    solved = jnp.zeros(rhs_here.shape, jnp.bfloat16)
    incoming = None
    for t in range(level_count):
        current = rhs_here.astype(jnp.float32)
        if t > 0:
            masked = incoming * keep_of(t)[..., None].astype(jnp.bfloat16)
            current = current - jnp.einsum(
                "kbr,krn->bn", left_here, masked, preferred_element_type=jnp.float32
            )
        lowered = current.astype(jnp.bfloat16)
        result = jnp.einsum(
            "ab,bn->an", inverse_here, lowered, preferred_element_type=jnp.float32
        ).astype(jnp.bfloat16)
        solved = jnp.where(my_row == t, result, solved)
        if t + 1 < level_count:
            out = jnp.einsum(
                "kbr,bn->krn", right_here, result, preferred_element_type=jnp.float32
            ).astype(jnp.bfloat16)
            piece = spread(out, t, row_count, my_row)
            routed = route(piece, mine_target[t + 1], mine_src[t + 1], block_count)
            incoming = collect(routed, t + 1, row_count)

    answer = jnp.zeros(rhs_here.shape, jnp.bfloat16)
    returning = None
    for t in reversed(range(level_count)):
        current = solved.astype(jnp.float32)
        if t + 1 < level_count:
            current = current - jnp.einsum(
                "kbr,krn->bn", right_here, returning, preferred_element_type=jnp.float32
            )
        upper = current.astype(jnp.bfloat16)
        result = jnp.einsum(
            "ba,bn->an", inverse_here, upper, preferred_element_type=jnp.float32
        ).astype(jnp.bfloat16)
        answer = jnp.where(my_row == t, result, answer)
        if t > 0:
            projected = jnp.einsum(
                "kbr,bn->krn", left_here, result, preferred_element_type=jnp.float32
            )
            out = (projected * keep_of(t)[..., None]).astype(jnp.bfloat16)
            piece = spread(out, t, row_count, my_row)
            routed = route(piece, mine_src[t], mine_target[t], block_count)
            returning = collect(routed, t - 1, row_count)
    return (solved[None, None], answer[None, None])


def solution(mesh):
    return jax.shard_map(
        local,
        mesh=mesh,
        in_specs=(
            P("lvl", "blk", None, None),
            P("lvl", "blk", None, None),
            P("lvl", "blk", None, None, None),
            P("lvl", "blk", None, None, None),
            P(),
            P(),
            P(),
        ),
        out_specs=(P("lvl", "blk", None, None), P("lvl", "blk", None, None)),
        check_vma=False,
    )
```

time: 458 us -> 260 us (0.57)
  waiting for transfers between devices: 315 us -> 45.2 us
  blocking collectives: 0 us -> 119 us
  local copies, waits for them, and re-layouts: 74.9 us -> 5.13 us
  matrix products: 6 us -> 31.9 us
    all_to_all x6 -> x0, waiting for transfers between devices: 234 us -> none  [route_lanes(): lax.all_to_all(holder, 'blk', split_axis=0, concat_axis=0, tiled=True)]
    all_to_all x0 -> x6, blocking collectives: none -> 119 us  [route(): lax.all_to_all(holder, 'blk', split_axis=0, concat_axis=0, tiled=True)]
    ppermute x6 -> x36, waiting for transfers between devices: 81 us -> 45.2 us  [the longest x18 31.8 us: spread(): got = lax.ppermute(part, 'lvl', [(src_row, r)])]
    all_to_all x6 -> x0, starting transfers between devices: 35.7 us -> none  [route_lanes(): lax.all_to_all(holder, 'blk', split_axis=0, concat_axis=0, tiled=True)]
    scatter x12 -> x0, local copies, waits for them, and re-layouts: 35.6 us -> none  [the longest x3 19.4 us: level_maps(): jnp.zeros(src_pos.shape, jnp.int32).at[src_pos, columns].set(targets)]
    ppermute x6 -> x36, starting transfers between devices: 18.8 us -> 51.9 us  [the longest x18 31.4 us: collect(): parts.append(lax.ppermute(routed, 'lvl', [(r, dst_row)]))]
    dot_general x3 -> x26, matrix products: 6 us -> 31.9 us  [the longest x4 10.3 us: local(): jnp.einsum('ab,bn->an', inverse_here, lowered, preferred_element_type=jnp...]
    gather x33 -> x0, local copies, waits for them, and re-layouts: 16.3 us -> none  [the longest x6 5.91 us: route_lanes(): return arrived[take_at]]
  transfers between devices with their start and end apart: 12 -> 36, of which waited for: 12 -> 13; matrix products, arithmetic and copies ran while one was open for 1% -> 1% of each run, Pallas kernels for 0% -> 0%
where the time goes in v1:
time: 260 us; the launch traced here: 258 us
  blocking collectives  119 us (46%)
  starting transfers between devices  51.9 us (20%)
  waiting for transfers between devices  45.2 us (17%)
  matrix products  31.9 us (12%)
  local copies, waits for them, and re-layouts  5.13 us (2%)
  other arithmetic  4.04 us (2%)
    all_to_all x6, blocking collectives, route(): lax.all_to_all(holder, 'blk', split_axis=0, concat_axis=0, tiled=True)  119 us
    ppermute x18, waiting for transfers between devices, spread(): got = lax.ppermute(part, 'lvl', [(src_row, r)])  31.8 us
    ppermute x18, starting transfers between devices, collect(): parts.append(lax.ppermute(routed, 'lvl', [(r, dst_row)]))  31.4 us
    ppermute x18, starting transfers between devices, spread(): got = lax.ppermute(part, 'lvl', [(src_row, r)])  20.5 us
    ppermute x18, waiting for transfers between devices, collect(): parts.append(lax.ppermute(routed, 'lvl', [(r, dst_row)]))  13.3 us
    dot_general x4, matrix products, local(): jnp.einsum('ab,bn->an', inverse_here, lowered, preferred_element_type=jnp...  10.3 us
    dot_general x4, matrix products, local(): jnp.einsum('ba,bn->an', inverse_here, upper, preferred_element_type=jnp.f...  10.2 us
  transfers between devices with their start and end apart: 36, of which 13 were waited for; matrix products, arithmetic and copies ran while one was open for 1% of the time, Pallas kernels for 0%

profile of v1, /device:TPU:1, one launch (start us, length us, event | category | flops | bytes accessed | tf_op | source)
XLA Modules:
  0.0 258.4 jit_solution(17651390096238394250)
XLA Ops:
  4.6 3.9 %collective-permute-start = (bf16[4,128,96]{1,2,0:T(8,128)(2,1)S(1)}, bf16[4,128,96]{1,2,0:T(8,128)(2,1)S(1)}, u32[]{:S(2)}, u32[]{:S(2)}) collective-permute-start(bf16[4,128,96]{1,2,0:T(8,128)(2,1)S(1)} %get-tuple-element.38), channel_id=1, source_target_pairs={{0,1},{4,5},{8,9},{12,13},{16,17},{20,21},{24,25},{28,29},{32,33},... | collective-permute-start | bytes 294920 | tf_op jit(solution)/shard_map/ppermute | solution.py:41
  14.9 23.4 %all_to_all.30 = bf16[32,128,96]{1,2,0:T(8,128)(2,1)S(1)} all-to-all(bf16[32,128,96]{1,2,0:T(8,128)(2,1)S(1)} %copy.44), channel_id=1, replica_groups=mesh['blk'=32,'lvl'=4] {'blk'}, dimensions={0} | all-to-all | bytes 1572864 | tf_op jit(solution)/shard_map/all_to_all | solution.py:60
  42.8 3.1 %convolution_convert_fusion.12 = bf16[384,768]{0,1:T(8,128)(2,1)} fusion(bf16[1,1,768,768]{3,2,1,0:T(8,128)(2,1)S(1)} %copy-done, bf16[1,1,4,768,128]{4,3,2,1,0:T(8,128)(2,1)} %param.9, bf16[1,1,768,384]{2,3,1,0:T(8,128)(2,1)S(1)} %copy.41, bf16[4,128,384]{1,0,2:T(4,128)(2,1)S(1)} %maximum_multiply_fusion), kind=kOutput, calls=%fused_computation.30 | convolution fusion | flops 756154368 | bytes 3538944 | tf_op jit(solution)/shard_map/ab,bn->an/dot_general | solution.py:97
  50.2 7.4 %collective-permute-done.6 = bf16[4,128,96]{1,2,0:T(8,128)(2,1)S(1)} collective-permute-done((bf16[4,128,96]{1,2,0:T(8,128)(2,1)S(1)}, bf16[4,128,96]{1,2,0:T(8,128)(2,1)S(1)}, u32[]{:S(2)}, u32[]{:S(2)}) %collective-permute-start.6) | collective-permute-done | bytes 98336 | tf_op jit(solution)/shard_map/ppermute | solution.py:41
  58.5 18.3 %all_to_all.31 = bf16[32,128,96]{1,2,0:T(8,128)(2,1)S(1)} all-to-all(bf16[32,128,96]{1,2,0:T(8,128)(2,1)S(1)} %copy.50), channel_id=1, replica_groups=mesh['blk'=32,'lvl'=4] {'blk'}, dimensions={0} | all-to-all | bytes 1572864 | tf_op jit(solution)/shard_map/all_to_all | solution.py:60
  78.4 6.2 %collective-permute-start.9 = (bf16[4,128,96]{1,0,2:T(4,128)(2,1)S(1)}, bf16[4,128,96]{1,0,2:T(4,128)(2,1)S(1)}, u32[]{:S(2)}, u32[]{:S(2)}) collective-permute-start(bf16[4,128,96]{1,0,2:T(4,128)(2,1)S(1)} %convolution_convert_fusion.21), channel_id=1, source_target_pairs={{0,2},{4,6},{8,10},{12,14},{16,18},{20,22},{24,26},{28,30},{32,34}... | collective-permute-start | bytes 294920 | tf_op jit(solution)/shard_map/ppermute | solution.py:52
  93.7 4.3 %collective-permute-done.12 = bf16[4,128,96]{1,2,0:T(8,128)(2,1)S(1)} collective-permute-done((bf16[4,128,96]{1,2,0:T(8,128)(2,1)S(1)}, bf16[4,128,96]{1,2,0:T(8,128)(2,1)S(1)}, u32[]{:S(2)}, u32[]{:S(2)}) %collective-permute-start.12) | collective-permute-done | bytes 98336 | tf_op jit(solution)/shard_map/ppermute | solution.py:41
  98.9 19.8 %all_to_all.32 = bf16[32,128,96]{1,2,0:T(8,128)(2,1)S(1)} all-to-all(bf16[32,128,96]{1,2,0:T(8,128)(2,1)S(1)} %copy.56), channel_id=1, replica_groups=mesh['blk'=32,'lvl'=4] {'blk'}, dimensions={0} | all-to-all | bytes 1572864 | tf_op jit(solution)/shard_map/all_to_all | solution.py:60
  119.0 4.3 %collective-permute-start.15 = (bf16[4,128,96]{1,0,2:T(4,128)(2,1)S(1)}, bf16[4,128,96]{1,0,2:T(4,128)(2,1)S(1)}, u32[]{:S(2)}, u32[]{:S(2)}) collective-permute-start(bf16[4,128,96]{1,0,2:T(4,128)(2,1)S(1)} %convolution_convert_fusion.20), channel_id=1, source_target_pairs={{0,3},{4,7},{8,11},{12,15},{16,19},{20,23},{24,27},{28,31},{32,35}... | collective-permute-start | bytes 294920 | tf_op jit(solution)/shard_map/ppermute | solution.py:52
  125.9 3.4 %fusion.10 = bf16[768,384]{1,0:T(8,128)(2,1)} fusion(bf16[1,1,768,768]{3,2,1,0:T(8,128)(2,1)S(1)} %copy-done, bf16[1,1,4,768,128]{4,3,2,1,0:T(8,128)(2,1)S(1)} %copy-done.6, bf16[384,768]{0,1:T(8,128)(2,1)} %convolution_convert_fusion.12, bf16[384,768]{0,1:T(8,128)(2,1)} %convolution_convert_fusion.11, bf16[1,1,768,384]{2,3,1,0:T(8,128)(2,1)S(1)} %copy.41, ...), kind=kOutput, calls=%fused_computation.39 | convolution fusion | flops 757334016 | bytes 5308420 | tf_op jit(solution)/shard_map/ab,bn->an/dot_general | solution.py:97
  134.2 6.0 %collective-permute-done.18 = bf16[4,128,96]{1,2,0:T(8,128)(2,1)S(1)} collective-permute-done((bf16[4,128,96]{1,2,0:T(8,128)(2,1)S(1)}, bf16[4,128,96]{1,2,0:T(8,128)(2,1)S(1)}, u32[]{:S(2)}, u32[]{:S(2)}) %collective-permute-start.18) | collective-permute-done | bytes 98336 | tf_op jit(solution)/shard_map/ppermute | solution.py:41
  141.0 19.5 %all_to_all.33 = bf16[32,128,96]{1,2,0:T(8,128)(2,1)S(1)} all-to-all(bf16[32,128,96]{1,2,0:T(8,128)(2,1)S(1)} %copy.61), channel_id=1, replica_groups=mesh['blk'=32,'lvl'=4] {'blk'}, dimensions={0} | all-to-all | bytes 1572864 | tf_op jit(solution)/shard_map/all_to_all | solution.py:60
  160.8 6.0 %collective-permute-start.21 = (bf16[4,128,96]{1,0,2:T(4,128)(2,1)S(1)}, bf16[4,128,96]{1,0,2:T(4,128)(2,1)S(1)}, u32[]{:S(2)}, u32[]{:S(2)}) collective-permute-start(bf16[4,128,96]{1,0,2:T(4,128)(2,1)S(1)} %convolution_convert_fusion.19), channel_id=1, source_target_pairs={{0,2},{4,6},{8,10},{12,14},{16,18},{20,22},{24,26},{28,30},{32,34}... | collective-permute-start | bytes 294920 | tf_op jit(solution)/shard_map/ppermute | solution.py:52
  169.4 2.7 %convolution_convert_fusion.8 = bf16[384,768]{1,0:T(8,128)(2,1)S(1)} fusion(bf16[768,384]{1,0:T(8,128)(2,1)} %fusion.10, bf16[1,1,768,768]{3,2,1,0:T(8,128)(2,1)S(1)} %copy-done, bf16[1,1,4,768,128]{4,3,2,1,0:T(8,128)(2,1)} %param.10, bf16[4,128,384]{1,0,2:T(4,128)(2,1)S(1)} %pad_maximum_fusion), kind=kOutput, calls=%fused_computation.26 | convolution fusion | flops 756154368 | bytes 3538944 | tf_op jit(solution)/shard_map/ba,bn->an/dot_general | solution.py:118
  175.6 6.7 %collective-permute-done.24 = bf16[4,128,96]{1,2,0:T(8,128)(2,1)S(1)} collective-permute-done((bf16[4,128,96]{1,2,0:T(8,128)(2,1)S(1)}, bf16[4,128,96]{1,2,0:T(8,128)(2,1)S(1)}, u32[]{:S(2)}, u32[]{:S(2)}) %collective-permute-start.24) | collective-permute-done | bytes 98336 | tf_op jit(solution)/shard_map/ppermute | solution.py:41
  183.2 18.8 %all_to_all.34 = bf16[32,128,96]{1,2,0:T(8,128)(2,1)S(1)} all-to-all(bf16[32,128,96]{1,2,0:T(8,128)(2,1)S(1)} %copy.66), channel_id=1, replica_groups=mesh['blk'=32,'lvl'=4] {'blk'}, dimensions={0} | all-to-all | bytes 1572864 | tf_op jit(solution)/shard_map/all_to_all | solution.py:60
  202.2 2.9 %collective-permute-start.27 = (bf16[4,128,96]{1,0,2:T(4,128)(2,1)S(1)}, bf16[4,128,96]{1,0,2:T(4,128)(2,1)S(1)}, u32[]{:S(2)}, u32[]{:S(2)}) collective-permute-start(bf16[4,128,96]{1,0,2:T(4,128)(2,1)S(1)} %convolution_convert_fusion.18), channel_id=1, source_target_pairs={{0,1},{4,5},{8,9},{12,13},{16,17},{20,21},{24,25},{28,29},{32,33},... | collective-permute-start | bytes 294920 | tf_op jit(solution)/shard_map/ppermute | solution.py:52
  207.7 3.3 %convolution_convert_fusion.7 = bf16[384,768]{1,0:T(8,128)(2,1)} fusion(bf16[768,384]{1,0:T(8,128)(2,1)} %fusion.10, bf16[1,1,768,768]{3,2,1,0:T(8,128)(2,1)S(1)} %copy-done, bf16[1,1,4,768,128]{4,3,2,1,0:T(8,128)(2,1)S(1)} %copy-done.9, bf16[4,128,384]{1,0,2:T(4,128)(2,1)S(1)} %pad_maximum_fusion.1), kind=kOutput, calls=%fused_computation.25 | convolution fusion | flops 756154368 | bytes 3538944 | tf_op jit(solution)/shard_map/ba,bn->an/dot_general | solution.py:118
  215.2 7.4 %collective-permute-done.30 = bf16[4,128,96]{1,2,0:T(8,128)(2,1)S(1)} collective-permute-done((bf16[4,128,96]{1,2,0:T(8,128)(2,1)S(1)}, bf16[4,128,96]{1,2,0:T(8,128)(2,1)S(1)}, u32[]{:S(2)}, u32[]{:S(2)}) %collective-permute-start.30) | collective-permute-done | bytes 98336 | tf_op jit(solution)/shard_map/ppermute | solution.py:41
  223.5 19.1 %all_to_all.35 = bf16[32,128,96]{1,2,0:T(8,128)(2,1)S(1)} all-to-all(bf16[32,128,96]{1,2,0:T(8,128)(2,1)S(1)} %copy.71), channel_id=1, replica_groups=mesh['blk'=32,'lvl'=4] {'blk'}, dimensions={0} | all-to-all | bytes 1572864 | tf_op jit(solution)/shard_map/all_to_all | solution.py:60
  246.8 2.5 collective-permute-done.33
  249.3 2.8 %collective-permute-done.34 = bf16[4,128,96]{1,0,2:T(4,128)(2,1)S(1)} collective-permute-done((bf16[4,128,96]{1,0,2:T(4,128)(2,1)S(1)}, bf16[4,128,96]{1,0,2:T(4,128)(2,1)S(1)}, u32[]{:S(2)}, u32[]{:S(2)}) %collective-permute-start.34) | collective-permute-done | bytes 98336 | tf_op jit(solution)/shard_map/ppermute | solution.py:52
  252.1 2.4 collective-permute-done.35
  254.8 2.5 fusion.12
  (153 shorter events, 60.4 us)
Async XLA Ops:
  4.6 9.4 %collective-permute-start = (bf16[4,128,96]{1,2,0:T(8,128)(2,1)S(1)}, bf16[4,128,96]{1,2,0:T(8,128)(2,1)S(1)}, u32[]{:S(2)}, u32[]{:S(2)}) collective-permute-start(bf16[4,128,96]{1,2,0:T(8,128)(2,1)S(1)} %get-tuple-element.38), channel_id=1, source_target_pairs={{0,1},{4,5},{8,9},{12,13},{16,17},{20,21},{24,25},{28,29},{32,33},... | collective-permute-start | bytes 294920 | tf_op jit(solution)/shard_map/ppermute | solution.py:41
  8.5 5.5 %collective-permute-start.1 = (bf16[4,128,96]{1,2,0:T(8,128)(2,1)S(1)}, bf16[4,128,96]{1,2,0:T(8,128)(2,1)S(1)}, u32[]{:S(2)}, u32[]{:S(2)}) collective-permute-start(bf16[4,128,96]{1,2,0:T(8,128)(2,1)S(1)} %get-tuple-element.40), channel_id=1, source_target_pairs={{0,2},{4,6},{8,10},{12,14},{16,18},{20,22},{24,26},{28,30},{32,34}... | collective-permute-start | bytes 294920 | tf_op jit(solution)/shard_map/ppermute | solution.py:41
  47.6 10.1 %collective-permute-start.6 = (bf16[4,128,96]{1,2,0:T(8,128)(2,1)S(1)}, bf16[4,128,96]{1,2,0:T(8,128)(2,1)S(1)}, u32[]{:S(2)}, u32[]{:S(2)}) collective-permute-start(bf16[4,128,96]{1,2,0:T(8,128)(2,1)S(1)} %get-tuple-element.35), channel_id=1, source_target_pairs={{1,0},{5,4},{9,8},{13,12},{17,16},{21,20},{25,24},{29,28},{33,32},... | collective-permute-start | bytes 294920 | tf_op jit(solution)/shard_map/ppermute | solution.py:41
  48.9 8.8 %collective-permute-start.7 = (bf16[4,128,96]{1,2,0:T(8,128)(2,1)S(1)}, bf16[4,128,96]{1,2,0:T(8,128)(2,1)S(1)}, u32[]{:S(2)}, u32[]{:S(2)}) collective-permute-start(bf16[4,128,96]{1,2,0:T(8,128)(2,1)S(1)} %get-tuple-element.37), channel_id=1, source_target_pairs={{1,2},{5,6},{9,10},{13,14},{17,18},{21,22},{25,26},{29,30},{33,34}... | collective-permute-start | bytes 294920 | tf_op jit(solution)/shard_map/ppermute | solution.py:41
  49.5 8.1 %collective-permute-start.8 = (bf16[4,128,96]{1,2,0:T(8,128)(2,1)S(1)}, bf16[4,128,96]{1,2,0:T(8,128)(2,1)S(1)}, u32[]{:S(2)}, u32[]{:S(2)}) collective-permute-start(bf16[4,128,96]{1,2,0:T(8,128)(2,1)S(1)} %get-tuple-element.36), channel_id=1, source_target_pairs={{1,3},{5,7},{9,11},{13,15},{17,19},{21,23},{25,27},{29,31},{33,35}... | collective-permute-start | bytes 294920 | tf_op jit(solution)/shard_map/ppermute | solution.py:41
  77.1 7.7 %collective-permute-start.10 = (bf16[4,128,96]{1,0,2:T(4,128)(2,1)S(1)}, bf16[4,128,96]{1,0,2:T(4,128)(2,1)S(1)}, u32[]{:S(2)}, u32[]{:S(2)}) collective-permute-start(bf16[4,128,96]{1,0,2:T(4,128)(2,1)S(1)} %convolution_convert_fusion.21), channel_id=1, source_target_pairs={{1,2},{5,6},{9,10},{13,14},{17,18},{21,22},{25,26},{29,30},{33,34}... | collective-permute-start | bytes 294920 | tf_op jit(solution)/shard_map/ppermute | solution.py:52
  77.8 7.0 %collective-permute-start.11 = (bf16[4,128,96]{1,0,2:T(4,128)(2,1)S(1)}, bf16[4,128,96]{1,0,2:T(4,128)(2,1)S(1)}, u32[]{:S(2)}, u32[]{:S(2)}) collective-permute-start(bf16[4,128,96]{1,0,2:T(4,128)(2,1)S(1)} %convolution_convert_fusion.21), channel_id=1, source_target_pairs={{3,2},{7,6},{11,10},{15,14},{19,18},{23,22},{27,26},{31,30},{35,34... | collective-permute-start | bytes 294920 | tf_op jit(solution)/shard_map/ppermute | solution.py:52
  78.4 8.5 %collective-permute-start.9 = (bf16[4,128,96]{1,0,2:T(4,128)(2,1)S(1)}, bf16[4,128,96]{1,0,2:T(4,128)(2,1)S(1)}, u32[]{:S(2)}, u32[]{:S(2)}) collective-permute-start(bf16[4,128,96]{1,0,2:T(4,128)(2,1)S(1)} %convolution_convert_fusion.21), channel_id=1, source_target_pairs={{0,2},{4,6},{8,10},{12,14},{16,18},{20,22},{24,26},{28,30},{32,34}... | collective-permute-start | bytes 294920 | tf_op jit(solution)/shard_map/ppermute | solution.py:52
  91.1 7.0 %collective-permute-start.12 = (bf16[4,128,96]{1,2,0:T(8,128)(2,1)S(1)}, bf16[4,128,96]{1,2,0:T(8,128)(2,1)S(1)}, u32[]{:S(2)}, u32[]{:S(2)}) collective-permute-start(bf16[4,128,96]{1,2,0:T(8,128)(2,1)S(1)} %get-tuple-element.34), channel_id=1, source_target_pairs={{2,0},{6,4},{10,8},{14,12},{18,16},{22,20},{26,24},{30,28},{34,32}... | collective-permute-start | bytes 294920 | tf_op jit(solution)/shard_map/ppermute | solution.py:41
  92.4 5.7 %collective-permute-start.13 = (bf16[4,128,96]{1,2,0:T(8,128)(2,1)S(1)}, bf16[4,128,96]{1,2,0:T(8,128)(2,1)S(1)}, u32[]{:S(2)}, u32[]{:S(2)}) collective-permute-start(bf16[4,128,96]{1,2,0:T(8,128)(2,1)S(1)} %get-tuple-element.32), channel_id=1, source_target_pairs={{2,1},{6,5},{10,9},{14,13},{18,17},{22,21},{26,25},{30,29},{34,33}... | collective-permute-start | bytes 294920 | tf_op jit(solution)/shard_map/ppermute | solution.py:41
  119.0 6.5 %collective-permute-start.15 = (bf16[4,128,96]{1,0,2:T(4,128)(2,1)S(1)}, bf16[4,128,96]{1,0,2:T(4,128)(2,1)S(1)}, u32[]{:S(2)}, u32[]{:S(2)}) collective-permute-start(bf16[4,128,96]{1,0,2:T(4,128)(2,1)S(1)} %convolution_convert_fusion.20), channel_id=1, source_target_pairs={{0,3},{4,7},{8,11},{12,15},{16,19},{20,23},{24,27},{28,31},{32,35}... | collective-permute-start | bytes 294920 | tf_op jit(solution)/shard_map/ppermute | solution.py:52
  131.6 8.6 %collective-permute-start.18 = (bf16[4,128,96]{1,2,0:T(8,128)(2,1)S(1)}, bf16[4,128,96]{1,2,0:T(8,128)(2,1)S(1)}, u32[]{:S(2)}, u32[]{:S(2)}) collective-permute-start(bf16[4,128,96]{1,2,0:T(8,128)(2,1)S(1)} %get-tuple-element.31), channel_id=1, source_target_pairs={{3,0},{7,4},{11,8},{15,12},{19,16},{23,20},{27,24},{31,28},{35,32}... | collective-permute-start | bytes 294920 | tf_op jit(solution)/shard_map/ppermute | solution.py:41
  132.9 7.3 %collective-permute-start.19 = (bf16[4,128,96]{1,2,0:T(8,128)(2,1)S(1)}, bf16[4,128,96]{1,2,0:T(8,128)(2,1)S(1)}, u32[]{:S(2)}, u32[]{:S(2)}) collective-permute-start(bf16[4,128,96]{1,2,0:T(8,128)(2,1)S(1)} %get-tuple-element.29), channel_id=1, source_target_pairs={{3,1},{7,5},{11,9},{15,13},{19,17},{23,21},{27,25},{31,29},{35,33}... | collective-permute-start | bytes 294920 | tf_op jit(solution)/shard_map/ppermute | solution.py:41
  133.5 6.6 %collective-permute-start.20 = (bf16[4,128,96]{1,2,0:T(8,128)(2,1)S(1)}, bf16[4,128,96]{1,2,0:T(8,128)(2,1)S(1)}, u32[]{:S(2)}, u32[]{:S(2)}) collective-permute-start(bf16[4,128,96]{1,2,0:T(8,128)(2,1)S(1)} %get-tuple-element.30), channel_id=1, source_target_pairs={{3,2},{7,6},{11,10},{15,14},{19,18},{23,22},{27,26},{31,30},{35,34... | collective-permute-start | bytes 294920 | tf_op jit(solution)/shard_map/ppermute | solution.py:41
  160.8 8.3 %collective-permute-start.21 = (bf16[4,128,96]{1,0,2:T(4,128)(2,1)S(1)}, bf16[4,128,96]{1,0,2:T(4,128)(2,1)S(1)}, u32[]{:S(2)}, u32[]{:S(2)}) collective-permute-start(bf16[4,128,96]{1,0,2:T(4,128)(2,1)S(1)} %convolution_convert_fusion.19), channel_id=1, source_target_pairs={{0,2},{4,6},{8,10},{12,14},{16,18},{20,22},{24,26},{28,30},{32,34}... | collective-permute-start | bytes 294920 | tf_op jit(solution)/shard_map/ppermute | solution.py:52
  173.0 9.3 %collective-permute-start.24 = (bf16[4,128,96]{1,2,0:T(8,128)(2,1)S(1)}, bf16[4,128,96]{1,2,0:T(8,128)(2,1)S(1)}, u32[]{:S(2)}, u32[]{:S(2)}) collective-permute-start(bf16[4,128,96]{1,2,0:T(8,128)(2,1)S(1)} %get-tuple-element.28), channel_id=1, source_target_pairs={{2,0},{6,4},{10,8},{14,12},{18,16},{22,20},{26,24},{30,28},{34,32}... | collective-permute-start | bytes 294920 | tf_op jit(solution)/shard_map/ppermute | solution.py:41
  174.3 8.0 %collective-permute-start.25 = (bf16[4,128,96]{1,2,0:T(8,128)(2,1)S(1)}, bf16[4,128,96]{1,2,0:T(8,128)(2,1)S(1)}, u32[]{:S(2)}, u32[]{:S(2)}) collective-permute-start(bf16[4,128,96]{1,2,0:T(8,128)(2,1)S(1)} %get-tuple-element.26), channel_id=1, source_target_pairs={{2,1},{6,5},{10,9},{14,13},{18,17},{22,21},{26,25},{30,29},{34,33}... | collective-permute-start | bytes 294920 | tf_op jit(solution)/shard_map/ppermute | solution.py:41
  174.9 7.4 %collective-permute-start.26 = (bf16[4,128,96]{1,2,0:T(8,128)(2,1)S(1)}, bf16[4,128,96]{1,2,0:T(8,128)(2,1)S(1)}, u32[]{:S(2)}, u32[]{:S(2)}) collective-permute-start(bf16[4,128,96]{1,2,0:T(8,128)(2,1)S(1)} %get-tuple-element.27), channel_id=1, source_target_pairs={{2,3},{6,7},{10,11},{14,15},{18,19},{22,23},{26,27},{30,31},{34,35... | collective-permute-start | bytes 294920 | tf_op jit(solution)/shard_map/ppermute | solution.py:41
  212.6 10.1 %collective-permute-start.30 = (bf16[4,128,96]{1,2,0:T(8,128)(2,1)S(1)}, bf16[4,128,96]{1,2,0:T(8,128)(2,1)S(1)}, u32[]{:S(2)}, u32[]{:S(2)}) collective-permute-start(bf16[4,128,96]{1,2,0:T(8,128)(2,1)S(1)} %get-tuple-element.23), channel_id=1, source_target_pairs={{1,0},{5,4},{9,8},{13,12},{17,16},{21,20},{25,24},{29,28},{33,32},... | collective-permute-start | bytes 294920 | tf_op jit(solution)/shard_map/ppermute | solution.py:41
  213.9 8.8 %collective-permute-start.31 = (bf16[4,128,96]{1,2,0:T(8,128)(2,1)S(1)}, bf16[4,128,96]{1,2,0:T(8,128)(2,1)S(1)}, u32[]{:S(2)}, u32[]{:S(2)}) collective-permute-start(bf16[4,128,96]{1,2,0:T(8,128)(2,1)S(1)} %get-tuple-element.25), channel_id=1, source_target_pairs={{1,2},{5,6},{9,10},{13,14},{17,18},{21,22},{25,26},{29,30},{33,34}... | collective-permute-start | bytes 294920 | tf_op jit(solution)/shard_map/ppermute | solution.py:41
  214.6 8.1 %collective-permute-start.32 = (bf16[4,128,96]{1,2,0:T(8,128)(2,1)S(1)}, bf16[4,128,96]{1,2,0:T(8,128)(2,1)S(1)}, u32[]{:S(2)}, u32[]{:S(2)}) collective-permute-start(bf16[4,128,96]{1,2,0:T(8,128)(2,1)S(1)} %get-tuple-element.24), channel_id=1, source_target_pairs={{1,3},{5,7},{9,11},{13,15},{17,19},{21,23},{25,27},{29,31},{33,35}... | collective-permute-start | bytes 294920 | tf_op jit(solution)/shard_map/ppermute | solution.py:41
  242.9 6.4 %collective-permute-start.33 = (bf16[4,128,96]{1,0,2:T(4,128)(2,1)S(1)}, bf16[4,128,96]{1,0,2:T(4,128)(2,1)S(1)}, u32[]{:S(2)}, u32[]{:S(2)}) collective-permute-start(bf16[4,128,96]{1,0,2:T(4,128)(2,1)S(1)} %convolution_convert_fusion.17), channel_id=1, source_target_pairs={{1,0},{5,4},{9,8},{13,12},{17,16},{21,20},{25,24},{29,28},{33,32},... | collective-permute-start | bytes 294920 | tf_op jit(solution)/shard_map/ppermute | solution.py:52
  244.2 7.9 %collective-permute-start.34 = (bf16[4,128,96]{1,0,2:T(4,128)(2,1)S(1)}, bf16[4,128,96]{1,0,2:T(4,128)(2,1)S(1)}, u32[]{:S(2)}, u32[]{:S(2)}) collective-permute-start(bf16[4,128,96]{1,0,2:T(4,128)(2,1)S(1)} %convolution_convert_fusion.17), channel_id=1, source_target_pairs={{2,0},{6,4},{10,8},{14,12},{18,16},{22,20},{26,24},{30,28},{34,32}... | collective-permute-start | bytes 294920 | tf_op jit(solution)/shard_map/ppermute | solution.py:52
  245.5 9.0 %collective-permute-start.35 = (bf16[4,128,96]{1,0,2:T(4,128)(2,1)S(1)}, bf16[4,128,96]{1,0,2:T(4,128)(2,1)S(1)}, u32[]{:S(2)}, u32[]{:S(2)}) collective-permute-start(bf16[4,128,96]{1,0,2:T(4,128)(2,1)S(1)} %convolution_convert_fusion.17), channel_id=1, source_target_pairs={{3,0},{7,4},{11,8},{15,12},{19,16},{23,20},{27,24},{31,28},{35,32}... | collective-permute-start | bytes 294920 | tf_op jit(solution)/shard_map/ppermute | solution.py:52
  (26 other events, 159.3 us)

commit v2 on v1

--- a/solution.py
+++ b/solution.py
@@ -30,10 +30,15 @@
     return (index[:, None] == jnp.arange(count, dtype=jnp.int32)[None, :]).astype(dtype)
 
 
+def hops(a, b, row_count):
+    d = (b - a) % row_count
+    return min(d, row_count - d)
+
+
 def spread(out, src_row, row_count, my_row):
     width = out.shape[-1] // row_count
     piece = None
-    for r in range(row_count):
+    for r in sorted(range(row_count), key=lambda r: -hops(src_row, r, row_count)):
         part = out[..., r * width:(r + 1) * width]
         if r == src_row:
             got = jnp.where(my_row == r, part, jnp.zeros_like(part))
@@ -44,12 +49,12 @@
 
 
 def collect(routed, dst_row, row_count):
-    parts = []
-    for r in range(row_count):
+    parts = [None] * row_count
+    for r in sorted(range(row_count), key=lambda r: -hops(r, dst_row, row_count)):
         if r == dst_row:
-            parts.append(routed)
+            parts[r] = routed
         else:
-            parts.append(lax.ppermute(routed, "lvl", [(r, dst_row)]))
+            parts[r] = lax.ppermute(routed, "lvl", [(r, dst_row)])
     return jnp.concatenate(parts, axis=-1)
 
 
@@ -80,28 +85,35 @@
     mine_rank = [None] + [mine(tables[t][1], me) for t in range(1, level_count)]
     mine_target = [None] + [mine(tables[t][2], me) for t in range(1, level_count)]
     lanes = jnp.arange(rank_width, dtype=jnp.int32)
-
-    def keep_of(t):
-        return (lanes[None, :] < mine_rank[t][:, None]).astype(jnp.float32)
+    tile_count, block_rows, _ = left_here.shape
+    my_rank = jnp.zeros((tile_count,), jnp.int32)
+    for t in range(1, level_count):
+        my_rank = jnp.where(my_row == t, mine_rank[t], my_rank)
+    keep = (lanes[None, :] < my_rank[:, None]).astype(left_here.dtype)
+    left_masked = left_here * keep[:, None, :]
+    left_flat = left_masked.transpose(1, 0, 2).reshape(block_rows, tile_count * rank_width)
+    right_flat = right_here.transpose(1, 0, 2).reshape(block_rows, tile_count * rank_width)
+    inverse_t = inverse_here.T
+    lane_shape = (tile_count, rank_width, rhs_here.shape[-1])
 
     solved = jnp.zeros(rhs_here.shape, jnp.bfloat16)
     incoming = None
     for t in range(level_count):
         current = rhs_here.astype(jnp.float32)
         if t > 0:
-            masked = incoming * keep_of(t)[..., None].astype(jnp.bfloat16)
-            current = current - jnp.einsum(
-                "kbr,krn->bn", left_here, masked, preferred_element_type=jnp.float32
+            current = current - jnp.dot(
+                left_flat, incoming.reshape(-1, incoming.shape[-1]),
+                preferred_element_type=jnp.float32,
             )
         lowered = current.astype(jnp.bfloat16)
-        result = jnp.einsum(
-            "ab,bn->an", inverse_here, lowered, preferred_element_type=jnp.float32
+        result = jnp.dot(
+            inverse_here, lowered, preferred_element_type=jnp.float32
         ).astype(jnp.bfloat16)
         solved = jnp.where(my_row == t, result, solved)
         if t + 1 < level_count:
             out = jnp.einsum(
-                "kbr,bn->krn", right_here, result, preferred_element_type=jnp.float32
-            ).astype(jnp.bfloat16)
+                "bm,bn->mn", right_flat, result, preferred_element_type=jnp.float32
+            ).astype(jnp.bfloat16).reshape(lane_shape)
             piece = spread(out, t, row_count, my_row)
             routed = route(piece, mine_target[t + 1], mine_src[t + 1], block_count)
             incoming = collect(routed, t + 1, row_count)
@@ -111,19 +123,19 @@
     for t in reversed(range(level_count)):
         current = solved.astype(jnp.float32)
         if t + 1 < level_count:
-            current = current - jnp.einsum(
-                "kbr,krn->bn", right_here, returning, preferred_element_type=jnp.float32
+            current = current - jnp.dot(
+                right_flat, returning.reshape(-1, returning.shape[-1]),
+                preferred_element_type=jnp.float32,
             )
         upper = current.astype(jnp.bfloat16)
-        result = jnp.einsum(
-            "ba,bn->an", inverse_here, upper, preferred_element_type=jnp.float32
+        result = jnp.dot(
+            inverse_t, upper, preferred_element_type=jnp.float32
         ).astype(jnp.bfloat16)
         answer = jnp.where(my_row == t, result, answer)
         if t > 0:
-            projected = jnp.einsum(
-                "kbr,bn->krn", left_here, result, preferred_element_type=jnp.float32
-            )
-            out = (projected * keep_of(t)[..., None]).astype(jnp.bfloat16)
+            out = jnp.einsum(
+                "bm,bn->mn", left_flat, result, preferred_element_type=jnp.float32
+            ).astype(jnp.bfloat16).reshape(lane_shape)
             piece = spread(out, t, row_count, my_row)
             routed = route(piece, mine_src[t], mine_target[t], block_count)
             returning = collect(routed, t - 1, row_count)

time: 260 us -> 267 us (1.027)
  blocking collectives: 119 us -> 94.3 us
  waiting for transfers between devices: 45.2 us -> 62.1 us
  starting transfers between devices: 51.9 us -> 60.8 us
  local copies, waits for them, and re-layouts: 5.13 us -> 9.38 us
    all_to_all x6 -> x5, blocking collectives: 119 us -> 94.3 us  [route(): lax.all_to_all(holder, 'blk', split_axis=0, concat_axis=0, tiled=True)]
    all_to_all x0 -> x1, waiting for transfers between devices: none -> 13.8 us  [route(): lax.all_to_all(holder, 'blk', split_axis=0, concat_axis=0, tiled=True)]
    all_to_all x0 -> x1, starting transfers between devices: none -> 9.18 us  [route(): lax.all_to_all(holder, 'blk', split_axis=0, concat_axis=0, tiled=True)]
    ppermute x18, waiting for transfers between devices: 13.3 us -> 18.4 us  [collect(): parts[r] = lax.ppermute(routed, 'lvl', [(r, dst_row)])]
    unnamed x30 -> x43, local copies, waits for them, and re-layouts: 3.14 us -> 5.51 us
  transfers between devices with their start and end apart: 36 -> 37, of which waited for: 13 -> 12; matrix products, arithmetic and copies ran while one was open for 1% -> 1% of each run, Pallas kernels for 0% -> 0%
where the time goes in v2:
time: 267 us; the launch traced here: 266 us
  blocking collectives  94.3 us (35%)
  waiting for transfers between devices  62.1 us (23%)
  starting transfers between devices  60.8 us (23%)
  matrix products  33.1 us (12%)
  local copies, waits for them, and re-layouts  9.38 us (4%)
  other arithmetic  4.3 us (2%)
    all_to_all x5, blocking collectives, route(): lax.all_to_all(holder, 'blk', split_axis=0, concat_axis=0, tiled=True)  94.3 us
    ppermute x18, waiting for transfers between devices, spread(): got = lax.ppermute(part, 'lvl', [(src_row, r)])  29.9 us
    ppermute x18, starting transfers between devices, collect(): parts[r] = lax.ppermute(routed, 'lvl', [(r, dst_row)])  29.8 us
    ppermute x18, starting transfers between devices, spread(): got = lax.ppermute(part, 'lvl', [(src_row, r)])  21.8 us
    ppermute x18, waiting for transfers between devices, collect(): parts[r] = lax.ppermute(routed, 'lvl', [(r, dst_row)])  18.4 us
    all_to_all x1, waiting for transfers between devices, route(): lax.all_to_all(holder, 'blk', split_axis=0, concat_axis=0, tiled=True)  13.8 us
    dot_general x4, matrix products, local(): jnp.dot(inverse_here, lowered, preferred_element_type=jnp.float32)  9.89 us
    dot_general x4, matrix products, local(): jnp.dot(inverse_t, upper, preferred_element_type=jnp.float32)  9.73 us
  transfers between devices with their start and end apart: 37, of which 12 were waited for; matrix products, arithmetic and copies ran while one was open for 1% of the time, Pallas kernels for 0%

profile of v2, /device:TPU:1, one launch (start us, length us, event | category | flops | bytes accessed | tf_op | source)
XLA Modules:
  0.0 265.5 jit_solution(15700982866321032842)
XLA Ops:
  4.6 3.9 %collective-permute-start.1 = (bf16[4,128,96]{1,0,2:T(4,128)(2,1)S(1)}, bf16[4,128,96]{1,0,2:T(4,128)(2,1)S(1)}, u32[]{:S(2)}, u32[]{:S(2)}) collective-permute-start(bf16[4,128,96]{1,0,2:T(4,128)(2,1)S(1)} %get-tuple-element.43), channel_id=1, source_target_pairs={{0,1},{4,5},{8,9},{12,13},{16,17},{20,21},{24,25},{28,29},{32,33},... | collective-permute-start | bytes 294920 | tf_op jit(solution)/shard_map/ppermute | solution.py:46
  16.0 9.2 %all-to-all-start = ((bf16[32,128,96]{1,2,0:T(8,128)(2,1)}), bf16[32,128,96]{1,2,0:T(8,128)(2,1)S(1)}, u32[]{:S(2)}, u32[]{:S(2)}) async-start(bf16[32,128,96]{1,2,0:T(8,128)(2,1)} %copy.108), calls=%async_computation | async-start | bytes 1572864 | tf_op jit(solution)/shard_map/all_to_all | solution.py:65
  25.6 13.8 %all-to-all-done = bf16[32,128,96]{1,2,0:T(8,128)(2,1)S(1)} async-done(((bf16[32,128,96]{1,2,0:T(8,128)(2,1)}), bf16[32,128,96]{1,2,0:T(8,128)(2,1)S(1)}, u32[]{:S(2)}, u32[]{:S(2)}) %all-to-all-start) | async-done | bytes 786464 | tf_op jit(solution)/shard_map/all_to_all | solution.py:65
  45.5 3.2 %convolution_convert_fusion.8 = bf16[384,768]{0,1:T(8,128)(2,1)} fusion(bf16[1,1,768,768]{3,2,1,0:T(8,128)(2,1)S(1)} %copy-done, bf16[4,768,128]{1,2,0:T(8,128)(2,1)S(1)} %bitcast_multiply_fusion, bf16[1,1,768,384]{3,2,1,0:T(8,128)(2,1)} %param.7, bf16[4,128,384]{1,0,2:T(4,128)(2,1)S(1)} %pad_maximum_fusion), kind=kOutput, calls=%fused_computation.26 | convolution fusion | flops 756154368 | bytes 3538944 | tf_op jit(solution)/shard_map/dot_general | solution.py:109
  53.1 5.1 %collective-permute-done.7 = bf16[4,128,96]{1,0,2:T(4,128)(2,1)S(1)} collective-permute-done((bf16[4,128,96]{1,0,2:T(4,128)(2,1)S(1)}, bf16[4,128,96]{1,0,2:T(4,128)(2,1)S(1)}, u32[]{:S(2)}, u32[]{:S(2)}) %collective-permute-start.7) | collective-permute-done | bytes 98336 | tf_op jit(solution)/shard_map/ppermute | solution.py:46
  59.1 18.4 %all_to_all.30 = bf16[32,128,96]{1,2,0:T(8,128)(2,1)S(1)} all-to-all(bf16[32,128,96]{1,2,0:T(8,128)(2,1)S(1)} %copy.113), channel_id=1, replica_groups=mesh['blk'=32,'lvl'=4] {'blk'}, dimensions={0} | all-to-all | bytes 1572864 | tf_op jit(solution)/shard_map/all_to_all | solution.py:65
  79.1 6.2 %collective-permute-start.9 = (bf16[4,128,96]{1,0,2:T(4,128)(2,1)S(1)}, bf16[4,128,96]{1,0,2:T(4,128)(2,1)S(1)}, u32[]{:S(2)}, u32[]{:S(2)}) collective-permute-start(bf16[4,128,96]{1,0,2:T(4,128)(2,1)S(1)} %convolution_convert_fusion.24), channel_id=1, source_target_pairs={{0,2},{4,6},{8,10},{12,14},{16,18},{20,22},{24,26},{28,30},{32,34}... | collective-permute-start | bytes 294920 | tf_op jit(solution)/shard_map/ppermute | solution.py:57
  88.0 3.1 %convolution_convert_fusion.7 = bf16[384,768]{0,1:T(8,128)(2,1)} fusion(bf16[1,1,768,768]{3,2,1,0:T(8,128)(2,1)S(1)} %copy-done, bf16[4,768,128]{1,2,0:T(8,128)(2,1)S(1)} %bitcast_multiply_fusion, bf16[1,1,768,384]{3,2,1,0:T(8,128)(2,1)} %param.7, bf16[4,128,384]{1,0,2:T(4,128)(2,1)S(1)} %pad_maximum_fusion.1), kind=kOutput, calls=%fused_computation.25 | convolution fusion | flops 756154368 | bytes 3538944 | tf_op jit(solution)/shard_map/dot_general | solution.py:109
  95.5 8.3 %collective-permute-done.12 = bf16[4,128,96]{1,0,2:T(4,128)(2,1)S(1)} collective-permute-done((bf16[4,128,96]{1,0,2:T(4,128)(2,1)S(1)}, bf16[4,128,96]{1,0,2:T(4,128)(2,1)S(1)}, u32[]{:S(2)}, u32[]{:S(2)}) %collective-permute-start.12) | collective-permute-done | bytes 98336 | tf_op jit(solution)/shard_map/ppermute | solution.py:46
  104.6 18.6 %all_to_all.31 = bf16[32,128,96]{1,2,0:T(8,128)(2,1)S(1)} all-to-all(bf16[32,128,96]{1,2,0:T(8,128)(2,1)S(1)} %copy.118), channel_id=1, replica_groups=mesh['blk'=32,'lvl'=4] {'blk'}, dimensions={0} | all-to-all | bytes 1572864 | tf_op jit(solution)/shard_map/all_to_all | solution.py:65
  127.1 3.6 %collective-permute-done.15 = bf16[4,128,96]{1,0,2:T(4,128)(2,1)S(1)} collective-permute-done((bf16[4,128,96]{1,0,2:T(4,128)(2,1)S(1)}, bf16[4,128,96]{1,0,2:T(4,128)(2,1)S(1)}, u32[]{:S(2)}, u32[]{:S(2)}) %collective-permute-start.15) | collective-permute-done | bytes 98336 | tf_op jit(solution)/shard_map/ppermute | solution.py:57
  131.0 2.8 %fusion.9 = bf16[768,384]{1,0:T(8,128)(2,1)S(1)} fusion(bf16[1,1,768,768]{3,2,1,0:T(8,128)(2,1)S(1)} %copy-done, bf16[4,768,128]{1,2,0:T(8,128)(2,1)S(1)} %bitcast_multiply_fusion, bf16[384,768]{0,1:T(8,128)(2,1)} %convolution_convert_fusion.8, bf16[384,768]{0,1:T(8,128)(2,1)} %convolution_convert_fusion.7, bf16[1,1,768,384]{3,2,1,0:T(8,128)(2,1)} %param.7, ...), kind=kOutput, calls=%fused_computation.35 | convolution fusion | flops 757334016 | bytes 5308420 | tf_op jit(solution)/shard_map/dot_general | solution.py:109
  138.7 7.1 %collective-permute-done.19 = bf16[4,128,96]{1,0,2:T(4,128)(2,1)S(1)} collective-permute-done((bf16[4,128,96]{1,0,2:T(4,128)(2,1)S(1)}, bf16[4,128,96]{1,0,2:T(4,128)(2,1)S(1)}, u32[]{:S(2)}, u32[]{:S(2)}) %collective-permute-start.19) | collective-permute-done | bytes 98336 | tf_op jit(solution)/shard_map/ppermute | solution.py:46
  146.6 18.4 %all_to_all.32 = bf16[32,128,96]{1,2,0:T(8,128)(2,1)S(1)} all-to-all(bf16[32,128,96]{1,2,0:T(8,128)(2,1)S(1)} %copy.127), channel_id=1, replica_groups=mesh['blk'=32,'lvl'=4] {'blk'}, dimensions={0} | all-to-all | bytes 1572864 | tf_op jit(solution)/shard_map/all_to_all | solution.py:65
  166.8 3.8 %collective-permute-start.21 = (bf16[4,128,96]{1,0,2:T(4,128)(2,1)S(1)}, bf16[4,128,96]{1,0,2:T(4,128)(2,1)S(1)}, u32[]{:S(2)}, u32[]{:S(2)}) collective-permute-start(bf16[4,128,96]{1,0,2:T(4,128)(2,1)S(1)} %convolution_convert_fusion.22), channel_id=1, source_target_pairs={{0,2},{4,6},{8,10},{12,14},{16,18},{20,22},{24,26},{28,30},{32,34}... | collective-permute-start | bytes 294920 | tf_op jit(solution)/shard_map/ppermute | solution.py:57
  173.2 3.3 %convolution_convert_fusion.11 = bf16[384,768]{1,0:T(8,128)(2,1)} fusion(bf16[768,384]{1,0:T(8,128)(2,1)} %copy-done.11, bf16[1,1,768,768]{3,2,1,0:T(8,128)(2,1)S(1)} %copy-done, bf16[1,1,4,768,128]{4,3,2,1,0:T(8,128)(2,1)S(1)} %copy-done.2, bf16[4,128,384]{1,0,2:T(4,128)(2,1)S(1)} %pad_maximum_fusion.3), kind=kOutput, calls=%fused_computation.29 | convolution fusion | flops 756154368 | bytes 3538944 | tf_op jit(solution)/shard_map/dot_general | solution.py:131
  182.7 3.0 %collective-permute-done.24 = bf16[4,128,96]{1,0,2:T(4,128)(2,1)S(1)} collective-permute-done((bf16[4,128,96]{1,0,2:T(4,128)(2,1)S(1)}, bf16[4,128,96]{1,0,2:T(4,128)(2,1)S(1)}, u32[]{:S(2)}, u32[]{:S(2)}) %collective-permute-start.24) | collective-permute-done | bytes 98336 | tf_op jit(solution)/shard_map/ppermute | solution.py:46
  187.5 20.2 %all_to_all.33 = bf16[32,128,96]{1,2,0:T(8,128)(2,1)S(1)} all-to-all(bf16[32,128,96]{1,2,0:T(8,128)(2,1)S(1)} %copy.136), channel_id=1, replica_groups=mesh['blk'=32,'lvl'=4] {'blk'}, dimensions={0} | all-to-all | bytes 1572864 | tf_op jit(solution)/shard_map/all_to_all | solution.py:65
  209.3 5.2 %collective-permute-start.27 = (bf16[4,128,96]{1,0,2:T(4,128)(2,1)S(1)}, bf16[4,128,96]{1,0,2:T(4,128)(2,1)S(1)}, u32[]{:S(2)}, u32[]{:S(2)}) collective-permute-start(bf16[4,128,96]{1,0,2:T(4,128)(2,1)S(1)} %convolution_convert_fusion.21), channel_id=1, source_target_pairs={{0,1},{4,5},{8,9},{12,13},{16,17},{20,21},{24,25},{28,29},{32,33},... | collective-permute-start | bytes 294920 | tf_op jit(solution)/shard_map/ppermute | solution.py:57
  217.1 3.3 %convolution_convert_fusion.10 = bf16[384,768]{1,0:T(8,128)(2,1)} fusion(bf16[768,384]{1,0:T(8,128)(2,1)} %copy-done.11, bf16[1,1,768,768]{3,2,1,0:T(8,128)(2,1)S(1)} %copy-done, bf16[1,1,4,768,128]{4,3,2,1,0:T(8,128)(2,1)S(1)} %copy-done.2, bf16[4,128,384]{1,0,2:T(4,128)(2,1)S(1)} %pad_maximum_fusion.4), kind=kOutput, calls=%fused_computation.28 | convolution fusion | flops 756154368 | bytes 3538944 | tf_op jit(solution)/shard_map/dot_general | solution.py:131
  225.7 6.4 %collective-permute-done.31 = bf16[4,128,96]{1,0,2:T(4,128)(2,1)S(1)} collective-permute-done((bf16[4,128,96]{1,0,2:T(4,128)(2,1)S(1)}, bf16[4,128,96]{1,0,2:T(4,128)(2,1)S(1)}, u32[]{:S(2)}, u32[]{:S(2)}) %collective-permute-start.31) | collective-permute-done | bytes 98336 | tf_op jit(solution)/shard_map/ppermute | solution.py:46
  232.9 18.8 %all_to_all.34 = bf16[32,128,96]{1,2,0:T(8,128)(2,1)S(1)} all-to-all(bf16[32,128,96]{1,2,0:T(8,128)(2,1)S(1)} %copy.145), channel_id=1, replica_groups=mesh['blk'=32,'lvl'=4] {'blk'}, dimensions={0} | all-to-all | bytes 1572864 | tf_op jit(solution)/shard_map/all_to_all | solution.py:65
  255.9 5.8 %collective-permute-done.35 = bf16[4,128,96]{1,0,2:T(4,128)(2,1)S(1)} collective-permute-done((bf16[4,128,96]{1,0,2:T(4,128)(2,1)S(1)}, bf16[4,128,96]{1,0,2:T(4,128)(2,1)S(1)}, u32[]{:S(2)}, u32[]{:S(2)}) %collective-permute-start.35) | collective-permute-done | bytes 98336 | tf_op jit(solution)/shard_map/ppermute | solution.py:57
  262.0 2.5 fusion.7
  (164 shorter events, 69.9 us)
Async XLA Ops:
  4.6 9.6 %collective-permute-start.1 = (bf16[4,128,96]{1,0,2:T(4,128)(2,1)S(1)}, bf16[4,128,96]{1,0,2:T(4,128)(2,1)S(1)}, u32[]{:S(2)}, u32[]{:S(2)}) collective-permute-start(bf16[4,128,96]{1,0,2:T(4,128)(2,1)S(1)} %get-tuple-element.43), channel_id=1, source_target_pairs={{0,1},{4,5},{8,9},{12,13},{16,17},{20,21},{24,25},{28,29},{32,33},... | collective-permute-start | bytes 294920 | tf_op jit(solution)/shard_map/ppermute | solution.py:46
  8.6 5.7 %collective-permute-start.2 = (bf16[4,128,96]{1,0,2:T(4,128)(2,1)S(1)}, bf16[4,128,96]{1,0,2:T(4,128)(2,1)S(1)}, u32[]{:S(2)}, u32[]{:S(2)}) collective-permute-start(bf16[4,128,96]{1,0,2:T(4,128)(2,1)S(1)} %get-tuple-element.44), channel_id=1, source_target_pairs={{0,3},{4,7},{8,11},{12,15},{16,19},{20,23},{24,27},{28,31},{32,35}... | collective-permute-start | bytes 294920 | tf_op jit(solution)/shard_map/ppermute | solution.py:46
  16.0 23.4 %all-to-all-start = ((bf16[32,128,96]{1,2,0:T(8,128)(2,1)}), bf16[32,128,96]{1,2,0:T(8,128)(2,1)S(1)}, u32[]{:S(2)}, u32[]{:S(2)}) async-start(bf16[32,128,96]{1,2,0:T(8,128)(2,1)} %copy.108), calls=%async_computation | async-start | bytes 1572864 | tf_op jit(solution)/shard_map/all_to_all | solution.py:65
  50.4 7.8 %collective-permute-start.7 = (bf16[4,128,96]{1,0,2:T(4,128)(2,1)S(1)}, bf16[4,128,96]{1,0,2:T(4,128)(2,1)S(1)}, u32[]{:S(2)}, u32[]{:S(2)}) collective-permute-start(bf16[4,128,96]{1,0,2:T(4,128)(2,1)S(1)} %get-tuple-element.40), channel_id=1, source_target_pairs={{1,0},{5,4},{9,8},{13,12},{17,16},{21,20},{25,24},{29,28},{33,32},... | collective-permute-start | bytes 294920 | tf_op jit(solution)/shard_map/ppermute | solution.py:46
  51.7 6.5 %collective-permute-start.8 = (bf16[4,128,96]{1,0,2:T(4,128)(2,1)S(1)}, bf16[4,128,96]{1,0,2:T(4,128)(2,1)S(1)}, u32[]{:S(2)}, u32[]{:S(2)}) collective-permute-start(bf16[4,128,96]{1,0,2:T(4,128)(2,1)S(1)} %get-tuple-element.41), channel_id=1, source_target_pairs={{1,2},{5,6},{9,10},{13,14},{17,18},{21,22},{25,26},{29,30},{33,34}... | collective-permute-start | bytes 294920 | tf_op jit(solution)/shard_map/ppermute | solution.py:46
  52.4 5.8 %collective-permute-start.6 = (bf16[4,128,96]{1,0,2:T(4,128)(2,1)S(1)}, bf16[4,128,96]{1,0,2:T(4,128)(2,1)S(1)}, u32[]{:S(2)}, u32[]{:S(2)}) collective-permute-start(bf16[4,128,96]{1,0,2:T(4,128)(2,1)S(1)} %get-tuple-element.42), channel_id=1, source_target_pairs={{1,3},{5,7},{9,11},{13,15},{17,19},{21,23},{25,27},{29,31},{33,35}... | collective-permute-start | bytes 294920 | tf_op jit(solution)/shard_map/ppermute | solution.py:46
  77.8 7.6 %collective-permute-start.11 = (bf16[4,128,96]{1,0,2:T(4,128)(2,1)S(1)}, bf16[4,128,96]{1,0,2:T(4,128)(2,1)S(1)}, u32[]{:S(2)}, u32[]{:S(2)}) collective-permute-start(bf16[4,128,96]{1,0,2:T(4,128)(2,1)S(1)} %convolution_convert_fusion.24), channel_id=1, source_target_pairs={{3,2},{7,6},{11,10},{15,14},{19,18},{23,22},{27,26},{31,30},{35,34... | collective-permute-start | bytes 294920 | tf_op jit(solution)/shard_map/ppermute | solution.py:57
  78.5 6.9 %collective-permute-start.10 = (bf16[4,128,96]{1,0,2:T(4,128)(2,1)S(1)}, bf16[4,128,96]{1,0,2:T(4,128)(2,1)S(1)}, u32[]{:S(2)}, u32[]{:S(2)}) collective-permute-start(bf16[4,128,96]{1,0,2:T(4,128)(2,1)S(1)} %convolution_convert_fusion.24), channel_id=1, source_target_pairs={{1,2},{5,6},{9,10},{13,14},{17,18},{21,22},{25,26},{29,30},{33,34}... | collective-permute-start | bytes 294920 | tf_op jit(solution)/shard_map/ppermute | solution.py:57
  79.1 8.5 %collective-permute-start.9 = (bf16[4,128,96]{1,0,2:T(4,128)(2,1)S(1)}, bf16[4,128,96]{1,0,2:T(4,128)(2,1)S(1)}, u32[]{:S(2)}, u32[]{:S(2)}) collective-permute-start(bf16[4,128,96]{1,0,2:T(4,128)(2,1)S(1)} %convolution_convert_fusion.24), channel_id=1, source_target_pairs={{0,2},{4,6},{8,10},{12,14},{16,18},{20,22},{24,26},{28,30},{32,34}... | collective-permute-start | bytes 294920 | tf_op jit(solution)/shard_map/ppermute | solution.py:57
  94.2 9.6 %collective-permute-start.12 = (bf16[4,128,96]{1,0,2:T(4,128)(2,1)S(1)}, bf16[4,128,96]{1,0,2:T(4,128)(2,1)S(1)}, u32[]{:S(2)}, u32[]{:S(2)}) collective-permute-start(bf16[4,128,96]{1,0,2:T(4,128)(2,1)S(1)} %get-tuple-element.39), channel_id=1, source_target_pairs={{2,0},{6,4},{10,8},{14,12},{18,16},{22,20},{26,24},{30,28},{34,32}... | collective-permute-start | bytes 294920 | tf_op jit(solution)/shard_map/ppermute | solution.py:46
  124.9 5.8 %collective-permute-start.15 = (bf16[4,128,96]{1,0,2:T(4,128)(2,1)S(1)}, bf16[4,128,96]{1,0,2:T(4,128)(2,1)S(1)}, u32[]{:S(2)}, u32[]{:S(2)}) collective-permute-start(bf16[4,128,96]{1,0,2:T(4,128)(2,1)S(1)} %convolution_convert_fusion.23), channel_id=1, source_target_pairs={{0,3},{4,7},{8,11},{12,15},{16,19},{20,23},{24,27},{28,31},{32,35}... | collective-permute-start | bytes 294920 | tf_op jit(solution)/shard_map/ppermute | solution.py:57
  137.2 8.6 %collective-permute-start.19 = (bf16[4,128,96]{1,0,2:T(4,128)(2,1)S(1)}, bf16[4,128,96]{1,0,2:T(4,128)(2,1)S(1)}, u32[]{:S(2)}, u32[]{:S(2)}) collective-permute-start(bf16[4,128,96]{1,0,2:T(4,128)(2,1)S(1)} %copy.173), channel_id=1, source_target_pairs={{3,0},{7,4},{11,8},{15,12},{19,16},{23,20},{27,24},{31,28},{35,32}... | collective-permute-start | bytes 294920 | tf_op jit(solution)/shard_map/ppermute | solution.py:46
  165.4 5.2 %collective-permute-start.23 = (bf16[4,128,96]{1,0,2:T(4,128)(2,1)S(1)}, bf16[4,128,96]{1,0,2:T(4,128)(2,1)S(1)}, u32[]{:S(2)}, u32[]{:S(2)}) collective-permute-start(bf16[4,128,96]{1,0,2:T(4,128)(2,1)S(1)} %convolution_convert_fusion.22), channel_id=1, source_target_pairs={{3,2},{7,6},{11,10},{15,14},{19,18},{23,22},{27,26},{31,30},{35,34... | collective-permute-start | bytes 294920 | tf_op jit(solution)/shard_map/ppermute | solution.py:57
  166.1 4.5 %collective-permute-start.22 = (bf16[4,128,96]{1,0,2:T(4,128)(2,1)S(1)}, bf16[4,128,96]{1,0,2:T(4,128)(2,1)S(1)}, u32[]{:S(2)}, u32[]{:S(2)}) collective-permute-start(bf16[4,128,96]{1,0,2:T(4,128)(2,1)S(1)} %convolution_convert_fusion.22), channel_id=1, source_target_pairs={{1,2},{5,6},{9,10},{13,14},{17,18},{21,22},{25,26},{29,30},{33,34}... | collective-permute-start | bytes 294920 | tf_op jit(solution)/shard_map/ppermute | solution.py:57
  166.8 6.1 %collective-permute-start.21 = (bf16[4,128,96]{1,0,2:T(4,128)(2,1)S(1)}, bf16[4,128,96]{1,0,2:T(4,128)(2,1)S(1)}, u32[]{:S(2)}, u32[]{:S(2)}) collective-permute-start(bf16[4,128,96]{1,0,2:T(4,128)(2,1)S(1)} %convolution_convert_fusion.22), channel_id=1, source_target_pairs={{0,2},{4,6},{8,10},{12,14},{16,18},{20,22},{24,26},{28,30},{32,34}... | collective-permute-start | bytes 294920 | tf_op jit(solution)/shard_map/ppermute | solution.py:57
  178.7 7.0 %collective-permute-start.24 = (bf16[4,128,96]{1,0,2:T(4,128)(2,1)S(1)}, bf16[4,128,96]{1,0,2:T(4,128)(2,1)S(1)}, u32[]{:S(2)}, u32[]{:S(2)}) collective-permute-start(bf16[4,128,96]{1,0,2:T(4,128)(2,1)S(1)} %copy.176), channel_id=1, source_target_pairs={{2,0},{6,4},{10,8},{14,12},{18,16},{22,20},{26,24},{30,28},{34,32}... | collective-permute-start | bytes 294920 | tf_op jit(solution)/shard_map/ppermute | solution.py:46
  180.0 5.7 %collective-permute-start.26 = (bf16[4,128,96]{1,0,2:T(4,128)(2,1)S(1)}, bf16[4,128,96]{1,0,2:T(4,128)(2,1)}, u32[]{:S(2)}, u32[]{:S(2)}) collective-permute-start(bf16[4,128,96]{1,0,2:T(4,128)(2,1)S(1)} %copy.178), channel_id=1, source_target_pairs={{2,3},{6,7},{10,11},{14,15},{18,19},{22,23},{26,27},{30,31},{34,35... | collective-permute-start | bytes 294920 | tf_op jit(solution)/shard_map/ppermute | solution.py:46
  208.0 6.6 %collective-permute-start.29 = (bf16[4,128,96]{1,0,2:T(4,128)(2,1)S(1)}, bf16[4,128,96]{1,0,2:T(4,128)(2,1)S(1)}, u32[]{:S(2)}, u32[]{:S(2)}) collective-permute-start(bf16[4,128,96]{1,0,2:T(4,128)(2,1)S(1)} %convolution_convert_fusion.21), channel_id=1, source_target_pairs={{3,1},{7,5},{11,9},{15,13},{19,17},{23,21},{27,25},{31,29},{35,33}... | collective-permute-start | bytes 294920 | tf_op jit(solution)/shard_map/ppermute | solution.py:57
  208.7 5.9 %collective-permute-start.28 = (bf16[4,128,96]{1,0,2:T(4,128)(2,1)S(1)}, bf16[4,128,96]{1,0,2:T(4,128)(2,1)S(1)}, u32[]{:S(2)}, u32[]{:S(2)}) collective-permute-start(bf16[4,128,96]{1,0,2:T(4,128)(2,1)S(1)} %convolution_convert_fusion.21), channel_id=1, source_target_pairs={{2,1},{6,5},{10,9},{14,13},{18,17},{22,21},{26,25},{30,29},{34,33}... | collective-permute-start | bytes 294920 | tf_op jit(solution)/shard_map/ppermute | solution.py:57
  209.3 7.5 %collective-permute-start.27 = (bf16[4,128,96]{1,0,2:T(4,128)(2,1)S(1)}, bf16[4,128,96]{1,0,2:T(4,128)(2,1)S(1)}, u32[]{:S(2)}, u32[]{:S(2)}) collective-permute-start(bf16[4,128,96]{1,0,2:T(4,128)(2,1)S(1)} %convolution_convert_fusion.21), channel_id=1, source_target_pairs={{0,1},{4,5},{8,9},{12,13},{16,17},{20,21},{24,25},{28,29},{32,33},... | collective-permute-start | bytes 294920 | tf_op jit(solution)/shard_map/ppermute | solution.py:57
  224.0 8.1 %collective-permute-start.31 = (bf16[4,128,96]{1,0,2:T(4,128)(2,1)S(1)}, bf16[4,128,96]{1,0,2:T(4,128)(2,1)S(1)}, u32[]{:S(2)}, u32[]{:S(2)}) collective-permute-start(bf16[4,128,96]{1,0,2:T(4,128)(2,1)S(1)} %copy.181), channel_id=1, source_target_pairs={{1,0},{5,4},{9,8},{13,12},{17,16},{21,20},{25,24},{29,28},{33,32},... | collective-permute-start | bytes 294920 | tf_op jit(solution)/shard_map/ppermute | solution.py:46
  252.0 9.7 %collective-permute-start.35 = (bf16[4,128,96]{1,0,2:T(4,128)(2,1)S(1)}, bf16[4,128,96]{1,0,2:T(4,128)(2,1)S(1)}, u32[]{:S(2)}, u32[]{:S(2)}) collective-permute-start(bf16[4,128,96]{1,0,2:T(4,128)(2,1)S(1)} %convolution_convert_fusion.20), channel_id=1, source_target_pairs={{3,0},{7,4},{11,8},{15,12},{19,16},{23,20},{27,24},{31,28},{35,32}... | collective-permute-start | bytes 294920 | tf_op jit(solution)/shard_map/ppermute | solution.py:57
  253.3 8.4 %collective-permute-start.34 = (bf16[4,128,96]{1,0,2:T(4,128)(2,1)S(1)}, bf16[4,128,96]{1,0,2:T(4,128)(2,1)S(1)}, u32[]{:S(2)}, u32[]{:S(2)}) collective-permute-start(bf16[4,128,96]{1,0,2:T(4,128)(2,1)S(1)} %convolution_convert_fusion.20), channel_id=1, source_target_pairs={{2,0},{6,4},{10,8},{14,12},{18,16},{22,20},{26,24},{30,28},{34,32}... | collective-permute-start | bytes 294920 | tf_op jit(solution)/shard_map/ppermute | solution.py:57
  254.6 7.1 %collective-permute-start.33 = (bf16[4,128,96]{1,0,2:T(4,128)(2,1)S(1)}, bf16[4,128,96]{1,0,2:T(4,128)(2,1)S(1)}, u32[]{:S(2)}, u32[]{:S(2)}) collective-permute-start(bf16[4,128,96]{1,0,2:T(4,128)(2,1)S(1)} %convolution_convert_fusion.20), channel_id=1, source_target_pairs={{1,0},{5,4},{9,8},{13,12},{17,16},{21,20},{25,24},{29,28},{33,32},... | collective-permute-start | bytes 294920 | tf_op jit(solution)/shard_map/ppermute | solution.py:57
  (27 other events, 121.7 us)

commit v3 on v1

--- a/solution.py
+++ b/solution.py
@@ -85,6 +85,7 @@
         return (lanes[None, :] < mine_rank[t][:, None]).astype(jnp.float32)
 
     solved = jnp.zeros(rhs_here.shape, jnp.bfloat16)
+    own_blocks = []
     incoming = None
     for t in range(level_count):
         current = rhs_here.astype(jnp.float32)
@@ -99,6 +100,7 @@
         ).astype(jnp.bfloat16)
         solved = jnp.where(my_row == t, result, solved)
         if t + 1 < level_count:
+            own_blocks.append(spread(result, t, row_count, my_row))
             out = jnp.einsum(
                 "kbr,bn->krn", right_here, result, preferred_element_type=jnp.float32
             ).astype(jnp.bfloat16)
@@ -106,27 +108,41 @@
             routed = route(piece, mine_target[t + 1], mine_src[t + 1], block_count)
             incoming = collect(routed, t + 1, row_count)
 
-    answer = jnp.zeros(rhs_here.shape, jnp.bfloat16)
-    returning = None
-    for t in reversed(range(level_count)):
-        current = solved.astype(jnp.float32)
-        if t + 1 < level_count:
-            current = current - jnp.einsum(
-                "kbr,krn->bn", right_here, returning, preferred_element_type=jnp.float32
-            )
+    last = level_count - 1
+    width = rhs_here.shape[-1] // row_count
+    inverse_all = lax.all_gather(inverse_here, "lvl")
+    right_all = lax.all_gather(right_here, "lvl")
+    left_all = lax.all_gather(left_here, "lvl")
+
+    result = jnp.einsum(
+        "ba,bn->an", inverse_here, solved, preferred_element_type=jnp.float32
+    ).astype(jnp.bfloat16)
+    top = result
+    projected = jnp.einsum(
+        "kbr,bn->krn", left_here, result, preferred_element_type=jnp.float32
+    )
+    out = (projected * keep_of(last)[..., None]).astype(jnp.bfloat16)
+    piece = spread(out, last, row_count, my_row)
+    returning = route(piece, mine_src[last], mine_target[last], block_count)
+    blocks = [None] * level_count
+    for t in reversed(range(last)):
+        current = own_blocks[t].astype(jnp.float32) - jnp.einsum(
+            "kbr,krn->bn", right_all[t], returning, preferred_element_type=jnp.float32
+        )
         upper = current.astype(jnp.bfloat16)
         result = jnp.einsum(
-            "ba,bn->an", inverse_here, upper, preferred_element_type=jnp.float32
+            "ba,bn->an", inverse_all[t], upper, preferred_element_type=jnp.float32
         ).astype(jnp.bfloat16)
-        answer = jnp.where(my_row == t, result, answer)
+        blocks[t] = result
         if t > 0:
             projected = jnp.einsum(
-                "kbr,bn->krn", left_here, result, preferred_element_type=jnp.float32
+                "kbr,bn->krn", left_all[t], result, preferred_element_type=jnp.float32
             )
             out = (projected * keep_of(t)[..., None]).astype(jnp.bfloat16)
-            piece = spread(out, t, row_count, my_row)
-            routed = route(piece, mine_src[t], mine_target[t], block_count)
-            returning = collect(routed, t - 1, row_count)
+            returning = route(out, mine_src[t], mine_target[t], block_count)
+    answer = top
+    for t in range(last):
+        answer = jnp.where(my_row == t, collect(blocks[t], t, row_count), answer)
     return (solved[None, None], answer[None, None])
 
 

time: 260 us -> 260 us (level)
  blocking collectives: 119 us -> 63.3 us
  starting transfers between devices: 51.9 us -> 76.3 us
  between operations: 1.45 us -> 14.6 us
  waiting for transfers between devices: 45.2 us -> 56.7 us
  local copies, waits for them, and re-layouts: 5.13 us -> 9.48 us
  other arithmetic: 4.04 us -> 7.99 us
    all_to_all x6 -> x3, blocking collectives: 119 us -> 63.3 us  [route(): lax.all_to_all(holder, 'blk', split_axis=0, concat_axis=0, tiled=True)]
    all_to_all x0 -> x3, waiting for transfers between devices: none -> 23.1 us  [route(): lax.all_to_all(holder, 'blk', split_axis=0, concat_axis=0, tiled=True)]
    ppermute x18 -> x21, waiting for transfers between devices: 31.8 us -> 15.5 us  [spread(): got = lax.ppermute(part, 'lvl', [(src_row, r)])]
    all_to_all x0 -> x3, starting transfers between devices: none -> 14.2 us  [route(): lax.all_to_all(holder, 'blk', split_axis=0, concat_axis=0, tiled=True)]
    ppermute x18 -> x21, starting transfers between devices: 20.5 us -> 33.4 us  [spread(): got = lax.ppermute(part, 'lvl', [(src_row, r)])]
    ppermute x18, waiting for transfers between devices: 13.3 us -> 17.3 us  [collect(): parts.append(lax.ppermute(routed, 'lvl', [(r, dst_row)]))]
    ppermute x18, starting transfers between devices: 31.4 us -> 28.6 us  [collect(): parts.append(lax.ppermute(routed, 'lvl', [(r, dst_row)]))]
    convert_element_type x6, local copies, waits for them, and re-layouts: 1.84 us -> 4.55 us  [route(): holder = holder.astype(piece.dtype)]
  transfers between devices with their start and end apart: 36 -> 45, of which waited for: 13 -> 11; matrix products, arithmetic and copies ran while one was open for 1% -> 14% of each run, Pallas kernels for 0% -> 0%
where the time goes in v3:
time: 260 us; the launch traced here: 259 us
  starting transfers between devices  76.3 us (29%)
  blocking collectives  63.3 us (24%)
  waiting for transfers between devices  56.7 us (22%)
  matrix products  30.4 us (12%)
  between operations  14.6 us (6%)
  local copies, waits for them, and re-layouts  9.48 us (4%)
  other arithmetic  7.99 us (3%)
    all_to_all x3, blocking collectives, route(): lax.all_to_all(holder, 'blk', split_axis=0, concat_axis=0, tiled=True)  63.3 us
    ppermute x21, starting transfers between devices, spread(): got = lax.ppermute(part, 'lvl', [(src_row, r)])  33.4 us
    ppermute x18, starting transfers between devices, collect(): parts.append(lax.ppermute(routed, 'lvl', [(r, dst_row)]))  28.6 us
    all_to_all x3, waiting for transfers between devices, route(): lax.all_to_all(holder, 'blk', split_axis=0, concat_axis=0, tiled=True)  23.1 us
    ppermute x18, waiting for transfers between devices, collect(): parts.append(lax.ppermute(routed, 'lvl', [(r, dst_row)]))  17.3 us
    ppermute x21, waiting for transfers between devices, spread(): got = lax.ppermute(part, 'lvl', [(src_row, r)])  15.5 us
    all_to_all x3, starting transfers between devices, route(): lax.all_to_all(holder, 'blk', split_axis=0, concat_axis=0, tiled=True)  14.2 us
    dot_general x4, matrix products, local(): jnp.einsum('ab,bn->an', inverse_here, lowered, preferred_element_type=jnp...  10.4 us
  transfers between devices with their start and end apart: 45, of which 11 were waited for; matrix products, arithmetic and copies ran while one was open for 14% of the time, Pallas kernels for 0%

profile of v3, /device:TPU:1, one launch (start us, length us, event | category | flops | bytes accessed | tf_op | source)
XLA Modules:
  0.0 258.8 jit_solution(4587593632477698513)
XLA Ops:
  11.5 3.9 %collective-permute-start = (bf16[4,128,96]{1,2,0:T(8,128)(2,1)S(1)}, bf16[4,128,96]{1,2,0:T(8,128)(2,1)S(1)}, u32[]{:S(2)}, u32[]{:S(2)}) collective-permute-start(bf16[4,128,96]{1,2,0:T(8,128)(2,1)S(1)} %get-tuple-element.41), channel_id=1, source_target_pairs={{0,1},{4,5},{8,9},{12,13},{16,17},{20,21},{24,25},{28,29},{32,33},... | collective-permute-start | bytes 294920 | tf_op jit(solution)/shard_map/ppermute | solution.py:41
  22.4 23.2 %all_to_all.30 = bf16[32,128,96]{1,2,0:T(8,128)(2,1)S(1)} all-to-all(bf16[32,128,96]{1,2,0:T(8,128)(2,1)S(1)} %copy.30), channel_id=1, replica_groups=mesh['blk'=32,'lvl'=4] {'blk'}, dimensions={0} | all-to-all | bytes 1572864 | tf_op jit(solution)/shard_map/all_to_all | solution.py:60
  53.1 2.9 %convolution_convert_fusion.9 = bf16[384,768]{1,0:T(8,128)(2,1)} fusion(bf16[1,1,768,768]{3,2,1,0:T(8,128)(2,1)S(1)} %copy-done, bf16[1,1,4,768,128]{4,3,2,1,0:T(8,128)(2,1)S(1)} %copy-done.2, bf16[1,1,768,384]{2,3,1,0:T(8,128)(2,1)} %copy.28, bf16[4,128,384]{1,0,2:T(4,128)(2,1)S(1)} %maximum_multiply_fusion), kind=kOutput, calls=%fused_computation.18 | convolution fusion | flops 756154368 | bytes 3538944 | tf_op jit(solution)/shard_map/ab,bn->an/dot_general | solution.py:98
  61.4 5.5 %collective-permute-done.6 = bf16[4,128,96]{1,2,0:T(8,128)(2,1)S(1)} collective-permute-done((bf16[4,128,96]{1,2,0:T(8,128)(2,1)S(1)}, bf16[4,128,96]{1,2,0:T(8,128)(2,1)S(1)}, u32[]{:S(2)}, u32[]{:S(2)}) %collective-permute-start.6) | collective-permute-done | bytes 98336 | tf_op jit(solution)/shard_map/ppermute | solution.py:41
  68.7 19.7 %all_to_all.31 = bf16[32,128,96]{1,2,0:T(8,128)(2,1)S(1)} all-to-all(bf16[32,128,96]{1,2,0:T(8,128)(2,1)S(1)} %copy.34), channel_id=1, replica_groups=mesh['blk'=32,'lvl'=4] {'blk'}, dimensions={0} | all-to-all | bytes 1572864 | tf_op jit(solution)/shard_map/all_to_all | solution.py:60
  90.1 6.4 %collective-permute-start.9 = (bf16[4,128,96]{1,0,2:T(4,128)(2,1)S(1)}, bf16[4,128,96]{1,0,2:T(4,128)(2,1)S(1)}, u32[]{:S(2)}, u32[]{:S(2)}) collective-permute-start(bf16[4,128,96]{1,0,2:T(4,128)(2,1)S(1)} %convolution_convert_fusion.18), channel_id=1, source_target_pairs={{0,2},{4,6},{8,10},{12,14},{16,18},{20,22},{24,26},{28,30},{32,34}... | collective-permute-start | bytes 294920 | tf_op jit(solution)/shard_map/ppermute | solution.py:52
  96.5 4.5 %collective-permute-done.9 = bf16[4,128,96]{1,0,2:T(4,128)(2,1)S(1)} collective-permute-done((bf16[4,128,96]{1,0,2:T(4,128)(2,1)S(1)}, bf16[4,128,96]{1,0,2:T(4,128)(2,1)S(1)}, u32[]{:S(2)}, u32[]{:S(2)}) %collective-permute-start.9) | collective-permute-done | bytes 98336 | tf_op jit(solution)/shard_map/ppermute | solution.py:52
  102.1 2.8 %convolution_convert_fusion.8 = bf16[384,768]{1,0:T(8,128)(2,1)} fusion(bf16[1,1,768,768]{3,2,1,0:T(8,128)(2,1)S(1)} %copy-done, bf16[1,1,4,768,128]{4,3,2,1,0:T(8,128)(2,1)S(1)} %copy-done.2, bf16[1,1,768,384]{2,3,1,0:T(8,128)(2,1)S(1)} %copy-done.5, bf16[4,128,384]{1,0,2:T(4,128)(2,1)} %maximum_multiply_fusion.1), kind=kOutput, calls=%fused_computation.17 | convolution fusion | flops 756154368 | bytes 3538944 | tf_op jit(solution)/shard_map/ab,bn->an/dot_general | solution.py:98
  109.2 4.6 %collective-permute-done.12 = bf16[4,128,96]{1,2,0:T(8,128)(2,1)S(1)} collective-permute-done((bf16[4,128,96]{1,2,0:T(8,128)(2,1)S(1)}, bf16[4,128,96]{1,2,0:T(8,128)(2,1)S(1)}, u32[]{:S(2)}, u32[]{:S(2)}) %collective-permute-start.12) | collective-permute-done | bytes 98336 | tf_op jit(solution)/shard_map/ppermute | solution.py:41
  114.7 20.4 %all_to_all.32 = bf16[32,128,96]{1,2,0:T(8,128)(2,1)S(1)} all-to-all(bf16[32,128,96]{1,2,0:T(8,128)(2,1)S(1)} %copy.38), channel_id=1, replica_groups=mesh['blk'=32,'lvl'=4] {'blk'}, dimensions={0} | all-to-all | bytes 1572864 | tf_op jit(solution)/shard_map/all_to_all | solution.py:60
  135.4 3.8 %collective-permute-start.15 = (bf16[4,128,96]{1,0,2:T(4,128)(2,1)S(1)}, bf16[4,128,96]{1,0,2:T(4,128)(2,1)S(1)}, u32[]{:S(2)}, u32[]{:S(2)}) collective-permute-start(bf16[4,128,96]{1,0,2:T(4,128)(2,1)S(1)} %convolution_convert_fusion.17), channel_id=1, source_target_pairs={{0,3},{4,7},{8,11},{12,15},{16,19},{20,23},{24,27},{28,31},{32,35}... | collective-permute-start | bytes 294920 | tf_op jit(solution)/shard_map/ppermute | solution.py:52
  140.8 4.1 %collective-permute-done.15 = bf16[4,128,96]{1,0,2:T(4,128)(2,1)S(1)} collective-permute-done((bf16[4,128,96]{1,0,2:T(4,128)(2,1)S(1)}, bf16[4,128,96]{1,0,2:T(4,128)(2,1)S(1)}, u32[]{:S(2)}, u32[]{:S(2)}) %collective-permute-start.15) | collective-permute-done | bytes 98336 | tf_op jit(solution)/shard_map/ppermute | solution.py:52
  146.1 2.5 fusion.5
  152.4 5.3 %collective-permute-done.21 = bf16[4,128,96]{1,2,0:T(8,128)(2,1)S(1)} collective-permute-done((bf16[4,128,96]{1,2,0:T(8,128)(2,1)S(1)}, bf16[4,128,96]{1,2,0:T(8,128)(2,1)S(1)}, u32[]{:S(2)}, u32[]{:S(2)}) %collective-permute-start.21) | collective-permute-done | bytes 98336 | tf_op jit(solution)/shard_map/ppermute | solution.py:41
  159.5 6.3 %all-to-all-start.3 = ((bf16[32,128,96]{1,2,0:T(8,128)(2,1)}), bf16[32,128,96]{1,2,0:T(8,128)(2,1)S(1)}, u32[]{:S(2)}, u32[]{:S(2)}) async-start(bf16[32,128,96]{1,2,0:T(8,128)(2,1)} %copy.42), calls=%async_computation.3 | async-start | bytes 1572864 | tf_op jit(solution)/shard_map/all_to_all | solution.py:60
  169.1 10.9 %all-to-all-done.3 = bf16[32,128,96]{1,2,0:T(8,128)(2,1)S(1)} async-done(((bf16[32,128,96]{1,2,0:T(8,128)(2,1)}), bf16[32,128,96]{1,2,0:T(8,128)(2,1)S(1)}, u32[]{:S(2)}, u32[]{:S(2)}) %all-to-all-start.3) | async-done | bytes 786464 | tf_op jit(solution)/shard_map/all_to_all | solution.py:60
  185.8 4.0 %all-to-all-start.4 = ((bf16[32,128,96]{1,2,0:T(8,128)(2,1)}), bf16[32,128,96]{1,2,0:T(8,128)(2,1)S(1)}, u32[]{:S(2)}, u32[]{:S(2)}) async-start(bf16[32,128,96]{1,2,0:T(8,128)(2,1)} %copy.46), calls=%async_computation.4 | async-start | bytes 1572864 | tf_op jit(solution)/shard_map/all_to_all | solution.py:60
  193.8 10.2 %all-to-all-done.4 = bf16[32,128,96]{1,2,0:T(8,128)(2,1)S(1)} async-done(((bf16[32,128,96]{1,2,0:T(8,128)(2,1)}), bf16[32,128,96]{1,2,0:T(8,128)(2,1)S(1)}, u32[]{:S(2)}, u32[]{:S(2)}) %all-to-all-start.4) | async-done | bytes 786464 | tf_op jit(solution)/shard_map/all_to_all | solution.py:60
  209.9 4.0 %all-to-all-start.5 = ((bf16[32,128,96]{1,2,0:T(8,128)(2,1)}), bf16[32,128,96]{1,2,0:T(8,128)(2,1)S(1)}, u32[]{:S(2)}, u32[]{:S(2)}) async-start(bf16[32,128,96]{1,2,0:T(8,128)(2,1)} %copy.50), calls=%async_computation.5 | async-start | bytes 1572864 | tf_op jit(solution)/shard_map/all_to_all | solution.py:60
  214.6 4.3 %collective-permute-start.33 = (bf16[768,96]{0,1:T(8,128)(2,1)S(1)}, bf16[768,96]{0,1:T(8,128)(2,1)}, u32[]{:S(2)}, u32[]{:S(2)}) collective-permute-start(bf16[768,96]{0,1:T(8,128)(2,1)S(1)} %get-tuple-element.23), channel_id=1, source_target_pairs={{0,1},{4,5},{8,9},{12,13},{16,17},{20,21},{24,25},{28,29},{32,33},... | collective-permute-start | bytes 442376 | tf_op jit(solution)/shard_map/ppermute | solution.py:41
  218.9 3.3 %collective-permute-start.34 = (bf16[768,96]{0,1:T(8,128)(2,1)}, bf16[768,96]{0,1:T(8,128)(2,1)}, u32[]{:S(2)}, u32[]{:S(2)}) collective-permute-start(bf16[768,96]{0,1:T(8,128)(2,1)} %get-tuple-element.25), channel_id=1, source_target_pairs={{0,2},{4,6},{8,10},{12,14},{16,18},{20,22},{24,26},{28,30},{32,34}... | collective-permute-start | bytes 442376 | tf_op jit(solution)/shard_map/ppermute | solution.py:41
  229.8 3.7 %collective-permute-start.30 = (bf16[768,96]{0,1:T(8,128)(2,1)S(1)}, bf16[768,96]{0,1:T(8,128)(2,1)S(1)}, u32[]{:S(2)}, u32[]{:S(2)}) collective-permute-start(bf16[768,96]{0,1:T(8,128)(2,1)S(1)} %bitcast.245), channel_id=1, source_target_pairs={{0,1},{4,5},{8,9},{12,13},{16,17},{20,21},{24,25},{28,29},{32,33},... | collective-permute-start | bytes 442376 | tf_op jit(solution)/shard_map/ppermute | solution.py:52
  244.4 2.8 %collective-permute-done.37 = bf16[768,96]{0,1:T(8,128)(2,1)S(1)} collective-permute-done((bf16[768,96]{0,1:T(8,128)(2,1)S(1)}, bf16[768,96]{0,1:T(8,128)(2,1)S(1)}, u32[]{:S(2)}, u32[]{:S(2)}) %collective-permute-start.37) | collective-permute-done | bytes 147488 | tf_op jit(solution)/shard_map/ppermute | solution.py:52
  247.2 3.6 %collective-permute-done.38 = bf16[768,96]{0,1:T(8,128)(2,1)S(1)} collective-permute-done((bf16[768,96]{0,1:T(8,128)(2,1)S(1)}, bf16[768,96]{0,1:T(8,128)(2,1)S(1)}, u32[]{:S(2)}, u32[]{:S(2)}) %collective-permute-start.38) | collective-permute-done | bytes 147488 | tf_op jit(solution)/shard_map/ppermute | solution.py:52
  (177 shorter events, 81.5 us)
Async XLA Ops:
  7.2 173.2 %all-gather.7.cloned.1.call-start = ((), (), s32[]{:S(2)}) async-start(), calls=%async_computation.6 | async-start | bytes 3932160 | tf_op jit(solution)/shard_map/all_gather | solution.py:114
  7.9 172.5 %all-gather.9.cloned.1.call-start = ((), (), s32[]{:S(2)}) async-start(), calls=%async_computation.7 | async-start | bytes 5898240 | tf_op jit(solution)/shard_map/all_gather | solution.py:113
  11.5 10.1 %collective-permute-start = (bf16[4,128,96]{1,2,0:T(8,128)(2,1)S(1)}, bf16[4,128,96]{1,2,0:T(8,128)(2,1)S(1)}, u32[]{:S(2)}, u32[]{:S(2)}) collective-permute-start(bf16[4,128,96]{1,2,0:T(8,128)(2,1)S(1)} %get-tuple-element.41), channel_id=1, source_target_pairs={{0,1},{4,5},{8,9},{12,13},{16,17},{20,21},{24,25},{28,29},{32,33},... | collective-permute-start | bytes 294920 | tf_op jit(solution)/shard_map/ppermute | solution.py:41
  19.0 163.8 %all-gather.11.cloned.1.call-start = ((), (), s32[]{:S(2)}) async-start(), calls=%async_computation.8 | async-start | bytes 3932160 | tf_op jit(solution)/shard_map/all_gather | solution.py:115
  57.5 9.4 %collective-permute-start.6 = (bf16[4,128,96]{1,2,0:T(8,128)(2,1)S(1)}, bf16[4,128,96]{1,2,0:T(8,128)(2,1)S(1)}, u32[]{:S(2)}, u32[]{:S(2)}) collective-permute-start(bf16[4,128,96]{1,2,0:T(8,128)(2,1)S(1)} %get-tuple-element.38), channel_id=1, source_target_pairs={{1,0},{5,4},{9,8},{13,12},{17,16},{21,20},{25,24},{29,28},{33,32},... | collective-permute-start | bytes 294920 | tf_op jit(solution)/shard_map/ppermute | solution.py:41
  90.1 10.9 %collective-permute-start.9 = (bf16[4,128,96]{1,0,2:T(4,128)(2,1)S(1)}, bf16[4,128,96]{1,0,2:T(4,128)(2,1)S(1)}, u32[]{:S(2)}, u32[]{:S(2)}) collective-permute-start(bf16[4,128,96]{1,0,2:T(4,128)(2,1)S(1)} %convolution_convert_fusion.18), channel_id=1, source_target_pairs={{0,2},{4,6},{8,10},{12,14},{16,18},{20,22},{24,26},{28,30},{32,34}... | collective-permute-start | bytes 294920 | tf_op jit(solution)/shard_map/ppermute | solution.py:52
  135.4 9.6 %collective-permute-start.15 = (bf16[4,128,96]{1,0,2:T(4,128)(2,1)S(1)}, bf16[4,128,96]{1,0,2:T(4,128)(2,1)S(1)}, u32[]{:S(2)}, u32[]{:S(2)}) collective-permute-start(bf16[4,128,96]{1,0,2:T(4,128)(2,1)S(1)} %convolution_convert_fusion.17), channel_id=1, source_target_pairs={{0,3},{4,7},{8,11},{12,15},{16,19},{20,23},{24,27},{28,31},{32,35}... | collective-permute-start | bytes 294920 | tf_op jit(solution)/shard_map/ppermute | solution.py:52
  159.5 20.5 %all-to-all-start.3 = ((bf16[32,128,96]{1,2,0:T(8,128)(2,1)}), bf16[32,128,96]{1,2,0:T(8,128)(2,1)S(1)}, u32[]{:S(2)}, u32[]{:S(2)}) async-start(bf16[32,128,96]{1,2,0:T(8,128)(2,1)} %copy.42), calls=%async_computation.3 | async-start | bytes 1572864 | tf_op jit(solution)/shard_map/all_to_all | solution.py:60
  165.8 14.5 %collective-permute-start.18 = (bf16[768,96]{0,1:T(8,128)(2,1)S(1)}, bf16[768,96]{0,1:T(8,128)(2,1)S(1)}, u32[]{:S(2)}, u32[]{:S(2)}) collective-permute-start(bf16[768,96]{0,1:T(8,128)(2,1)S(1)} %get-tuple-element.30), channel_id=1, source_target_pairs={{2,0},{6,4},{10,8},{14,12},{18,16},{22,20},{26,24},{30,28},{34,32}... | collective-permute-start | bytes 442376 | tf_op jit(solution)/shard_map/ppermute | solution.py:41
  167.1 13.2 %collective-permute-start.19 = (bf16[768,96]{0,1:T(8,128)(2,1)S(1)}, bf16[768,96]{0,1:T(8,128)(2,1)S(1)}, u32[]{:S(2)}, u32[]{:S(2)}) collective-permute-start(bf16[768,96]{0,1:T(8,128)(2,1)S(1)} %get-tuple-element.29), channel_id=1, source_target_pairs={{2,1},{6,5},{10,9},{14,13},{18,17},{22,21},{26,25},{30,29},{34,33}... | collective-permute-start | bytes 442376 | tf_op jit(solution)/shard_map/ppermute | solution.py:41
  167.8 12.6 %collective-permute-start.20 = (bf16[768,96]{0,1:T(8,128)(2,1)S(1)}, bf16[768,96]{0,1:T(8,128)(2,1)}, u32[]{:S(2)}, u32[]{:S(2)}) collective-permute-start(bf16[768,96]{0,1:T(8,128)(2,1)S(1)} %get-tuple-element.31), channel_id=1, source_target_pairs={{2,3},{6,7},{10,11},{14,15},{18,19},{22,23},{26,27},{30,31},{34,35... | collective-permute-start | bytes 442376 | tf_op jit(solution)/shard_map/ppermute | solution.py:41
  185.8 18.2 %all-to-all-start.4 = ((bf16[32,128,96]{1,2,0:T(8,128)(2,1)}), bf16[32,128,96]{1,2,0:T(8,128)(2,1)S(1)}, u32[]{:S(2)}, u32[]{:S(2)}) async-start(bf16[32,128,96]{1,2,0:T(8,128)(2,1)} %copy.46), calls=%async_computation.4 | async-start | bytes 1572864 | tf_op jit(solution)/shard_map/all_to_all | solution.py:60
  189.8 14.5 %collective-permute-start.27 = (bf16[768,96]{0,1:T(8,128)(2,1)S(1)}, bf16[768,96]{0,1:T(8,128)(2,1)S(1)}, u32[]{:S(2)}, u32[]{:S(2)}) collective-permute-start(bf16[768,96]{0,1:T(8,128)(2,1)S(1)} %get-tuple-element.26), channel_id=1, source_target_pairs={{1,0},{5,4},{9,8},{13,12},{17,16},{21,20},{25,24},{29,28},{33,32},... | collective-permute-start | bytes 442376 | tf_op jit(solution)/shard_map/ppermute | solution.py:41
  191.1 13.2 %collective-permute-start.28 = (bf16[768,96]{0,1:T(8,128)(2,1)S(1)}, bf16[768,96]{0,1:T(8,128)(2,1)}, u32[]{:S(2)}, u32[]{:S(2)}) collective-permute-start(bf16[768,96]{0,1:T(8,128)(2,1)S(1)} %get-tuple-element.27), channel_id=1, source_target_pairs={{1,2},{5,6},{9,10},{13,14},{17,18},{21,22},{25,26},{29,30},{33,34}... | collective-permute-start | bytes 442376 | tf_op jit(solution)/shard_map/ppermute | solution.py:41
  192.5 11.9 %collective-permute-start.29 = (bf16[768,96]{0,1:T(8,128)(2,1)S(1)}, bf16[768,96]{0,1:T(8,128)(2,1)}, u32[]{:S(2)}, u32[]{:S(2)}) collective-permute-start(bf16[768,96]{0,1:T(8,128)(2,1)S(1)} %get-tuple-element.28), channel_id=1, source_target_pairs={{1,3},{5,7},{9,11},{13,15},{17,19},{21,23},{25,27},{29,31},{33,35}... | collective-permute-start | bytes 442376 | tf_op jit(solution)/shard_map/ppermute | solution.py:41
  209.9 18.2 %all-to-all-start.5 = ((bf16[32,128,96]{1,2,0:T(8,128)(2,1)}), bf16[32,128,96]{1,2,0:T(8,128)(2,1)S(1)}, u32[]{:S(2)}, u32[]{:S(2)}) async-start(bf16[32,128,96]{1,2,0:T(8,128)(2,1)} %copy.50), calls=%async_computation.5 | async-start | bytes 1572864 | tf_op jit(solution)/shard_map/all_to_all | solution.py:60
  214.6 14.5 %collective-permute-start.33 = (bf16[768,96]{0,1:T(8,128)(2,1)S(1)}, bf16[768,96]{0,1:T(8,128)(2,1)}, u32[]{:S(2)}, u32[]{:S(2)}) collective-permute-start(bf16[768,96]{0,1:T(8,128)(2,1)S(1)} %get-tuple-element.23), channel_id=1, source_target_pairs={{0,1},{4,5},{8,9},{12,13},{16,17},{20,21},{24,25},{28,29},{32,33},... | collective-permute-start | bytes 442376 | tf_op jit(solution)/shard_map/ppermute | solution.py:41
  218.9 10.9 %collective-permute-start.34 = (bf16[768,96]{0,1:T(8,128)(2,1)}, bf16[768,96]{0,1:T(8,128)(2,1)}, u32[]{:S(2)}, u32[]{:S(2)}) collective-permute-start(bf16[768,96]{0,1:T(8,128)(2,1)} %get-tuple-element.25), channel_id=1, source_target_pairs={{0,2},{4,6},{8,10},{12,14},{16,18},{20,22},{24,26},{28,30},{32,34}... | collective-permute-start | bytes 442376 | tf_op jit(solution)/shard_map/ppermute | solution.py:41
  222.2 11.2 %collective-permute-start.35 = (bf16[768,96]{0,1:T(8,128)(2,1)S(1)}, bf16[768,96]{0,1:T(8,128)(2,1)}, u32[]{:S(2)}, u32[]{:S(2)}) collective-permute-start(bf16[768,96]{0,1:T(8,128)(2,1)S(1)} %get-tuple-element.24), channel_id=1, source_target_pairs={{0,3},{4,7},{8,11},{12,15},{16,19},{20,23},{24,27},{28,31},{32,35}... | collective-permute-start | bytes 442376 | tf_op jit(solution)/shard_map/ppermute | solution.py:41
  224.2 12.3 %collective-permute-start.24 = (bf16[768,96]{0,1:T(8,128)(2,1)S(1)}, bf16[768,96]{0,1:T(8,128)(2,1)S(1)}, u32[]{:S(2)}, u32[]{:S(2)}) collective-permute-start(bf16[768,96]{0,1:T(8,128)(2,1)S(1)} %bitcast.241), channel_id=1, source_target_pairs={{0,2},{4,6},{8,10},{12,14},{16,18},{20,22},{24,26},{28,30},{32,34}... | collective-permute-start | bytes 442376 | tf_op jit(solution)/shard_map/ppermute | solution.py:52
  225.5 11.7 %collective-permute-start.25 = (bf16[768,96]{0,1:T(8,128)(2,1)S(1)}, bf16[768,96]{0,1:T(8,128)(2,1)S(1)}, u32[]{:S(2)}, u32[]{:S(2)}) collective-permute-start(bf16[768,96]{0,1:T(8,128)(2,1)S(1)} %bitcast.242), channel_id=1, source_target_pairs={{1,2},{5,6},{9,10},{13,14},{17,18},{21,22},{25,26},{29,30},{33,34}... | collective-permute-start | bytes 442376 | tf_op jit(solution)/shard_map/ppermute | solution.py:52
  229.1 9.4 %collective-permute-start.26 = (bf16[768,96]{0,1:T(8,128)(2,1)S(1)}, bf16[768,96]{0,1:T(8,128)(2,1)S(1)}, u32[]{:S(2)}, u32[]{:S(2)}) collective-permute-start(bf16[768,96]{0,1:T(8,128)(2,1)S(1)} %bitcast.243), channel_id=1, source_target_pairs={{3,2},{7,6},{11,10},{15,14},{19,18},{23,22},{27,26},{31,30},{35,34... | collective-permute-start | bytes 442376 | tf_op jit(solution)/shard_map/ppermute | solution.py:52
  229.8 10.0 %collective-permute-start.30 = (bf16[768,96]{0,1:T(8,128)(2,1)S(1)}, bf16[768,96]{0,1:T(8,128)(2,1)S(1)}, u32[]{:S(2)}, u32[]{:S(2)}) collective-permute-start(bf16[768,96]{0,1:T(8,128)(2,1)S(1)} %bitcast.245), channel_id=1, source_target_pairs={{0,1},{4,5},{8,9},{12,13},{16,17},{20,21},{24,25},{28,29},{32,33},... | collective-permute-start | bytes 442376 | tf_op jit(solution)/shard_map/ppermute | solution.py:52
  239.8 11.1 %collective-permute-start.38 = (bf16[768,96]{0,1:T(8,128)(2,1)S(1)}, bf16[768,96]{0,1:T(8,128)(2,1)S(1)}, u32[]{:S(2)}, u32[]{:S(2)}) collective-permute-start(bf16[768,96]{0,1:T(8,128)(2,1)S(1)} %fusion.21), channel_id=1, source_target_pairs={{3,0},{7,4},{11,8},{15,12},{19,16},{23,20},{27,24},{31,28},{35,32}... | collective-permute-start | bytes 442376 | tf_op jit(solution)/shard_map/ppermute | solution.py:52
  (39 other events, 325.7 us)
Sparse Core Ops, SparseCore 0:
  9.7 42.7 all-gather.6
  54.1 55.7 all-gather.8
  111.6 44.1 all-gather.10

commit v4 on v3

--- a/solution.py
+++ b/solution.py
@@ -51,6 +51,22 @@
         else:
             parts.append(lax.ppermute(routed, "lvl", [(r, dst_row)]))
     return jnp.concatenate(parts, axis=-1)
+
+
+def shift(array, by, row_count):
+    return lax.ppermute(array, "lvl", [(i, (i + by) % row_count) for i in range(row_count)])
+
+
+def one_hot_rows(index, count, dtype):
+    return (jnp.arange(count, dtype=jnp.int32) == index).astype(dtype)
+
+
+def blocks_of(level_blocks, my_row, by, row_count):
+    wanted = lax.rem(my_row + by, row_count)
+    chosen = level_blocks[0]
+    for t in range(1, len(level_blocks)):
+        chosen = jnp.where(wanted == t, level_blocks[t], chosen)
+    return chosen
 
 
 def route(piece, send_to, take_from, block_count):
@@ -84,8 +100,33 @@
     def keep_of(t):
         return (lanes[None, :] < mine_rank[t][:, None]).astype(jnp.float32)
 
+    last = level_count - 1
+    tile_count, block_rows, _ = left_here.shape
+    columns = rhs_here.shape[-1]
+    width = columns // row_count
+    flat = tile_count * rank_width
+    packed = jnp.concatenate(
+        [
+            inverse_here,
+            right_here.transpose(1, 0, 2).reshape(block_rows, flat),
+            left_here.transpose(1, 0, 2).reshape(block_rows, flat),
+        ],
+        axis=1,
+    )
+    shifted = [packed] + [shift(packed, d, row_count) for d in range(1, row_count)]
+
+    def level_data(t):
+        pick = lax.rem(my_row - t + row_count, row_count)
+        data = shifted[row_count - 1]
+        for d in reversed(range(row_count - 1)):
+            data = jnp.where(pick == d, shifted[d], data)
+        return (
+            data[:, :block_rows],
+            data[:, block_rows:block_rows + flat],
+            data[:, block_rows + flat:],
+        )
+
     solved = jnp.zeros(rhs_here.shape, jnp.bfloat16)
-    own_blocks = []
     incoming = None
     for t in range(level_count):
         current = rhs_here.astype(jnp.float32)
@@ -100,49 +141,63 @@
         ).astype(jnp.bfloat16)
         solved = jnp.where(my_row == t, result, solved)
         if t + 1 < level_count:
-            own_blocks.append(spread(result, t, row_count, my_row))
             out = jnp.einsum(
                 "kbr,bn->krn", right_here, result, preferred_element_type=jnp.float32
             ).astype(jnp.bfloat16)
             piece = spread(out, t, row_count, my_row)
             routed = route(piece, mine_target[t + 1], mine_src[t + 1], block_count)
             incoming = collect(routed, t + 1, row_count)
-
-    last = level_count - 1
-    width = rhs_here.shape[-1] // row_count
-    inverse_all = lax.all_gather(inverse_here, "lvl")
-    right_all = lax.all_gather(right_here, "lvl")
-    left_all = lax.all_gather(left_here, "lvl")
-
-    result = jnp.einsum(
+        if t == last - 1:
+            by_block = solved.reshape(block_rows, row_count, width)
+            sent = [by_block[:, 0, :] * 0]
+            for d in range(1, row_count):
+                wanted = lax.rem(my_row + d, row_count)
+                part = jnp.sum(
+                    by_block * one_hot_rows(wanted, row_count, by_block.dtype)[None, :, None], axis=1
+                ).astype(by_block.dtype)
+                sent.append(shift(part, d, row_count))
+            own = jnp.sum(
+                by_block * one_hot_rows(my_row, row_count, by_block.dtype)[None, :, None], axis=1
+            ).astype(by_block.dtype)
+
+    def forward_block(t):
+        pick = lax.rem(my_row - t + row_count, row_count)
+        block = own
+        for d in range(1, row_count):
+            block = jnp.where(pick == d, sent[d], block)
+        return block
+
+    top = jnp.einsum(
         "ba,bn->an", inverse_here, solved, preferred_element_type=jnp.float32
     ).astype(jnp.bfloat16)
-    top = result
-    projected = jnp.einsum(
-        "kbr,bn->krn", left_here, result, preferred_element_type=jnp.float32
-    )
+    projected = jnp.einsum("kbr,bn->krn", left_here, top, preferred_element_type=jnp.float32)
     out = (projected * keep_of(last)[..., None]).astype(jnp.bfloat16)
     piece = spread(out, last, row_count, my_row)
     returning = route(piece, mine_src[last], mine_target[last], block_count)
     blocks = [None] * level_count
     for t in reversed(range(last)):
-        current = own_blocks[t].astype(jnp.float32) - jnp.einsum(
-            "kbr,krn->bn", right_all[t], returning, preferred_element_type=jnp.float32
+        inverse_t, right_t, left_t = level_data(t)
+        current = forward_block(t).astype(jnp.float32) - jnp.dot(
+            right_t, returning.reshape(flat, width), preferred_element_type=jnp.float32
         )
         upper = current.astype(jnp.bfloat16)
         result = jnp.einsum(
-            "ba,bn->an", inverse_all[t], upper, preferred_element_type=jnp.float32
+            "ba,bn->an", inverse_t, upper, preferred_element_type=jnp.float32
         ).astype(jnp.bfloat16)
         blocks[t] = result
         if t > 0:
             projected = jnp.einsum(
-                "kbr,bn->krn", left_all[t], result, preferred_element_type=jnp.float32
-            )
+                "bm,bn->mn", left_t, result, preferred_element_type=jnp.float32
+            ).reshape(tile_count, rank_width, width)
             out = (projected * keep_of(t)[..., None]).astype(jnp.bfloat16)
             returning = route(out, mine_src[t], mine_target[t], block_count)
-    answer = top
-    for t in range(last):
-        answer = jnp.where(my_row == t, collect(blocks[t], t, row_count), answer)
+    mine_blocks = blocks[:last] + [jnp.zeros_like(blocks[0])]
+    placed = one_hot_rows(my_row, row_count, jnp.bfloat16)[None, :, None] * blocks_of(mine_blocks, my_row, 0, row_count)[:, None, :]
+    for d in range(1, row_count):
+        got = shift(blocks_of(mine_blocks, my_row, d, row_count), d, row_count)
+        origin = lax.rem(my_row - d + row_count, row_count)
+        placed = placed + one_hot_rows(origin, row_count, jnp.bfloat16)[None, :, None] * got[:, None, :]
+    answer = jnp.where(my_row == last, top, placed.reshape(block_rows, columns))
     return (solved[None, None], answer[None, None])
 
 

time: 260 us -> 359 us (1.38)
  waiting for transfers between devices: 56.7 us -> 170 us
  blocking collectives: 63.3 us -> 41.5 us
  other arithmetic: 7.99 us -> 25.4 us
  between operations: 14.6 us -> 1.54 us
  starting transfers between devices: 76.3 us -> 68.5 us
  local copies, waits for them, and re-layouts: 9.48 us -> 15.3 us
  matrix products: 30.4 us -> 35 us
    ppermute x18 -> x9, waiting for transfers between devices: 17.3 us -> 110 us  [collect(): parts.append(lax.ppermute(routed, 'lvl', [(r, dst_row)]))]
    all_to_all x3 -> x2, blocking collectives: 63.3 us -> 41.5 us  [route(): lax.all_to_all(holder, 'blk', split_axis=0, concat_axis=0, tiled=True)]
    ppermute x21 -> x12, starting transfers between devices: 33.4 us -> 16.6 us  [spread(): got = lax.ppermute(part, 'lvl', [(src_row, r)])]
    all_to_all x3 -> x4, waiting for transfers between devices: 23.1 us -> 36.9 us  [route(): lax.all_to_all(holder, 'blk', split_axis=0, concat_axis=0, tiled=True)]
    ppermute x18 -> x9, starting transfers between devices: 28.6 us -> 18.3 us  [collect(): parts.append(lax.ppermute(routed, 'lvl', [(r, dst_row)]))]
    select_n x0 -> x3, other arithmetic: none -> 10.1 us  [the longest x2 9.79 us: level_data(): data = jnp.where(pick == d, shifted[d], data)]
    ppermute x0 -> x9, starting transfers between devices: none -> 9.95 us  [shift(): lax.ppermute(array, 'lvl', [(i, (i + by) % row_count) for i in range(row_...]
    all_to_all x3 -> x4, starting transfers between devices: 14.2 us -> 23.7 us  [route(): lax.all_to_all(holder, 'blk', split_axis=0, concat_axis=0, tiled=True)]
  transfers between devices with their start and end apart: 45 -> 34, of which waited for: 11 -> 11; matrix products, arithmetic and copies ran while one was open for 14% -> 11% of each run, Pallas kernels for 0% -> 0%
where the time goes in v4:
time: 359 us; the launch traced here: 358 us
  waiting for transfers between devices  170 us (47%)
  starting transfers between devices  68.5 us (19%)
  blocking collectives  41.5 us (12%)
  matrix products  35 us (10%)
  other arithmetic  25.4 us (7%)
  local copies, waits for them, and re-layouts  15.3 us (4%)
    ppermute x9, waiting for transfers between devices, collect(): parts.append(lax.ppermute(routed, 'lvl', [(r, dst_row)]))  110 us
    all_to_all x2, blocking collectives, route(): lax.all_to_all(holder, 'blk', split_axis=0, concat_axis=0, tiled=True)  41.5 us
    all_to_all x4, waiting for transfers between devices, route(): lax.all_to_all(holder, 'blk', split_axis=0, concat_axis=0, tiled=True)  36.9 us
    all_to_all x4, starting transfers between devices, route(): lax.all_to_all(holder, 'blk', split_axis=0, concat_axis=0, tiled=True)  23.7 us
    ppermute x9, starting transfers between devices, collect(): parts.append(lax.ppermute(routed, 'lvl', [(r, dst_row)]))  18.3 us
    ppermute x12, waiting for transfers between devices, spread(): got = lax.ppermute(part, 'lvl', [(src_row, r)])  17.8 us
    ppermute x12, starting transfers between devices, spread(): got = lax.ppermute(part, 'lvl', [(src_row, r)])  16.6 us
    dot_general x4, matrix products, local(): jnp.einsum('ab,bn->an', inverse_here, lowered, preferred_element_type=jnp...  11.9 us
  transfers between devices with their start and end apart: 34, of which 11 were waited for; matrix products, arithmetic and copies ran while one was open for 11% of the time, Pallas kernels for 0%

profile of v4, /device:TPU:1, one launch (start us, length us, event | category | flops | bytes accessed | tf_op | source)
XLA Modules:
  0.0 357.7 jit_solution(1871397093726965536)
XLA Ops:
  3.4 3.9 %collective-permute-start = (bf16[4,128,96]{1,2,0:T(8,128)(2,1)S(1)}, bf16[4,128,96]{1,2,0:T(8,128)(2,1)S(1)}, u32[]{:S(2)}, u32[]{:S(2)}) collective-permute-start(bf16[4,128,96]{1,2,0:T(8,128)(2,1)S(1)} %get-tuple-element.44), channel_id=1, source_target_pairs={{0,1},{4,5},{8,9},{12,13},{16,17},{20,21},{24,25},{28,29},{32,33},... | collective-permute-start | bytes 294920 | tf_op jit(solution)/shard_map/ppermute | solution.py:41
  14.7 23.2 %all_to_all.30 = bf16[32,128,96]{1,2,0:T(8,128)(2,1)S(1)} all-to-all(bf16[32,128,96]{1,2,0:T(8,128)(2,1)S(1)} %copy.76), channel_id=1, replica_groups=mesh['blk'=32,'lvl'=4] {'blk'}, dimensions={0} | all-to-all | bytes 1572864 | tf_op jit(solution)/shard_map/all_to_all | solution.py:76
  53.5 4.3 %collective-permute-done.6 = bf16[4,128,96]{1,2,0:T(8,128)(2,1)S(1)} collective-permute-done((bf16[4,128,96]{1,2,0:T(8,128)(2,1)S(1)}, bf16[4,128,96]{1,2,0:T(8,128)(2,1)S(1)}, u32[]{:S(2)}, u32[]{:S(2)}) %collective-permute-start.6) | collective-permute-done | bytes 98336 | tf_op jit(solution)/shard_map/ppermute | solution.py:41
  59.6 18.3 %all_to_all.31 = bf16[32,128,96]{1,2,0:T(8,128)(2,1)S(1)} all-to-all(bf16[32,128,96]{1,2,0:T(8,128)(2,1)S(1)} %copy.83), channel_id=1, replica_groups=mesh['blk'=32,'lvl'=4] {'blk'}, dimensions={0} | all-to-all | bytes 1572864 | tf_op jit(solution)/shard_map/all_to_all | solution.py:76
  80.2 6.4 %collective-permute-start.9 = (bf16[4,128,96]{1,0,2:T(4,128)(2,1)S(1)}, bf16[4,128,96]{1,0,2:T(4,128)(2,1)}, u32[]{:S(2)}, u32[]{:S(2)}) collective-permute-start(bf16[4,128,96]{1,0,2:T(4,128)(2,1)S(1)} %convolution_convert_fusion.18), channel_id=1, source_target_pairs={{0,2},{4,6},{8,10},{12,14},{16,18},{20,22},{24,26},{28,30},{32,34}... | collective-permute-start | bytes 294920 | tf_op jit(solution)/shard_map/ppermute | solution.py:52
  90.2 3.4 fusion.57
  97.8 4.3 %collective-permute-done.12 = bf16[4,128,96]{1,2,0:T(8,128)(2,1)S(1)} collective-permute-done((bf16[4,128,96]{1,2,0:T(8,128)(2,1)S(1)}, bf16[4,128,96]{1,2,0:T(8,128)(2,1)S(1)}, u32[]{:S(2)}, u32[]{:S(2)}) %collective-permute-start.12) | collective-permute-done | bytes 98336 | tf_op jit(solution)/shard_map/ppermute | solution.py:41
  103.8 5.5 %all-to-all-start.2 = ((bf16[32,128,96]{1,2,0:T(8,128)(2,1)}), bf16[32,128,96]{1,2,0:T(8,128)(2,1)S(1)}, u32[]{:S(2)}, u32[]{:S(2)}) async-start(bf16[32,128,96]{1,2,0:T(8,128)(2,1)} %copy.89), calls=%async_computation.2 | async-start | bytes 1572864 | tf_op jit(solution)/shard_map/all_to_all | solution.py:76
  116.3 3.1 collective-permute-start.19
  119.4 4.2 %all-to-all-done.2 = bf16[32,128,96]{1,2,0:T(8,128)(2,1)S(1)} async-done(((bf16[32,128,96]{1,2,0:T(8,128)(2,1)}), bf16[32,128,96]{1,2,0:T(8,128)(2,1)S(1)}, u32[]{:S(2)}, u32[]{:S(2)}) %all-to-all-start.2) | async-done | bytes 786464 | tf_op jit(solution)/shard_map/all_to_all | solution.py:76
  125.2 4.8 %collective-permute-start.15 = (bf16[4,128,96]{1,0,2:T(4,128)(2,1)}, bf16[4,128,96]{1,0,2:T(4,128)(2,1)S(1)}, u32[]{:S(2)}, u32[]{:S(2)}) collective-permute-start(bf16[4,128,96]{1,0,2:T(4,128)(2,1)} %convolution_convert_fusion.17), channel_id=1, source_target_pairs={{0,3},{4,7},{8,11},{12,15},{16,19},{20,23},{24,27},{28,31},{32,35}... | collective-permute-start | bytes 294920 | tf_op jit(solution)/shard_map/ppermute | solution.py:52
  131.9 109.5 %collective-permute-done.15 = bf16[4,128,96]{1,0,2:T(4,128)(2,1)S(1)} collective-permute-done((bf16[4,128,96]{1,0,2:T(4,128)(2,1)}, bf16[4,128,96]{1,0,2:T(4,128)(2,1)S(1)}, u32[]{:S(2)}, u32[]{:S(2)}) %collective-permute-start.15) | collective-permute-done | bytes 98336 | tf_op jit(solution)/shard_map/ppermute | solution.py:52
  244.5 3.5 fusion.5
  252.6 9.2 %collective-permute-done.24 = bf16[4,128,96]{1,2,0:T(8,128)(2,1)S(1)} collective-permute-done((bf16[4,128,96]{1,2,0:T(8,128)(2,1)S(1)}, bf16[4,128,96]{1,2,0:T(8,128)(2,1)S(1)}, u32[]{:S(2)}, u32[]{:S(2)}) %collective-permute-start.24) | collective-permute-done | bytes 98336 | tf_op jit(solution)/shard_map/ppermute | solution.py:41
  264.0 2.9 collective-permute-start.22
  268.6 10.3 %all-to-all-start.3 = ((bf16[32,128,96]{1,2,0:T(8,128)(2,1)}), bf16[32,128,96]{1,2,0:T(8,128)(2,1)S(1)}, u32[]{:S(2)}, u32[]{:S(2)}) async-start(bf16[32,128,96]{1,2,0:T(8,128)(2,1)} %copy.97), calls=%async_computation.3 | async-start | bytes 1572864 | tf_op jit(solution)/shard_map/all_to_all | solution.py:76
  279.1 3.8 %select_select_fusion.2 = bf16[768,1792]{1,0:T(8,128)(2,1)} fusion(bf16[768,1792]{1,0:T(8,128)(2,1)} %collective-permute-done.18, bf16[768,1792]{1,0:T(8,128)(2,1)} %collective-permute-done.19, bf16[768,1792]{1,0:T(8,128)(2,1)} %collective-permute-done.20, pred[]{:T(512)S(6)} %eq.478, pred[]{:T(512)S(6)} %eq.477, pred[]{:T(512)S(6)} %eq.476, ...), kind=kLoop, calls=%fused_computation.3 | loop fusion | flops 12386304 | bytes 13762563 | tf_op jit(solution)/shard_map/jit(_where)/select_n | solution.py:122
  282.9 10.3 %all-to-all-done.3 = bf16[32,128,96]{1,2,0:T(8,128)(2,1)S(1)} async-done(((bf16[32,128,96]{1,2,0:T(8,128)(2,1)}), bf16[32,128,96]{1,2,0:T(8,128)(2,1)S(1)}, u32[]{:S(2)}, u32[]{:S(2)}) %all-to-all-start.3) | async-done | bytes 786464 | tf_op jit(solution)/shard_map/all_to_all | solution.py:76
  301.0 3.8 %all-to-all-start.4 = ((bf16[32,128,96]{1,2,0:T(8,128)(2,1)}), bf16[32,128,96]{1,2,0:T(8,128)(2,1)S(1)}, u32[]{:S(2)}, u32[]{:S(2)}) async-start(bf16[32,128,96]{1,2,0:T(8,128)(2,1)} %copy.99), calls=%async_computation.4 | async-start | bytes 1572864 | tf_op jit(solution)/shard_map/all_to_all | solution.py:76
  304.8 6.0 %select_select_fusion = (bf16[768,1792]{1,0:T(8,128)(2,1)}, bf16[768,1792]{1,0:T(8,128)(2,1)}) fusion(bf16[768,1792]{1,0:T(8,128)(2,1)} %collective-permute-done.18, bf16[768,1792]{1,0:T(8,128)(2,1)} %collective-permute-done.19, bf16[768,1792]{1,0:T(8,128)(2,1)} %collective-permute-done.20, pred[]{:T(512)S(6)} %eq.493, pred[]{:T(512)S(6)} %eq.492, ...), kind=kLoop, calls=%fused_computation.1 | loop fusion | flops 16515072 | bytes 16515078 | tf_op jit(solution)/shard_map/jit(_where)/select_n | solution.py:122
  310.8 8.2 %all-to-all-done.4 = bf16[32,128,96]{1,2,0:T(8,128)(2,1)S(1)} async-done(((bf16[32,128,96]{1,2,0:T(8,128)(2,1)}), bf16[32,128,96]{1,2,0:T(8,128)(2,1)S(1)}, u32[]{:S(2)}, u32[]{:S(2)}) %all-to-all-start.4) | async-done | bytes 786464 | tf_op jit(solution)/shard_map/all_to_all | solution.py:76
  324.9 4.1 %all-to-all-start.5 = ((bf16[32,128,96]{1,2,0:T(8,128)(2,1)}), bf16[32,128,96]{1,2,0:T(8,128)(2,1)S(1)}, u32[]{:S(2)}, u32[]{:S(2)}) async-start(bf16[32,128,96]{1,2,0:T(8,128)(2,1)} %copy.101), calls=%async_computation.5 | async-start | bytes 1572864 | tf_op jit(solution)/shard_map/all_to_all | solution.py:76
  329.0 14.2 %all-to-all-done.5 = bf16[32,128,96]{1,2,0:T(8,128)(2,1)S(1)} async-done(((bf16[32,128,96]{1,2,0:T(8,128)(2,1)}), bf16[32,128,96]{1,2,0:T(8,128)(2,1)S(1)}, u32[]{:S(2)}, u32[]{:S(2)}) %all-to-all-start.5) | async-done | bytes 786464 | tf_op jit(solution)/shard_map/all_to_all | solution.py:76
  350.4 5.5 %collective-permute-done.27 = bf16[768,96]{0,1:T(8,128)(2,1)S(1)} collective-permute-done((bf16[768,96]{0,1:T(8,128)(2,1)S(1)}, bf16[768,96]{0,1:T(8,128)(2,1)S(1)}, u32[]{:S(2)}, u32[]{:S(2)}) %collective-permute-start.27) | collective-permute-done | bytes 147488 | tf_op jit(solution)/shard_map/ppermute | solution.py:57
  (196 shorter events, 83.6 us)
Async XLA Ops:
  3.4 10.0 %collective-permute-start = (bf16[4,128,96]{1,2,0:T(8,128)(2,1)S(1)}, bf16[4,128,96]{1,2,0:T(8,128)(2,1)S(1)}, u32[]{:S(2)}, u32[]{:S(2)}) collective-permute-start(bf16[4,128,96]{1,2,0:T(8,128)(2,1)S(1)} %get-tuple-element.44), channel_id=1, source_target_pairs={{0,1},{4,5},{8,9},{12,13},{16,17},{20,21},{24,25},{28,29},{32,33},... | collective-permute-start | bytes 294920 | tf_op jit(solution)/shard_map/ppermute | solution.py:41
  49.6 8.2 %collective-permute-start.6 = (bf16[4,128,96]{1,2,0:T(8,128)(2,1)S(1)}, bf16[4,128,96]{1,2,0:T(8,128)(2,1)S(1)}, u32[]{:S(2)}, u32[]{:S(2)}) collective-permute-start(bf16[4,128,96]{1,2,0:T(8,128)(2,1)S(1)} %get-tuple-element.41), channel_id=1, source_target_pairs={{1,0},{5,4},{9,8},{13,12},{17,16},{21,20},{25,24},{29,28},{33,32},... | collective-permute-start | bytes 294920 | tf_op jit(solution)/shard_map/ppermute | solution.py:41
  50.9 6.9 %collective-permute-start.7 = (bf16[4,128,96]{1,2,0:T(8,128)(2,1)S(1)}, bf16[4,128,96]{1,2,0:T(8,128)(2,1)}, u32[]{:S(2)}, u32[]{:S(2)}) collective-permute-start(bf16[4,128,96]{1,2,0:T(8,128)(2,1)S(1)} %get-tuple-element.43), channel_id=1, source_target_pairs={{1,2},{5,6},{9,10},{13,14},{17,18},{21,22},{25,26},{29,30},{33,34}... | collective-permute-start | bytes 294920 | tf_op jit(solution)/shard_map/ppermute | solution.py:41
  78.2 9.6 %collective-permute-start.10 = (bf16[4,128,96]{1,0,2:T(4,128)(2,1)S(1)}, bf16[4,128,96]{1,0,2:T(4,128)(2,1)S(1)}, u32[]{:S(2)}, u32[]{:S(2)}) collective-permute-start(bf16[4,128,96]{1,0,2:T(4,128)(2,1)S(1)} %convolution_convert_fusion.18), channel_id=1, source_target_pairs={{1,2},{5,6},{9,10},{13,14},{17,18},{21,22},{25,26},{29,30},{33,34}... | collective-permute-start | bytes 294920 | tf_op jit(solution)/shard_map/ppermute | solution.py:52
  78.9 9.0 %collective-permute-start.11 = (bf16[4,128,96]{1,0,2:T(4,128)(2,1)S(1)}, bf16[4,128,96]{1,0,2:T(4,128)(2,1)}, u32[]{:S(2)}, u32[]{:S(2)}) collective-permute-start(bf16[4,128,96]{1,0,2:T(4,128)(2,1)S(1)} %convolution_convert_fusion.18), channel_id=1, source_target_pairs={{3,2},{7,6},{11,10},{15,14},{19,18},{23,22},{27,26},{31,30},{35,34... | collective-permute-start | bytes 294920 | tf_op jit(solution)/shard_map/ppermute | solution.py:52
  80.2 8.0 %collective-permute-start.9 = (bf16[4,128,96]{1,0,2:T(4,128)(2,1)S(1)}, bf16[4,128,96]{1,0,2:T(4,128)(2,1)}, u32[]{:S(2)}, u32[]{:S(2)}) collective-permute-start(bf16[4,128,96]{1,0,2:T(4,128)(2,1)S(1)} %convolution_convert_fusion.18), channel_id=1, source_target_pairs={{0,2},{4,6},{8,10},{12,14},{16,18},{20,22},{24,26},{28,30},{32,34}... | collective-permute-start | bytes 294920 | tf_op jit(solution)/shard_map/ppermute | solution.py:52
  95.2 6.9 %collective-permute-start.12 = (bf16[4,128,96]{1,2,0:T(8,128)(2,1)S(1)}, bf16[4,128,96]{1,2,0:T(8,128)(2,1)S(1)}, u32[]{:S(2)}, u32[]{:S(2)}) collective-permute-start(bf16[4,128,96]{1,2,0:T(8,128)(2,1)S(1)} %get-tuple-element.40), channel_id=1, source_target_pairs={{2,0},{6,4},{10,8},{14,12},{18,16},{22,20},{26,24},{30,28},{34,32}... | collective-permute-start | bytes 294920 | tf_op jit(solution)/shard_map/ppermute | solution.py:41
  103.8 19.7 %all-to-all-start.2 = ((bf16[32,128,96]{1,2,0:T(8,128)(2,1)}), bf16[32,128,96]{1,2,0:T(8,128)(2,1)S(1)}, u32[]{:S(2)}, u32[]{:S(2)}) async-start(bf16[32,128,96]{1,2,0:T(8,128)(2,1)} %copy.89), calls=%async_computation.2 | async-start | bytes 1572864 | tf_op jit(solution)/shard_map/all_to_all | solution.py:76
  115.4 163.6 %collective-permute-start.18 = (bf16[768,1792]{1,0:T(8,128)(2,1)}, bf16[768,1792]{1,0:T(8,128)(2,1)}, u32[]{:S(2)}, u32[]{:S(2)}) collective-permute-start(bf16[768,1792]{1,0:T(8,128)(2,1)} %pad_maximum_fusion), channel_id=1, source_target_pairs={{0,1},{1,2},{2,3},{3,0},{4,5},{5,6},{6,7},{7,4},{8,9},{9,10},{10,1... | collective-permute-start | bytes 8257544 | tf_op jit(solution)/shard_map/ppermute | solution.py:57
  116.3 162.8 %collective-permute-start.19 = (bf16[768,1792]{1,0:T(8,128)(2,1)}, bf16[768,1792]{1,0:T(8,128)(2,1)}, u32[]{:S(2)}, u32[]{:S(2)}) collective-permute-start(bf16[768,1792]{1,0:T(8,128)(2,1)} %pad_maximum_fusion), channel_id=1, source_target_pairs={{0,2},{1,3},{2,0},{3,1},{4,6},{5,7},{6,4},{7,5},{8,10},{9,11},{10,... | collective-permute-start | bytes 8257544 | tf_op jit(solution)/shard_map/ppermute | solution.py:57
  119.4 159.7 %collective-permute-start.20 = (bf16[768,1792]{1,0:T(8,128)(2,1)}, bf16[768,1792]{1,0:T(8,128)(2,1)}, u32[]{:S(2)}, u32[]{:S(2)}) collective-permute-start(bf16[768,1792]{1,0:T(8,128)(2,1)} %pad_maximum_fusion), channel_id=1, source_target_pairs={{0,3},{1,0},{2,1},{3,2},{4,7},{5,4},{6,5},{7,6},{8,11},{9,8},{10,9... | collective-permute-start | bytes 8257544 | tf_op jit(solution)/shard_map/ppermute | solution.py:57
  125.2 116.2 %collective-permute-start.15 = (bf16[4,128,96]{1,0,2:T(4,128)(2,1)}, bf16[4,128,96]{1,0,2:T(4,128)(2,1)S(1)}, u32[]{:S(2)}, u32[]{:S(2)}) collective-permute-start(bf16[4,128,96]{1,0,2:T(4,128)(2,1)} %convolution_convert_fusion.17), channel_id=1, source_target_pairs={{0,3},{4,7},{8,11},{12,15},{16,19},{20,23},{24,27},{28,31},{32,35}... | collective-permute-start | bytes 294920 | tf_op jit(solution)/shard_map/ppermute | solution.py:52
  131.2 111.3 %collective-permute-start.16 = (bf16[4,128,96]{1,0,2:T(4,128)(2,1)}, bf16[4,128,96]{1,0,2:T(4,128)(2,1)S(1)}, u32[]{:S(2)}, u32[]{:S(2)}) collective-permute-start(bf16[4,128,96]{1,0,2:T(4,128)(2,1)} %convolution_convert_fusion.17), channel_id=1, source_target_pairs={{1,3},{5,7},{9,11},{13,15},{17,19},{21,23},{25,27},{29,31},{33,35}... | collective-permute-start | bytes 294920 | tf_op jit(solution)/shard_map/ppermute | solution.py:52
  250.6 11.2 %collective-permute-start.24 = (bf16[4,128,96]{1,2,0:T(8,128)(2,1)S(1)}, bf16[4,128,96]{1,2,0:T(8,128)(2,1)S(1)}, u32[]{:S(2)}, u32[]{:S(2)}) collective-permute-start(bf16[4,128,96]{1,2,0:T(8,128)(2,1)S(1)} %get-tuple-element.37), channel_id=1, source_target_pairs={{3,0},{7,4},{11,8},{15,12},{19,16},{23,20},{27,24},{31,28},{35,32}... | collective-permute-start | bytes 294920 | tf_op jit(solution)/shard_map/ppermute | solution.py:41
  251.9 11.8 %collective-permute-start.25 = (bf16[4,128,96]{1,2,0:T(8,128)(2,1)S(1)}, bf16[4,128,96]{1,2,0:T(8,128)(2,1)S(1)}, u32[]{:S(2)}, u32[]{:S(2)}) collective-permute-start(bf16[4,128,96]{1,2,0:T(8,128)(2,1)S(1)} %get-tuple-element.35), channel_id=1, source_target_pairs={{3,1},{7,5},{11,9},{15,13},{19,17},{23,21},{27,25},{31,29},{35,33}... | collective-permute-start | bytes 294920 | tf_op jit(solution)/shard_map/ppermute | solution.py:41
  263.7 31.1 %collective-permute-start.21 = (bf16[768,96]{0,1:T(8,128)(2,1)}, bf16[768,96]{0,1:T(8,128)(2,1)}, u32[]{:S(2)}, u32[]{:S(2)}) collective-permute-start(bf16[768,96]{0,1:T(8,128)(2,1)} %get-tuple-element.13), channel_id=1, source_target_pairs={{0,3},{1,0},{2,1},{3,2},{4,7},{5,4},{6,5},{7,6},{8,11},{9,8},{10,9... | collective-permute-start | bytes 442376 | tf_op jit(solution)/shard_map/ppermute | solution.py:57
  264.0 30.8 %collective-permute-start.22 = (bf16[768,96]{0,1:T(8,128)(2,1)}, bf16[768,96]{0,1:T(8,128)(2,1)}, u32[]{:S(2)}, u32[]{:S(2)}) collective-permute-start(bf16[768,96]{0,1:T(8,128)(2,1)} %get-tuple-element.12), channel_id=1, source_target_pairs={{0,2},{1,3},{2,0},{3,1},{4,6},{5,7},{6,4},{7,5},{8,10},{9,11},{10,... | collective-permute-start | bytes 442376 | tf_op jit(solution)/shard_map/ppermute | solution.py:57
  268.6 24.5 %all-to-all-start.3 = ((bf16[32,128,96]{1,2,0:T(8,128)(2,1)}), bf16[32,128,96]{1,2,0:T(8,128)(2,1)S(1)}, u32[]{:S(2)}, u32[]{:S(2)}) async-start(bf16[32,128,96]{1,2,0:T(8,128)(2,1)} %copy.97), calls=%async_computation.3 | async-start | bytes 1572864 | tf_op jit(solution)/shard_map/all_to_all | solution.py:76
  279.0 15.9 %collective-permute-start.23 = (bf16[768,96]{0,1:T(8,128)(2,1)}, bf16[768,96]{0,1:T(8,128)(2,1)}, u32[]{:S(2)}, u32[]{:S(2)}) collective-permute-start(bf16[768,96]{0,1:T(8,128)(2,1)} %get-tuple-element.11), channel_id=1, source_target_pairs={{0,1},{1,2},{2,3},{3,0},{4,5},{5,6},{6,7},{7,4},{8,9},{9,10},{10,1... | collective-permute-start | bytes 442376 | tf_op jit(solution)/shard_map/ppermute | solution.py:57
  301.0 18.1 %all-to-all-start.4 = ((bf16[32,128,96]{1,2,0:T(8,128)(2,1)}), bf16[32,128,96]{1,2,0:T(8,128)(2,1)S(1)}, u32[]{:S(2)}, u32[]{:S(2)}) async-start(bf16[32,128,96]{1,2,0:T(8,128)(2,1)} %copy.99), calls=%async_computation.4 | async-start | bytes 1572864 | tf_op jit(solution)/shard_map/all_to_all | solution.py:76
  324.9 18.3 %all-to-all-start.5 = ((bf16[32,128,96]{1,2,0:T(8,128)(2,1)}), bf16[32,128,96]{1,2,0:T(8,128)(2,1)S(1)}, u32[]{:S(2)}, u32[]{:S(2)}) async-start(bf16[32,128,96]{1,2,0:T(8,128)(2,1)} %copy.101), calls=%async_computation.5 | async-start | bytes 1572864 | tf_op jit(solution)/shard_map/all_to_all | solution.py:76
  346.0 10.0 %collective-permute-start.27 = (bf16[768,96]{0,1:T(8,128)(2,1)S(1)}, bf16[768,96]{0,1:T(8,128)(2,1)S(1)}, u32[]{:S(2)}, u32[]{:S(2)}) collective-permute-start(bf16[768,96]{0,1:T(8,128)(2,1)S(1)} %get-tuple-element.34), channel_id=1, source_target_pairs={{0,1},{1,2},{2,3},{3,0},{4,5},{5,6},{6,7},{7,4},{8,9},{9,10},{10,1... | collective-permute-start | bytes 442376 | tf_op jit(solution)/shard_map/ppermute | solution.py:57
  346.1 9.9 %collective-permute-start.28 = (bf16[768,96]{0,1:T(8,128)(2,1)S(1)}, bf16[768,96]{0,1:T(8,128)(2,1)S(1)}, u32[]{:S(2)}, u32[]{:S(2)}) collective-permute-start(bf16[768,96]{0,1:T(8,128)(2,1)S(1)} %get-tuple-element.33), channel_id=1, source_target_pairs={{0,2},{1,3},{2,0},{3,1},{4,6},{5,7},{6,4},{7,5},{8,10},{9,11},{10,... | collective-permute-start | bytes 442376 | tf_op jit(solution)/shard_map/ppermute | solution.py:57
  347.5 8.8 %collective-permute-start.29 = (bf16[768,96]{0,1:T(8,128)(2,1)S(1)}, bf16[768,96]{0,1:T(8,128)(2,1)S(1)}, u32[]{:S(2)}, u32[]{:S(2)}) collective-permute-start(bf16[768,96]{0,1:T(8,128)(2,1)S(1)} %get-tuple-element.32), channel_id=1, source_target_pairs={{0,3},{1,0},{2,1},{3,2},{4,7},{5,4},{6,5},{7,6},{8,11},{9,8},{10,9... | collective-permute-start | bytes 442376 | tf_op jit(solution)/shard_map/ppermute | solution.py:57
  (42 other events, 481.3 us)

commit v5 on v4

--- a/solution.py
+++ b/solution.py
@@ -113,13 +113,10 @@
         ],
         axis=1,
     )
-    shifted = [packed] + [shift(packed, d, row_count) for d in range(1, row_count)]
+    gathered = lax.all_gather(packed, "lvl")
 
     def level_data(t):
-        pick = lax.rem(my_row - t + row_count, row_count)
-        data = shifted[row_count - 1]
-        for d in reversed(range(row_count - 1)):
-            data = jnp.where(pick == d, shifted[d], data)
+        data = gathered[t]
         return (
             data[:, :block_rows],
             data[:, block_rows:block_rows + flat],
@@ -148,24 +145,13 @@
             routed = route(piece, mine_target[t + 1], mine_src[t + 1], block_count)
             incoming = collect(routed, t + 1, row_count)
         if t == last - 1:
-            by_block = solved.reshape(block_rows, row_count, width)
-            sent = [by_block[:, 0, :] * 0]
-            for d in range(1, row_count):
-                wanted = lax.rem(my_row + d, row_count)
-                part = jnp.sum(
-                    by_block * one_hot_rows(wanted, row_count, by_block.dtype)[None, :, None], axis=1
-                ).astype(by_block.dtype)
-                sent.append(shift(part, d, row_count))
-            own = jnp.sum(
-                by_block * one_hot_rows(my_row, row_count, by_block.dtype)[None, :, None], axis=1
-            ).astype(by_block.dtype)
+            forward_all = lax.all_gather(solved, "lvl")
 
     def forward_block(t):
-        pick = lax.rem(my_row - t + row_count, row_count)
-        block = own
-        for d in range(1, row_count):
-            block = jnp.where(pick == d, sent[d], block)
-        return block
+        by_block = forward_all[t].reshape(block_rows, row_count, width)
+        return jnp.sum(
+            by_block * one_hot_rows(my_row, row_count, by_block.dtype)[None, :, None], axis=1
+        ).astype(by_block.dtype)
 
     top = jnp.einsum(
         "ba,bn->an", inverse_here, solved, preferred_element_type=jnp.float32

time: 359 us -> 317 us (0.88)
  waiting for transfers between devices: 170 us -> 107 us
  blocking collectives: 41.5 us -> 83.2 us
  starting transfers between devices: 68.5 us -> 52.8 us
  between operations: 1.54 us -> 14.8 us
  other arithmetic: 25.4 us -> 13.7 us
  matrix products: 35 us -> 31.2 us
    ppermute x9, waiting for transfers between devices: 110 us -> 1.28 us  [collect(): parts.append(lax.ppermute(routed, 'lvl', [(r, dst_row)]))]
    all_gather x0 -> x2, waiting for transfers between devices: none -> 55.2 us  [the longest x1 55.2 us: local(): gathered = lax.all_gather(packed, 'lvl')]
    all_to_all x2 -> x4, blocking collectives: 41.5 us -> 83.2 us  [route(): lax.all_to_all(holder, 'blk', split_axis=0, concat_axis=0, tiled=True)]
    all_to_all x4 -> x2, starting transfers between devices: 23.7 us -> 8.99 us  [route(): lax.all_to_all(holder, 'blk', split_axis=0, concat_axis=0, tiled=True)]
    select_n x3 -> x0, other arithmetic: 10.1 us -> none  [the longest x2 9.79 us: level_data(): data = jnp.where(pick == d, shifted[d], data)]
    all_to_all x4 -> x2, waiting for transfers between devices: 36.9 us -> 28.5 us  [route(): lax.all_to_all(holder, 'blk', split_axis=0, concat_axis=0, tiled=True)]
    unnamed x69 -> x53, local copies, waits for them, and re-layouts: 7.34 us -> 4.34 us
    ppermute x9 -> x3, starting transfers between devices: 9.95 us -> 7.04 us  [shift(): lax.ppermute(array, 'lvl', [(i, (i + by) % row_count) for i in range(row_...]
  transfers between devices with their start and end apart: 34 -> 28, of which waited for: 11 -> 9; matrix products, arithmetic and copies ran while one was open for 11% -> 8% of each run, Pallas kernels for 0% -> 0%
where the time goes in v5:
time: 317 us; the launch traced here: 316 us
  waiting for transfers between devices  107 us (34%)
  blocking collectives  83.2 us (26%)
  starting transfers between devices  52.8 us (17%)
  matrix products  31.2 us (10%)
  between operations  14.8 us (5%)
  other arithmetic  13.7 us (4%)
  local copies, waits for them, and re-layouts  13.2 us (4%)
    all_to_all x4, blocking collectives, route(): lax.all_to_all(holder, 'blk', split_axis=0, concat_axis=0, tiled=True)  83.2 us
    all_gather x1, waiting for transfers between devices, local(): gathered = lax.all_gather(packed, 'lvl')  55.2 us
    all_to_all x2, waiting for transfers between devices, route(): lax.all_to_all(holder, 'blk', split_axis=0, concat_axis=0, tiled=True)  28.5 us
    ppermute x9, starting transfers between devices, collect(): parts.append(lax.ppermute(routed, 'lvl', [(r, dst_row)]))  20.1 us
    ppermute x12, waiting for transfers between devices, spread(): got = lax.ppermute(part, 'lvl', [(src_row, r)])  17.9 us
    ppermute x12, starting transfers between devices, spread(): got = lax.ppermute(part, 'lvl', [(src_row, r)])  16.6 us
    dot_general x4, matrix products, local(): jnp.einsum('ab,bn->an', inverse_here, lowered, preferred_element_type=jnp...  11.8 us
    all_to_all x2, starting transfers between devices, route(): lax.all_to_all(holder, 'blk', split_axis=0, concat_axis=0, tiled=True)  8.99 us
  transfers between devices with their start and end apart: 28, of which 9 were waited for; matrix products, arithmetic and copies ran while one was open for 8% of the time, Pallas kernels for 0%

profile of v5, /device:TPU:1, one launch (start us, length us, event | category | flops | bytes accessed | tf_op | source)
XLA Modules:
  0.0 316.0 jit_solution(4063997317909385169)
XLA Ops:
  7.2 2.3 convolution_convert_fusion.10
  10.9 4.0 %collective-permute-start = (bf16[4,128,96]{1,2,0:T(8,128)(2,1)S(1)}, bf16[4,128,96]{1,2,0:T(8,128)(2,1)S(1)}, u32[]{:S(2)}, u32[]{:S(2)}) collective-permute-start(bf16[4,128,96]{1,2,0:T(8,128)(2,1)S(1)} %get-tuple-element.36), channel_id=1, source_target_pairs={{0,1},{4,5},{8,9},{12,13},{16,17},{20,21},{24,25},{28,29},{32,33},... | collective-permute-start | bytes 294920 | tf_op jit(solution)/shard_map/ppermute | solution.py:41
  22.2 23.2 %all_to_all.30 = bf16[32,128,96]{1,2,0:T(8,128)(2,1)S(1)} all-to-all(bf16[32,128,96]{1,2,0:T(8,128)(2,1)S(1)} %copy.113), channel_id=1, replica_groups=mesh['blk'=32,'lvl'=4] {'blk'}, dimensions={0} | all-to-all | bytes 1572864 | tf_op jit(solution)/shard_map/all_to_all | solution.py:76
  52.8 3.0 convolution_convert_fusion.9
  61.3 4.3 %collective-permute-done.6 = bf16[4,128,96]{1,2,0:T(8,128)(2,1)S(1)} collective-permute-done((bf16[4,128,96]{1,2,0:T(8,128)(2,1)S(1)}, bf16[4,128,96]{1,2,0:T(8,128)(2,1)S(1)}, u32[]{:S(2)}, u32[]{:S(2)}) %collective-permute-start.6) | collective-permute-done | bytes 98336 | tf_op jit(solution)/shard_map/ppermute | solution.py:41
  67.4 18.3 %all_to_all.31 = bf16[32,128,96]{1,2,0:T(8,128)(2,1)S(1)} all-to-all(bf16[32,128,96]{1,2,0:T(8,128)(2,1)S(1)} %copy.122), channel_id=1, replica_groups=mesh['blk'=32,'lvl'=4] {'blk'}, dimensions={0} | all-to-all | bytes 1572864 | tf_op jit(solution)/shard_map/all_to_all | solution.py:76
  88.0 6.4 %collective-permute-start.9 = (bf16[4,128,96]{1,0,2:T(4,128)(2,1)S(1)}, bf16[4,128,96]{1,0,2:T(4,128)(2,1)}, u32[]{:S(2)}, u32[]{:S(2)}) collective-permute-start(bf16[4,128,96]{1,0,2:T(4,128)(2,1)S(1)} %convolution_convert_fusion.18), channel_id=1, source_target_pairs={{0,2},{4,6},{8,10},{12,14},{16,18},{20,22},{24,26},{28,30},{32,34}... | collective-permute-start | bytes 294920 | tf_op jit(solution)/shard_map/ppermute | solution.py:52
  98.0 3.5 %fusion.57 = (bf16[768,384]{1,0:T(8,128)(2,1)}, bf16[384,768]{0,1:T(8,128)(2,1)}) fusion(bf16[384,768]{0,1:T(8,128)(2,1)} %convolution_convert_fusion.9, bf16[768,384]{1,0:T(8,128)(2,1)} %copy-done.23, pred[]{:T(512)S(6)} %eq.425, pred[]{:T(512)S(6)} %eq.426, pred[]{:T(512)S(6)} %eq.427, bf16[1,1,768,768]{3,2,1,0:T(8,128)(2,1)S(1)} %copy-done, ...), kind=kOutput, calls=%fused_computation.78 | convolution fusion | flops 757039104 | bytes 5308419 | tf_op jit(solution)/shard_map/ab,bn->an/dot_general | solution.py:136
  109.1 4.3 %collective-permute-done.12 = bf16[4,128,96]{1,2,0:T(8,128)(2,1)S(1)} collective-permute-done((bf16[4,128,96]{1,2,0:T(8,128)(2,1)S(1)}, bf16[4,128,96]{1,2,0:T(8,128)(2,1)S(1)}, u32[]{:S(2)}, u32[]{:S(2)}) %collective-permute-start.12) | collective-permute-done | bytes 98336 | tf_op jit(solution)/shard_map/ppermute | solution.py:41
  114.2 20.0 %all_to_all.32 = bf16[32,128,96]{1,2,0:T(8,128)(2,1)S(1)} all-to-all(bf16[32,128,96]{1,2,0:T(8,128)(2,1)S(1)} %copy.130), channel_id=1, replica_groups=mesh['blk'=32,'lvl'=4] {'blk'}, dimensions={0} | all-to-all | bytes 1572864 | tf_op jit(solution)/shard_map/all_to_all | solution.py:76
  134.6 6.4 %collective-permute-start.15 = (bf16[4,128,96]{1,0,2:T(4,128)(2,1)S(1)}, bf16[4,128,96]{1,0,2:T(4,128)(2,1)S(1)}, u32[]{:S(2)}, u32[]{:S(2)}) collective-permute-start(bf16[4,128,96]{1,0,2:T(4,128)(2,1)S(1)} %convolution_convert_fusion.17), channel_id=1, source_target_pairs={{0,3},{4,7},{8,11},{12,15},{16,19},{20,23},{24,27},{28,31},{32,35}... | collective-permute-start | bytes 294920 | tf_op jit(solution)/shard_map/ppermute | solution.py:52
  145.1 3.0 fusion.5
  153.2 9.3 %collective-permute-done.18 = bf16[4,128,96]{1,2,0:T(8,128)(2,1)S(1)} collective-permute-done((bf16[4,128,96]{1,2,0:T(8,128)(2,1)S(1)}, bf16[4,128,96]{1,2,0:T(8,128)(2,1)S(1)}, u32[]{:S(2)}, u32[]{:S(2)}) %collective-permute-start.18) | collective-permute-done | bytes 98336 | tf_op jit(solution)/shard_map/ppermute | solution.py:41
  164.3 5.0 %all-to-all-start.3 = ((bf16[32,128,96]{1,2,0:T(8,128)(2,1)}), bf16[32,128,96]{1,2,0:T(8,128)(2,1)S(1)}, u32[]{:S(2)}, u32[]{:S(2)}) async-start(bf16[32,128,96]{1,2,0:T(8,128)(2,1)} %copy.142), calls=%async_computation.3 | async-start | bytes 1572864 | tf_op jit(solution)/shard_map/all_to_all | solution.py:76
  169.3 14.3 %all-to-all-done.3 = bf16[32,128,96]{1,2,0:T(8,128)(2,1)S(1)} async-done(((bf16[32,128,96]{1,2,0:T(8,128)(2,1)}), bf16[32,128,96]{1,2,0:T(8,128)(2,1)S(1)}, u32[]{:S(2)}, u32[]{:S(2)}) %all-to-all-start.3) | async-done | bytes 786464 | tf_op jit(solution)/shard_map/all_to_all | solution.py:76
  186.9 55.2 %all-gather.5.cloned.1.call-done = bf16[3072,1792]{1,0:T(8,128)(2,1)} async-done(((bf16[768,1792]{1,0:T(8,128)(2,1)}), bf16[3072,1792]{1,0:T(8,128)(2,1)}) %all-gather.5.cloned.1.call-update) | async-done | bytes 11010064 | tf_op jit(solution)/shard_map/all_gather | solution.py:116
  242.1 2.2 fusion.19
  246.6 21.8 %all_to_all.33 = bf16[32,128,96]{1,2,0:T(8,128)(2,1)S(1)} all-to-all(bf16[32,128,96]{1,2,0:T(8,128)(2,1)S(1)} %copy.145), channel_id=1, replica_groups=mesh['blk'=32,'lvl'=4] {'blk'}, dimensions={0} | all-to-all | bytes 1572864 | tf_op jit(solution)/shard_map/all_to_all | solution.py:76
  268.7 2.2 fusion.22
  274.1 4.0 %all-to-all-start.5 = ((bf16[32,128,96]{1,2,0:T(8,128)(2,1)}), bf16[32,128,96]{1,2,0:T(8,128)(2,1)S(1)}, u32[]{:S(2)}, u32[]{:S(2)}) async-start(bf16[32,128,96]{1,2,0:T(8,128)(2,1)} %copy.148), calls=%async_computation.5 | async-start | bytes 1572864 | tf_op jit(solution)/shard_map/all_to_all | solution.py:76
  278.1 14.2 %all-to-all-done.5 = bf16[32,128,96]{1,2,0:T(8,128)(2,1)S(1)} async-done(((bf16[32,128,96]{1,2,0:T(8,128)(2,1)}), bf16[32,128,96]{1,2,0:T(8,128)(2,1)S(1)}, u32[]{:S(2)}, u32[]{:S(2)}) %all-to-all-start.5) | async-done | bytes 786464 | tf_op jit(solution)/shard_map/all_to_all | solution.py:76
  292.7 2.2 select_select_fusion.3
  296.5 3.5 %collective-permute-start.22 = (bf16[768,96]{0,1:T(8,128)(2,1)S(1)}, bf16[768,96]{0,1:T(8,128)(2,1)S(1)}, u32[]{:S(2)}, u32[]{:S(2)}) collective-permute-start(bf16[768,96]{0,1:T(8,128)(2,1)S(1)} %get-tuple-element.25), channel_id=1, source_target_pairs={{0,2},{1,3},{2,0},{3,1},{4,6},{5,7},{6,4},{7,5},{8,10},{9,11},{10,... | collective-permute-start | bytes 442376 | tf_op jit(solution)/shard_map/ppermute | solution.py:57
  303.3 4.1 %collective-permute-done.22 = bf16[768,96]{0,1:T(8,128)(2,1)S(1)} collective-permute-done((bf16[768,96]{0,1:T(8,128)(2,1)S(1)}, bf16[768,96]{0,1:T(8,128)(2,1)S(1)}, u32[]{:S(2)}, u32[]{:S(2)}) %collective-permute-start.22) | collective-permute-done | bytes 147488 | tf_op jit(solution)/shard_map/ppermute | solution.py:57
  (184 shorter events, 64.7 us)
Async XLA Ops:
  7.2 176.9 %all-gather.7.cloned.1.call-start = ((), (), s32[]{:S(2)}) async-start(), calls=%async_computation.7 | async-start | bytes 2949120 | tf_op jit(solution)/shard_map/all_gather | solution.py:148
  10.9 10.0 %collective-permute-start = (bf16[4,128,96]{1,2,0:T(8,128)(2,1)S(1)}, bf16[4,128,96]{1,2,0:T(8,128)(2,1)S(1)}, u32[]{:S(2)}, u32[]{:S(2)}) collective-permute-start(bf16[4,128,96]{1,2,0:T(8,128)(2,1)S(1)} %get-tuple-element.36), channel_id=1, source_target_pairs={{0,1},{4,5},{8,9},{12,13},{16,17},{20,21},{24,25},{28,29},{32,33},... | collective-permute-start | bytes 294920 | tf_op jit(solution)/shard_map/ppermute | solution.py:41
  14.8 6.0 %collective-permute-start.1 = (bf16[4,128,96]{1,2,0:T(8,128)(2,1)S(1)}, bf16[4,128,96]{1,2,0:T(8,128)(2,1)S(1)}, u32[]{:S(2)}, u32[]{:S(2)}) collective-permute-start(bf16[4,128,96]{1,2,0:T(8,128)(2,1)S(1)} %get-tuple-element.38), channel_id=1, source_target_pairs={{0,2},{4,6},{8,10},{12,14},{16,18},{20,22},{24,26},{28,30},{32,34}... | collective-permute-start | bytes 294920 | tf_op jit(solution)/shard_map/ppermute | solution.py:41
  45.8 5.7 %collective-permute-start.3 = (bf16[4,128,96]{1,0,2:T(4,128)(2,1)S(1)}, bf16[4,128,96]{1,0,2:T(4,128)(2,1)S(1)}, u32[]{:S(2)}, u32[]{:S(2)}) collective-permute-start(bf16[4,128,96]{1,0,2:T(4,128)(2,1)S(1)} %convolution_convert_fusion.19), channel_id=1, source_target_pairs={{0,1},{4,5},{8,9},{12,13},{16,17},{20,21},{24,25},{28,29},{32,33},... | collective-permute-start | bytes 294920 | tf_op jit(solution)/shard_map/ppermute | solution.py:52
  47.3 4.3 %collective-permute-start.4 = (bf16[4,128,96]{1,0,2:T(4,128)(2,1)S(1)}, bf16[4,128,96]{1,0,2:T(4,128)(2,1)}, u32[]{:S(2)}, u32[]{:S(2)}) collective-permute-start(bf16[4,128,96]{1,0,2:T(4,128)(2,1)S(1)} %convolution_convert_fusion.19), channel_id=1, source_target_pairs={{2,1},{6,5},{10,9},{14,13},{18,17},{22,21},{26,25},{30,29},{34,33}... | collective-permute-start | bytes 294920 | tf_op jit(solution)/shard_map/ppermute | solution.py:52
  57.5 8.1 %collective-permute-start.6 = (bf16[4,128,96]{1,2,0:T(8,128)(2,1)S(1)}, bf16[4,128,96]{1,2,0:T(8,128)(2,1)S(1)}, u32[]{:S(2)}, u32[]{:S(2)}) collective-permute-start(bf16[4,128,96]{1,2,0:T(8,128)(2,1)S(1)} %get-tuple-element.33), channel_id=1, source_target_pairs={{1,0},{5,4},{9,8},{13,12},{17,16},{21,20},{25,24},{29,28},{33,32},... | collective-permute-start | bytes 294920 | tf_op jit(solution)/shard_map/ppermute | solution.py:41
  58.8 6.8 %collective-permute-start.7 = (bf16[4,128,96]{1,2,0:T(8,128)(2,1)S(1)}, bf16[4,128,96]{1,2,0:T(8,128)(2,1)}, u32[]{:S(2)}, u32[]{:S(2)}) collective-permute-start(bf16[4,128,96]{1,2,0:T(8,128)(2,1)S(1)} %get-tuple-element.35), channel_id=1, source_target_pairs={{1,2},{5,6},{9,10},{13,14},{17,18},{21,22},{25,26},{29,30},{33,34}... | collective-permute-start | bytes 294920 | tf_op jit(solution)/shard_map/ppermute | solution.py:41
  60.1 5.5 %collective-permute-start.8 = (bf16[4,128,96]{1,2,0:T(8,128)(2,1)S(1)}, bf16[4,128,96]{1,2,0:T(8,128)(2,1)}, u32[]{:S(2)}, u32[]{:S(2)}) collective-permute-start(bf16[4,128,96]{1,2,0:T(8,128)(2,1)S(1)} %get-tuple-element.34), channel_id=1, source_target_pairs={{1,3},{5,7},{9,11},{13,15},{17,19},{21,23},{25,27},{29,31},{33,35}... | collective-permute-start | bytes 294920 | tf_op jit(solution)/shard_map/ppermute | solution.py:41
  86.0 9.0 %collective-permute-start.10 = (bf16[4,128,96]{1,0,2:T(4,128)(2,1)S(1)}, bf16[4,128,96]{1,0,2:T(4,128)(2,1)S(1)}, u32[]{:S(2)}, u32[]{:S(2)}) collective-permute-start(bf16[4,128,96]{1,0,2:T(4,128)(2,1)S(1)} %convolution_convert_fusion.18), channel_id=1, source_target_pairs={{1,2},{5,6},{9,10},{13,14},{17,18},{21,22},{25,26},{29,30},{33,34}... | collective-permute-start | bytes 294920 | tf_op jit(solution)/shard_map/ppermute | solution.py:52
  86.7 8.3 %collective-permute-start.11 = (bf16[4,128,96]{1,0,2:T(4,128)(2,1)S(1)}, bf16[4,128,96]{1,0,2:T(4,128)(2,1)}, u32[]{:S(2)}, u32[]{:S(2)}) collective-permute-start(bf16[4,128,96]{1,0,2:T(4,128)(2,1)S(1)} %convolution_convert_fusion.18), channel_id=1, source_target_pairs={{3,2},{7,6},{11,10},{15,14},{19,18},{23,22},{27,26},{31,30},{35,34... | collective-permute-start | bytes 294920 | tf_op jit(solution)/shard_map/ppermute | solution.py:52
  88.0 8.0 %collective-permute-start.9 = (bf16[4,128,96]{1,0,2:T(4,128)(2,1)S(1)}, bf16[4,128,96]{1,0,2:T(4,128)(2,1)}, u32[]{:S(2)}, u32[]{:S(2)}) collective-permute-start(bf16[4,128,96]{1,0,2:T(4,128)(2,1)S(1)} %convolution_convert_fusion.18), channel_id=1, source_target_pairs={{0,2},{4,6},{8,10},{12,14},{16,18},{20,22},{24,26},{28,30},{32,34}... | collective-permute-start | bytes 294920 | tf_op jit(solution)/shard_map/ppermute | solution.py:52
  101.6 140.6 %all-gather.5.cloned.1.call-start = ((), (), s32[]{:S(2)}) async-start(), calls=%async_computation.6 | async-start | bytes 13762560 | tf_op jit(solution)/shard_map/all_gather | solution.py:116
  106.4 6.9 %collective-permute-start.12 = (bf16[4,128,96]{1,2,0:T(8,128)(2,1)S(1)}, bf16[4,128,96]{1,2,0:T(8,128)(2,1)S(1)}, u32[]{:S(2)}, u32[]{:S(2)}) collective-permute-start(bf16[4,128,96]{1,2,0:T(8,128)(2,1)S(1)} %get-tuple-element.32), channel_id=1, source_target_pairs={{2,0},{6,4},{10,8},{14,12},{18,16},{22,20},{26,24},{30,28},{34,32}... | collective-permute-start | bytes 294920 | tf_op jit(solution)/shard_map/ppermute | solution.py:41
  107.7 5.6 %collective-permute-start.13 = (bf16[4,128,96]{1,2,0:T(8,128)(2,1)S(1)}, bf16[4,128,96]{1,2,0:T(8,128)(2,1)S(1)}, u32[]{:S(2)}, u32[]{:S(2)}) collective-permute-start(bf16[4,128,96]{1,2,0:T(8,128)(2,1)S(1)} %get-tuple-element.30), channel_id=1, source_target_pairs={{2,1},{6,5},{10,9},{14,13},{18,17},{22,21},{26,25},{30,29},{34,33}... | collective-permute-start | bytes 294920 | tf_op jit(solution)/shard_map/ppermute | solution.py:41
  108.4 4.9 %collective-permute-start.14 = (bf16[4,128,96]{1,2,0:T(8,128)(2,1)S(1)}, bf16[4,128,96]{1,2,0:T(8,128)(2,1)S(1)}, u32[]{:S(2)}, u32[]{:S(2)}) collective-permute-start(bf16[4,128,96]{1,2,0:T(8,128)(2,1)S(1)} %get-tuple-element.31), channel_id=1, source_target_pairs={{2,3},{6,7},{10,11},{14,15},{18,19},{22,23},{26,27},{30,31},{34,35... | collective-permute-start | bytes 294920 | tf_op jit(solution)/shard_map/ppermute | solution.py:41
  134.6 8.7 %collective-permute-start.15 = (bf16[4,128,96]{1,0,2:T(4,128)(2,1)S(1)}, bf16[4,128,96]{1,0,2:T(4,128)(2,1)S(1)}, u32[]{:S(2)}, u32[]{:S(2)}) collective-permute-start(bf16[4,128,96]{1,0,2:T(4,128)(2,1)S(1)} %convolution_convert_fusion.17), channel_id=1, source_target_pairs={{0,3},{4,7},{8,11},{12,15},{16,19},{20,23},{24,27},{28,31},{32,35}... | collective-permute-start | bytes 294920 | tf_op jit(solution)/shard_map/ppermute | solution.py:52
  150.6 12.0 %collective-permute-start.18 = (bf16[4,128,96]{1,2,0:T(8,128)(2,1)S(1)}, bf16[4,128,96]{1,2,0:T(8,128)(2,1)S(1)}, u32[]{:S(2)}, u32[]{:S(2)}) collective-permute-start(bf16[4,128,96]{1,2,0:T(8,128)(2,1)S(1)} %get-tuple-element.29), channel_id=1, source_target_pairs={{3,0},{7,4},{11,8},{15,12},{19,16},{23,20},{27,24},{31,28},{35,32}... | collective-permute-start | bytes 294920 | tf_op jit(solution)/shard_map/ppermute | solution.py:41
  151.9 10.7 %collective-permute-start.19 = (bf16[4,128,96]{1,2,0:T(8,128)(2,1)S(1)}, bf16[4,128,96]{1,2,0:T(8,128)(2,1)S(1)}, u32[]{:S(2)}, u32[]{:S(2)}) collective-permute-start(bf16[4,128,96]{1,2,0:T(8,128)(2,1)S(1)} %get-tuple-element.27), channel_id=1, source_target_pairs={{3,1},{7,5},{11,9},{15,13},{19,17},{23,21},{27,25},{31,29},{35,33}... | collective-permute-start | bytes 294920 | tf_op jit(solution)/shard_map/ppermute | solution.py:41
  152.5 10.0 %collective-permute-start.20 = (bf16[4,128,96]{1,2,0:T(8,128)(2,1)S(1)}, bf16[4,128,96]{1,2,0:T(8,128)(2,1)S(1)}, u32[]{:S(2)}, u32[]{:S(2)}) collective-permute-start(bf16[4,128,96]{1,2,0:T(8,128)(2,1)S(1)} %get-tuple-element.28), channel_id=1, source_target_pairs={{3,2},{7,6},{11,10},{15,14},{19,18},{23,22},{27,26},{31,30},{35,34... | collective-permute-start | bytes 294920 | tf_op jit(solution)/shard_map/ppermute | solution.py:41
  164.3 19.4 %all-to-all-start.3 = ((bf16[32,128,96]{1,2,0:T(8,128)(2,1)}), bf16[32,128,96]{1,2,0:T(8,128)(2,1)S(1)}, u32[]{:S(2)}, u32[]{:S(2)}) async-start(bf16[32,128,96]{1,2,0:T(8,128)(2,1)} %copy.142), calls=%async_computation.3 | async-start | bytes 1572864 | tf_op jit(solution)/shard_map/all_to_all | solution.py:76
  274.1 18.2 %all-to-all-start.5 = ((bf16[32,128,96]{1,2,0:T(8,128)(2,1)}), bf16[32,128,96]{1,2,0:T(8,128)(2,1)S(1)}, u32[]{:S(2)}, u32[]{:S(2)}) async-start(bf16[32,128,96]{1,2,0:T(8,128)(2,1)} %copy.148), calls=%async_computation.5 | async-start | bytes 1572864 | tf_op jit(solution)/shard_map/all_to_all | solution.py:76
  294.9 8.1 %collective-permute-start.21 = (bf16[768,96]{0,1:T(8,128)(2,1)S(1)}, bf16[768,96]{0,1:T(8,128)(2,1)S(1)}, u32[]{:S(2)}, u32[]{:S(2)}) collective-permute-start(bf16[768,96]{0,1:T(8,128)(2,1)S(1)} %get-tuple-element.26), channel_id=1, source_target_pairs={{0,1},{1,2},{2,3},{3,0},{4,5},{5,6},{6,7},{7,4},{8,9},{9,10},{10,1... | collective-permute-start | bytes 442376 | tf_op jit(solution)/shard_map/ppermute | solution.py:57
  296.5 10.9 %collective-permute-start.22 = (bf16[768,96]{0,1:T(8,128)(2,1)S(1)}, bf16[768,96]{0,1:T(8,128)(2,1)S(1)}, u32[]{:S(2)}, u32[]{:S(2)}) collective-permute-start(bf16[768,96]{0,1:T(8,128)(2,1)S(1)} %get-tuple-element.25), channel_id=1, source_target_pairs={{0,2},{1,3},{2,0},{3,1},{4,6},{5,7},{6,4},{7,5},{8,10},{9,11},{10,... | collective-permute-start | bytes 442376 | tf_op jit(solution)/shard_map/ppermute | solution.py:57
  300.0 7.8 %collective-permute-start.23 = (bf16[768,96]{0,1:T(8,128)(2,1)S(1)}, bf16[768,96]{0,1:T(8,128)(2,1)S(1)}, u32[]{:S(2)}, u32[]{:S(2)}) collective-permute-start(bf16[768,96]{0,1:T(8,128)(2,1)S(1)} %get-tuple-element.24), channel_id=1, source_target_pairs={{0,3},{1,0},{2,1},{3,2},{4,7},{5,4},{6,5},{7,6},{8,11},{9,8},{10,9... | collective-permute-start | bytes 442376 | tf_op jit(solution)/shard_map/ppermute | solution.py:57
  (29 other events, 351.3 us)
Sparse Core Ops, SparseCore 0:
  101.7 32.3 all-gather.6
  135.7 106.3 all-gather.4

commit v6 on v4

--- a/solution.py
+++ b/solution.py
@@ -113,13 +113,10 @@
         ],
         axis=1,
     )
-    shifted = [packed] + [shift(packed, d, row_count) for d in range(1, row_count)]
+    gathered = lax.all_gather(packed, "lvl")
 
     def level_data(t):
-        pick = lax.rem(my_row - t + row_count, row_count)
-        data = shifted[row_count - 1]
-        for d in reversed(range(row_count - 1)):
-            data = jnp.where(pick == d, shifted[d], data)
+        data = gathered[t]
         return (
             data[:, :block_rows],
             data[:, block_rows:block_rows + flat],
@@ -149,7 +146,7 @@
             incoming = collect(routed, t + 1, row_count)
         if t == last - 1:
             by_block = solved.reshape(block_rows, row_count, width)
-            sent = [by_block[:, 0, :] * 0]
+            sent = [None]
             for d in range(1, row_count):
                 wanted = lax.rem(my_row + d, row_count)
                 part = jnp.sum(

time: 359 us -> 262 us (0.73)
  waiting for transfers between devices: 170 us -> 77.3 us
  blocking collectives: 41.5 us -> 61.6 us
  starting transfers between devices: 68.5 us -> 51.4 us
  other arithmetic: 25.4 us -> 11.8 us
  between operations: 1.54 us -> 14.8 us
  matrix products: 35 us -> 28.2 us
    ppermute x9, waiting for transfers between devices: 110 us -> 9.65 us  [collect(): parts.append(lax.ppermute(routed, 'lvl', [(r, dst_row)]))]
    all_to_all x2 -> x3, blocking collectives: 41.5 us -> 61.6 us  [route(): lax.all_to_all(holder, 'blk', split_axis=0, concat_axis=0, tiled=True)]
    select_n x2 -> x0, other arithmetic: 9.79 us -> none  [level_data(): data = jnp.where(pick == d, shifted[d], data)]
    all_to_all x4 -> x3, starting transfers between devices: 23.7 us -> 14 us  [route(): lax.all_to_all(holder, 'blk', split_axis=0, concat_axis=0, tiled=True)]
    ppermute x12, waiting for transfers between devices: 17.8 us -> 23.4 us  [spread(): got = lax.ppermute(part, 'lvl', [(src_row, r)])]
    ppermute x9, starting transfers between devices: 18.3 us -> 14.2 us  [collect(): parts.append(lax.ppermute(routed, 'lvl', [(r, dst_row)]))]
    ppermute x9 -> x6, starting transfers between devices: 9.95 us -> 6.87 us  [shift(): lax.ppermute(array, 'lvl', [(i, (i + by) % row_count) for i in range(row_...]
    all_to_all x4 -> x3, waiting for transfers between devices: 36.9 us -> 38.4 us  [route(): lax.all_to_all(holder, 'blk', split_axis=0, concat_axis=0, tiled=True)]
  transfers between devices with their start and end apart: 34 -> 31, of which waited for: 11 -> 12; matrix products, arithmetic and copies ran while one was open for 11% -> 13% of each run, Pallas kernels for 0% -> 0%
where the time goes in v6:
time: 262 us; the launch traced here: 260 us
  waiting for transfers between devices  77.3 us (30%)
  blocking collectives  61.6 us (24%)
  starting transfers between devices  51.4 us (20%)
  matrix products  28.2 us (11%)
  local copies, waits for them, and re-layouts  15.4 us (6%)
  between operations  14.8 us (6%)
  other arithmetic  11.8 us (5%)
    all_to_all x3, blocking collectives, route(): lax.all_to_all(holder, 'blk', split_axis=0, concat_axis=0, tiled=True)  61.6 us
    all_to_all x3, waiting for transfers between devices, route(): lax.all_to_all(holder, 'blk', split_axis=0, concat_axis=0, tiled=True)  38.4 us
    ppermute x12, waiting for transfers between devices, spread(): got = lax.ppermute(part, 'lvl', [(src_row, r)])  23.4 us
    ppermute x12, starting transfers between devices, spread(): got = lax.ppermute(part, 'lvl', [(src_row, r)])  16.3 us
    ppermute x9, starting transfers between devices, collect(): parts.append(lax.ppermute(routed, 'lvl', [(r, dst_row)]))  14.2 us
    all_to_all x3, starting transfers between devices, route(): lax.all_to_all(holder, 'blk', split_axis=0, concat_axis=0, tiled=True)  14 us
    ppermute x9, waiting for transfers between devices, collect(): parts.append(lax.ppermute(routed, 'lvl', [(r, dst_row)]))  9.65 us
    dot_general x4, matrix products, local(): jnp.einsum('ab,bn->an', inverse_here, lowered, preferred_element_type=jnp...  9.08 us
  transfers between devices with their start and end apart: 31, of which 12 were waited for; matrix products, arithmetic and copies ran while one was open for 13% of the time, Pallas kernels for 0%

profile of v6, /device:TPU:1, one launch (start us, length us, event | category | flops | bytes accessed | tf_op | source)
XLA Modules:
  0.0 260.4 jit_solution(2832444726913492115)
XLA Ops:
  16.1 5.2 %collective-permute-start.2 = (bf16[4,128,96]{1,2,0:T(8,128)(2,1)S(1)}, bf16[4,128,96]{1,2,0:T(8,128)(2,1)S(1)}, u32[]{:S(2)}, u32[]{:S(2)}) collective-permute-start(bf16[4,128,96]{1,2,0:T(8,128)(2,1)S(1)} %get-tuple-element.43), channel_id=1, source_target_pairs={{0,3},{4,7},{8,11},{12,15},{16,19},{20,23},{24,27},{28,31},{32,35}... | collective-permute-start | bytes 294920 | tf_op jit(solution)/shard_map/ppermute | solution.py:41
  28.2 23.1 %all_to_all.30 = bf16[32,128,96]{1,2,0:T(8,128)(2,1)S(1)} all-to-all(bf16[32,128,96]{1,2,0:T(8,128)(2,1)S(1)} %copy.76), channel_id=1, replica_groups=mesh['blk'=32,'lvl'=4] {'blk'}, dimensions={0} | all-to-all | bytes 1572864 | tf_op jit(solution)/shard_map/all_to_all | solution.py:76
  53.7 4.9 %collective-permute-start.3 = (bf16[4,128,96]{1,0,2:T(4,128)(2,1)S(1)}, bf16[4,128,96]{1,0,2:T(4,128)(2,1)}, u32[]{:S(2)}, u32[]{:S(2)}) collective-permute-start(bf16[4,128,96]{1,0,2:T(4,128)(2,1)S(1)} %convolution_convert_fusion.19), channel_id=1, source_target_pairs={{0,1},{4,5},{8,9},{12,13},{16,17},{20,21},{24,25},{28,29},{32,33},... | collective-permute-start | bytes 294920 | tf_op jit(solution)/shard_map/ppermute | solution.py:52
  60.4 2.2 collective-permute-done.3
  63.9 2.9 %convolution_convert_fusion.9 = bf16[384,768]{1,0:T(8,128)(2,1)} fusion(bf16[1,1,4,768,128]{4,3,2,1,0:T(8,128)(2,1)S(1)} %copy-done.3, bf16[1,1,768,384]{2,3,1,0:T(8,128)(2,1)} %copy.72, bf16[4,128,384]{1,0,2:T(4,128)(2,1)S(1)} %maximum_multiply_fusion, bf16[1,1,768,768]{3,2,1,0:T(8,128)(2,1)S(1)} %copy-done), kind=kOutput, calls=%fused_computation.19 | convolution fusion | flops 756154368 | bytes 3538944 | tf_op jit(solution)/shard_map/ab,bn->an/dot_general | solution.py:136
  71.6 10.5 %collective-permute-done.6 = bf16[4,128,96]{1,2,0:T(8,128)(2,1)} collective-permute-done((bf16[4,128,96]{1,2,0:T(8,128)(2,1)S(1)}, bf16[4,128,96]{1,2,0:T(8,128)(2,1)}, u32[]{:S(2)}, u32[]{:S(2)}) %collective-permute-start.6) | collective-permute-done | bytes 98336 | tf_op jit(solution)/shard_map/ppermute | solution.py:41
  84.0 18.8 %all_to_all.31 = bf16[32,128,96]{1,2,0:T(8,128)(2,1)S(1)} all-to-all(bf16[32,128,96]{1,2,0:T(8,128)(2,1)S(1)} %copy.83), channel_id=1, replica_groups=mesh['blk'=32,'lvl'=4] {'blk'}, dimensions={0} | all-to-all | bytes 1572864 | tf_op jit(solution)/shard_map/all_to_all | solution.py:76
  107.8 3.3 %collective-permute-done.9 = bf16[4,128,96]{1,0,2:T(4,128)(2,1)} collective-permute-done((bf16[4,128,96]{1,0,2:T(4,128)(2,1)S(1)}, bf16[4,128,96]{1,0,2:T(4,128)(2,1)}, u32[]{:S(2)}, u32[]{:S(2)}) %collective-permute-start.9) | collective-permute-done | bytes 98336 | tf_op jit(solution)/shard_map/ppermute | solution.py:52
  113.1 3.4 %fusion.57 = (bf16[768,384]{0,1:T(8,128)(2,1)}, bf16[384,768]{1,0:T(8,128)(2,1)}) fusion(bf16[384,768]{1,0:T(8,128)(2,1)} %convolution_convert_fusion.9, bf16[768,384]{0,1:T(8,128)(2,1)} %copy-done.20, pred[]{:T(512)S(6)} %eq.454, pred[]{:T(512)S(6)} %eq.455, pred[]{:T(512)S(6)} %eq.456, bf16[1,1,768,768]{3,2,1,0:T(8,128)(2,1)S(1)} %copy-done, ...), kind=kOutput, calls=%fused_computation.81 | convolution fusion | flops 757039104 | bytes 5308419 | tf_op jit(solution)/shard_map/ab,bn->an/dot_general | solution.py:136
  120.6 6.9 %collective-permute-done.12 = bf16[4,128,96]{1,2,0:T(8,128)(2,1)S(1)} collective-permute-done((bf16[4,128,96]{1,2,0:T(8,128)(2,1)S(1)}, bf16[4,128,96]{1,2,0:T(8,128)(2,1)S(1)}, u32[]{:S(2)}, u32[]{:S(2)}) %collective-permute-start.12) | collective-permute-done | bytes 98336 | tf_op jit(solution)/shard_map/ppermute | solution.py:41
  128.4 19.7 %all_to_all.32 = bf16[32,128,96]{1,2,0:T(8,128)(2,1)S(1)} all-to-all(bf16[32,128,96]{1,2,0:T(8,128)(2,1)S(1)} %copy.89), channel_id=1, replica_groups=mesh['blk'=32,'lvl'=4] {'blk'}, dimensions={0} | all-to-all | bytes 1572864 | tf_op jit(solution)/shard_map/all_to_all | solution.py:76
  151.7 4.1 %collective-permute-done.15 = bf16[4,128,96]{1,0,2:T(4,128)(2,1)S(1)} collective-permute-done((bf16[4,128,96]{1,0,2:T(4,128)(2,1)S(1)}, bf16[4,128,96]{1,0,2:T(4,128)(2,1)S(1)}, u32[]{:S(2)}, u32[]{:S(2)}) %collective-permute-start.15) | collective-permute-done | bytes 98336 | tf_op jit(solution)/shard_map/ppermute | solution.py:52
  162.9 5.9 %collective-permute-done.21 = bf16[4,128,96]{1,2,0:T(8,128)(2,1)S(1)} collective-permute-done((bf16[4,128,96]{1,2,0:T(8,128)(2,1)S(1)}, bf16[4,128,96]{1,2,0:T(8,128)(2,1)S(1)}, u32[]{:S(2)}, u32[]{:S(2)}) %collective-permute-start.21) | collective-permute-done | bytes 98336 | tf_op jit(solution)/shard_map/ppermute | solution.py:41
  170.5 5.0 %all-to-all-start.3 = ((bf16[32,128,96]{1,2,0:T(8,128)(2,1)}), bf16[32,128,96]{1,2,0:T(8,128)(2,1)S(1)}, u32[]{:S(2)}, u32[]{:S(2)}) async-start(bf16[32,128,96]{1,2,0:T(8,128)(2,1)} %copy.97), calls=%async_computation.3 | async-start | bytes 1572864 | tf_op jit(solution)/shard_map/all_to_all | solution.py:76
  176.8 3.1 %collective-permute-start.19 = (bf16[768,96]{0,1:T(8,128)(2,1)S(1)}, bf16[768,96]{0,1:T(8,128)(2,1)S(1)}, u32[]{:S(2)}, u32[]{:S(2)}) collective-permute-start(bf16[768,96]{0,1:T(8,128)(2,1)S(1)} %get-tuple-element.12), channel_id=1, source_target_pairs={{0,2},{1,3},{2,0},{3,1},{4,6},{5,7},{6,4},{7,5},{8,10},{9,11},{10,... | collective-permute-start | bytes 442376 | tf_op jit(solution)/shard_map/ppermute | solution.py:57
  179.9 10.0 %all-to-all-done.3 = bf16[32,128,96]{1,2,0:T(8,128)(2,1)S(1)} async-done(((bf16[32,128,96]{1,2,0:T(8,128)(2,1)}), bf16[32,128,96]{1,2,0:T(8,128)(2,1)S(1)}, u32[]{:S(2)}, u32[]{:S(2)}) %all-to-all-start.3) | async-done | bytes 786464 | tf_op jit(solution)/shard_map/all_to_all | solution.py:76
  190.3 2.2 fusion.16
  195.7 5.1 %all-to-all-start.4 = ((bf16[32,128,96]{1,2,0:T(8,128)(2,1)}), bf16[32,128,96]{1,2,0:T(8,128)(2,1)S(1)}, u32[]{:S(2)}, u32[]{:S(2)}) async-start(bf16[32,128,96]{1,2,0:T(8,128)(2,1)} %copy.99), calls=%async_computation.4 | async-start | bytes 1572864 | tf_op jit(solution)/shard_map/all_to_all | solution.py:76
  200.8 14.2 %all-to-all-done.4 = bf16[32,128,96]{1,2,0:T(8,128)(2,1)S(1)} async-done(((bf16[32,128,96]{1,2,0:T(8,128)(2,1)}), bf16[32,128,96]{1,2,0:T(8,128)(2,1)S(1)}, u32[]{:S(2)}, u32[]{:S(2)}) %all-to-all-start.4) | async-done | bytes 786464 | tf_op jit(solution)/shard_map/all_to_all | solution.py:76
  220.8 4.0 %all-to-all-start.5 = ((bf16[32,128,96]{1,2,0:T(8,128)(2,1)}), bf16[32,128,96]{1,2,0:T(8,128)(2,1)S(1)}, u32[]{:S(2)}, u32[]{:S(2)}) async-start(bf16[32,128,96]{1,2,0:T(8,128)(2,1)} %copy.101), calls=%async_computation.5 | async-start | bytes 1572864 | tf_op jit(solution)/shard_map/all_to_all | solution.py:76
  224.8 14.2 %all-to-all-done.5 = bf16[32,128,96]{1,2,0:T(8,128)(2,1)S(1)} async-done(((bf16[32,128,96]{1,2,0:T(8,128)(2,1)}), bf16[32,128,96]{1,2,0:T(8,128)(2,1)S(1)}, u32[]{:S(2)}, u32[]{:S(2)}) %all-to-all-start.5) | async-done | bytes 786464 | tf_op jit(solution)/shard_map/all_to_all | solution.py:76
  239.3 2.2 select_select_fusion.3
  242.0 2.7 %collective-permute-start.25 = (bf16[768,96]{0,1:T(8,128)(2,1)S(1)}, bf16[768,96]{0,1:T(8,128)(2,1)S(1)}, u32[]{:S(2)}, u32[]{:S(2)}) collective-permute-start(bf16[768,96]{0,1:T(8,128)(2,1)S(1)} %get-tuple-element.31), channel_id=1, source_target_pairs={{0,2},{1,3},{2,0},{3,1},{4,6},{5,7},{6,4},{7,5},{8,10},{9,11},{10,... | collective-permute-start | bytes 442376 | tf_op jit(solution)/shard_map/ppermute | solution.py:57
  248.8 3.4 %collective-permute-done.24 = bf16[768,96]{0,1:T(8,128)(2,1)S(1)} collective-permute-done((bf16[768,96]{0,1:T(8,128)(2,1)S(1)}, bf16[768,96]{0,1:T(8,128)(2,1)S(1)}, u32[]{:S(2)}, u32[]{:S(2)}) %collective-permute-start.24) | collective-permute-done | bytes 147488 | tf_op jit(solution)/shard_map/ppermute | solution.py:57
  (168 shorter events, 68.6 us)
Async XLA Ops:
  7.2 183.1 %all-gather.3.cloned.1.call-start = ((), (), s32[]{:S(2)}) async-start(), calls=%async_computation.6 | async-start | bytes 13762560 | tf_op jit(solution)/shard_map/all_gather | solution.py:116
  16.1 11.1 %collective-permute-start.2 = (bf16[4,128,96]{1,2,0:T(8,128)(2,1)S(1)}, bf16[4,128,96]{1,2,0:T(8,128)(2,1)S(1)}, u32[]{:S(2)}, u32[]{:S(2)}) collective-permute-start(bf16[4,128,96]{1,2,0:T(8,128)(2,1)S(1)} %get-tuple-element.43), channel_id=1, source_target_pairs={{0,3},{4,7},{8,11},{12,15},{16,19},{20,23},{24,27},{28,31},{32,35}... | collective-permute-start | bytes 294920 | tf_op jit(solution)/shard_map/ppermute | solution.py:41
  21.4 5.9 %collective-permute-start.1 = (bf16[4,128,96]{1,2,0:T(8,128)(2,1)S(1)}, bf16[4,128,96]{1,2,0:T(8,128)(2,1)S(1)}, u32[]{:S(2)}, u32[]{:S(2)}) collective-permute-start(bf16[4,128,96]{1,2,0:T(8,128)(2,1)S(1)} %get-tuple-element.44), channel_id=1, source_target_pairs={{0,2},{4,6},{8,10},{12,14},{16,18},{20,22},{24,26},{28,30},{32,34}... | collective-permute-start | bytes 294920 | tf_op jit(solution)/shard_map/ppermute | solution.py:41
  22.7 4.6 %collective-permute-start = (bf16[4,128,96]{1,2,0:T(8,128)(2,1)S(1)}, bf16[4,128,96]{1,2,0:T(8,128)(2,1)S(1)}, u32[]{:S(2)}, u32[]{:S(2)}) collective-permute-start(bf16[4,128,96]{1,2,0:T(8,128)(2,1)S(1)} %get-tuple-element.42), channel_id=1, source_target_pairs={{0,1},{4,5},{8,9},{12,13},{16,17},{20,21},{24,25},{28,29},{32,33},... | collective-permute-start | bytes 294920 | tf_op jit(solution)/shard_map/ppermute | solution.py:41
  51.6 8.8 %collective-permute-start.5 = (bf16[4,128,96]{1,0,2:T(4,128)(2,1)S(1)}, bf16[4,128,96]{1,0,2:T(4,128)(2,1)S(1)}, u32[]{:S(2)}, u32[]{:S(2)}) collective-permute-start(bf16[4,128,96]{1,0,2:T(4,128)(2,1)S(1)} %convolution_convert_fusion.19), channel_id=1, source_target_pairs={{3,1},{7,5},{11,9},{15,13},{19,17},{23,21},{27,25},{31,29},{35,33}... | collective-permute-start | bytes 294920 | tf_op jit(solution)/shard_map/ppermute | solution.py:52
  52.4 8.0 %collective-permute-start.4 = (bf16[4,128,96]{1,0,2:T(4,128)(2,1)S(1)}, bf16[4,128,96]{1,0,2:T(4,128)(2,1)}, u32[]{:S(2)}, u32[]{:S(2)}) collective-permute-start(bf16[4,128,96]{1,0,2:T(4,128)(2,1)S(1)} %convolution_convert_fusion.19), channel_id=1, source_target_pairs={{2,1},{6,5},{10,9},{14,13},{18,17},{22,21},{26,25},{30,29},{34,33}... | collective-permute-start | bytes 294920 | tf_op jit(solution)/shard_map/ppermute | solution.py:52
  53.7 8.9 %collective-permute-start.3 = (bf16[4,128,96]{1,0,2:T(4,128)(2,1)S(1)}, bf16[4,128,96]{1,0,2:T(4,128)(2,1)}, u32[]{:S(2)}, u32[]{:S(2)}) collective-permute-start(bf16[4,128,96]{1,0,2:T(4,128)(2,1)S(1)} %convolution_convert_fusion.19), channel_id=1, source_target_pairs={{0,1},{4,5},{8,9},{12,13},{16,17},{20,21},{24,25},{28,29},{32,33},... | collective-permute-start | bytes 294920 | tf_op jit(solution)/shard_map/ppermute | solution.py:52
  70.3 11.8 %collective-permute-start.6 = (bf16[4,128,96]{1,2,0:T(8,128)(2,1)S(1)}, bf16[4,128,96]{1,2,0:T(8,128)(2,1)}, u32[]{:S(2)}, u32[]{:S(2)}) collective-permute-start(bf16[4,128,96]{1,2,0:T(8,128)(2,1)S(1)} %get-tuple-element.39), channel_id=1, source_target_pairs={{1,0},{5,4},{9,8},{13,12},{17,16},{21,20},{25,24},{29,28},{33,32},... | collective-permute-start | bytes 294920 | tf_op jit(solution)/shard_map/ppermute | solution.py:41
  103.1 4.7 %collective-permute-start.11 = (bf16[4,128,96]{1,0,2:T(4,128)(2,1)S(1)}, bf16[4,128,96]{1,0,2:T(4,128)(2,1)S(1)}, u32[]{:S(2)}, u32[]{:S(2)}) collective-permute-start(bf16[4,128,96]{1,0,2:T(4,128)(2,1)S(1)} %convolution_convert_fusion.18), channel_id=1, source_target_pairs={{3,2},{7,6},{11,10},{15,14},{19,18},{23,22},{27,26},{31,30},{35,34... | collective-permute-start | bytes 294920 | tf_op jit(solution)/shard_map/ppermute | solution.py:52
  105.1 6.0 %collective-permute-start.9 = (bf16[4,128,96]{1,0,2:T(4,128)(2,1)S(1)}, bf16[4,128,96]{1,0,2:T(4,128)(2,1)}, u32[]{:S(2)}, u32[]{:S(2)}) collective-permute-start(bf16[4,128,96]{1,0,2:T(4,128)(2,1)S(1)} %convolution_convert_fusion.18), channel_id=1, source_target_pairs={{0,2},{4,6},{8,10},{12,14},{16,18},{20,22},{24,26},{28,30},{32,34}... | collective-permute-start | bytes 294920 | tf_op jit(solution)/shard_map/ppermute | solution.py:52
  118.7 8.9 %collective-permute-start.12 = (bf16[4,128,96]{1,2,0:T(8,128)(2,1)S(1)}, bf16[4,128,96]{1,2,0:T(8,128)(2,1)S(1)}, u32[]{:S(2)}, u32[]{:S(2)}) collective-permute-start(bf16[4,128,96]{1,2,0:T(8,128)(2,1)S(1)} %get-tuple-element.38), channel_id=1, source_target_pairs={{2,0},{6,4},{10,8},{14,12},{18,16},{22,20},{26,24},{30,28},{34,32}... | collective-permute-start | bytes 294920 | tf_op jit(solution)/shard_map/ppermute | solution.py:41
  120.0 7.6 %collective-permute-start.13 = (bf16[4,128,96]{1,2,0:T(8,128)(2,1)S(1)}, bf16[4,128,96]{1,2,0:T(8,128)(2,1)S(1)}, u32[]{:S(2)}, u32[]{:S(2)}) collective-permute-start(bf16[4,128,96]{1,2,0:T(8,128)(2,1)S(1)} %get-tuple-element.36), channel_id=1, source_target_pairs={{2,1},{6,5},{10,9},{14,13},{18,17},{22,21},{26,25},{30,29},{34,33}... | collective-permute-start | bytes 294920 | tf_op jit(solution)/shard_map/ppermute | solution.py:41
  149.8 6.0 %collective-permute-start.15 = (bf16[4,128,96]{1,0,2:T(4,128)(2,1)S(1)}, bf16[4,128,96]{1,0,2:T(4,128)(2,1)S(1)}, u32[]{:S(2)}, u32[]{:S(2)}) collective-permute-start(bf16[4,128,96]{1,0,2:T(4,128)(2,1)S(1)} %convolution_convert_fusion.17), channel_id=1, source_target_pairs={{0,3},{4,7},{8,11},{12,15},{16,19},{20,23},{24,27},{28,31},{32,35}... | collective-permute-start | bytes 294920 | tf_op jit(solution)/shard_map/ppermute | solution.py:52
  160.9 7.9 %collective-permute-start.21 = (bf16[4,128,96]{1,2,0:T(8,128)(2,1)S(1)}, bf16[4,128,96]{1,2,0:T(8,128)(2,1)S(1)}, u32[]{:S(2)}, u32[]{:S(2)}) collective-permute-start(bf16[4,128,96]{1,2,0:T(8,128)(2,1)S(1)} %get-tuple-element.35), channel_id=1, source_target_pairs={{3,0},{7,4},{11,8},{15,12},{19,16},{23,20},{27,24},{31,28},{35,32}... | collective-permute-start | bytes 294920 | tf_op jit(solution)/shard_map/ppermute | solution.py:41
  162.2 6.6 %collective-permute-start.22 = (bf16[4,128,96]{1,2,0:T(8,128)(2,1)S(1)}, bf16[4,128,96]{1,2,0:T(8,128)(2,1)S(1)}, u32[]{:S(2)}, u32[]{:S(2)}) collective-permute-start(bf16[4,128,96]{1,2,0:T(8,128)(2,1)S(1)} %get-tuple-element.33), channel_id=1, source_target_pairs={{3,1},{7,5},{11,9},{15,13},{19,17},{23,21},{27,25},{31,29},{35,33}... | collective-permute-start | bytes 294920 | tf_op jit(solution)/shard_map/ppermute | solution.py:41
  170.5 19.3 %all-to-all-start.3 = ((bf16[32,128,96]{1,2,0:T(8,128)(2,1)}), bf16[32,128,96]{1,2,0:T(8,128)(2,1)S(1)}, u32[]{:S(2)}, u32[]{:S(2)}) async-start(bf16[32,128,96]{1,2,0:T(8,128)(2,1)} %copy.97), calls=%async_computation.3 | async-start | bytes 1572864 | tf_op jit(solution)/shard_map/all_to_all | solution.py:76
  176.1 14.1 %collective-permute-start.18 = (bf16[768,96]{0,1:T(8,128)(2,1)S(1)}, bf16[768,96]{0,1:T(8,128)(2,1)S(1)}, u32[]{:S(2)}, u32[]{:S(2)}) collective-permute-start(bf16[768,96]{0,1:T(8,128)(2,1)S(1)} %get-tuple-element.13), channel_id=1, source_target_pairs={{0,3},{1,0},{2,1},{3,2},{4,7},{5,4},{6,5},{7,6},{8,11},{9,8},{10,9... | collective-permute-start | bytes 442376 | tf_op jit(solution)/shard_map/ppermute | solution.py:57
  176.8 13.4 %collective-permute-start.19 = (bf16[768,96]{0,1:T(8,128)(2,1)S(1)}, bf16[768,96]{0,1:T(8,128)(2,1)S(1)}, u32[]{:S(2)}, u32[]{:S(2)}) collective-permute-start(bf16[768,96]{0,1:T(8,128)(2,1)S(1)} %get-tuple-element.12), channel_id=1, source_target_pairs={{0,2},{1,3},{2,0},{3,1},{4,6},{5,7},{6,4},{7,5},{8,10},{9,11},{10,... | collective-permute-start | bytes 442376 | tf_op jit(solution)/shard_map/ppermute | solution.py:57
  179.9 10.3 %collective-permute-start.20 = (bf16[768,96]{0,1:T(8,128)(2,1)S(1)}, bf16[768,96]{0,1:T(8,128)(2,1)S(1)}, u32[]{:S(2)}, u32[]{:S(2)}) collective-permute-start(bf16[768,96]{0,1:T(8,128)(2,1)S(1)} %get-tuple-element.11), channel_id=1, source_target_pairs={{0,1},{1,2},{2,3},{3,0},{4,5},{5,6},{6,7},{7,4},{8,9},{9,10},{10,1... | collective-permute-start | bytes 442376 | tf_op jit(solution)/shard_map/ppermute | solution.py:57
  195.7 19.3 %all-to-all-start.4 = ((bf16[32,128,96]{1,2,0:T(8,128)(2,1)}), bf16[32,128,96]{1,2,0:T(8,128)(2,1)S(1)}, u32[]{:S(2)}, u32[]{:S(2)}) async-start(bf16[32,128,96]{1,2,0:T(8,128)(2,1)} %copy.99), calls=%async_computation.4 | async-start | bytes 1572864 | tf_op jit(solution)/shard_map/all_to_all | solution.py:76
  220.8 18.2 %all-to-all-start.5 = ((bf16[32,128,96]{1,2,0:T(8,128)(2,1)}), bf16[32,128,96]{1,2,0:T(8,128)(2,1)S(1)}, u32[]{:S(2)}, u32[]{:S(2)}) async-start(bf16[32,128,96]{1,2,0:T(8,128)(2,1)} %copy.101), calls=%async_computation.5 | async-start | bytes 1572864 | tf_op jit(solution)/shard_map/all_to_all | solution.py:76
  241.6 5.6 %collective-permute-start.26 = (bf16[768,96]{0,1:T(8,128)(2,1)S(1)}, bf16[768,96]{0,1:T(8,128)(2,1)S(1)}, u32[]{:S(2)}, u32[]{:S(2)}) collective-permute-start(bf16[768,96]{0,1:T(8,128)(2,1)S(1)} %get-tuple-element.30), channel_id=1, source_target_pairs={{0,3},{1,0},{2,1},{3,2},{4,7},{5,4},{6,5},{7,6},{8,11},{9,8},{10,9... | collective-permute-start | bytes 442376 | tf_op jit(solution)/shard_map/ppermute | solution.py:57
  242.0 6.8 %collective-permute-start.25 = (bf16[768,96]{0,1:T(8,128)(2,1)S(1)}, bf16[768,96]{0,1:T(8,128)(2,1)S(1)}, u32[]{:S(2)}, u32[]{:S(2)}) collective-permute-start(bf16[768,96]{0,1:T(8,128)(2,1)S(1)} %get-tuple-element.31), channel_id=1, source_target_pairs={{0,2},{1,3},{2,0},{3,1},{4,6},{5,7},{6,4},{7,5},{8,10},{9,11},{10,... | collective-permute-start | bytes 442376 | tf_op jit(solution)/shard_map/ppermute | solution.py:57
  244.7 7.5 %collective-permute-start.24 = (bf16[768,96]{0,1:T(8,128)(2,1)S(1)}, bf16[768,96]{0,1:T(8,128)(2,1)S(1)}, u32[]{:S(2)}, u32[]{:S(2)}) collective-permute-start(bf16[768,96]{0,1:T(8,128)(2,1)S(1)} %get-tuple-element.32), channel_id=1, source_target_pairs={{0,1},{1,2},{2,3},{3,0},{4,5},{5,6},{6,7},{7,4},{8,9},{9,10},{10,1... | collective-permute-start | bytes 442376 | tf_op jit(solution)/shard_map/ppermute | solution.py:57
  (28 other events, 275.2 us)
Sparse Core Ops, SparseCore 0:
  13.3 112.6 all-gather.2

commit v7 on v1

--- a/solution.py
+++ b/solution.py
@@ -51,6 +51,35 @@
         else:
             parts.append(lax.ppermute(routed, "lvl", [(r, dst_row)]))
     return jnp.concatenate(parts, axis=-1)
+
+
+def shift(array, by, row_count):
+    return lax.ppermute(array, "lvl", [(i, (i + by) % row_count) for i in range(row_count)])
+
+
+def one_hot_rows(index, count, dtype):
+    return (jnp.arange(count, dtype=jnp.int32) == index).astype(dtype)
+
+
+def blocks_of(level_blocks, my_row, by, row_count):
+    wanted = lax.rem(my_row + by, row_count)
+    chosen = level_blocks[0]
+    for t in range(1, len(level_blocks)):
+        chosen = jnp.where(wanted == t, level_blocks[t], chosen)
+    return chosen
+
+
+def pick_block(blocks, index, count):
+    hot = (jnp.arange(count, dtype=jnp.int32) == index).astype(blocks.dtype)
+    return jnp.sum(blocks * hot[None, :, None], axis=1).astype(blocks.dtype)
+
+
+def frees_at(parts, my_row, t, row_count):
+    pick = lax.rem(my_row - t + row_count, row_count)
+    chosen = parts[0]
+    for d in range(1, row_count):
+        chosen = jnp.where(pick == d, parts[d], chosen)
+    return chosen
 
 
 def route(piece, send_to, take_from, block_count):
@@ -84,49 +113,106 @@
     def keep_of(t):
         return (lanes[None, :] < mine_rank[t][:, None]).astype(jnp.float32)
 
-    solved = jnp.zeros(rhs_here.shape, jnp.bfloat16)
-    incoming = None
-    for t in range(level_count):
-        current = rhs_here.astype(jnp.float32)
+    last = level_count - 1
+    tile_count, block_rows, _ = left_here.shape
+    columns = rhs_here.shape[-1]
+    width = columns // row_count
+    flat = tile_count * rank_width
+    my_rank = jnp.zeros((tile_count,), jnp.int32)
+    for t in range(1, level_count):
+        my_rank = jnp.where(my_row == t, mine_rank[t], my_rank)
+    keep = (lanes[None, :] < my_rank[:, None]).astype(left_here.dtype)
+    left_flat = (left_here * keep[:, None, :]).transpose(1, 0, 2).reshape(block_rows, flat)
+    right_flat = right_here.transpose(1, 0, 2).reshape(block_rows, flat)
+
+    def dot(a, b, spec):
+        return jnp.einsum(spec, a, b, preferred_element_type=jnp.float32)
+
+    inv_left = dot(inverse_here, left_flat, "ab,bm->am").astype(jnp.bfloat16)
+    couple = dot(right_flat, inv_left, "bq,bm->qm").astype(jnp.bfloat16)
+    inv_rhs = dot(inverse_here, rhs_here, "ab,bn->an").astype(jnp.bfloat16)
+    free = dot(right_flat, inv_rhs, "bq,bn->qn").astype(jnp.bfloat16)
+    couples = [couple] + [shift(couple, d, row_count) for d in range(1, row_count)]
+    free_blocks = free.reshape(flat, row_count, width)
+    frees = [pick_block(free_blocks, my_row, row_count)]
+    for d in range(1, row_count):
+        frees.append(shift(pick_block(free_blocks, lax.rem(my_row + d, row_count), row_count), d, row_count))
+
+    def from_row(parts, t):
+        pick = lax.rem(my_row - t + row_count, row_count)
+        chosen = parts[row_count - 1]
+        for d in reversed(range(row_count - 1)):
+            chosen = jnp.where(pick == d, parts[d], chosen)
+        return chosen
+
+    def solve_forward(coef_full):
+        lower = rhs_here.astype(jnp.float32) - dot(
+            left_flat, coef_full.reshape(flat, columns), "bm,mn->bn"
+        )
+        return dot(inverse_here, lower.astype(jnp.bfloat16), "ab,bn->an").astype(jnp.bfloat16)
+
+    def solve_backward(fwd, back_full):
+        upper = fwd.astype(jnp.float32) - dot(
+            right_flat, back_full.reshape(flat, columns), "bm,mn->bn"
+        )
+        return dot(inverse_here, upper.astype(jnp.bfloat16), "ba,bn->an").astype(jnp.bfloat16)
+
+    lane_shape = (tile_count, rank_width, width)
+    first = dot(inverse_here, rhs_here, "ab,bn->an").astype(jnp.bfloat16)
+    out = dot(right_flat, first, "bq,bn->qn").astype(jnp.bfloat16)
+    piece = spread(out.reshape(tile_count, rank_width, columns), 0, row_count, my_row)
+    chain = [None] * level_count
+    chain[1] = route(piece, mine_target[1], mine_src[1], block_count)
+    couple_at = [None] + [from_row(couples, t) for t in range(1, last)]
+    for t in range(1, last):
+        step = frees_at(frees, my_row, t, row_count).astype(jnp.float32) - dot(
+            couple_at[t], chain[t].reshape(flat, width), "qm,mn->qn"
+        )
+        chain[t + 1] = route(step.astype(jnp.bfloat16).reshape(lane_shape), mine_target[t + 1], mine_src[t + 1], block_count)
+
+    solved = jnp.where(my_row == 0, first, jnp.zeros_like(first))
+    back_free = [None] * level_count
+    for t in range(1, last):
+        coef_full = collect(chain[t], t, row_count)
+
+        def owner(coef_full):
+            fwd = solve_forward(coef_full)
+            back_in = dot(inverse_here, fwd, "ba,bn->an").astype(jnp.bfloat16)
+            return fwd, dot(left_flat, back_in, "bm,bn->mn").astype(jnp.bfloat16)
+
+        def other(coef_full):
+            return jnp.zeros_like(rhs_here), jnp.zeros((flat, columns), jnp.bfloat16)
+
+        fwd, back_term = lax.cond(my_row == t, owner, other, coef_full)
+        solved = jnp.where(my_row == t, fwd, solved)
+        back_free[t] = spread(back_term.reshape(tile_count, rank_width, columns), t, row_count, my_row)
+
+    top_fwd = solve_forward(collect(chain[last], last, row_count))
+    solved = jnp.where(my_row == last, top_fwd, solved)
+    top = dot(inverse_here, top_fwd, "ba,bn->an").astype(jnp.bfloat16)
+    out = dot(left_flat, top, "bm,bn->mn").astype(jnp.bfloat16)
+    piece = spread(out.reshape(tile_count, rank_width, columns), last, row_count, my_row)
+    back = [None] * level_count
+    back[last - 1] = route(piece, mine_src[last], mine_target[last], block_count)
+    for t in reversed(range(1, last)):
+        step = back_free[t].reshape(flat, width).astype(jnp.float32) - dot(
+            couple_at[t], back[t].reshape(flat, width), "mq,mn->qn"
+        )
+        back[t - 1] = route(step.astype(jnp.bfloat16).reshape(lane_shape), mine_src[t], mine_target[t], block_count)
+
+    answer = jnp.where(my_row == last, top, jnp.zeros_like(top))
+    for t in reversed(range(last)):
+        back_full = collect(back[t], t, row_count)
         if t > 0:
-            masked = incoming * keep_of(t)[..., None].astype(jnp.bfloat16)
-            current = current - jnp.einsum(
-                "kbr,krn->bn", left_here, masked, preferred_element_type=jnp.float32
+            result = lax.cond(
+                my_row == t,
+                lambda ops: solve_backward(*ops),
+                lambda ops: jnp.zeros_like(rhs_here),
+                (solved, back_full),
             )
-        lowered = current.astype(jnp.bfloat16)
-        result = jnp.einsum(
-            "ab,bn->an", inverse_here, lowered, preferred_element_type=jnp.float32
-        ).astype(jnp.bfloat16)
-        solved = jnp.where(my_row == t, result, solved)
-        if t + 1 < level_count:
-            out = jnp.einsum(
-                "kbr,bn->krn", right_here, result, preferred_element_type=jnp.float32
-            ).astype(jnp.bfloat16)
-            piece = spread(out, t, row_count, my_row)
-            routed = route(piece, mine_target[t + 1], mine_src[t + 1], block_count)
-            incoming = collect(routed, t + 1, row_count)
-
-    answer = jnp.zeros(rhs_here.shape, jnp.bfloat16)
-    returning = None
-    for t in reversed(range(level_count)):
-        current = solved.astype(jnp.float32)
-        if t + 1 < level_count:
-            current = current - jnp.einsum(
-                "kbr,krn->bn", right_here, returning, preferred_element_type=jnp.float32
-            )
-        upper = current.astype(jnp.bfloat16)
-        result = jnp.einsum(
-            "ba,bn->an", inverse_here, upper, preferred_element_type=jnp.float32
-        ).astype(jnp.bfloat16)
+        else:
+            result = solve_backward(solved, back_full)
         answer = jnp.where(my_row == t, result, answer)
-        if t > 0:
-            projected = jnp.einsum(
-                "kbr,bn->krn", left_here, result, preferred_element_type=jnp.float32
-            )
-            out = (projected * keep_of(t)[..., None]).astype(jnp.bfloat16)
-            piece = spread(out, t, row_count, my_row)
-            routed = route(piece, mine_src[t], mine_target[t], block_count)
-            returning = collect(routed, t - 1, row_count)
     return (solved[None, None], answer[None, None])
 
 

time: 260 us -> 226 us (0.87)
  blocking collectives: 119 us -> 17.9 us
  starting transfers between devices: 51.9 us -> 93.1 us
  local copies, waits for them, and re-layouts: 5.13 us -> 17.2 us
  other arithmetic: 4.04 us -> 15.7 us
  waiting for transfers between devices: 45.2 us -> 55.3 us
  matrix products: 31.9 us -> 21.9 us
    all_to_all x6 -> x1, blocking collectives: 119 us -> 17.9 us  [route(): lax.all_to_all(holder, 'blk', split_axis=0, concat_axis=0, tiled=True)]
    all_to_all x0 -> x5, starting transfers between devices: none -> 41.2 us  [route(): lax.all_to_all(holder, 'blk', split_axis=0, concat_axis=0, tiled=True)]
    all_to_all x0 -> x5, waiting for transfers between devices: none -> 15.6 us  [route(): lax.all_to_all(holder, 'blk', split_axis=0, concat_axis=0, tiled=True)]
    ppermute x0 -> x6, waiting for transfers between devices: none -> 12.6 us  [shift(): lax.ppermute(array, 'lvl', [(i, (i + by) % row_count) for i in range(row_...]
    ppermute x18 -> x12, waiting for transfers between devices: 31.8 us -> 19.4 us  [spread(): got = lax.ppermute(part, 'lvl', [(src_row, r)])]
    dot_general x14 -> x11, matrix products: 26.9 us -> 16.9 us  [dot(): return jnp.einsum(spec, a, b, preferred_element_type=jnp.float32)]
    ppermute x18, waiting for transfers between devices: 13.3 us -> 7.7 us  [collect(): parts.append(lax.ppermute(routed, 'lvl', [(r, dst_row)]))]
    ppermute x0 -> x6, starting transfers between devices: none -> 5.37 us  [shift(): lax.ppermute(array, 'lvl', [(i, (i + by) % row_count) for i in range(row_...]
  transfers between devices with their start and end apart: 36 -> 41, of which waited for: 13 -> 10; matrix products, arithmetic and copies ran while one was open for 1% -> 15% of each run, Pallas kernels for 0% -> 0%
where the time goes in v7:
time: 226 us; the launch traced here: 223 us
  starting transfers between devices  93.1 us (41%)
  waiting for transfers between devices  55.3 us (24%)
  matrix products  21.9 us (10%)
  blocking collectives  17.9 us (8%)
  local copies, waits for them, and re-layouts  17.2 us (8%)
  other arithmetic  15.7 us (7%)
    all_to_all x5, starting transfers between devices, route(): lax.all_to_all(holder, 'blk', split_axis=0, concat_axis=0, tiled=True)  41.2 us
    ppermute x18, starting transfers between devices, collect(): parts.append(lax.ppermute(routed, 'lvl', [(r, dst_row)]))  30.7 us
    ppermute x12, waiting for transfers between devices, spread(): got = lax.ppermute(part, 'lvl', [(src_row, r)])  19.4 us
    all_to_all x1, blocking collectives, route(): lax.all_to_all(holder, 'blk', split_axis=0, concat_axis=0, tiled=True)  17.9 us
    dot_general x11, matrix products, dot(): return jnp.einsum(spec, a, b, preferred_element_type=jnp.float32)  16.9 us
    ppermute x12, starting transfers between devices, spread(): got = lax.ppermute(part, 'lvl', [(src_row, r)])  15.8 us
    all_to_all x5, waiting for transfers between devices, route(): lax.all_to_all(holder, 'blk', split_axis=0, concat_axis=0, tiled=True)  15.6 us
    ppermute x6, waiting for transfers between devices, shift(): lax.ppermute(array, 'lvl', [(i, (i + by) % row_count) for i in range(row_...  12.6 us
  transfers between devices with their start and end apart: 41, of which 10 were waited for; matrix products, arithmetic and copies ran while one was open for 15% of the time, Pallas kernels for 0%

profile of v7, /device:TPU:1, one launch (start us, length us, event | category | flops | bytes accessed | tf_op | source)
XLA Modules:
  0.0 222.7 jit_solution(12790506470682879883)
XLA Ops:
  0.6 2.3 %convolution_convert_fusion.16 = bf16[768,384]{1,0:T(8,128)(2,1)S(1)} fusion(bf16[1,1,768,768]{3,2,1,0:T(8,128)(2,1)} %param.16, bf16[1,1,768,384]{3,2,1,0:T(8,128)(2,1)} %param.15), kind=kOutput, calls=%fused_computation.42 | convolution fusion | flops 453279744 | bytes 2359296 | tf_op jit(solution)/shard_map/ab,bn->an/dot_general | solution.py:129
  4.0 5.3 %collective-permute-start.8 = (bf16[4,128,96]{1,0,2:T(4,128)(2,1)S(1)}, bf16[4,128,96]{1,0,2:T(4,128)(2,1)S(1)}, u32[]{:S(2)}, u32[]{:S(2)}) collective-permute-start(bf16[4,128,96]{1,0,2:T(4,128)(2,1)S(1)} %get-tuple-element.148), channel_id=1, source_target_pairs={{0,3},{4,7},{8,11},{12,15},{16,19},{20,23},{24,27},{28,31},{32,35}... | collective-permute-start | bytes 294920 | tf_op jit(solution)/shard_map/ppermute | solution.py:41
  14.4 2.5 %fusion.23 = bf16[512,512]{0,1:T(8,128)(2,1)S(1)} fusion(bf16[1,1,768,768]{3,2,1,0:T(8,128)(2,1)} %param.16, bf16[1,1,4,768,128]{4,3,2,1,0:T(8,128)(2,1)S(1)} %copy-done, bf16[1,1,4,768,128]{4,3,2,1,0:T(8,128)(2,1)S(1)} %copy-done.1, bf16[4,128]{1,0:T(4,128)(2,1)S(1)} %fusion.87), kind=kOutput, calls=%fused_computation.49 | convolution fusion | flops 1007681536 | bytes 3277824 | tf_op jit(solution)/shard_map/bq,bm->qm/dot_general | solution.py:129
  17.1 2.6 %collective-permute-start.5 = (bf16[512,512]{0,1:T(8,128)(2,1)S(1)}, bf16[512,512]{0,1:T(8,128)(2,1)}, u32[]{:S(2)}, u32[]{:S(2)}) collective-permute-start(bf16[512,512]{0,1:T(8,128)(2,1)S(1)} %fusion.23), channel_id=1, source_target_pairs={{0,3},{1,0},{2,1},{3,2},{4,7},{5,4},{6,5},{7,6},{8,11},{9,8},{10,9... | collective-permute-start | bytes 1572872 | tf_op jit(solution)/shard_map/ppermute | solution.py:57
  21.4 9.6 %all-to-all-start = ((bf16[32,128,96]{1,2,0:T(8,128)(2,1)}), bf16[32,128,96]{1,2,0:T(8,128)(2,1)S(1)}, u32[]{:S(2)}, u32[]{:S(2)}) async-start(bf16[32,128,96]{1,2,0:T(8,128)(2,1)} %copy.63), calls=%async_computation | async-start | bytes 1572864 | tf_op jit(solution)/shard_map/all_to_all | solution.py:89
  34.7 9.4 %collective-permute-done.3 = bf16[512,512]{0,1:T(8,128)(2,1)} collective-permute-done((bf16[512,512]{0,1:T(8,128)(2,1)S(1)}, bf16[512,512]{0,1:T(8,128)(2,1)}, u32[]{:S(2)}, u32[]{:S(2)}) %collective-permute-start.3) | collective-permute-done | bytes 524320 | tf_op jit(solution)/shard_map/ppermute | solution.py:57
  46.0 3.1 %collective-permute-done.2 = bf16[512,96]{0,1:T(8,128)(2,1)} collective-permute-done((bf16[512,96]{0,1:T(8,128)(2,1)}, bf16[512,96]{0,1:T(8,128)(2,1)}, u32[]{:S(2)}, u32[]{:S(2)}) %collective-permute-start.2) | collective-permute-done | bytes 98336 | tf_op jit(solution)/shard_map/ppermute | solution.py:57
  51.1 11.1 %all-to-all-start.1 = ((bf16[32,128,96]{1,2,0:T(8,128)(2,1)}), bf16[32,128,96]{1,2,0:T(8,128)(2,1)S(1)}, u32[]{:S(2)}, u32[]{:S(2)}) async-start(bf16[32,128,96]{1,2,0:T(8,128)(2,1)} %copy.65), calls=%async_computation.1 | async-start | bytes 1572864 | tf_op jit(solution)/shard_map/all_to_all | solution.py:89
  62.2 14.2 %all-to-all-done.1 = bf16[32,128,96]{1,2,0:T(8,128)(2,1)S(1)} async-done(((bf16[32,128,96]{1,2,0:T(8,128)(2,1)}), bf16[32,128,96]{1,2,0:T(8,128)(2,1)S(1)}, u32[]{:S(2)}, u32[]{:S(2)}) %all-to-all-start.1) | async-done | bytes 786464 | tf_op jit(solution)/shard_map/all_to_all | solution.py:89
  78.8 17.9 %all_to_all.30 = bf16[32,128,96]{1,2,0:T(8,128)(2,1)S(1)} all-to-all(bf16[32,128,96]{1,2,0:T(8,128)(2,1)S(1)} %copy.67), channel_id=1, replica_groups=mesh['blk'=32,'lvl'=4] {'blk'}, dimensions={0} | all-to-all | bytes 1572864 | tf_op jit(solution)/shard_map/all_to_all | solution.py:89
  98.3 2.7 %collective-permute-start.9 = (bf16[4,128,96]{1,0,2:T(4,128)(2,1)S(1)}, bf16[4,128,96]{1,0,2:T(4,128)(2,1)S(1)}, u32[]{:S(2)}, u32[]{:S(2)}) collective-permute-start(bf16[4,128,96]{1,0,2:T(4,128)(2,1)S(1)} %convolution_convert_fusion.23), channel_id=1, source_target_pairs={{0,3},{4,7},{8,11},{12,15},{16,19},{20,23},{24,27},{28,31},{32,35}... | collective-permute-start | bytes 294920 | tf_op jit(solution)/shard_map/ppermute | solution.py:52
  101.0 3.5 %collective-permute-done.9 = bf16[4,128,96]{1,0,2:T(4,128)(2,1)S(1)} collective-permute-done((bf16[4,128,96]{1,0,2:T(4,128)(2,1)S(1)}, bf16[4,128,96]{1,0,2:T(4,128)(2,1)S(1)}, u32[]{:S(2)}, u32[]{:S(2)}) %collective-permute-start.9) | collective-permute-done | bytes 98336 | tf_op jit(solution)/shard_map/ppermute | solution.py:52
  105.5 2.7 %convolution_convert_fusion.13 = bf16[384,768]{0,1:T(8,128)(2,1)S(1)} fusion(bf16[1,1,4,768,128]{4,3,2,1,0:T(8,128)(2,1)S(1)} %copy-done.2, bf16[4,128,384]{1,0,2:T(4,128)(2,1)} %pad_maximum_fusion, bf16[4,128]{1,0:T(4,128)(2,1)S(1)} %copy-done.16, bf16[1,1,768,768]{3,2,1,0:T(8,128)(2,1)} %param.16, bf16[1,1,768,384]{3,2,1,0:T(8,128)(2,1)} %param.15), kind=kOutput, calls=%fused_computation.39 | convolution fusion | flops 756547584 | bytes 3539968 | tf_op jit(solution)/shard_map/ab,bn->an/dot_general | solution.py:129
  116.7 6.2 %collective-permute-start.12 = (bf16[4,128,96]{1,0,2:T(4,128)(2,1)S(1)}, bf16[4,128,96]{1,0,2:T(4,128)(2,1)S(1)}, u32[]{:S(2)}, u32[]{:S(2)}) collective-permute-start(bf16[4,128,96]{1,0,2:T(4,128)(2,1)S(1)} %convolution_convert_fusion.24), channel_id=1, source_target_pairs={{0,2},{4,6},{8,10},{12,14},{16,18},{20,22},{24,26},{28,30},{32,34}... | collective-permute-start | bytes 294920 | tf_op jit(solution)/shard_map/ppermute | solution.py:52
  124.7 4.8 %all-to-all-start.3 = ((bf16[32,128,96]{1,2,0:T(8,128)(2,1)}), bf16[32,128,96]{1,2,0:T(8,128)(2,1)S(1)}, u32[]{:S(2)}, u32[]{:S(2)}) async-start(bf16[32,128,96]{1,2,0:T(8,128)(2,1)} %copy.80), calls=%async_computation.3 | async-start | bytes 1572864 | tf_op jit(solution)/shard_map/all_to_all | solution.py:89
  129.5 2.2 copy_bitcast_fusion
  141.1 3.8 %collective-permute-start.15 = (bf16[4,128,96]{1,0,2:T(4,128)(2,1)S(1)}, bf16[4,128,96]{1,0,2:T(4,128)(2,1)}, u32[]{:S(2)}, u32[]{:S(2)}) collective-permute-start(bf16[4,128,96]{1,0,2:T(4,128)(2,1)S(1)} %convolution_convert_fusion.25), channel_id=1, source_target_pairs={{0,1},{4,5},{8,9},{12,13},{16,17},{20,21},{24,25},{28,29},{32,33},... | collective-permute-start | bytes 294920 | tf_op jit(solution)/shard_map/ppermute | solution.py:52
  144.9 6.0 %collective-permute-done.21 = bf16[4,128,96]{1,0,2:T(4,128)(2,1)S(1)} collective-permute-done((bf16[4,128,96]{1,0,2:T(4,128)(2,1)S(1)}, bf16[4,128,96]{1,0,2:T(4,128)(2,1)S(1)}, u32[]{:S(2)}, u32[]{:S(2)}) %collective-permute-start.21) | collective-permute-done | bytes 98336 | tf_op jit(solution)/shard_map/ppermute | solution.py:41
  155.8 8.0 %all-to-all-start.4 = ((bf16[32,128,96]{1,2,0:T(8,128)(2,1)}), bf16[32,128,96]{1,2,0:T(8,128)(2,1)S(1)}, u32[]{:S(2)}, u32[]{:S(2)}) async-start(bf16[32,128,96]{1,2,0:T(8,128)(2,1)} %copy.82), calls=%async_computation.4 | async-start | bytes 1572864 | tf_op jit(solution)/shard_map/all_to_all | solution.py:89
  170.6 13.4 %collective-permute-done.18 = bf16[4,128,96]{1,0,2:T(4,128)(2,1)S(1)} collective-permute-done((bf16[4,128,96]{1,0,2:T(4,128)(2,1)S(1)}, bf16[4,128,96]{1,0,2:T(4,128)(2,1)S(1)}, u32[]{:S(2)}, u32[]{:S(2)}) %collective-permute-start.18) | collective-permute-done | bytes 98336 | tf_op jit(solution)/shard_map/ppermute | solution.py:41
  187.5 7.7 %all-to-all-start.5 = ((bf16[32,128,96]{1,2,0:T(8,128)(2,1)}), bf16[32,128,96]{1,2,0:T(8,128)(2,1)S(1)}, u32[]{:S(2)}, u32[]{:S(2)}) async-start(bf16[32,128,96]{1,2,0:T(8,128)(2,1)} %copy.84), calls=%async_computation.5 | async-start | bytes 1572864 | tf_op jit(solution)/shard_map/all_to_all | solution.py:89
  196.8 3.7 %collective-permute-start.33 = (bf16[4,128,96]{1,0,2:T(4,128)(2,1)S(1)}, bf16[4,128,96]{1,0,2:T(4,128)(2,1)S(1)}, u32[]{:S(2)}, u32[]{:S(2)}) collective-permute-start(bf16[4,128,96]{1,0,2:T(4,128)(2,1)S(1)} %convolution_convert_fusion.22), channel_id=1, source_target_pairs={{0,2},{4,6},{8,10},{12,14},{16,18},{20,22},{24,26},{28,30},{32,34}... | collective-permute-start | bytes 294920 | tf_op jit(solution)/shard_map/ppermute | solution.py:52
  205.1 3.0 %collective-permute-start.30 = (bf16[4,128,96]{1,0,2:T(4,128)(2,1)S(1)}, bf16[4,128,96]{1,0,2:T(4,128)(2,1)}, u32[]{:S(2)}, u32[]{:S(2)}) collective-permute-start(bf16[4,128,96]{1,0,2:T(4,128)(2,1)S(1)} %convolution_convert_fusion.21), channel_id=1, source_target_pairs={{0,1},{4,5},{8,9},{12,13},{16,17},{20,21},{24,25},{28,29},{32,33},... | collective-permute-start | bytes 294920 | tf_op jit(solution)/shard_map/ppermute | solution.py:52
  219.4 3.4 %fusion.22 = bf16[1,1,768,384]{3,2,1,0:T(8,128)(2,1)} fusion(bf16[768,384]{1,0:T(8,128)(2,1)S(1)} %copy-done.7, bf16[1,1,4,768,128]{4,3,2,1,0:T(8,128)(2,1)S(1)} %copy-done, bf16[768,384]{1,0:T(8,128)(2,1)} %get-tuple-element.114, bf16[768,384]{1,0:T(8,128)(2,1)} %get-tuple-element.115, bf16[384,768]{0,1:T(8,128)(2,1)} %copy-done.17, pred[]{:T(512)S(6)} %eq.172, ...), kind=kOutput, calls=%fused_computation.46 | convolution fusion | flops 757334016 | bytes 5308420 | tf_op jit(solution)/shard_map/ba,bn->an/dot_general | solution.py:129
  (180 shorter events, 75.7 us)
Async XLA Ops:
  4.0 13.1 %collective-permute-start.8 = (bf16[4,128,96]{1,0,2:T(4,128)(2,1)S(1)}, bf16[4,128,96]{1,0,2:T(4,128)(2,1)S(1)}, u32[]{:S(2)}, u32[]{:S(2)}) collective-permute-start(bf16[4,128,96]{1,0,2:T(4,128)(2,1)S(1)} %get-tuple-element.148), channel_id=1, source_target_pairs={{0,3},{4,7},{8,11},{12,15},{16,19},{20,23},{24,27},{28,31},{32,35}... | collective-permute-start | bytes 294920 | tf_op jit(solution)/shard_map/ppermute | solution.py:41
  9.3 10.3 %collective-permute-start.7 = (bf16[4,128,96]{1,0,2:T(4,128)(2,1)S(1)}, bf16[4,128,96]{1,0,2:T(4,128)(2,1)S(1)}, u32[]{:S(2)}, u32[]{:S(2)}) collective-permute-start(bf16[4,128,96]{1,0,2:T(4,128)(2,1)S(1)} %get-tuple-element.149), channel_id=1, source_target_pairs={{0,2},{4,6},{8,10},{12,14},{16,18},{20,22},{24,26},{28,30},{32,34}... | collective-permute-start | bytes 294920 | tf_op jit(solution)/shard_map/ppermute | solution.py:41
  10.7 9.0 %collective-permute-start.6 = (bf16[4,128,96]{1,0,2:T(4,128)(2,1)S(1)}, bf16[4,128,96]{1,0,2:T(4,128)(2,1)S(1)}, u32[]{:S(2)}, u32[]{:S(2)}) collective-permute-start(bf16[4,128,96]{1,0,2:T(4,128)(2,1)S(1)} %get-tuple-element.147), channel_id=1, source_target_pairs={{0,1},{4,5},{8,9},{12,13},{16,17},{20,21},{24,25},{28,29},{32,33},... | collective-permute-start | bytes 294920 | tf_op jit(solution)/shard_map/ppermute | solution.py:41
  16.9 27.2 %collective-permute-start.3 = (bf16[512,512]{0,1:T(8,128)(2,1)S(1)}, bf16[512,512]{0,1:T(8,128)(2,1)}, u32[]{:S(2)}, u32[]{:S(2)}) collective-permute-start(bf16[512,512]{0,1:T(8,128)(2,1)S(1)} %fusion.23), channel_id=1, source_target_pairs={{0,1},{1,2},{2,3},{3,0},{4,5},{5,6},{6,7},{7,4},{8,9},{9,10},{10,1... | collective-permute-start | bytes 1572872 | tf_op jit(solution)/shard_map/ppermute | solution.py:57
  17.0 27.1 %collective-permute-start.4 = (bf16[512,512]{0,1:T(8,128)(2,1)S(1)}, bf16[512,512]{0,1:T(8,128)(2,1)}, u32[]{:S(2)}, u32[]{:S(2)}) collective-permute-start(bf16[512,512]{0,1:T(8,128)(2,1)S(1)} %fusion.23), channel_id=1, source_target_pairs={{0,2},{1,3},{2,0},{3,1},{4,6},{5,7},{6,4},{7,5},{8,10},{9,11},{10,... | collective-permute-start | bytes 1572872 | tf_op jit(solution)/shard_map/ppermute | solution.py:57
  17.1 27.0 %collective-permute-start.5 = (bf16[512,512]{0,1:T(8,128)(2,1)S(1)}, bf16[512,512]{0,1:T(8,128)(2,1)}, u32[]{:S(2)}, u32[]{:S(2)}) collective-permute-start(bf16[512,512]{0,1:T(8,128)(2,1)S(1)} %fusion.23), channel_id=1, source_target_pairs={{0,3},{1,0},{2,1},{3,2},{4,7},{5,4},{6,5},{7,6},{8,11},{9,8},{10,9... | collective-permute-start | bytes 1572872 | tf_op jit(solution)/shard_map/ppermute | solution.py:57
  21.4 24.2 %all-to-all-start = ((bf16[32,128,96]{1,2,0:T(8,128)(2,1)}), bf16[32,128,96]{1,2,0:T(8,128)(2,1)S(1)}, u32[]{:S(2)}, u32[]{:S(2)}) async-start(bf16[32,128,96]{1,2,0:T(8,128)(2,1)} %copy.63), calls=%async_computation | async-start | bytes 1572864 | tf_op jit(solution)/shard_map/all_to_all | solution.py:89
  32.0 13.9 %collective-permute-start = (bf16[512,96]{0,1:T(8,128)(2,1)}, bf16[512,96]{0,1:T(8,128)(2,1)S(1)}, u32[]{:S(2)}, u32[]{:S(2)}) collective-permute-start(bf16[512,96]{0,1:T(8,128)(2,1)} %get-tuple-element.119), channel_id=1, source_target_pairs={{0,3},{1,0},{2,1},{3,2},{4,7},{5,4},{6,5},{7,6},{8,11},{9,8},{10,9... | collective-permute-start | bytes 294920 | tf_op jit(solution)/shard_map/ppermute | solution.py:57
  32.7 13.2 %collective-permute-start.1 = (bf16[512,96]{0,1:T(8,128)(2,1)}, bf16[512,96]{0,1:T(8,128)(2,1)S(1)}, u32[]{:S(2)}, u32[]{:S(2)}) collective-permute-start(bf16[512,96]{0,1:T(8,128)(2,1)} %get-tuple-element.118), channel_id=1, source_target_pairs={{0,2},{1,3},{2,0},{3,1},{4,6},{5,7},{6,4},{7,5},{8,10},{9,11},{10,... | collective-permute-start | bytes 294920 | tf_op jit(solution)/shard_map/ppermute | solution.py:57
  51.1 25.3 %all-to-all-start.1 = ((bf16[32,128,96]{1,2,0:T(8,128)(2,1)}), bf16[32,128,96]{1,2,0:T(8,128)(2,1)S(1)}, u32[]{:S(2)}, u32[]{:S(2)}) async-start(bf16[32,128,96]{1,2,0:T(8,128)(2,1)} %copy.65), calls=%async_computation.1 | async-start | bytes 1572864 | tf_op jit(solution)/shard_map/all_to_all | solution.py:89
  113.1 9.8 %collective-permute-start.24 = (bf16[4,128,96]{1,0,2:T(4,128)(2,1)S(1)}, bf16[4,128,96]{1,0,2:T(4,128)(2,1)S(1)}, u32[]{:S(2)}, u32[]{:S(2)}) collective-permute-start(bf16[4,128,96]{1,0,2:T(4,128)(2,1)S(1)} %copy.106), channel_id=1, source_target_pairs={{3,0},{7,4},{11,8},{15,12},{19,16},{23,20},{27,24},{31,28},{35,32}... | collective-permute-start | bytes 294920 | tf_op jit(solution)/shard_map/ppermute | solution.py:41
  115.2 16.4 %collective-permute-start.14 = (bf16[4,128,96]{1,0,2:T(4,128)(2,1)S(1)}, bf16[4,128,96]{1,0,2:T(4,128)(2,1)S(1)}, u32[]{:S(2)}, u32[]{:S(2)}) collective-permute-start(bf16[4,128,96]{1,0,2:T(4,128)(2,1)S(1)} %convolution_convert_fusion.24), channel_id=1, source_target_pairs={{3,2},{7,6},{11,10},{15,14},{19,18},{23,22},{27,26},{31,30},{35,34... | collective-permute-start | bytes 294920 | tf_op jit(solution)/shard_map/ppermute | solution.py:52
  115.9 15.7 %collective-permute-start.13 = (bf16[4,128,96]{1,0,2:T(4,128)(2,1)S(1)}, bf16[4,128,96]{1,0,2:T(4,128)(2,1)S(1)}, u32[]{:S(2)}, u32[]{:S(2)}) collective-permute-start(bf16[4,128,96]{1,0,2:T(4,128)(2,1)S(1)} %convolution_convert_fusion.24), channel_id=1, source_target_pairs={{1,2},{5,6},{9,10},{13,14},{17,18},{21,22},{25,26},{29,30},{33,34}... | collective-permute-start | bytes 294920 | tf_op jit(solution)/shard_map/ppermute | solution.py:52
  116.7 14.9 %collective-permute-start.12 = (bf16[4,128,96]{1,0,2:T(4,128)(2,1)S(1)}, bf16[4,128,96]{1,0,2:T(4,128)(2,1)S(1)}, u32[]{:S(2)}, u32[]{:S(2)}) collective-permute-start(bf16[4,128,96]{1,0,2:T(4,128)(2,1)S(1)} %convolution_convert_fusion.24), channel_id=1, source_target_pairs={{0,2},{4,6},{8,10},{12,14},{16,18},{20,22},{24,26},{28,30},{32,34}... | collective-permute-start | bytes 294920 | tf_op jit(solution)/shard_map/ppermute | solution.py:52
  124.7 27.9 %all-to-all-start.3 = ((bf16[32,128,96]{1,2,0:T(8,128)(2,1)}), bf16[32,128,96]{1,2,0:T(8,128)(2,1)S(1)}, u32[]{:S(2)}, u32[]{:S(2)}) async-start(bf16[32,128,96]{1,2,0:T(8,128)(2,1)} %copy.80), calls=%async_computation.3 | async-start | bytes 1572864 | tf_op jit(solution)/shard_map/all_to_all | solution.py:89
  137.2 13.7 %collective-permute-start.21 = (bf16[4,128,96]{1,0,2:T(4,128)(2,1)S(1)}, bf16[4,128,96]{1,0,2:T(4,128)(2,1)S(1)}, u32[]{:S(2)}, u32[]{:S(2)}) collective-permute-start(bf16[4,128,96]{1,0,2:T(4,128)(2,1)S(1)} %get-tuple-element.146), channel_id=1, source_target_pairs={{2,0},{6,4},{10,8},{14,12},{18,16},{22,20},{26,24},{30,28},{34,32}... | collective-permute-start | bytes 294920 | tf_op jit(solution)/shard_map/ppermute | solution.py:41
  138.5 12.4 %collective-permute-start.22 = (bf16[4,128,96]{1,0,2:T(4,128)(2,1)S(1)}, bf16[4,128,96]{1,0,2:T(4,128)(2,1)S(1)}, u32[]{:S(2)}, u32[]{:S(2)}) collective-permute-start(bf16[4,128,96]{1,0,2:T(4,128)(2,1)S(1)} %get-tuple-element.144), channel_id=1, source_target_pairs={{2,1},{6,5},{10,9},{14,13},{18,17},{22,21},{26,25},{30,29},{34,33}... | collective-permute-start | bytes 294920 | tf_op jit(solution)/shard_map/ppermute | solution.py:41
  139.1 24.7 %collective-permute-start.17 = (bf16[4,128,96]{1,0,2:T(4,128)(2,1)S(1)}, bf16[4,128,96]{1,0,2:T(4,128)(2,1)S(1)}, u32[]{:S(2)}, u32[]{:S(2)}) collective-permute-start(bf16[4,128,96]{1,0,2:T(4,128)(2,1)S(1)} %convolution_convert_fusion.25), channel_id=1, source_target_pairs={{3,1},{7,5},{11,9},{15,13},{19,17},{23,21},{27,25},{31,29},{35,33}... | collective-permute-start | bytes 294920 | tf_op jit(solution)/shard_map/ppermute | solution.py:52
  139.8 24.1 %collective-permute-start.16 = (bf16[4,128,96]{1,0,2:T(4,128)(2,1)S(1)}, bf16[4,128,96]{1,0,2:T(4,128)(2,1)}, u32[]{:S(2)}, u32[]{:S(2)}) collective-permute-start(bf16[4,128,96]{1,0,2:T(4,128)(2,1)S(1)} %convolution_convert_fusion.25), channel_id=1, source_target_pairs={{2,1},{6,5},{10,9},{14,13},{18,17},{22,21},{26,25},{30,29},{34,33}... | collective-permute-start | bytes 294920 | tf_op jit(solution)/shard_map/ppermute | solution.py:52
  141.1 22.8 %collective-permute-start.15 = (bf16[4,128,96]{1,0,2:T(4,128)(2,1)S(1)}, bf16[4,128,96]{1,0,2:T(4,128)(2,1)}, u32[]{:S(2)}, u32[]{:S(2)}) collective-permute-start(bf16[4,128,96]{1,0,2:T(4,128)(2,1)S(1)} %convolution_convert_fusion.25), channel_id=1, source_target_pairs={{0,1},{4,5},{8,9},{12,13},{16,17},{20,21},{24,25},{28,29},{32,33},... | collective-permute-start | bytes 294920 | tf_op jit(solution)/shard_map/ppermute | solution.py:52
  155.8 29.2 %all-to-all-start.4 = ((bf16[32,128,96]{1,2,0:T(8,128)(2,1)}), bf16[32,128,96]{1,2,0:T(8,128)(2,1)S(1)}, u32[]{:S(2)}, u32[]{:S(2)}) async-start(bf16[32,128,96]{1,2,0:T(8,128)(2,1)} %copy.82), calls=%async_computation.4 | async-start | bytes 1572864 | tf_op jit(solution)/shard_map/all_to_all | solution.py:89
  169.3 14.8 %collective-permute-start.18 = (bf16[4,128,96]{1,0,2:T(4,128)(2,1)S(1)}, bf16[4,128,96]{1,0,2:T(4,128)(2,1)S(1)}, u32[]{:S(2)}, u32[]{:S(2)}) collective-permute-start(bf16[4,128,96]{1,0,2:T(4,128)(2,1)S(1)} %get-tuple-element.137), channel_id=1, source_target_pairs={{1,0},{5,4},{9,8},{13,12},{17,16},{21,20},{25,24},{29,28},{33,32},... | collective-permute-start | bytes 294920 | tf_op jit(solution)/shard_map/ppermute | solution.py:41
  187.5 22.0 %all-to-all-start.5 = ((bf16[32,128,96]{1,2,0:T(8,128)(2,1)}), bf16[32,128,96]{1,2,0:T(8,128)(2,1)S(1)}, u32[]{:S(2)}, u32[]{:S(2)}) async-start(bf16[32,128,96]{1,2,0:T(8,128)(2,1)} %copy.84), calls=%async_computation.5 | async-start | bytes 1572864 | tf_op jit(solution)/shard_map/all_to_all | solution.py:89
  204.4 9.3 %collective-permute-start.31 = (bf16[4,128,96]{1,0,2:T(4,128)(2,1)S(1)}, bf16[4,128,96]{1,0,2:T(4,128)(2,1)S(1)}, u32[]{:S(2)}, u32[]{:S(2)}) collective-permute-start(bf16[4,128,96]{1,0,2:T(4,128)(2,1)S(1)} %convolution_convert_fusion.21), channel_id=1, source_target_pairs={{2,1},{6,5},{10,9},{14,13},{18,17},{22,21},{26,25},{30,29},{34,33}... | collective-permute-start | bytes 294920 | tf_op jit(solution)/shard_map/ppermute | solution.py:52
  (34 other events, 218.3 us)

commit v8 on v7

--- a/solution.py
+++ b/solution.py
@@ -67,6 +67,26 @@
     for t in range(1, len(level_blocks)):
         chosen = jnp.where(wanted == t, level_blocks[t], chosen)
     return chosen
+
+
+def of_level(parts, index):
+    chosen = parts[0]
+    for t in range(1, len(parts)):
+        chosen = jnp.where(index == t, parts[t], chosen)
+    return chosen
+
+
+def take_block(full, index, count):
+    width = full.shape[-1] // count
+    blocks = full.reshape(full.shape[:-1] + (count, width))
+    hot = (jnp.arange(count, dtype=jnp.int32) == index).astype(full.dtype)
+    return jnp.sum(blocks * hot[:, None], axis=-2).astype(full.dtype)
+
+
+def put_block(part, index, count):
+    hot = (jnp.arange(count, dtype=jnp.int32) == index).astype(part.dtype)
+    full = part[..., None, :] * hot[:, None]
+    return full.reshape(part.shape[:-1] + (count * part.shape[-1],))
 
 
 def pick_block(blocks, index, count):
@@ -158,10 +178,19 @@
         return dot(inverse_here, upper.astype(jnp.bfloat16), "ba,bn->an").astype(jnp.bfloat16)
 
     lane_shape = (tile_count, rank_width, width)
+    zero_block = jnp.zeros(lane_shape, jnp.bfloat16)
+
+    def own_level_blocks(parts):
+        full = put_block(of_level(parts, my_row), my_row, row_count)
+        for d in range(1, row_count):
+            got = shift(of_level(parts, lax.rem(my_row + d, row_count)), d, row_count)
+            full = full + put_block(got, lax.rem(my_row - d + row_count, row_count), row_count)
+        return full
+
     first = dot(inverse_here, rhs_here, "ab,bn->an").astype(jnp.bfloat16)
     out = dot(right_flat, first, "bq,bn->qn").astype(jnp.bfloat16)
     piece = spread(out.reshape(tile_count, rank_width, columns), 0, row_count, my_row)
-    chain = [None] * level_count
+    chain = [zero_block] * level_count
     chain[1] = route(piece, mine_target[1], mine_src[1], block_count)
     couple_at = [None] + [from_row(couples, t) for t in range(1, last)]
     for t in range(1, last):
@@ -170,49 +199,27 @@
         )
         chain[t + 1] = route(step.astype(jnp.bfloat16).reshape(lane_shape), mine_target[t + 1], mine_src[t + 1], block_count)
 
-    solved = jnp.where(my_row == 0, first, jnp.zeros_like(first))
-    back_free = [None] * level_count
-    for t in range(1, last):
-        coef_full = collect(chain[t], t, row_count)
-
-        def owner(coef_full):
-            fwd = solve_forward(coef_full)
-            back_in = dot(inverse_here, fwd, "ba,bn->an").astype(jnp.bfloat16)
-            return fwd, dot(left_flat, back_in, "bm,bn->mn").astype(jnp.bfloat16)
-
-        def other(coef_full):
-            return jnp.zeros_like(rhs_here), jnp.zeros((flat, columns), jnp.bfloat16)
-
-        fwd, back_term = lax.cond(my_row == t, owner, other, coef_full)
-        solved = jnp.where(my_row == t, fwd, solved)
-        back_free[t] = spread(back_term.reshape(tile_count, rank_width, columns), t, row_count, my_row)
-
-    top_fwd = solve_forward(collect(chain[last], last, row_count))
-    solved = jnp.where(my_row == last, top_fwd, solved)
-    top = dot(inverse_here, top_fwd, "ba,bn->an").astype(jnp.bfloat16)
-    out = dot(left_flat, top, "bm,bn->mn").astype(jnp.bfloat16)
-    piece = spread(out.reshape(tile_count, rank_width, columns), last, row_count, my_row)
-    back = [None] * level_count
-    back[last - 1] = route(piece, mine_src[last], mine_target[last], block_count)
+    mine_fwd = solve_forward(own_level_blocks(chain))
+    solved = jnp.where(my_row == 0, first, mine_fwd)
+    top = dot(inverse_here, solved, "ba,bn->an").astype(jnp.bfloat16)
+    back_term = dot(left_flat, top, "bm,bn->mn").astype(jnp.bfloat16)
+    back_parts = [take_block(back_term, my_row, row_count)]
+    for d in range(1, row_count):
+        back_parts.append(shift(take_block(back_term, lax.rem(my_row + d, row_count), row_count), d, row_count))
+
+    def back_free(t):
+        return frees_at(back_parts, my_row, t, row_count)
+
+    back = [zero_block] * level_count
+    back[last - 1] = route(back_free(last).reshape(lane_shape), mine_src[last], mine_target[last], block_count)
     for t in reversed(range(1, last)):
-        step = back_free[t].reshape(flat, width).astype(jnp.float32) - dot(
-            couple_at[t], back[t].reshape(flat, width), "mq,mn->qn"
+        step = back_free(t).astype(jnp.float32) - dot(
+            couple_at[t], back[t - 0].reshape(flat, width), "mq,mn->qn"
         )
         back[t - 1] = route(step.astype(jnp.bfloat16).reshape(lane_shape), mine_src[t], mine_target[t], block_count)
 
-    answer = jnp.where(my_row == last, top, jnp.zeros_like(top))
-    for t in reversed(range(last)):
-        back_full = collect(back[t], t, row_count)
-        if t > 0:
-            result = lax.cond(
-                my_row == t,
-                lambda ops: solve_backward(*ops),
-                lambda ops: jnp.zeros_like(rhs_here),
-                (solved, back_full),
-            )
-        else:
-            result = solve_backward(solved, back_full)
-        answer = jnp.where(my_row == t, result, answer)
+    mine_back = solve_backward(solved, own_level_blocks(back[:last] + [zero_block]))
+    answer = jnp.where(my_row == last, top, mine_back)
     return (solved[None, None], answer[None, None])
 
 

time: 226 us -> 202 us (0.89); the launches traced: 223 us -> 201 us
  starting transfers between devices: 93.1 us -> 47 us
  blocking collectives: 17.9 us -> 54.1 us
  other arithmetic: 15.7 us -> 8.29 us
  local copies, waits for them, and re-layouts: 17.2 us -> 11.2 us
  waiting for transfers between devices: 55.3 us -> 58.2 us
    all_to_all x1 -> x3, blocking collectives: 17.9 us -> 54.1 us  [route(): lax.all_to_all(holder, 'blk', split_axis=0, concat_axis=0, tiled=True)]
    ppermute x18 -> x0, starting transfers between devices: 30.7 us -> none  [collect(): parts.append(lax.ppermute(routed, 'lvl', [(r, dst_row)]))]
    ppermute x12 -> x3, waiting for transfers between devices: 19.4 us -> 0.01 us  [spread(): got = lax.ppermute(part, 'lvl', [(src_row, r)])]
    ppermute x6 -> x15, waiting for transfers between devices: 12.6 us -> 29.5 us  [shift(): lax.ppermute(array, 'lvl', [(i, (i + by) % row_count) for i in range(row_...]
    all_to_all x5 -> x3, starting transfers between devices: 41.2 us -> 24.7 us  [route(): lax.all_to_all(holder, 'blk', split_axis=0, concat_axis=0, tiled=True)]
    all_to_all x5 -> x3, waiting for transfers between devices: 15.6 us -> 28.7 us  [route(): lax.all_to_all(holder, 'blk', split_axis=0, concat_axis=0, tiled=True)]
    ppermute x18 -> x0, waiting for transfers between devices: 7.7 us -> none  [collect(): parts.append(lax.ppermute(routed, 'lvl', [(r, dst_row)]))]
    ppermute x6 -> x15, starting transfers between devices: 5.37 us -> 13 us  [shift(): lax.ppermute(array, 'lvl', [(i, (i + by) % row_count) for i in range(row_...]
  transfers between devices with their start and end apart: 41 -> 21, of which waited for: 10 -> 13; matrix products, arithmetic and copies ran while one was open for 15% -> 7% of each run, Pallas kernels for 0% -> 0%
where the time goes in v8:
time: 202 us; the launch traced here: 201 us
  waiting for transfers between devices  58.2 us (29%)
  blocking collectives  54.1 us (27%)
  starting transfers between devices  47 us (23%)
  matrix products  21.2 us (10%)
  local copies, waits for them, and re-layouts  11.2 us (6%)
  other arithmetic  8.29 us (4%)
    all_to_all x3, blocking collectives, route(): lax.all_to_all(holder, 'blk', split_axis=0, concat_axis=0, tiled=True)  54.1 us
    ppermute x15, waiting for transfers between devices, shift(): lax.ppermute(array, 'lvl', [(i, (i + by) % row_count) for i in range(row_...  29.5 us
    all_to_all x3, waiting for transfers between devices, route(): lax.all_to_all(holder, 'blk', split_axis=0, concat_axis=0, tiled=True)  28.7 us
    all_to_all x3, starting transfers between devices, route(): lax.all_to_all(holder, 'blk', split_axis=0, concat_axis=0, tiled=True)  24.7 us
    dot_general x11, matrix products, dot(): return jnp.einsum(spec, a, b, preferred_element_type=jnp.float32)  13.4 us
    ppermute x15, starting transfers between devices, shift(): lax.ppermute(array, 'lvl', [(i, (i + by) % row_count) for i in range(row_...  13 us
    ppermute x3, starting transfers between devices, spread(): got = lax.ppermute(part, 'lvl', [(src_row, r)])  9.33 us
    dot_general x6, matrix products, route(): jnp.einsum('kj,krn->jrn', send, piece, preferred_element_type=jnp.float32)  4.88 us
  transfers between devices with their start and end apart: 21, of which 13 were waited for; matrix products, arithmetic and copies ran while one was open for 7% of the time, Pallas kernels for 0%

profile of v8, /device:TPU:1, one launch (start us, length us, event | category | flops | bytes accessed | tf_op | source)
XLA Modules:
  0.0 201.1 jit_solution(8730816413397577135)
XLA Ops:
  4.8 4.6 %collective-permute-start.6 = (bf16[4,128,96]{1,0,2:T(4,128)(2,1)}, bf16[4,128,96]{1,0,2:T(4,128)(2,1)}, u32[]{:S(2)}, u32[]{:S(2)}) collective-permute-start(bf16[4,128,96]{1,0,2:T(4,128)(2,1)} %get-tuple-element.35), channel_id=1, source_target_pairs={{0,1},{4,5},{8,9},{12,13},{16,17},{20,21},{24,25},{28,29},{32,33},... | collective-permute-start | bytes 294920 | tf_op jit(solution)/shard_map/ppermute | solution.py:41
  9.4 2.8 %collective-permute-start.7 = (bf16[4,128,96]{1,0,2:T(4,128)(2,1)}, bf16[4,128,96]{1,0,2:T(4,128)(2,1)}, u32[]{:S(2)}, u32[]{:S(2)}) collective-permute-start(bf16[4,128,96]{1,0,2:T(4,128)(2,1)} %get-tuple-element.37), channel_id=1, source_target_pairs={{0,2},{4,6},{8,10},{12,14},{16,18},{20,22},{24,26},{28,30},{32,34}... | collective-permute-start | bytes 294920 | tf_op jit(solution)/shard_map/ppermute | solution.py:41
  19.2 3.1 %fusion.8 = bf16[512,512]{0,1:T(8,128)(2,1)} fusion(bf16[768,512]{0,1:T(8,128)(2,1)S(1)} %bitcast.223, bf16[768,512]{0,1:T(8,128)(2,1)} %bitcast.224, bf16[1,1,768,768]{3,2,1,0:T(8,128)(2,1)S(1)} %copy-done), kind=kOutput, calls=%fused_computation.24 | convolution fusion | flops 1007288320 | bytes 3276800 | tf_op jit(solution)/shard_map/bq,bm->qm/dot_general | solution.py:149
  22.4 2.7 %collective-permute-start.5 = (bf16[512,512]{0,1:T(8,128)(2,1)}, bf16[512,512]{0,1:T(8,128)(2,1)}, u32[]{:S(2)}, u32[]{:S(2)}) collective-permute-start(bf16[512,512]{0,1:T(8,128)(2,1)} %fusion.8), channel_id=1, source_target_pairs={{0,3},{1,0},{2,1},{3,2},{4,7},{5,4},{6,5},{7,6},{8,11},{9,8},{10,9... | collective-permute-start | bytes 1572872 | tf_op jit(solution)/shard_map/ppermute | solution.py:57
  27.7 9.6 %all-to-all-start = ((bf16[32,128,96]{1,2,0:T(8,128)(2,1)}), bf16[32,128,96]{1,2,0:T(8,128)(2,1)S(1)}, u32[]{:S(2)}, u32[]{:S(2)}) async-start(bf16[32,128,96]{1,2,0:T(8,128)(2,1)} %copy.79), calls=%async_computation | async-start | bytes 1572864 | tf_op jit(solution)/shard_map/all_to_all | solution.py:109
  39.0 2.1 %collective-permute-start.1 = (bf16[512,96]{0,1:T(8,128)(2,1)}, bf16[512,96]{0,1:T(8,128)(2,1)S(1)}, u32[]{:S(2)}, u32[]{:S(2)}) collective-permute-start(bf16[512,96]{0,1:T(8,128)(2,1)} %get-tuple-element.16), channel_id=1, source_target_pairs={{0,2},{1,3},{2,0},{3,1},{4,6},{5,7},{6,4},{7,5},{8,10},{9,11},{10,... | collective-permute-start | bytes 294920 | tf_op jit(solution)/shard_map/ppermute | solution.py:57
  41.0 8.7 %collective-permute-done.3 = bf16[512,512]{0,1:T(8,128)(2,1)} collective-permute-done((bf16[512,512]{0,1:T(8,128)(2,1)}, bf16[512,512]{0,1:T(8,128)(2,1)}, u32[]{:S(2)}, u32[]{:S(2)}) %collective-permute-start.3) | collective-permute-done | bytes 524320 | tf_op jit(solution)/shard_map/ppermute | solution.py:57
  51.9 2.7 %collective-permute-done.2 = bf16[512,96]{0,1:T(8,128)(2,1)S(1)} collective-permute-done((bf16[512,96]{0,1:T(8,128)(2,1)}, bf16[512,96]{0,1:T(8,128)(2,1)S(1)}, u32[]{:S(2)}, u32[]{:S(2)}) %collective-permute-start.2) | collective-permute-done | bytes 98336 | tf_op jit(solution)/shard_map/ppermute | solution.py:57
  58.1 11.1 %all-to-all-start.1 = ((bf16[32,128,96]{1,2,0:T(8,128)(2,1)}), bf16[32,128,96]{1,2,0:T(8,128)(2,1)S(1)}, u32[]{:S(2)}, u32[]{:S(2)}) async-start(bf16[32,128,96]{1,2,0:T(8,128)(2,1)} %copy.81), calls=%async_computation.1 | async-start | bytes 1572864 | tf_op jit(solution)/shard_map/all_to_all | solution.py:109
  69.2 14.2 %all-to-all-done.1 = bf16[32,128,96]{1,2,0:T(8,128)(2,1)S(1)} async-done(((bf16[32,128,96]{1,2,0:T(8,128)(2,1)}), bf16[32,128,96]{1,2,0:T(8,128)(2,1)S(1)}, u32[]{:S(2)}, u32[]{:S(2)}) %all-to-all-start.1) | async-done | bytes 786464 | tf_op jit(solution)/shard_map/all_to_all | solution.py:109
  86.4 4.0 %all-to-all-start.2 = ((bf16[32,128,96]{1,2,0:T(8,128)(2,1)}), bf16[32,128,96]{1,2,0:T(8,128)(2,1)S(1)}, u32[]{:S(2)}, u32[]{:S(2)}) async-start(bf16[32,128,96]{1,2,0:T(8,128)(2,1)} %copy.83), calls=%async_computation.2 | async-start | bytes 1572864 | tf_op jit(solution)/shard_map/all_to_all | solution.py:109
  90.4 14.2 %all-to-all-done.2 = bf16[32,128,96]{1,2,0:T(8,128)(2,1)S(1)} async-done(((bf16[32,128,96]{1,2,0:T(8,128)(2,1)}), bf16[32,128,96]{1,2,0:T(8,128)(2,1)S(1)}, u32[]{:S(2)}, u32[]{:S(2)}) %all-to-all-start.2) | async-done | bytes 786464 | tf_op jit(solution)/shard_map/all_to_all | solution.py:109
  106.4 2.0 %collective-permute-start.11 = (bf16[4,128,96]{1,0,2:T(4,128)(2,1)}, bf16[4,128,96]{1,0,2:T(4,128)(2,1)S(1)}, u32[]{:S(2)}, u32[]{:S(2)}) collective-permute-start(bf16[4,128,96]{1,0,2:T(4,128)(2,1)} %get-tuple-element.43), channel_id=1, source_target_pairs={{0,3},{1,0},{2,1},{3,2},{4,7},{5,4},{6,5},{7,6},{8,11},{9,8},{10,9... | collective-permute-start | bytes 294920 | tf_op jit(solution)/shard_map/ppermute | solution.py:57
  109.1 4.7 %collective-permute-done.9 = bf16[4,128,96]{1,0,2:T(4,128)(2,1)S(1)} collective-permute-done((bf16[4,128,96]{1,0,2:T(4,128)(2,1)}, bf16[4,128,96]{1,0,2:T(4,128)(2,1)S(1)}, u32[]{:S(2)}, u32[]{:S(2)}) %collective-permute-start.9) | collective-permute-done | bytes 98336 | tf_op jit(solution)/shard_map/ppermute | solution.py:57
  114.4 3.3 %fusion.7 = bf16[768,384]{1,0:T(8,128)(2,1)} fusion(bf16[768,384]{1,0:T(8,128)(2,1)} %copy-done.14, bf16[4,128,384]{1,2,0:T(8,128)(2,1)S(1)} %fusion.32, bf16[1,1,768,768]{3,2,1,0:T(8,128)(2,1)S(1)} %copy-done, bf16[4,768,128]{1,2,0:T(8,128)(2,1)S(1)} %copy-done.5, bf16[1,1,768,384]{3,2,1,0:T(8,128)(2,1)} %param.7, pred[]{:T(512)S(6)} %eq.194), kind=kOutput, calls=%fused_computation.21 | convolution fusion | flops 756449280 | bytes 4128769 | tf_op jit(solution)/shard_map/ab,bn->an/dot_general | solution.py:149
  120.7 2.2 %collective-permute-start.12 = (bf16[512,96]{0,1:T(8,128)(2,1)S(1)}, bf16[512,96]{0,1:T(8,128)(2,1)S(1)}, u32[]{:S(2)}, u32[]{:S(2)}) collective-permute-start(bf16[512,96]{0,1:T(8,128)(2,1)S(1)} %get-tuple-element.13), channel_id=1, source_target_pairs={{0,3},{1,0},{2,1},{3,2},{4,7},{5,4},{6,5},{7,6},{8,11},{9,8},{10,9... | collective-permute-start | bytes 294920 | tf_op jit(solution)/shard_map/ppermute | solution.py:57
  125.2 2.7 %collective-permute-done.13 = bf16[512,96]{0,1:T(8,128)(2,1)S(1)} collective-permute-done((bf16[512,96]{0,1:T(8,128)(2,1)S(1)}, bf16[512,96]{0,1:T(8,128)(2,1)S(1)}, u32[]{:S(2)}, u32[]{:S(2)}) %collective-permute-start.13) | collective-permute-done | bytes 98336 | tf_op jit(solution)/shard_map/ppermute | solution.py:57
  127.9 2.6 %collective-permute-done.14 = bf16[512,96]{0,1:T(8,128)(2,1)S(1)} collective-permute-done((bf16[512,96]{0,1:T(8,128)(2,1)S(1)}, bf16[512,96]{0,1:T(8,128)(2,1)S(1)}, u32[]{:S(2)}, u32[]{:S(2)}) %collective-permute-start.14) | collective-permute-done | bytes 98336 | tf_op jit(solution)/shard_map/ppermute | solution.py:57
  131.4 18.4 %all_to_all.30 = bf16[32,128,96]{1,2,0:T(8,128)(2,1)S(1)} all-to-all(bf16[32,128,96]{1,2,0:T(8,128)(2,1)S(1)} %copy.92), channel_id=1, replica_groups=mesh['blk'=32,'lvl'=4] {'blk'}, dimensions={0} | all-to-all | bytes 1572864 | tf_op jit(solution)/shard_map/all_to_all | solution.py:109
  151.2 17.9 %all_to_all.31 = bf16[32,128,96]{1,2,0:T(8,128)(2,1)S(1)} all-to-all(bf16[32,128,96]{1,2,0:T(8,128)(2,1)S(1)} %copy.94), channel_id=1, replica_groups=mesh['blk'=32,'lvl'=4] {'blk'}, dimensions={0} | all-to-all | bytes 1572864 | tf_op jit(solution)/shard_map/all_to_all | solution.py:109
  170.6 17.9 %all_to_all.32 = bf16[32,128,96]{1,2,0:T(8,128)(2,1)S(1)} all-to-all(bf16[32,128,96]{1,2,0:T(8,128)(2,1)S(1)} %copy.96), channel_id=1, replica_groups=mesh['blk'=32,'lvl'=4] {'blk'}, dimensions={0} | all-to-all | bytes 1572864 | tf_op jit(solution)/shard_map/all_to_all | solution.py:109
  191.0 3.9 %collective-permute-done.16 = bf16[4,128,96]{1,0,2:T(4,128)(2,1)S(1)} collective-permute-done((bf16[4,128,96]{1,0,2:T(4,128)(2,1)S(1)}, bf16[4,128,96]{1,0,2:T(4,128)(2,1)S(1)}, u32[]{:S(2)}, u32[]{:S(2)}) %collective-permute-start.16) | collective-permute-done | bytes 98336 | tf_op jit(solution)/shard_map/ppermute | solution.py:57
  195.3 2.0 collective-permute-done.15
  197.6 2.5 %fusion.5 = bf16[1,1,768,384]{2,3,1,0:T(8,128)(2,1)S(1)} fusion(bf16[384,768]{1,0:T(8,128)(2,1)} %copy-done.15, bf16[1,1,768,768]{3,2,1,0:T(8,128)(2,1)S(1)} %copy-done, bf16[4,128,384]{1,2,0:T(8,128)(2,1)S(1)} %fusion.29, bf16[768,384]{1,0:T(8,128)(2,1)} %fusion.7, bf16[1,1,4,768,128]{4,3,2,1,0:T(8,128)(2,1)S(1)} %copy-done.2, pred[]{:T(512)S(6)} %eq.195), kind=kOutput, calls=%fused_computation.19 | convolution fusion | flops 756449280 | bytes 4128769 | tf_op jit(solution)/shard_map/ba,bn->an/dot_general | solution.py:149
  (135 shorter events, 40.4 us)
Async XLA Ops:
  3.9 13.3 %copy-start.1 = (bf16[1,1,4,768,128]{4,3,2,1,0:T(8,128)(2,1)S(1)}, bf16[1,1,4,768,128]{4,3,2,1,0:T(8,128)(2,1)}, u32[]{:S(2)}) copy-start(bf16[1,1,4,768,128]{4,3,2,1,0:T(8,128)(2,1)} %param.9) | copy-start | bytes 2359300
  4.8 17.6 %collective-permute-start.6 = (bf16[4,128,96]{1,0,2:T(4,128)(2,1)}, bf16[4,128,96]{1,0,2:T(4,128)(2,1)}, u32[]{:S(2)}, u32[]{:S(2)}) collective-permute-start(bf16[4,128,96]{1,0,2:T(4,128)(2,1)} %get-tuple-element.35), channel_id=1, source_target_pairs={{0,1},{4,5},{8,9},{12,13},{16,17},{20,21},{24,25},{28,29},{32,33},... | collective-permute-start | bytes 294920 | tf_op jit(solution)/shard_map/ppermute | solution.py:41
  9.4 15.7 %collective-permute-start.7 = (bf16[4,128,96]{1,0,2:T(4,128)(2,1)}, bf16[4,128,96]{1,0,2:T(4,128)(2,1)}, u32[]{:S(2)}, u32[]{:S(2)}) collective-permute-start(bf16[4,128,96]{1,0,2:T(4,128)(2,1)} %get-tuple-element.37), channel_id=1, source_target_pairs={{0,2},{4,6},{8,10},{12,14},{16,18},{20,22},{24,26},{28,30},{32,34}... | collective-permute-start | bytes 294920 | tf_op jit(solution)/shard_map/ppermute | solution.py:41
  12.2 12.8 %collective-permute-start.8 = (bf16[4,128,96]{1,0,2:T(4,128)(2,1)}, bf16[4,128,96]{1,0,2:T(4,128)(2,1)}, u32[]{:S(2)}, u32[]{:S(2)}) collective-permute-start(bf16[4,128,96]{1,0,2:T(4,128)(2,1)} %get-tuple-element.36), channel_id=1, source_target_pairs={{0,3},{4,7},{8,11},{12,15},{16,19},{20,23},{24,27},{28,31},{32,35}... | collective-permute-start | bytes 294920 | tf_op jit(solution)/shard_map/ppermute | solution.py:41
  22.4 27.3 %collective-permute-start.3 = (bf16[512,512]{0,1:T(8,128)(2,1)}, bf16[512,512]{0,1:T(8,128)(2,1)}, u32[]{:S(2)}, u32[]{:S(2)}) collective-permute-start(bf16[512,512]{0,1:T(8,128)(2,1)} %fusion.8), channel_id=1, source_target_pairs={{0,1},{1,2},{2,3},{3,0},{4,5},{5,6},{6,7},{7,4},{8,9},{9,10},{10,1... | collective-permute-start | bytes 1572872 | tf_op jit(solution)/shard_map/ppermute | solution.py:57
  22.4 27.3 %collective-permute-start.4 = (bf16[512,512]{0,1:T(8,128)(2,1)}, bf16[512,512]{0,1:T(8,128)(2,1)}, u32[]{:S(2)}, u32[]{:S(2)}) collective-permute-start(bf16[512,512]{0,1:T(8,128)(2,1)} %fusion.8), channel_id=1, source_target_pairs={{0,2},{1,3},{2,0},{3,1},{4,6},{5,7},{6,4},{7,5},{8,10},{9,11},{10,... | collective-permute-start | bytes 1572872 | tf_op jit(solution)/shard_map/ppermute | solution.py:57
  22.4 27.3 %collective-permute-start.5 = (bf16[512,512]{0,1:T(8,128)(2,1)}, bf16[512,512]{0,1:T(8,128)(2,1)}, u32[]{:S(2)}, u32[]{:S(2)}) collective-permute-start(bf16[512,512]{0,1:T(8,128)(2,1)} %fusion.8), channel_id=1, source_target_pairs={{0,3},{1,0},{2,1},{3,2},{4,7},{5,4},{6,5},{7,6},{8,11},{9,8},{10,9... | collective-permute-start | bytes 1572872 | tf_op jit(solution)/shard_map/ppermute | solution.py:57
  27.7 23.8 %all-to-all-start = ((bf16[32,128,96]{1,2,0:T(8,128)(2,1)}), bf16[32,128,96]{1,2,0:T(8,128)(2,1)S(1)}, u32[]{:S(2)}, u32[]{:S(2)}) async-start(bf16[32,128,96]{1,2,0:T(8,128)(2,1)} %copy.79), calls=%async_computation | async-start | bytes 1572864 | tf_op jit(solution)/shard_map/all_to_all | solution.py:109
  38.4 13.5 %collective-permute-start = (bf16[512,96]{0,1:T(8,128)(2,1)}, bf16[512,96]{0,1:T(8,128)(2,1)S(1)}, u32[]{:S(2)}, u32[]{:S(2)}) collective-permute-start(bf16[512,96]{0,1:T(8,128)(2,1)} %get-tuple-element.17), channel_id=1, source_target_pairs={{0,3},{1,0},{2,1},{3,2},{4,7},{5,4},{6,5},{7,6},{8,11},{9,8},{10,9... | collective-permute-start | bytes 294920 | tf_op jit(solution)/shard_map/ppermute | solution.py:57
  39.0 12.9 %collective-permute-start.1 = (bf16[512,96]{0,1:T(8,128)(2,1)}, bf16[512,96]{0,1:T(8,128)(2,1)S(1)}, u32[]{:S(2)}, u32[]{:S(2)}) collective-permute-start(bf16[512,96]{0,1:T(8,128)(2,1)} %get-tuple-element.16), channel_id=1, source_target_pairs={{0,2},{1,3},{2,0},{3,1},{4,6},{5,7},{6,4},{7,5},{8,10},{9,11},{10,... | collective-permute-start | bytes 294920 | tf_op jit(solution)/shard_map/ppermute | solution.py:57
  49.7 4.9 %collective-permute-start.2 = (bf16[512,96]{0,1:T(8,128)(2,1)}, bf16[512,96]{0,1:T(8,128)(2,1)S(1)}, u32[]{:S(2)}, u32[]{:S(2)}) collective-permute-start(bf16[512,96]{0,1:T(8,128)(2,1)} %get-tuple-element.15), channel_id=1, source_target_pairs={{0,1},{1,2},{2,3},{3,0},{4,5},{5,6},{6,7},{7,4},{8,9},{9,10},{10,1... | collective-permute-start | bytes 294920 | tf_op jit(solution)/shard_map/ppermute | solution.py:57
  58.1 25.3 %all-to-all-start.1 = ((bf16[32,128,96]{1,2,0:T(8,128)(2,1)}), bf16[32,128,96]{1,2,0:T(8,128)(2,1)S(1)}, u32[]{:S(2)}, u32[]{:S(2)}) async-start(bf16[32,128,96]{1,2,0:T(8,128)(2,1)} %copy.81), calls=%async_computation.1 | async-start | bytes 1572864 | tf_op jit(solution)/shard_map/all_to_all | solution.py:109
  86.4 18.2 %copy-start.7 = (bf16[4,128,96]{1,0,2:T(4,128)(2,1)S(1)}, bf16[4,128,96]{1,0,2:T(4,128)(2,1)}, u32[]{:S(2)}) copy-start(bf16[4,128,96]{1,0,2:T(4,128)(2,1)} %copy-done.6) | copy-start | bytes 294916
  86.4 18.2 %copy-start.11 = (s32[4]{0:T(128)S(1)}, s32[4]{0:T(128)}, u32[]{:S(2)}) copy-start(s32[4]{0:T(128)} %get-tuple-element.24) | copy-start | bytes 52
  86.4 18.2 %all-to-all-start.2 = ((bf16[32,128,96]{1,2,0:T(8,128)(2,1)}), bf16[32,128,96]{1,2,0:T(8,128)(2,1)S(1)}, u32[]{:S(2)}, u32[]{:S(2)}) async-start(bf16[32,128,96]{1,2,0:T(8,128)(2,1)} %copy.83), calls=%async_computation.2 | async-start | bytes 1572864 | tf_op jit(solution)/shard_map/all_to_all | solution.py:109
  105.7 8.0 %collective-permute-start.9 = (bf16[4,128,96]{1,0,2:T(4,128)(2,1)}, bf16[4,128,96]{1,0,2:T(4,128)(2,1)S(1)}, u32[]{:S(2)}, u32[]{:S(2)}) collective-permute-start(bf16[4,128,96]{1,0,2:T(4,128)(2,1)} %get-tuple-element.45), channel_id=1, source_target_pairs={{0,1},{1,2},{2,3},{3,0},{4,5},{5,6},{6,7},{7,4},{8,9},{9,10},{10,1... | collective-permute-start | bytes 294920 | tf_op jit(solution)/shard_map/ppermute | solution.py:57
  105.7 8.1 %collective-permute-start.10 = (bf16[4,128,96]{1,0,2:T(4,128)(2,1)}, bf16[4,128,96]{1,0,2:T(4,128)(2,1)S(1)}, u32[]{:S(2)}, u32[]{:S(2)}) collective-permute-start(bf16[4,128,96]{1,0,2:T(4,128)(2,1)} %get-tuple-element.44), channel_id=1, source_target_pairs={{0,2},{1,3},{2,0},{3,1},{4,6},{5,7},{6,4},{7,5},{8,10},{9,11},{10,... | collective-permute-start | bytes 294920 | tf_op jit(solution)/shard_map/ppermute | solution.py:57
  106.4 7.8 %collective-permute-start.11 = (bf16[4,128,96]{1,0,2:T(4,128)(2,1)}, bf16[4,128,96]{1,0,2:T(4,128)(2,1)S(1)}, u32[]{:S(2)}, u32[]{:S(2)}) collective-permute-start(bf16[4,128,96]{1,0,2:T(4,128)(2,1)} %get-tuple-element.43), channel_id=1, source_target_pairs={{0,3},{1,0},{2,1},{3,2},{4,7},{5,4},{6,5},{7,6},{8,11},{9,8},{10,9... | collective-permute-start | bytes 294920 | tf_op jit(solution)/shard_map/ppermute | solution.py:57
  120.7 4.6 %collective-permute-start.12 = (bf16[512,96]{0,1:T(8,128)(2,1)S(1)}, bf16[512,96]{0,1:T(8,128)(2,1)S(1)}, u32[]{:S(2)}, u32[]{:S(2)}) collective-permute-start(bf16[512,96]{0,1:T(8,128)(2,1)S(1)} %get-tuple-element.13), channel_id=1, source_target_pairs={{0,3},{1,0},{2,1},{3,2},{4,7},{5,4},{6,5},{7,6},{8,11},{9,8},{10,9... | collective-permute-start | bytes 294920 | tf_op jit(solution)/shard_map/ppermute | solution.py:57
  122.8 5.1 %collective-permute-start.13 = (bf16[512,96]{0,1:T(8,128)(2,1)S(1)}, bf16[512,96]{0,1:T(8,128)(2,1)S(1)}, u32[]{:S(2)}, u32[]{:S(2)}) collective-permute-start(bf16[512,96]{0,1:T(8,128)(2,1)S(1)} %get-tuple-element.12), channel_id=1, source_target_pairs={{0,2},{1,3},{2,0},{3,1},{4,6},{5,7},{6,4},{7,5},{8,10},{9,11},{10,... | collective-permute-start | bytes 294920 | tf_op jit(solution)/shard_map/ppermute | solution.py:57
  122.8 7.7 %collective-permute-start.14 = (bf16[512,96]{0,1:T(8,128)(2,1)S(1)}, bf16[512,96]{0,1:T(8,128)(2,1)S(1)}, u32[]{:S(2)}, u32[]{:S(2)}) collective-permute-start(bf16[512,96]{0,1:T(8,128)(2,1)S(1)} %get-tuple-element.11), channel_id=1, source_target_pairs={{0,1},{1,2},{2,3},{3,0},{4,5},{5,6},{6,7},{7,4},{8,9},{9,10},{10,1... | collective-permute-start | bytes 294920 | tf_op jit(solution)/shard_map/ppermute | solution.py:57
  188.9 6.1 %collective-permute-start.16 = (bf16[4,128,96]{1,0,2:T(4,128)(2,1)S(1)}, bf16[4,128,96]{1,0,2:T(4,128)(2,1)S(1)}, u32[]{:S(2)}, u32[]{:S(2)}) collective-permute-start(bf16[4,128,96]{1,0,2:T(4,128)(2,1)S(1)} %get-tuple-element.40), channel_id=1, source_target_pairs={{0,2},{1,3},{2,0},{3,1},{4,6},{5,7},{6,4},{7,5},{8,10},{9,11},{10,... | collective-permute-start | bytes 294920 | tf_op jit(solution)/shard_map/ppermute | solution.py:57
  189.6 5.7 %collective-permute-start.17 = (bf16[4,128,96]{1,0,2:T(4,128)(2,1)S(1)}, bf16[4,128,96]{1,0,2:T(4,128)(2,1)S(1)}, u32[]{:S(2)}, u32[]{:S(2)}) collective-permute-start(bf16[4,128,96]{1,0,2:T(4,128)(2,1)S(1)} %get-tuple-element.39), channel_id=1, source_target_pairs={{0,3},{1,0},{2,1},{3,2},{4,7},{5,4},{6,5},{7,6},{8,11},{9,8},{10,9... | collective-permute-start | bytes 294920 | tf_op jit(solution)/shard_map/ppermute | solution.py:57
  190.1 7.2 %collective-permute-start.15 = (bf16[4,128,96]{1,0,2:T(4,128)(2,1)S(1)}, bf16[4,128,96]{1,0,2:T(4,128)(2,1)S(1)}, u32[]{:S(2)}, u32[]{:S(2)}) collective-permute-start(bf16[4,128,96]{1,0,2:T(4,128)(2,1)S(1)} %get-tuple-element.41), channel_id=1, source_target_pairs={{0,1},{1,2},{2,3},{3,0},{4,5},{5,6},{6,7},{7,4},{8,9},{9,10},{10,1... | collective-permute-start | bytes 294920 | tf_op jit(solution)/shard_map/ppermute | solution.py:57
  (13 other events, 64.3 us)

commit v9 on v8

--- a/solution.py
+++ b/solution.py
@@ -152,6 +152,11 @@
     couple = dot(right_flat, inv_left, "bq,bm->qm").astype(jnp.bfloat16)
     inv_rhs = dot(inverse_here, rhs_here, "ab,bn->an").astype(jnp.bfloat16)
     free = dot(right_flat, inv_rhs, "bq,bn->qn").astype(jnp.bfloat16)
+    inv_left_f = inv_left
+    gram = dot(inv_left_f, inv_left_f, "bq,bm->qm").astype(jnp.bfloat16)
+    turn = dot(inv_left_f, inv_rhs, "bq,bn->qn").astype(jnp.bfloat16)
+    couple = jnp.where(my_row == last, gram, couple)
+    free = jnp.where(my_row == last, turn, free)
     couples = [couple] + [shift(couple, d, row_count) for d in range(1, row_count)]
     free_blocks = free.reshape(flat, row_count, width)
     frees = [pick_block(free_blocks, my_row, row_count)]
@@ -187,12 +192,11 @@
             full = full + put_block(got, lax.rem(my_row - d + row_count, row_count), row_count)
         return full
 
-    first = dot(inverse_here, rhs_here, "ab,bn->an").astype(jnp.bfloat16)
-    out = dot(right_flat, first, "bq,bn->qn").astype(jnp.bfloat16)
-    piece = spread(out.reshape(tile_count, rank_width, columns), 0, row_count, my_row)
+    first = inv_rhs
     chain = [zero_block] * level_count
-    chain[1] = route(piece, mine_target[1], mine_src[1], block_count)
-    couple_at = [None] + [from_row(couples, t) for t in range(1, last)]
+    start_block = frees_at(frees, my_row, 0, row_count).reshape(lane_shape)
+    chain[1] = route(start_block, mine_target[1], mine_src[1], block_count)
+    couple_at = [None] + [from_row(couples, t) for t in range(1, level_count)]
     for t in range(1, last):
         step = frees_at(frees, my_row, t, row_count).astype(jnp.float32) - dot(
             couple_at[t], chain[t].reshape(flat, width), "qm,mn->qn"
@@ -211,7 +215,10 @@
         return frees_at(back_parts, my_row, t, row_count)
 
     back = [zero_block] * level_count
-    back[last - 1] = route(back_free(last).reshape(lane_shape), mine_src[last], mine_target[last], block_count)
+    turned = frees_at(frees, my_row, last, row_count).astype(jnp.float32) - dot(
+        couple_at[last], chain[last].reshape(flat, width), "qm,mn->qn"
+    )
+    back[last - 1] = route(turned.astype(jnp.bfloat16).reshape(lane_shape), mine_src[last], mine_target[last], block_count)
     for t in reversed(range(1, last)):
         step = back_free(t).astype(jnp.float32) - dot(
             couple_at[t], back[t - 0].reshape(flat, width), "mq,mn->qn"

time: 202 us -> 187 us (0.926)
  waiting for transfers between devices: 58.2 us -> 43.4 us
  blocking collectives: 54.1 us -> 40 us
  local copies, waits for them, and re-layouts: 11.2 us -> 21.6 us
  matrix products: 21.2 us -> 26.9 us
  other arithmetic: 8.29 us -> 5.92 us
    all_to_all x3 -> x2, blocking collectives: 54.1 us -> 40 us  [route(): lax.all_to_all(holder, 'blk', split_axis=0, concat_axis=0, tiled=True)]
    ppermute x15, waiting for transfers between devices: 29.5 us -> 18.8 us  [shift(): lax.ppermute(array, 'lvl', [(i, (i + by) % row_count) for i in range(row_...]
    ppermute x3 -> x0, starting transfers between devices: 9.33 us -> none  [spread(): got = lax.ppermute(part, 'lvl', [(src_row, r)])]
    ppermute x15, starting transfers between devices: 13 us -> 20.5 us  [shift(): lax.ppermute(array, 'lvl', [(i, (i + by) % row_count) for i in range(row_...]
    dot_general x11 -> x15, matrix products: 13.4 us -> 19.2 us  [dot(): return jnp.einsum(spec, a, b, preferred_element_type=jnp.float32)]
    mul x8, local copies, waits for them, and re-layouts: 0.64 us -> 5.68 us  [put_block(): full = part[..., None, :] * hot[:, None]]
    all_to_all x3 -> x4, waiting for transfers between devices: 28.7 us -> 24.6 us  [route(): lax.all_to_all(holder, 'blk', split_axis=0, concat_axis=0, tiled=True)]
    ppermute x6, local copies, waits for them, and re-layouts: 0.09 us -> 2.77 us  [shift(): lax.ppermute(array, 'lvl', [(i, (i + by) % row_count) for i in range(row_...]
  transfers between devices with their start and end apart: 21 -> 19, of which waited for: 13 -> 10; matrix products, arithmetic and copies ran while one was open for 7% -> 13% of each run, Pallas kernels for 0% -> 0%
where the time goes in v9:
time: 187 us; the launch traced here: 186 us
  starting transfers between devices  46.9 us (25%)
  waiting for transfers between devices  43.4 us (23%)
  blocking collectives  40 us (21%)
  matrix products  26.9 us (14%)
  local copies, waits for them, and re-layouts  21.6 us (12%)
  other arithmetic  5.92 us (3%)
    all_to_all x2, blocking collectives, route(): lax.all_to_all(holder, 'blk', split_axis=0, concat_axis=0, tiled=True)  40 us
    all_to_all x4, starting transfers between devices, route(): lax.all_to_all(holder, 'blk', split_axis=0, concat_axis=0, tiled=True)  26.4 us
    all_to_all x4, waiting for transfers between devices, route(): lax.all_to_all(holder, 'blk', split_axis=0, concat_axis=0, tiled=True)  24.6 us
    ppermute x15, starting transfers between devices, shift(): lax.ppermute(array, 'lvl', [(i, (i + by) % row_count) for i in range(row_...  20.5 us
    dot_general x15, matrix products, dot(): return jnp.einsum(spec, a, b, preferred_element_type=jnp.float32)  19.2 us
    ppermute x15, waiting for transfers between devices, shift(): lax.ppermute(array, 'lvl', [(i, (i + by) % row_count) for i in range(row_...  18.8 us
    mul x8, local copies, waits for them, and re-layouts, put_block(): full = part[..., None, :] * hot[:, None]  5.68 us
    convert_element_type x6, local copies, waits for them, and re-layouts, route(): holder = holder.astype(piece.dtype)  5.39 us
  transfers between devices with their start and end apart: 19, of which 10 were waited for; matrix products, arithmetic and copies ran while one was open for 13% of the time, Pallas kernels for 0%

profile of v9, /device:TPU:1, one launch (start us, length us, event | category | flops | bytes accessed | tf_op | source)
XLA Modules:
  0.0 186.2 jit_solution(15602424856633896854)
XLA Ops:
  6.9 1.7 convolution_convert_fusion
  8.6 1.6 convolution_convert_fusion.10
  10.6 1.7 fusion.11
  14.4 3.3 %collective-permute-start = (bf16[512,96]{0,1:T(8,128)(2,1)S(1)}, bf16[512,96]{0,1:T(8,128)(2,1)S(1)}, u32[]{:S(2)}, u32[]{:S(2)}) collective-permute-start(bf16[512,96]{0,1:T(8,128)(2,1)S(1)} %get-tuple-element.17), channel_id=1, source_target_pairs={{0,3},{1,0},{2,1},{3,2},{4,7},{5,4},{6,5},{7,6},{8,11},{9,8},{10,9... | collective-permute-start | bytes 294920 | tf_op jit(solution)/shard_map/ppermute | solution.py:57
  21.7 1.7 collective-permute-start.4
  27.2 10.0 %all-to-all-start = ((bf16[32,128,96]{1,2,0:T(8,128)(2,1)}), bf16[32,128,96]{1,2,0:T(8,128)(2,1)S(1)}, u32[]{:S(2)}, u32[]{:S(2)}) async-start(bf16[32,128,96]{1,2,0:T(8,128)(2,1)} %copy.83), calls=%async_computation | async-start | bytes 1572864 | tf_op jit(solution)/shard_map/all_to_all | solution.py:109
  37.4 9.7 %collective-permute-done.4 = bf16[512,512]{1,0:T(8,128)(2,1)S(1)} collective-permute-done((bf16[512,512]{1,0:T(8,128)(2,1)S(1)}, bf16[512,512]{1,0:T(8,128)(2,1)S(1)}, u32[]{:S(2)}, u32[]{:S(2)}) %collective-permute-start.4) | collective-permute-done | bytes 524320 | tf_op jit(solution)/shard_map/ppermute | solution.py:57
  49.5 1.9 %all-to-all-done = bf16[32,128,96]{1,2,0:T(8,128)(2,1)S(1)} async-done(((bf16[32,128,96]{1,2,0:T(8,128)(2,1)}), bf16[32,128,96]{1,2,0:T(8,128)(2,1)S(1)}, u32[]{:S(2)}, u32[]{:S(2)}) %all-to-all-start) | async-done | bytes 786464 | tf_op jit(solution)/shard_map/all_to_all | solution.py:109
  55.3 8.1 %all-to-all-start.1 = ((bf16[32,128,96]{1,2,0:T(8,128)(2,1)}), bf16[32,128,96]{1,2,0:T(8,128)(2,1)S(1)}, u32[]{:S(2)}, u32[]{:S(2)}) async-start(bf16[32,128,96]{1,2,0:T(8,128)(2,1)} %copy.85), calls=%async_computation.1 | async-start | bytes 1572864 | tf_op jit(solution)/shard_map/all_to_all | solution.py:109
  63.4 14.2 %all-to-all-done.1 = bf16[32,128,96]{1,2,0:T(8,128)(2,1)S(1)} async-done(((bf16[32,128,96]{1,2,0:T(8,128)(2,1)}), bf16[32,128,96]{1,2,0:T(8,128)(2,1)S(1)}, u32[]{:S(2)}, u32[]{:S(2)}) %all-to-all-start.1) | async-done | bytes 786464 | tf_op jit(solution)/shard_map/all_to_all | solution.py:109
  81.6 3.9 %all-to-all-start.2 = ((bf16[32,128,96]{1,2,0:T(8,128)(2,1)}), bf16[32,128,96]{1,2,0:T(8,128)(2,1)S(1)}, u32[]{:S(2)}, u32[]{:S(2)}) async-start(bf16[32,128,96]{1,2,0:T(8,128)(2,1)} %copy.87), calls=%async_computation.2 | async-start | bytes 1572864 | tf_op jit(solution)/shard_map/all_to_all | solution.py:109
  91.2 8.5 %all-to-all-done.2 = bf16[32,128,96]{1,2,0:T(8,128)(2,1)S(1)} async-done(((bf16[32,128,96]{1,2,0:T(8,128)(2,1)}), bf16[32,128,96]{1,2,0:T(8,128)(2,1)S(1)}, u32[]{:S(2)}, u32[]{:S(2)}) %all-to-all-start.2) | async-done | bytes 786464 | tf_op jit(solution)/shard_map/all_to_all | solution.py:109
  99.7 2.3 %select_select_fusion.9 = (bf16[4,128,96]{1,0,2:T(4,128)(2,1)}, bf16[4,128,96]{1,0,2:T(4,128)(2,1)}, bf16[4,128,96]{1,0,2:T(4,128)(2,1)}, bf16[4,128,96]{1,0,2:T(4,128)(2,1)}, bf16[4,128,96]{1,0,2:T(4,128)(2,1)S(1)}) fusion(bf16[4,128,96]{1,0,2:T(4,128)(2,1)} %copy-done.12, bf16[4,128,96]{1,0,2:T(4,128)(2,1)} %copy-done.11, pred[]{:T(512)S(6)} %eq.215, ...), kind=kOutput, calls=%fused_computation.110 | convolution fusion | flops 3784832 | bytes 1474588 | tf_op jit(solution)/shard_map/kj,jrn->krn/dot_general | solution.py:111
  107.9 4.5 %all-to-all-start.3 = ((bf16[32,128,96]{1,2,0:T(8,128)(2,1)}), bf16[32,128,96]{1,2,0:T(8,128)(2,1)S(1)}, u32[]{:S(2)}, u32[]{:S(2)}) async-start(bf16[32,128,96]{1,2,0:T(8,128)(2,1)} %copy.96), calls=%async_computation.3 | async-start | bytes 1572864 | tf_op jit(solution)/shard_map/all_to_all | solution.py:109
  115.4 3.5 %fusion.7 = bf16[768,384]{1,0:T(8,128)(2,1)} fusion(bf16[768,384]{1,0:T(8,128)(2,1)} %convolution_convert_fusion.10, bf16[4,128,384]{1,2,0:T(8,128)(2,1)S(1)} %fusion.40, bf16[1,1,768,768]{3,2,1,0:T(8,128)(2,1)S(1)} %copy-done, bf16[4,768,128]{1,2,0:T(8,128)(2,1)} %copy-done.3, bf16[1,1,768,384]{3,2,1,0:T(8,128)(2,1)} %param.7, pred[]{:T(512)S(6)} %eq.202), kind=kOutput, calls=%fused_computation.22 | convolution fusion | flops 756449280 | bytes 4128769 | tf_op jit(solution)/shard_map/ab,bn->an/dot_general | solution.py:149
  118.9 1.8 convolution_convert_fusion.9
  122.5 2.4 %collective-permute-start.10 = (bf16[512,96]{0,1:T(8,128)(2,1)}, bf16[512,96]{0,1:T(8,128)(2,1)S(1)}, u32[]{:S(2)}, u32[]{:S(2)}) collective-permute-start(bf16[512,96]{0,1:T(8,128)(2,1)} %get-tuple-element.12), channel_id=1, source_target_pairs={{0,2},{1,3},{2,0},{3,1},{4,6},{5,7},{6,4},{7,5},{8,10},{9,11},{10,... | collective-permute-start | bytes 294920 | tf_op jit(solution)/shard_map/ppermute | solution.py:57
  124.8 2.7 %collective-permute-start.9 = (bf16[512,96]{0,1:T(8,128)(2,1)}, bf16[512,96]{0,1:T(8,128)(2,1)S(1)}, u32[]{:S(2)}, u32[]{:S(2)}) collective-permute-start(bf16[512,96]{0,1:T(8,128)(2,1)} %get-tuple-element.13), channel_id=1, source_target_pairs={{0,3},{1,0},{2,1},{3,2},{4,7},{5,4},{6,5},{7,6},{8,11},{9,8},{10,9... | collective-permute-start | bytes 294920 | tf_op jit(solution)/shard_map/ppermute | solution.py:57
  128.3 2.4 %collective-permute-done.11 = bf16[512,96]{0,1:T(8,128)(2,1)S(1)} collective-permute-done((bf16[512,96]{0,1:T(8,128)(2,1)}, bf16[512,96]{0,1:T(8,128)(2,1)S(1)}, u32[]{:S(2)}, u32[]{:S(2)}) %collective-permute-start.11) | collective-permute-done | bytes 98336 | tf_op jit(solution)/shard_map/ppermute | solution.py:57
  132.5 22.2 %all_to_all.30 = bf16[32,128,96]{1,2,0:T(8,128)(2,1)S(1)} all-to-all(bf16[32,128,96]{1,2,0:T(8,128)(2,1)S(1)} %copy.98), channel_id=1, replica_groups=mesh['blk'=32,'lvl'=4] {'blk'}, dimensions={0} | all-to-all | bytes 1572864 | tf_op jit(solution)/shard_map/all_to_all | solution.py:109
  156.1 17.9 %all_to_all.31 = bf16[32,128,96]{1,2,0:T(8,128)(2,1)S(1)} all-to-all(bf16[32,128,96]{1,2,0:T(8,128)(2,1)S(1)} %copy.100), channel_id=1, replica_groups=mesh['blk'=32,'lvl'=4] {'blk'}, dimensions={0} | all-to-all | bytes 1572864 | tf_op jit(solution)/shard_map/all_to_all | solution.py:109
  175.1 3.2 %collective-permute-start.13 = (bf16[4,128,96]{1,0,2:T(4,128)(2,1)S(1)}, bf16[4,128,96]{1,0,2:T(4,128)(2,1)S(1)}, u32[]{:S(2)}, u32[]{:S(2)}) collective-permute-start(bf16[4,128,96]{1,0,2:T(4,128)(2,1)S(1)} %get-tuple-element.37), channel_id=1, source_target_pairs={{0,2},{1,3},{2,0},{3,1},{4,6},{5,7},{6,4},{7,5},{8,10},{9,11},{10,... | collective-permute-start | bytes 294920 | tf_op jit(solution)/shard_map/ppermute | solution.py:57
  178.3 1.9 %collective-permute-done.12 = bf16[4,128,96]{1,0,2:T(4,128)(2,1)S(1)} collective-permute-done((bf16[4,128,96]{1,0,2:T(4,128)(2,1)S(1)}, bf16[4,128,96]{1,0,2:T(4,128)(2,1)S(1)}, u32[]{:S(2)}, u32[]{:S(2)}) %collective-permute-start.12) | collective-permute-done | bytes 98336 | tf_op jit(solution)/shard_map/ppermute | solution.py:57
  180.3 3.2 %collective-permute-done.13 = bf16[4,128,96]{1,0,2:T(4,128)(2,1)S(1)} collective-permute-done((bf16[4,128,96]{1,0,2:T(4,128)(2,1)S(1)}, bf16[4,128,96]{1,0,2:T(4,128)(2,1)S(1)}, u32[]{:S(2)}, u32[]{:S(2)}) %collective-permute-start.13) | collective-permute-done | bytes 98336 | tf_op jit(solution)/shard_map/ppermute | solution.py:57
  (196 shorter events, 50.7 us)
Async XLA Ops:
  5.2 46.1 %copy-start.20 = (s32[4]{0:T(128)}, s32[4]{0:T(128)S(1)}, u32[]{:S(2)}) copy-start(s32[4]{0:T(128)S(1)} %get-tuple-element.30) | copy-start | bytes 52
  5.2 48.4 %copy-start.22 = (s32[4]{0:T(128)}, s32[4]{0:T(128)S(1)}, u32[]{:S(2)}) copy-start(s32[4]{0:T(128)S(1)} %get-tuple-element.29) | copy-start | bytes 52
  5.2 72.4 %copy-start.24 = (s32[4]{0:T(128)}, s32[4]{0:T(128)S(1)}, u32[]{:S(2)}) copy-start(s32[4]{0:T(128)S(1)} %get-tuple-element.28) | copy-start | bytes 52
  5.2 74.6 %copy-start.25 = (s32[4]{0:T(128)}, s32[4]{0:T(128)S(1)}, u32[]{:S(2)}) copy-start(s32[4]{0:T(128)S(1)} %get-tuple-element.27) | copy-start | bytes 52
  14.4 9.0 %collective-permute-start = (bf16[512,96]{0,1:T(8,128)(2,1)S(1)}, bf16[512,96]{0,1:T(8,128)(2,1)S(1)}, u32[]{:S(2)}, u32[]{:S(2)}) collective-permute-start(bf16[512,96]{0,1:T(8,128)(2,1)S(1)} %get-tuple-element.17), channel_id=1, source_target_pairs={{0,3},{1,0},{2,1},{3,2},{4,7},{5,4},{6,5},{7,6},{8,11},{9,8},{10,9... | collective-permute-start | bytes 294920 | tf_op jit(solution)/shard_map/ppermute | solution.py:57
  17.7 6.9 %collective-permute-start.1 = (bf16[512,96]{0,1:T(8,128)(2,1)S(1)}, bf16[512,96]{0,1:T(8,128)(2,1)S(1)}, u32[]{:S(2)}, u32[]{:S(2)}) collective-permute-start(bf16[512,96]{0,1:T(8,128)(2,1)S(1)} %get-tuple-element.16), channel_id=1, source_target_pairs={{0,2},{1,3},{2,0},{3,1},{4,6},{5,7},{6,4},{7,5},{8,10},{9,11},{10,... | collective-permute-start | bytes 294920 | tf_op jit(solution)/shard_map/ppermute | solution.py:57
  18.2 7.1 %collective-permute-start.2 = (bf16[512,96]{0,1:T(8,128)(2,1)S(1)}, bf16[512,96]{0,1:T(8,128)(2,1)S(1)}, u32[]{:S(2)}, u32[]{:S(2)}) collective-permute-start(bf16[512,96]{0,1:T(8,128)(2,1)S(1)} %get-tuple-element.15), channel_id=1, source_target_pairs={{0,1},{1,2},{2,3},{3,0},{4,5},{5,6},{6,7},{7,4},{8,9},{9,10},{10,1... | collective-permute-start | bytes 294920 | tf_op jit(solution)/shard_map/ppermute | solution.py:57
  20.1 17.4 %collective-permute-start.3 = (bf16[512,512]{1,0:T(8,128)(2,1)S(1)}, bf16[512,512]{1,0:T(8,128)(2,1)S(1)}, u32[]{:S(2)}, u32[]{:S(2)}) collective-permute-start(bf16[512,512]{1,0:T(8,128)(2,1)S(1)} %fusion.8), channel_id=1, source_target_pairs={{0,1},{1,2},{2,3},{3,0},{4,5},{5,6},{6,7},{7,4},{8,9},{9,10},{10,1... | collective-permute-start | bytes 1572872 | tf_op jit(solution)/shard_map/ppermute | solution.py:57
  21.7 25.5 %collective-permute-start.4 = (bf16[512,512]{1,0:T(8,128)(2,1)S(1)}, bf16[512,512]{1,0:T(8,128)(2,1)S(1)}, u32[]{:S(2)}, u32[]{:S(2)}) collective-permute-start(bf16[512,512]{1,0:T(8,128)(2,1)S(1)} %fusion.8), channel_id=1, source_target_pairs={{0,2},{1,3},{2,0},{3,1},{4,6},{5,7},{6,4},{7,5},{8,10},{9,11},{10,... | collective-permute-start | bytes 1572872 | tf_op jit(solution)/shard_map/ppermute | solution.py:57
  23.4 24.6 %collective-permute-start.5 = (bf16[512,512]{1,0:T(8,128)(2,1)S(1)}, bf16[512,512]{1,0:T(8,128)(2,1)}, u32[]{:S(2)}, u32[]{:S(2)}) collective-permute-start(bf16[512,512]{1,0:T(8,128)(2,1)S(1)} %fusion.8), channel_id=1, source_target_pairs={{0,3},{1,0},{2,1},{3,2},{4,7},{5,4},{6,5},{7,6},{8,11},{9,8},{10,9... | collective-permute-start | bytes 1572872 | tf_op jit(solution)/shard_map/ppermute | solution.py:57
  27.2 24.2 %all-to-all-start = ((bf16[32,128,96]{1,2,0:T(8,128)(2,1)}), bf16[32,128,96]{1,2,0:T(8,128)(2,1)S(1)}, u32[]{:S(2)}, u32[]{:S(2)}) async-start(bf16[32,128,96]{1,2,0:T(8,128)(2,1)} %copy.83), calls=%async_computation | async-start | bytes 1572864 | tf_op jit(solution)/shard_map/all_to_all | solution.py:109
  55.3 22.3 %all-to-all-start.1 = ((bf16[32,128,96]{1,2,0:T(8,128)(2,1)}), bf16[32,128,96]{1,2,0:T(8,128)(2,1)S(1)}, u32[]{:S(2)}, u32[]{:S(2)}) async-start(bf16[32,128,96]{1,2,0:T(8,128)(2,1)} %copy.85), calls=%async_computation.1 | async-start | bytes 1572864 | tf_op jit(solution)/shard_map/all_to_all | solution.py:109
  81.6 18.1 %all-to-all-start.2 = ((bf16[32,128,96]{1,2,0:T(8,128)(2,1)}), bf16[32,128,96]{1,2,0:T(8,128)(2,1)S(1)}, u32[]{:S(2)}, u32[]{:S(2)}) async-start(bf16[32,128,96]{1,2,0:T(8,128)(2,1)} %copy.87), calls=%async_computation.2 | async-start | bytes 1572864 | tf_op jit(solution)/shard_map/all_to_all | solution.py:109
  102.0 10.4 %collective-permute-start.6 = (bf16[4,128,96]{1,0,2:T(4,128)(2,1)}, bf16[4,128,96]{1,0,2:T(4,128)(2,1)}, u32[]{:S(2)}, u32[]{:S(2)}) collective-permute-start(bf16[4,128,96]{1,0,2:T(4,128)(2,1)} %get-tuple-element.42), channel_id=1, source_target_pairs={{0,1},{1,2},{2,3},{3,0},{4,5},{5,6},{6,7},{7,4},{8,9},{9,10},{10,1... | collective-permute-start | bytes 294920 | tf_op jit(solution)/shard_map/ppermute | solution.py:57
  102.0 11.3 %collective-permute-start.7 = (bf16[4,128,96]{1,0,2:T(4,128)(2,1)}, bf16[4,128,96]{1,0,2:T(4,128)(2,1)}, u32[]{:S(2)}, u32[]{:S(2)}) collective-permute-start(bf16[4,128,96]{1,0,2:T(4,128)(2,1)} %get-tuple-element.41), channel_id=1, source_target_pairs={{0,2},{1,3},{2,0},{3,1},{4,6},{5,7},{6,4},{7,5},{8,10},{9,11},{10,... | collective-permute-start | bytes 294920 | tf_op jit(solution)/shard_map/ppermute | solution.py:57
  103.3 10.9 %collective-permute-start.8 = (bf16[4,128,96]{1,0,2:T(4,128)(2,1)}, bf16[4,128,96]{1,0,2:T(4,128)(2,1)}, u32[]{:S(2)}, u32[]{:S(2)}) collective-permute-start(bf16[4,128,96]{1,0,2:T(4,128)(2,1)} %get-tuple-element.40), channel_id=1, source_target_pairs={{0,3},{1,0},{2,1},{3,2},{4,7},{5,4},{6,5},{7,6},{8,11},{9,8},{10,9... | collective-permute-start | bytes 294920 | tf_op jit(solution)/shard_map/ppermute | solution.py:57
  107.9 19.6 %all-to-all-start.3 = ((bf16[32,128,96]{1,2,0:T(8,128)(2,1)}), bf16[32,128,96]{1,2,0:T(8,128)(2,1)S(1)}, u32[]{:S(2)}, u32[]{:S(2)}) async-start(bf16[32,128,96]{1,2,0:T(8,128)(2,1)} %copy.96), calls=%async_computation.3 | async-start | bytes 1572864 | tf_op jit(solution)/shard_map/all_to_all | solution.py:109
  122.5 5.9 %collective-permute-start.10 = (bf16[512,96]{0,1:T(8,128)(2,1)}, bf16[512,96]{0,1:T(8,128)(2,1)S(1)}, u32[]{:S(2)}, u32[]{:S(2)}) collective-permute-start(bf16[512,96]{0,1:T(8,128)(2,1)} %get-tuple-element.12), channel_id=1, source_target_pairs={{0,2},{1,3},{2,0},{3,1},{4,6},{5,7},{6,4},{7,5},{8,10},{9,11},{10,... | collective-permute-start | bytes 294920 | tf_op jit(solution)/shard_map/ppermute | solution.py:57
  124.8 5.9 %collective-permute-start.11 = (bf16[512,96]{0,1:T(8,128)(2,1)}, bf16[512,96]{0,1:T(8,128)(2,1)S(1)}, u32[]{:S(2)}, u32[]{:S(2)}) collective-permute-start(bf16[512,96]{0,1:T(8,128)(2,1)} %get-tuple-element.11), channel_id=1, source_target_pairs={{0,1},{1,2},{2,3},{3,0},{4,5},{5,6},{6,7},{7,4},{8,9},{9,10},{10,1... | collective-permute-start | bytes 294920 | tf_op jit(solution)/shard_map/ppermute | solution.py:57
  124.8 5.9 %collective-permute-start.9 = (bf16[512,96]{0,1:T(8,128)(2,1)}, bf16[512,96]{0,1:T(8,128)(2,1)S(1)}, u32[]{:S(2)}, u32[]{:S(2)}) collective-permute-start(bf16[512,96]{0,1:T(8,128)(2,1)} %get-tuple-element.13), channel_id=1, source_target_pairs={{0,3},{1,0},{2,1},{3,2},{4,7},{5,4},{6,5},{7,6},{8,11},{9,8},{10,9... | collective-permute-start | bytes 294920 | tf_op jit(solution)/shard_map/ppermute | solution.py:57
  132.5 22.2 %copy-start.23 = (s32[4]{0:T(128)S(1)}, s32[4]{0:T(128)}, u32[]{:S(2)}) copy-start(s32[4]{0:T(128)} %copy-done.22) | copy-start | bytes 52
  174.5 5.8 %collective-permute-start.12 = (bf16[4,128,96]{1,0,2:T(4,128)(2,1)S(1)}, bf16[4,128,96]{1,0,2:T(4,128)(2,1)S(1)}, u32[]{:S(2)}, u32[]{:S(2)}) collective-permute-start(bf16[4,128,96]{1,0,2:T(4,128)(2,1)S(1)} %get-tuple-element.38), channel_id=1, source_target_pairs={{0,1},{1,2},{2,3},{3,0},{4,5},{5,6},{6,7},{7,4},{8,9},{9,10},{10,1... | collective-permute-start | bytes 294920 | tf_op jit(solution)/shard_map/ppermute | solution.py:57
  175.1 8.4 %collective-permute-start.13 = (bf16[4,128,96]{1,0,2:T(4,128)(2,1)S(1)}, bf16[4,128,96]{1,0,2:T(4,128)(2,1)S(1)}, u32[]{:S(2)}, u32[]{:S(2)}) collective-permute-start(bf16[4,128,96]{1,0,2:T(4,128)(2,1)S(1)} %get-tuple-element.37), channel_id=1, source_target_pairs={{0,2},{1,3},{2,0},{3,1},{4,6},{5,7},{6,4},{7,5},{8,10},{9,11},{10,... | collective-permute-start | bytes 294920 | tf_op jit(solution)/shard_map/ppermute | solution.py:57
  178.3 5.2 %collective-permute-start.14 = (bf16[4,128,96]{1,0,2:T(4,128)(2,1)S(1)}, bf16[4,128,96]{1,0,2:T(4,128)(2,1)S(1)}, u32[]{:S(2)}, u32[]{:S(2)}) collective-permute-start(bf16[4,128,96]{1,0,2:T(4,128)(2,1)S(1)} %get-tuple-element.36), channel_id=1, source_target_pairs={{0,3},{1,0},{2,1},{3,2},{4,7},{5,4},{6,5},{7,6},{8,11},{9,8},{10,9... | collective-permute-start | bytes 294920 | tf_op jit(solution)/shard_map/ppermute | solution.py:57
  (42 other events, 190.4 us)

commit v10 on v8

--- a/solution.py
+++ b/solution.py
@@ -152,11 +152,19 @@
     couple = dot(right_flat, inv_left, "bq,bm->qm").astype(jnp.bfloat16)
     inv_rhs = dot(inverse_here, rhs_here, "ab,bn->an").astype(jnp.bfloat16)
     free = dot(right_flat, inv_rhs, "bq,bn->qn").astype(jnp.bfloat16)
+    gram = dot(inv_left, inv_left, "bq,bm->qm").astype(jnp.bfloat16)
+    turn = dot(inv_left, inv_rhs, "bq,bn->qn").astype(jnp.bfloat16)
     couples = [couple] + [shift(couple, d, row_count) for d in range(1, row_count)]
-    free_blocks = free.reshape(flat, row_count, width)
-    frees = [pick_block(free_blocks, my_row, row_count)]
+    grams = [gram] + [shift(gram, d, row_count) for d in range(1, row_count)]
+
+    def both_blocks(index):
+        return jnp.concatenate(
+            [take_block(free, index, row_count), take_block(turn, index, row_count)], axis=1
+        )
+
+    frees = [both_blocks(my_row)]
     for d in range(1, row_count):
-        frees.append(shift(pick_block(free_blocks, lax.rem(my_row + d, row_count), row_count), d, row_count))
+        frees.append(shift(both_blocks(lax.rem(my_row + d, row_count)), d, row_count))
 
     def from_row(parts, t):
         pick = lax.rem(my_row - t + row_count, row_count)
@@ -187,14 +195,13 @@
             full = full + put_block(got, lax.rem(my_row - d + row_count, row_count), row_count)
         return full
 
-    first = dot(inverse_here, rhs_here, "ab,bn->an").astype(jnp.bfloat16)
-    out = dot(right_flat, first, "bq,bn->qn").astype(jnp.bfloat16)
-    piece = spread(out.reshape(tile_count, rank_width, columns), 0, row_count, my_row)
+    first = inv_rhs
     chain = [zero_block] * level_count
-    chain[1] = route(piece, mine_target[1], mine_src[1], block_count)
-    couple_at = [None] + [from_row(couples, t) for t in range(1, last)]
+    start_block = frees_at(frees, my_row, 0, row_count)[:, :width].reshape(lane_shape)
+    chain[1] = route(start_block, mine_target[1], mine_src[1], block_count)
+    couple_at = [None] + [from_row(couples, t) for t in range(1, level_count)]
     for t in range(1, last):
-        step = frees_at(frees, my_row, t, row_count).astype(jnp.float32) - dot(
+        step = frees_at(frees, my_row, t, row_count)[:, :width].astype(jnp.float32) - dot(
             couple_at[t], chain[t].reshape(flat, width), "qm,mn->qn"
         )
         chain[t + 1] = route(step.astype(jnp.bfloat16).reshape(lane_shape), mine_target[t + 1], mine_src[t + 1], block_count)
@@ -202,18 +209,19 @@
     mine_fwd = solve_forward(own_level_blocks(chain))
     solved = jnp.where(my_row == 0, first, mine_fwd)
     top = dot(inverse_here, solved, "ba,bn->an").astype(jnp.bfloat16)
-    back_term = dot(left_flat, top, "bm,bn->mn").astype(jnp.bfloat16)
-    back_parts = [take_block(back_term, my_row, row_count)]
-    for d in range(1, row_count):
-        back_parts.append(shift(take_block(back_term, lax.rem(my_row + d, row_count), row_count), d, row_count))
+    gram_at = [None] + [from_row(grams, t) for t in range(1, level_count)]
 
     def back_free(t):
-        return frees_at(back_parts, my_row, t, row_count)
+        return frees_at(frees, my_row, t, row_count)[:, width:].astype(jnp.float32) - dot(
+            gram_at[t], chain[t].reshape(flat, width), "qm,mn->qn"
+        )
+
+    back_terms = [None] + [back_free(t) for t in range(1, level_count)]
 
     back = [zero_block] * level_count
-    back[last - 1] = route(back_free(last).reshape(lane_shape), mine_src[last], mine_target[last], block_count)
+    back[last - 1] = route(back_terms[last].astype(jnp.bfloat16).reshape(lane_shape), mine_src[last], mine_target[last], block_count)
     for t in reversed(range(1, last)):
-        step = back_free(t).astype(jnp.float32) - dot(
+        step = back_terms[t] - dot(
             couple_at[t], back[t - 0].reshape(flat, width), "mq,mn->qn"
         )
         back[t - 1] = route(step.astype(jnp.bfloat16).reshape(lane_shape), mine_src[t], mine_target[t], block_count)

time: 202 us -> 208 us (1.030)
  blocking collectives: 54.1 us -> 18 us
  starting transfers between devices: 47 us -> 62.9 us
  waiting for transfers between devices: 58.2 us -> 74.1 us
  matrix products: 21.2 us -> 30.3 us
    all_to_all x3 -> x1, blocking collectives: 54.1 us -> 18 us  [route(): lax.all_to_all(holder, 'blk', split_axis=0, concat_axis=0, tiled=True)]
    all_to_all x3 -> x5, waiting for transfers between devices: 28.7 us -> 55.1 us  [route(): lax.all_to_all(holder, 'blk', split_axis=0, concat_axis=0, tiled=True)]
    ppermute x15, starting transfers between devices: 13 us -> 32 us  [shift(): lax.ppermute(array, 'lvl', [(i, (i + by) % row_count) for i in range(row_...]
    ppermute x15, waiting for transfers between devices: 29.5 us -> 19 us  [shift(): lax.ppermute(array, 'lvl', [(i, (i + by) % row_count) for i in range(row_...]
    dot_general x11 -> x16, matrix products: 13.4 us -> 23.4 us  [dot(): return jnp.einsum(spec, a, b, preferred_element_type=jnp.float32)]
    ppermute x3 -> x0, starting transfers between devices: 9.33 us -> none  [spread(): got = lax.ppermute(part, 'lvl', [(src_row, r)])]
    all_to_all x3 -> x5, starting transfers between devices: 24.7 us -> 31 us  [route(): lax.all_to_all(holder, 'blk', split_axis=0, concat_axis=0, tiled=True)]
    unnamed x35 -> x61, local copies, waits for them, and re-layouts: 4.22 us -> 5.31 us
  transfers between devices with their start and end apart: 21 -> 20, of which waited for: 13 -> 10; matrix products, arithmetic and copies ran while one was open for 7% -> 8% of each run, Pallas kernels for 0% -> 0%
where the time goes in v10:
time: 208 us; the launch traced here: 207 us
  waiting for transfers between devices  74.1 us (36%)
  starting transfers between devices  62.9 us (30%)
  matrix products  30.3 us (15%)
  blocking collectives  18 us (9%)
  local copies, waits for them, and re-layouts  12.6 us (6%)
  other arithmetic  8.02 us (4%)
    all_to_all x5, waiting for transfers between devices, route(): lax.all_to_all(holder, 'blk', split_axis=0, concat_axis=0, tiled=True)  55.1 us
    ppermute x15, starting transfers between devices, shift(): lax.ppermute(array, 'lvl', [(i, (i + by) % row_count) for i in range(row_...  32 us
    all_to_all x5, starting transfers between devices, route(): lax.all_to_all(holder, 'blk', split_axis=0, concat_axis=0, tiled=True)  31 us
    dot_general x16, matrix products, dot(): return jnp.einsum(spec, a, b, preferred_element_type=jnp.float32)  23.4 us
    ppermute x15, waiting for transfers between devices, shift(): lax.ppermute(array, 'lvl', [(i, (i + by) % row_count) for i in range(row_...  19 us
    all_to_all x1, blocking collectives, route(): lax.all_to_all(holder, 'blk', split_axis=0, concat_axis=0, tiled=True)  18 us
    convert_element_type x6, local copies, waits for them, and re-layouts, route(): holder = holder.astype(piece.dtype)  6.33 us
    unnamed x61, local copies, waits for them, and re-layouts  5.31 us
  transfers between devices with their start and end apart: 20, of which 10 were waited for; matrix products, arithmetic and copies ran while one was open for 8% of the time, Pallas kernels for 0%

profile of v10, /device:TPU:1, one launch (start us, length us, event | category | flops | bytes accessed | tf_op | source)
XLA Modules:
  0.0 207.3 jit_solution(4424169024555518)
XLA Ops:
  11.8 3.3 %collective-permute-start = (bf16[512,192]{0,1:T(8,128)(2,1)}, bf16[512,192]{0,1:T(8,128)(2,1)S(1)}, u32[]{:S(2)}, u32[]{:S(2)}) collective-permute-start(bf16[512,192]{0,1:T(8,128)(2,1)} %pad_maximum_fusion.1), channel_id=1, source_target_pairs={{0,3},{1,0},{2,1},{3,2},{4,7},{5,4},{6,5},{7,6},{8,11},{9,8},{10,9... | collective-permute-start | bytes 589832 | tf_op jit(solution)/shard_map/ppermute | solution.py:57
  21.0 15.9 %collective-permute-start.5 = (bf16[512,512]{0,1:T(8,128)(2,1)S(1)}, bf16[512,512]{0,1:T(8,128)(2,1)}, u32[]{:S(2)}, u32[]{:S(2)}) collective-permute-start(bf16[512,512]{0,1:T(8,128)(2,1)S(1)} %fusion.8), channel_id=1, source_target_pairs={{0,3},{1,0},{2,1},{3,2},{4,7},{5,4},{6,5},{7,6},{8,11},{9,8},{10,9... | collective-permute-start | bytes 1572872 | tf_op jit(solution)/shard_map/ppermute | solution.py:57
  38.7 10.8 %all-to-all-start = ((bf16[32,128,96]{1,2,0:T(8,128)(2,1)}), bf16[32,128,96]{1,2,0:T(8,128)(2,1)S(1)}, u32[]{:S(2)}, u32[]{:S(2)}) async-start(bf16[32,128,96]{1,2,0:T(8,128)(2,1)} %copy.82), calls=%async_computation | async-start | bytes 1572864 | tf_op jit(solution)/shard_map/all_to_all | solution.py:109
  49.6 2.0 select_select_fusion.2
  53.8 9.9 %all-to-all-done = bf16[32,128,96]{1,2,0:T(8,128)(2,1)S(1)} async-done(((bf16[32,128,96]{1,2,0:T(8,128)(2,1)}), bf16[32,128,96]{1,2,0:T(8,128)(2,1)S(1)}, u32[]{:S(2)}, u32[]{:S(2)}) %all-to-all-start) | async-done | bytes 786464 | tf_op jit(solution)/shard_map/all_to_all | solution.py:109
  65.2 18.0 %all_to_all.30 = bf16[32,128,96]{1,2,0:T(8,128)(2,1)S(1)} all-to-all(bf16[32,128,96]{1,2,0:T(8,128)(2,1)S(1)} %copy.84), channel_id=1, replica_groups=mesh['blk'=32,'lvl'=4] {'blk'}, dimensions={0} | all-to-all | bytes 1572864 | tf_op jit(solution)/shard_map/all_to_all | solution.py:109
  85.5 3.9 %all-to-all-start.2 = ((bf16[32,128,96]{1,2,0:T(8,128)(2,1)}), bf16[32,128,96]{1,2,0:T(8,128)(2,1)S(1)}, u32[]{:S(2)}, u32[]{:S(2)}) async-start(bf16[32,128,96]{1,2,0:T(8,128)(2,1)} %copy.86), calls=%async_computation.2 | async-start | bytes 1572864 | tf_op jit(solution)/shard_map/all_to_all | solution.py:109
  89.4 2.8 %convolution_convert_fusion.11 = bf16[512,512]{0,1:T(8,128)(2,1)} fusion(bf16[512,768]{1,0:T(8,128)(2,1)} %convolution_convert_fusion), kind=kOutput, calls=%fused_computation.17 | convolution fusion | flops 402915328 | bytes 1310720 | tf_op jit(solution)/shard_map/bq,bm->qm/dot_general | solution.py:149
  94.8 8.7 %all-to-all-done.2 = bf16[32,128,96]{1,2,0:T(8,128)(2,1)S(1)} async-done(((bf16[32,128,96]{1,2,0:T(8,128)(2,1)}), bf16[32,128,96]{1,2,0:T(8,128)(2,1)S(1)}, u32[]{:S(2)}, u32[]{:S(2)}) %all-to-all-start.2) | async-done | bytes 786464 | tf_op jit(solution)/shard_map/all_to_all | solution.py:109
  103.6 2.2 %select_select_fusion.11 = (bf16[4,128,96]{1,0,2:T(4,128)(2,1)}, bf16[4,128,96]{1,0,2:T(4,128)(2,1)}, bf16[4,128,96]{1,0,2:T(4,128)(2,1)}, bf16[4,128,96]{1,0,2:T(4,128)(2,1)}, bf16[4,128,96]{1,0,2:T(4,128)(2,1)S(1)}) fusion(bf16[4,128,96]{1,0,2:T(4,128)(2,1)} %copy-done.16, bf16[4,128,96]{1,0,2:T(4,128)(2,1)S(1)} %convolution_convert_fusion.20, ...), kind=kOutput, calls=%fused_computation.139 | convolution fusion | flops 3784832 | bytes 1474588 | tf_op jit(solution)/shard_map/kj,jrn->krn/dot_general | solution.py:111
  105.7 12.3 %collective-permute-done.9 = bf16[512,512]{0,1:T(8,128)(2,1)} collective-permute-done((bf16[512,512]{0,1:T(8,128)(2,1)}, bf16[512,512]{0,1:T(8,128)(2,1)}, u32[]{:S(2)}, u32[]{:S(2)}) %collective-permute-start.9) | collective-permute-done | bytes 524320 | tf_op jit(solution)/shard_map/ppermute | solution.py:57
  121.6 8.5 %all-to-all-start.3 = ((bf16[32,128,96]{1,2,0:T(8,128)(2,1)}), bf16[32,128,96]{1,2,0:T(8,128)(2,1)S(1)}, u32[]{:S(2)}, u32[]{:S(2)}) async-start(bf16[32,128,96]{1,2,0:T(8,128)(2,1)} %copy.96), calls=%async_computation.3 | async-start | bytes 1572864 | tf_op jit(solution)/shard_map/all_to_all | solution.py:109
  130.1 2.1 fusion.32
  132.2 12.2 %all-to-all-done.3 = bf16[32,128,96]{1,2,0:T(8,128)(2,1)S(1)} async-done(((bf16[32,128,96]{1,2,0:T(8,128)(2,1)}), bf16[32,128,96]{1,2,0:T(8,128)(2,1)S(1)}, u32[]{:S(2)}, u32[]{:S(2)}) %all-to-all-start.3) | async-done | bytes 786464 | tf_op jit(solution)/shard_map/all_to_all | solution.py:109
  148.3 3.8 %all-to-all-start.4 = ((bf16[32,128,96]{1,2,0:T(8,128)(2,1)}), bf16[32,128,96]{1,2,0:T(8,128)(2,1)S(1)}, u32[]{:S(2)}, u32[]{:S(2)}) async-start(bf16[32,128,96]{1,2,0:T(8,128)(2,1)} %copy.98), calls=%async_computation.4 | async-start | bytes 1572864 | tf_op jit(solution)/shard_map/all_to_all | solution.py:109
  153.4 12.9 %all-to-all-done.4 = bf16[32,128,96]{1,2,0:T(8,128)(2,1)S(1)} async-done(((bf16[32,128,96]{1,2,0:T(8,128)(2,1)}), bf16[32,128,96]{1,2,0:T(8,128)(2,1)S(1)}, u32[]{:S(2)}, u32[]{:S(2)}) %all-to-all-start.4) | async-done | bytes 786464 | tf_op jit(solution)/shard_map/all_to_all | solution.py:109
  168.8 4.0 %all-to-all-start.5 = ((bf16[32,128,96]{1,2,0:T(8,128)(2,1)}), bf16[32,128,96]{1,2,0:T(8,128)(2,1)S(1)}, u32[]{:S(2)}, u32[]{:S(2)}) async-start(bf16[32,128,96]{1,2,0:T(8,128)(2,1)} %copy.100), calls=%async_computation.5 | async-start | bytes 1572864 | tf_op jit(solution)/shard_map/all_to_all | solution.py:109
  172.7 2.1 %collective-permute-start.8 = (bf16[4,128,96]{1,0,2:T(4,128)(2,1)S(1)}, bf16[4,128,96]{1,0,2:T(4,128)(2,1)S(1)}, u32[]{:S(2)}, u32[]{:S(2)}) collective-permute-start(bf16[4,128,96]{1,0,2:T(4,128)(2,1)S(1)} %copy-done.26), channel_id=1, source_target_pairs={{0,3},{1,0},{2,1},{3,2},{4,7},{5,4},{6,5},{7,6},{8,11},{9,8},{10,9... | collective-permute-start | bytes 294920 | tf_op jit(solution)/shard_map/ppermute | solution.py:57
  175.6 11.4 %all-to-all-done.5 = bf16[32,128,96]{1,2,0:T(8,128)(2,1)S(1)} async-done(((bf16[32,128,96]{1,2,0:T(8,128)(2,1)}), bf16[32,128,96]{1,2,0:T(8,128)(2,1)S(1)}, u32[]{:S(2)}, u32[]{:S(2)}) %all-to-all-start.5) | async-done | bytes 786464 | tf_op jit(solution)/shard_map/all_to_all | solution.py:109
  187.4 2.1 %collective-permute-start.14 = (bf16[4,128,96]{1,0,2:T(4,128)(2,1)S(1)}, bf16[4,128,96]{1,0,2:T(4,128)(2,1)S(1)}, u32[]{:S(2)}, u32[]{:S(2)}) collective-permute-start(bf16[4,128,96]{1,0,2:T(4,128)(2,1)S(1)} %get-tuple-element.42), channel_id=1, source_target_pairs={{0,3},{1,0},{2,1},{3,2},{4,7},{5,4},{6,5},{7,6},{8,11},{9,8},{10,9... | collective-permute-start | bytes 294920 | tf_op jit(solution)/shard_map/ppermute | solution.py:57
  191.0 2.8 %collective-permute-done.14 = bf16[4,128,96]{1,0,2:T(4,128)(2,1)S(1)} collective-permute-done((bf16[4,128,96]{1,0,2:T(4,128)(2,1)S(1)}, bf16[4,128,96]{1,0,2:T(4,128)(2,1)S(1)}, u32[]{:S(2)}, u32[]{:S(2)}) %collective-permute-start.14) | collective-permute-done | bytes 98336 | tf_op jit(solution)/shard_map/ppermute | solution.py:57
  195.4 2.0 collective-permute-done.12
  197.7 3.4 %fusion.7 = bf16[768,384]{1,0:T(8,128)(2,1)} fusion(bf16[768,384]{1,0:T(8,128)(2,1)} %copy-done.28, bf16[4,128,384]{1,2,0:T(8,128)(2,1)S(1)} %get-tuple-element.56, bf16[1,1,768,768]{3,2,1,0:T(8,128)(2,1)S(1)} %copy-done, bf16[4,768,128]{1,2,0:T(8,128)(2,1)S(1)} %copy-done.4, bf16[1,1,768,384]{3,2,1,0:T(8,128)(2,1)} %param.7, pred[]{:T(512)S(6)} %eq.202), kind=kOutput, calls=%fused_computation.22 | convolution fusion | flops 756449280 | bytes 4128769 | tf_op jit(solution)/shard_map/ab,bn->an/dot_general | solution.py:149
  201.0 3.3 %convolution_convert_fusion.8 = bf16[384,768]{1,0:T(8,128)(2,1)} fusion(bf16[4,128,384]{1,2,0:T(8,128)(2,1)S(1)} %get-tuple-element.55, bf16[1,1,768,768]{3,2,1,0:T(8,128)(2,1)S(1)} %copy-done, bf16[768,384]{1,0:T(8,128)(2,1)} %fusion.7, bf16[1,1,4,768,128]{4,3,2,1,0:T(8,128)(2,1)S(1)} %copy-done.2), kind=kOutput, calls=%fused_computation.14 | convolution fusion | flops 756154368 | bytes 3538944 | tf_op jit(solution)/shard_map/ba,bn->an/dot_general | solution.py:149
  (163 shorter events, 45.7 us)
Async XLA Ops:
  11.8 9.2 %collective-permute-start = (bf16[512,192]{0,1:T(8,128)(2,1)}, bf16[512,192]{0,1:T(8,128)(2,1)S(1)}, u32[]{:S(2)}, u32[]{:S(2)}) collective-permute-start(bf16[512,192]{0,1:T(8,128)(2,1)} %pad_maximum_fusion.1), channel_id=1, source_target_pairs={{0,3},{1,0},{2,1},{3,2},{4,7},{5,4},{6,5},{7,6},{8,11},{9,8},{10,9... | collective-permute-start | bytes 589832 | tf_op jit(solution)/shard_map/ppermute | solution.py:57
  15.1 21.7 %collective-permute-start.1 = (bf16[512,192]{0,1:T(8,128)(2,1)S(1)}, bf16[512,192]{0,1:T(8,128)(2,1)S(1)}, u32[]{:S(2)}, u32[]{:S(2)}) collective-permute-start(bf16[512,192]{0,1:T(8,128)(2,1)S(1)} %pad_maximum_fusion.2), channel_id=1, source_target_pairs={{0,2},{1,3},{2,0},{3,1},{4,6},{5,7},{6,4},{7,5},{8,10},{9,11},{10,... | collective-permute-start | bytes 589832 | tf_op jit(solution)/shard_map/ppermute | solution.py:57
  16.4 20.4 %collective-permute-start.2 = (bf16[512,192]{0,1:T(8,128)(2,1)}, bf16[512,192]{0,1:T(8,128)(2,1)S(1)}, u32[]{:S(2)}, u32[]{:S(2)}) collective-permute-start(bf16[512,192]{0,1:T(8,128)(2,1)} %pad_maximum_fusion.3), channel_id=1, source_target_pairs={{0,1},{1,2},{2,3},{3,0},{4,5},{5,6},{6,7},{7,4},{8,9},{9,10},{10,1... | collective-permute-start | bytes 589832 | tf_op jit(solution)/shard_map/ppermute | solution.py:57
  17.6 21.0 %copy-start.7 = (bf16[512,512]{0,1:T(8,128)(2,1)}, bf16[512,512]{0,1:T(8,128)(2,1)S(1)}, u32[]{:S(2)}) copy-start(bf16[512,512]{0,1:T(8,128)(2,1)S(1)} %fusion.8) | copy-start | bytes 1572868
  17.6 33.9 %collective-permute-start.3 = (bf16[512,512]{0,1:T(8,128)(2,1)S(1)}, bf16[512,512]{0,1:T(8,128)(2,1)S(1)}, u32[]{:S(2)}, u32[]{:S(2)}) collective-permute-start(bf16[512,512]{0,1:T(8,128)(2,1)S(1)} %fusion.8), channel_id=1, source_target_pairs={{0,1},{1,2},{2,3},{3,0},{4,5},{5,6},{6,7},{7,4},{8,9},{9,10},{10,1... | collective-permute-start | bytes 1572872 | tf_op jit(solution)/shard_map/ppermute | solution.py:57
  19.2 32.3 %collective-permute-start.4 = (bf16[512,512]{0,1:T(8,128)(2,1)S(1)}, bf16[512,512]{0,1:T(8,128)(2,1)}, u32[]{:S(2)}, u32[]{:S(2)}) collective-permute-start(bf16[512,512]{0,1:T(8,128)(2,1)S(1)} %fusion.8), channel_id=1, source_target_pairs={{0,2},{1,3},{2,0},{3,1},{4,6},{5,7},{6,4},{7,5},{8,10},{9,11},{10,... | collective-permute-start | bytes 1572872 | tf_op jit(solution)/shard_map/ppermute | solution.py:57
  21.0 17.7 %copy-start.10 = (bf16[512,192]{0,1:T(8,128)(2,1)}, bf16[512,192]{0,1:T(8,128)(2,1)S(1)}, u32[]{:S(2)}) copy-start(bf16[512,192]{0,1:T(8,128)(2,1)S(1)} %collective-permute-done) | copy-start | bytes 589828
  21.0 31.4 %collective-permute-start.5 = (bf16[512,512]{0,1:T(8,128)(2,1)S(1)}, bf16[512,512]{0,1:T(8,128)(2,1)}, u32[]{:S(2)}, u32[]{:S(2)}) collective-permute-start(bf16[512,512]{0,1:T(8,128)(2,1)S(1)} %fusion.8), channel_id=1, source_target_pairs={{0,3},{1,0},{2,1},{3,2},{4,7},{5,4},{6,5},{7,6},{8,11},{9,8},{10,9... | collective-permute-start | bytes 1572872 | tf_op jit(solution)/shard_map/ppermute | solution.py:57
  38.7 25.1 %all-to-all-start = ((bf16[32,128,96]{1,2,0:T(8,128)(2,1)}), bf16[32,128,96]{1,2,0:T(8,128)(2,1)S(1)}, u32[]{:S(2)}, u32[]{:S(2)}) async-start(bf16[32,128,96]{1,2,0:T(8,128)(2,1)} %copy.82), calls=%async_computation | async-start | bytes 1572864 | tf_op jit(solution)/shard_map/all_to_all | solution.py:109
  65.2 18.3 %copy-start.5 = (bf16[512,192]{0,1:T(8,128)(2,1)S(1)}, bf16[512,192]{0,1:T(8,128)(2,1)}, u32[]{:S(2)}) copy-start(bf16[512,192]{0,1:T(8,128)(2,1)} %get-tuple-element.40) | copy-start | bytes 589828
  85.5 18.1 %all-to-all-start.2 = ((bf16[32,128,96]{1,2,0:T(8,128)(2,1)}), bf16[32,128,96]{1,2,0:T(8,128)(2,1)S(1)}, u32[]{:S(2)}, u32[]{:S(2)}) async-start(bf16[32,128,96]{1,2,0:T(8,128)(2,1)} %copy.86), calls=%async_computation.2 | async-start | bytes 1572864 | tf_op jit(solution)/shard_map/all_to_all | solution.py:109
  92.2 25.9 %collective-permute-start.9 = (bf16[512,512]{0,1:T(8,128)(2,1)}, bf16[512,512]{0,1:T(8,128)(2,1)}, u32[]{:S(2)}, u32[]{:S(2)}) collective-permute-start(bf16[512,512]{0,1:T(8,128)(2,1)} %convolution_convert_fusion.11), channel_id=1, source_target_pairs={{0,1},{1,2},{2,3},{3,0},{4,5},{5,6},{6,7},{7,4},{8,9},{9,10},{10,1... | collective-permute-start | bytes 1572872 | tf_op jit(solution)/shard_map/ppermute | solution.py:57
  92.2 25.9 %collective-permute-start.10 = (bf16[512,512]{0,1:T(8,128)(2,1)}, bf16[512,512]{0,1:T(8,128)(2,1)}, u32[]{:S(2)}, u32[]{:S(2)}) collective-permute-start(bf16[512,512]{0,1:T(8,128)(2,1)} %convolution_convert_fusion.11), channel_id=1, source_target_pairs={{0,2},{1,3},{2,0},{3,1},{4,6},{5,7},{6,4},{7,5},{8,10},{9,11},{10,... | collective-permute-start | bytes 1572872 | tf_op jit(solution)/shard_map/ppermute | solution.py:57
  93.1 25.3 %collective-permute-start.11 = (bf16[512,512]{0,1:T(8,128)(2,1)}, bf16[512,512]{0,1:T(8,128)(2,1)}, u32[]{:S(2)}, u32[]{:S(2)}) collective-permute-start(bf16[512,512]{0,1:T(8,128)(2,1)} %convolution_convert_fusion.11), channel_id=1, source_target_pairs={{0,3},{1,0},{2,1},{3,2},{4,7},{5,4},{6,5},{7,6},{8,11},{9,8},{10,9... | collective-permute-start | bytes 1572872 | tf_op jit(solution)/shard_map/ppermute | solution.py:57
  121.6 22.7 %all-to-all-start.3 = ((bf16[32,128,96]{1,2,0:T(8,128)(2,1)}), bf16[32,128,96]{1,2,0:T(8,128)(2,1)S(1)}, u32[]{:S(2)}, u32[]{:S(2)}) async-start(bf16[32,128,96]{1,2,0:T(8,128)(2,1)} %copy.96), calls=%async_computation.3 | async-start | bytes 1572864 | tf_op jit(solution)/shard_map/all_to_all | solution.py:109
  148.3 18.1 %all-to-all-start.4 = ((bf16[32,128,96]{1,2,0:T(8,128)(2,1)}), bf16[32,128,96]{1,2,0:T(8,128)(2,1)S(1)}, u32[]{:S(2)}, u32[]{:S(2)}) async-start(bf16[32,128,96]{1,2,0:T(8,128)(2,1)} %copy.98), calls=%async_computation.4 | async-start | bytes 1572864 | tf_op jit(solution)/shard_map/all_to_all | solution.py:109
  168.7 18.2 %copy-start.18 = (bf16[4,128,96]{1,0,2:T(4,128)(2,1)S(1)}, bf16[4,128,96]{1,0,2:T(4,128)(2,1)}, u32[]{:S(2)}) copy-start(bf16[4,128,96]{1,0,2:T(4,128)(2,1)} %copy-done.17) | copy-start | bytes 294916
  168.8 18.2 %all-to-all-start.5 = ((bf16[32,128,96]{1,2,0:T(8,128)(2,1)}), bf16[32,128,96]{1,2,0:T(8,128)(2,1)S(1)}, u32[]{:S(2)}, u32[]{:S(2)}) async-start(bf16[32,128,96]{1,2,0:T(8,128)(2,1)} %copy.100), calls=%async_computation.5 | async-start | bytes 1572864 | tf_op jit(solution)/shard_map/all_to_all | solution.py:109
  172.7 16.8 %collective-permute-start.8 = (bf16[4,128,96]{1,0,2:T(4,128)(2,1)S(1)}, bf16[4,128,96]{1,0,2:T(4,128)(2,1)S(1)}, u32[]{:S(2)}, u32[]{:S(2)}) collective-permute-start(bf16[4,128,96]{1,0,2:T(4,128)(2,1)S(1)} %copy-done.26), channel_id=1, source_target_pairs={{0,3},{1,0},{2,1},{3,2},{4,7},{5,4},{6,5},{7,6},{8,11},{9,8},{10,9... | collective-permute-start | bytes 294920 | tf_op jit(solution)/shard_map/ppermute | solution.py:57
  174.9 16.0 %collective-permute-start.7 = (bf16[4,128,96]{1,0,2:T(4,128)(2,1)S(1)}, bf16[4,128,96]{1,0,2:T(4,128)(2,1)S(1)}, u32[]{:S(2)}, u32[]{:S(2)}) collective-permute-start(bf16[4,128,96]{1,0,2:T(4,128)(2,1)S(1)} %copy-done.25), channel_id=1, source_target_pairs={{0,2},{1,3},{2,0},{3,1},{4,6},{5,7},{6,4},{7,5},{8,10},{9,11},{10,... | collective-permute-start | bytes 294920 | tf_op jit(solution)/shard_map/ppermute | solution.py:57
  174.9 16.1 %collective-permute-start.6 = (bf16[4,128,96]{1,0,2:T(4,128)(2,1)S(1)}, bf16[4,128,96]{1,0,2:T(4,128)(2,1)S(1)}, u32[]{:S(2)}, u32[]{:S(2)}) collective-permute-start(bf16[4,128,96]{1,0,2:T(4,128)(2,1)S(1)} %copy-done.24), channel_id=1, source_target_pairs={{0,1},{1,2},{2,3},{3,0},{4,5},{5,6},{6,7},{7,4},{8,9},{9,10},{10,1... | collective-permute-start | bytes 294920 | tf_op jit(solution)/shard_map/ppermute | solution.py:57
  187.4 6.4 %collective-permute-start.14 = (bf16[4,128,96]{1,0,2:T(4,128)(2,1)S(1)}, bf16[4,128,96]{1,0,2:T(4,128)(2,1)S(1)}, u32[]{:S(2)}, u32[]{:S(2)}) collective-permute-start(bf16[4,128,96]{1,0,2:T(4,128)(2,1)S(1)} %get-tuple-element.42), channel_id=1, source_target_pairs={{0,3},{1,0},{2,1},{3,2},{4,7},{5,4},{6,5},{7,6},{8,11},{9,8},{10,9... | collective-permute-start | bytes 294920 | tf_op jit(solution)/shard_map/ppermute | solution.py:57
  189.5 5.8 %collective-permute-start.13 = (bf16[4,128,96]{1,0,2:T(4,128)(2,1)S(1)}, bf16[4,128,96]{1,0,2:T(4,128)(2,1)S(1)}, u32[]{:S(2)}, u32[]{:S(2)}) collective-permute-start(bf16[4,128,96]{1,0,2:T(4,128)(2,1)S(1)} %get-tuple-element.43), channel_id=1, source_target_pairs={{0,2},{1,3},{2,0},{3,1},{4,6},{5,7},{6,4},{7,5},{8,10},{9,11},{10,... | collective-permute-start | bytes 294920 | tf_op jit(solution)/shard_map/ppermute | solution.py:57
  189.5 7.8 %collective-permute-start.12 = (bf16[4,128,96]{1,0,2:T(4,128)(2,1)S(1)}, bf16[4,128,96]{1,0,2:T(4,128)(2,1)S(1)}, u32[]{:S(2)}, u32[]{:S(2)}) collective-permute-start(bf16[4,128,96]{1,0,2:T(4,128)(2,1)S(1)} %get-tuple-element.44), channel_id=1, source_target_pairs={{0,1},{1,2},{2,3},{3,0},{4,5},{5,6},{6,7},{7,4},{8,9},{9,10},{10,1... | collective-permute-start | bytes 294920 | tf_op jit(solution)/shard_map/ppermute | solution.py:57
  (25 other events, 137.9 us)

commit v11 on v9

--- a/solution.py
+++ b/solution.py
@@ -152,11 +152,8 @@
     couple = dot(right_flat, inv_left, "bq,bm->qm").astype(jnp.bfloat16)
     inv_rhs = dot(inverse_here, rhs_here, "ab,bn->an").astype(jnp.bfloat16)
     free = dot(right_flat, inv_rhs, "bq,bn->qn").astype(jnp.bfloat16)
-    inv_left_f = inv_left
-    gram = dot(inv_left_f, inv_left_f, "bq,bm->qm").astype(jnp.bfloat16)
-    turn = dot(inv_left_f, inv_rhs, "bq,bn->qn").astype(jnp.bfloat16)
-    couple = jnp.where(my_row == last, gram, couple)
-    free = jnp.where(my_row == last, turn, free)
+    gram = dot(inv_left, inv_left, "bq,bm->qm").astype(jnp.bfloat16)
+    turn = dot(inv_left, inv_rhs, "bq,bn->qn").astype(jnp.bfloat16)
     couples = [couple] + [shift(couple, d, row_count) for d in range(1, row_count)]
     free_blocks = free.reshape(flat, row_count, width)
     frees = [pick_block(free_blocks, my_row, row_count)]
@@ -197,6 +194,22 @@
     start_block = frees_at(frees, my_row, 0, row_count).reshape(lane_shape)
     chain[1] = route(start_block, mine_target[1], mine_src[1], block_count)
     couple_at = [None] + [from_row(couples, t) for t in range(1, level_count)]
+    grams = []
+    for d in range(row_count):
+        part = jnp.concatenate(
+            [gram, take_block(turn, lax.rem(my_row + d, row_count), row_count)], axis=1
+        )
+        if d:
+            part, _ = lax.optimization_barrier((part, chain[1]))
+            part = shift(part, d, row_count)
+        grams.append(part)
+    gram_at = [None] + [from_row(grams, t) for t in range(1, level_count)]
+
+    def back_free(t):
+        return gram_at[t][:, flat:].astype(jnp.float32) - dot(
+            gram_at[t][:, :flat], chain[t].reshape(flat, width), "qm,mn->qn"
+        )
+
     for t in range(1, last):
         step = frees_at(frees, my_row, t, row_count).astype(jnp.float32) - dot(
             couple_at[t], chain[t].reshape(flat, width), "qm,mn->qn"
@@ -206,21 +219,11 @@
     mine_fwd = solve_forward(own_level_blocks(chain))
     solved = jnp.where(my_row == 0, first, mine_fwd)
     top = dot(inverse_here, solved, "ba,bn->an").astype(jnp.bfloat16)
-    back_term = dot(left_flat, top, "bm,bn->mn").astype(jnp.bfloat16)
-    back_parts = [take_block(back_term, my_row, row_count)]
-    for d in range(1, row_count):
-        back_parts.append(shift(take_block(back_term, lax.rem(my_row + d, row_count), row_count), d, row_count))
-
-    def back_free(t):
-        return frees_at(back_parts, my_row, t, row_count)
 
     back = [zero_block] * level_count
-    turned = frees_at(frees, my_row, last, row_count).astype(jnp.float32) - dot(
-        couple_at[last], chain[last].reshape(flat, width), "qm,mn->qn"
-    )
-    back[last - 1] = route(turned.astype(jnp.bfloat16).reshape(lane_shape), mine_src[last], mine_target[last], block_count)
+    back[last - 1] = route(back_free(last).astype(jnp.bfloat16).reshape(lane_shape), mine_src[last], mine_target[last], block_count)
     for t in reversed(range(1, last)):
-        step = back_free(t).astype(jnp.float32) - dot(
+        step = back_free(t) - dot(
             couple_at[t], back[t - 0].reshape(flat, width), "mq,mn->qn"
         )
         back[t - 1] = route(step.astype(jnp.bfloat16).reshape(lane_shape), mine_src[t], mine_target[t], block_count)

time: 187 us -> 190 us (1.016)
  blocking collectives: 40 us -> 0 us
  waiting for transfers between devices: 43.4 us -> 79.1 us
  local copies, waits for them, and re-layouts: 21.6 us -> 15.2 us
  starting transfers between devices: 46.9 us -> 52.9 us
  other arithmetic: 5.92 us -> 11.8 us
    all_to_all x2 -> x0, blocking collectives: 40 us -> none  [route(): lax.all_to_all(holder, 'blk', split_axis=0, concat_axis=0, tiled=True)]
    all_to_all x4 -> x6, waiting for transfers between devices: 24.6 us -> 50 us  [route(): lax.all_to_all(holder, 'blk', split_axis=0, concat_axis=0, tiled=True)]
    all_to_all x4 -> x6, starting transfers between devices: 26.4 us -> 37.5 us  [route(): lax.all_to_all(holder, 'blk', split_axis=0, concat_axis=0, tiled=True)]
    ppermute x15, waiting for transfers between devices: 18.8 us -> 29.1 us  [shift(): lax.ppermute(array, 'lvl', [(i, (i + by) % row_count) for i in range(row_...]
    ppermute x15, starting transfers between devices: 20.5 us -> 15.4 us  [shift(): lax.ppermute(array, 'lvl', [(i, (i + by) % row_count) for i in range(row_...]
    mul x8, local copies, waits for them, and re-layouts: 5.68 us -> 0.64 us  [put_block(): full = part[..., None, :] * hot[:, None]]
    select_n x1 -> x2, other arithmetic: 1.47 us -> 4.9 us  [from_row(): chosen = jnp.where(pick == d, parts[d], chosen)]
    ppermute x6, local copies, waits for them, and re-layouts: 2.77 us -> 0.09 us  [shift(): lax.ppermute(array, 'lvl', [(i, (i + by) % row_count) for i in range(row_...]
  transfers between devices with their start and end apart: 19 -> 21, of which waited for: 10 -> 12; matrix products, arithmetic and copies ran while one was open for 13% -> 9% of each run, Pallas kernels for 0% -> 0%
where the time goes in v11:
time: 190 us; the launch traced here: 188 us
  waiting for transfers between devices  79.1 us (42%)
  starting transfers between devices  52.9 us (28%)
  matrix products  28 us (15%)
  local copies, waits for them, and re-layouts  15.2 us (8%)
  other arithmetic  11.8 us (6%)
    all_to_all x6, waiting for transfers between devices, route(): lax.all_to_all(holder, 'blk', split_axis=0, concat_axis=0, tiled=True)  50 us
    all_to_all x6, starting transfers between devices, route(): lax.all_to_all(holder, 'blk', split_axis=0, concat_axis=0, tiled=True)  37.5 us
    ppermute x15, waiting for transfers between devices, shift(): lax.ppermute(array, 'lvl', [(i, (i + by) % row_count) for i in range(row_...  29.1 us
    dot_general x16, matrix products, dot(): return jnp.einsum(spec, a, b, preferred_element_type=jnp.float32)  20.2 us
    ppermute x15, starting transfers between devices, shift(): lax.ppermute(array, 'lvl', [(i, (i + by) % row_count) for i in range(row_...  15.4 us
    convert_element_type x6, local copies, waits for them, and re-layouts, route(): holder = holder.astype(piece.dtype)  7.25 us
    select_n x2, other arithmetic, from_row(): chosen = jnp.where(pick == d, parts[d], chosen)  4.9 us
    dot_general x6, matrix products, route(): jnp.einsum('kj,jrn->krn', take, arrived, preferred_element_type=jnp.float32)  4.88 us
  transfers between devices with their start and end apart: 21, of which 12 were waited for; matrix products, arithmetic and copies ran while one was open for 9% of the time, Pallas kernels for 0%

profile of v11, /device:TPU:1, one launch (start us, length us, event | category | flops | bytes accessed | tf_op | source)
XLA Modules:
  0.0 188.4 jit_solution(3341491526017837808)
XLA Ops:
  15.2 3.3 %collective-permute-start = (bf16[512,96]{0,1:T(8,128)(2,1)S(1)}, bf16[512,96]{0,1:T(8,128)(2,1)S(1)}, u32[]{:S(2)}, u32[]{:S(2)}) collective-permute-start(bf16[512,96]{0,1:T(8,128)(2,1)S(1)} %get-tuple-element.67), channel_id=1, source_target_pairs={{0,3},{1,0},{2,1},{3,2},{4,7},{5,4},{6,5},{7,6},{8,11},{9,8},{10,9... | collective-permute-start | bytes 294920 | tf_op jit(solution)/shard_map/ppermute | solution.py:57
  21.9 1.7 collective-permute-start.4
  28.0 10.0 %all-to-all-start = ((bf16[32,128,96]{1,2,0:T(8,128)(2,1)}), bf16[32,128,96]{1,2,0:T(8,128)(2,1)S(1)}, u32[]{:S(2)}, u32[]{:S(2)}) async-start(bf16[32,128,96]{1,2,0:T(8,128)(2,1)} %copy.79), calls=%async_computation | async-start | bytes 1572864 | tf_op jit(solution)/shard_map/all_to_all | solution.py:109
  38.3 9.8 %collective-permute-done.4 = bf16[512,512]{0,1:T(8,128)(2,1)} collective-permute-done((bf16[512,512]{0,1:T(8,128)(2,1)S(1)}, bf16[512,512]{0,1:T(8,128)(2,1)}, u32[]{:S(2)}, u32[]{:S(2)}) %collective-permute-start.4) | collective-permute-done | bytes 524320 | tf_op jit(solution)/shard_map/ppermute | solution.py:57
  49.7 2.5 %all-to-all-done = bf16[32,128,96]{1,2,0:T(8,128)(2,1)S(1)} async-done(((bf16[32,128,96]{1,2,0:T(8,128)(2,1)}), bf16[32,128,96]{1,2,0:T(8,128)(2,1)S(1)}, u32[]{:S(2)}, u32[]{:S(2)}) %all-to-all-start) | async-done | bytes 786464 | tf_op jit(solution)/shard_map/all_to_all | solution.py:109
  55.1 7.5 %all-to-all-start.1 = ((bf16[32,128,96]{1,2,0:T(8,128)(2,1)}), bf16[32,128,96]{1,2,0:T(8,128)(2,1)S(1)}, u32[]{:S(2)}, u32[]{:S(2)}) async-start(bf16[32,128,96]{1,2,0:T(8,128)(2,1)} %copy.81), calls=%async_computation.1 | async-start | bytes 1572864 | tf_op jit(solution)/shard_map/all_to_all | solution.py:109
  62.7 2.0 %convolution_convert_fusion.11 = bf16[512,512]{0,1:T(8,128)(2,1)S(1)} fusion(bf16[512,768]{1,0:T(8,128)(2,1)} %copy-done.40), kind=kOutput, calls=%fused_computation.17 | convolution fusion | flops 402915328 | bytes 1310720 | tf_op jit(solution)/shard_map/bq,bm->qm/dot_general | solution.py:149
  67.6 9.3 %all-to-all-done.1 = bf16[32,128,96]{1,2,0:T(8,128)(2,1)S(1)} async-done(((bf16[32,128,96]{1,2,0:T(8,128)(2,1)}), bf16[32,128,96]{1,2,0:T(8,128)(2,1)S(1)}, u32[]{:S(2)}, u32[]{:S(2)}) %all-to-all-start.1) | async-done | bytes 786464 | tf_op jit(solution)/shard_map/all_to_all | solution.py:109
  80.8 4.5 %all-to-all-start.2 = ((bf16[32,128,96]{1,2,0:T(8,128)(2,1)}), bf16[32,128,96]{1,2,0:T(8,128)(2,1)}, u32[]{:S(2)}, u32[]{:S(2)}) async-start(bf16[32,128,96]{1,2,0:T(8,128)(2,1)} %copy.83), calls=%async_computation.2 | async-start | bytes 1572864 | tf_op jit(solution)/shard_map/all_to_all | solution.py:109
  85.4 12.1 %collective-permute-done.9 = bf16[512,608]{0,1:T(8,128)(2,1)} collective-permute-done((bf16[512,608]{0,1:T(8,128)(2,1)}, bf16[512,608]{0,1:T(8,128)(2,1)}, u32[]{:S(2)}, u32[]{:S(2)}) %collective-permute-start.9) | collective-permute-done | bytes 622624 | tf_op jit(solution)/shard_map/ppermute | solution.py:57
  97.5 3.3 %select_select_fusion = (bf16[512,608]{0,1:T(8,128)(2,1)}, bf16[512,608]{0,1:T(8,128)(2,1)}, bf16[512,608]{0,1:T(8,128)(2,1)}) fusion(bf16[512,608]{0,1:T(8,128)(2,1)} %collective-permute-done.9, bf16[512,608]{0,1:T(8,128)(2,1)} %collective-permute-done.10, bf16[512,608]{0,1:T(8,128)(2,1)} %collective-permute-done.11, pred[]{:T(512)S(6)} %eq.515, ...), kind=kLoop, calls=%fused_computation.52 | loop fusion | flops 4046848 | bytes 4358153 | tf_op jit(solution)/shard_map/jit(_where)/select_n | solution.py:167
  100.8 2.4 %select_select_fusion.12 = (bf16[4,128,96]{1,0,2:T(4,128)(2,1)}, bf16[4,128,96]{1,0,2:T(4,128)(2,1)}, bf16[4,128,96]{1,0,2:T(4,128)(2,1)}, bf16[4,128,96]{1,0,2:T(4,128)(2,1)}, bf16[4,128,96]{1,0,2:T(4,128)(2,1)S(1)}) fusion(bf16[4,128,96]{1,0,2:T(4,128)(2,1)S(1)} %copy-done.6, bf16[4,128,96]{1,0,2:T(4,128)(2,1)S(1)} %copy-done.4, pred[]{:T(512)S(6)} %eq.223, ...), kind=kOutput, calls=%fused_computation.113 | convolution fusion | flops 3784832 | bytes 1474588 | tf_op jit(solution)/shard_map/kj,jrn->krn/dot_general | solution.py:111
  105.2 7.5 %all-to-all-start.3 = ((bf16[32,128,96]{1,2,0:T(8,128)(2,1)}), bf16[32,128,96]{1,2,0:T(8,128)(2,1)S(1)}, u32[]{:S(2)}, u32[]{:S(2)}) async-start(bf16[32,128,96]{1,2,0:T(8,128)(2,1)} %copy.92), calls=%async_computation.3 | async-start | bytes 1572864 | tf_op jit(solution)/shard_map/all_to_all | solution.py:109
  114.0 13.0 %all-to-all-done.3 = bf16[32,128,96]{1,2,0:T(8,128)(2,1)S(1)} async-done(((bf16[32,128,96]{1,2,0:T(8,128)(2,1)}), bf16[32,128,96]{1,2,0:T(8,128)(2,1)S(1)}, u32[]{:S(2)}, u32[]{:S(2)}) %all-to-all-start.3) | async-done | bytes 786464 | tf_op jit(solution)/shard_map/all_to_all | solution.py:109
  130.2 4.0 %all-to-all-start.4 = ((bf16[32,128,96]{1,2,0:T(8,128)(2,1)}), bf16[32,128,96]{1,2,0:T(8,128)(2,1)S(1)}, u32[]{:S(2)}, u32[]{:S(2)}) async-start(bf16[32,128,96]{1,2,0:T(8,128)(2,1)} %copy.94), calls=%async_computation.4 | async-start | bytes 1572864 | tf_op jit(solution)/shard_map/all_to_all | solution.py:109
  134.4 14.0 %all-to-all-done.4 = bf16[32,128,96]{1,2,0:T(8,128)(2,1)S(1)} async-done(((bf16[32,128,96]{1,2,0:T(8,128)(2,1)}), bf16[32,128,96]{1,2,0:T(8,128)(2,1)S(1)}, u32[]{:S(2)}, u32[]{:S(2)}) %all-to-all-start.4) | async-done | bytes 786464 | tf_op jit(solution)/shard_map/all_to_all | solution.py:109
  150.8 4.0 %all-to-all-start.5 = ((bf16[32,128,96]{1,2,0:T(8,128)(2,1)}), bf16[32,128,96]{1,2,0:T(8,128)(2,1)S(1)}, u32[]{:S(2)}, u32[]{:S(2)}) async-start(bf16[32,128,96]{1,2,0:T(8,128)(2,1)} %copy.96), calls=%async_computation.5 | async-start | bytes 1572864 | tf_op jit(solution)/shard_map/all_to_all | solution.py:109
  154.9 1.8 collective-permute-start.7
  157.8 11.2 %all-to-all-done.5 = bf16[32,128,96]{1,2,0:T(8,128)(2,1)S(1)} async-done(((bf16[32,128,96]{1,2,0:T(8,128)(2,1)}), bf16[32,128,96]{1,2,0:T(8,128)(2,1)S(1)}, u32[]{:S(2)}, u32[]{:S(2)}) %all-to-all-start.5) | async-done | bytes 786464 | tf_op jit(solution)/shard_map/all_to_all | solution.py:109
  173.2 3.2 %collective-permute-done.13 = bf16[4,128,96]{1,0,2:T(4,128)(2,1)S(1)} collective-permute-done((bf16[4,128,96]{1,0,2:T(4,128)(2,1)}, bf16[4,128,96]{1,0,2:T(4,128)(2,1)S(1)}, u32[]{:S(2)}, u32[]{:S(2)}) %collective-permute-start.13) | collective-permute-done | bytes 98336 | tf_op jit(solution)/shard_map/ppermute | solution.py:57
  176.8 1.8 collective-permute-done.12
  178.9 3.4 %fusion.7 = bf16[768,384]{1,0:T(8,128)(2,1)} fusion(bf16[768,384]{1,0:T(8,128)(2,1)} %convolution_convert_fusion.10, bf16[4,128,384]{1,2,0:T(8,128)(2,1)S(1)} %get-tuple-element.62, bf16[1,1,768,768]{3,2,1,0:T(8,128)(2,1)S(1)} %copy-done, bf16[4,768,128]{1,2,0:T(8,128)(2,1)S(1)} %copy-done.15, bf16[1,1,768,384]{3,2,1,0:T(8,128)(2,1)} %param.7, pred[]{:T(512)S(6)} %eq.210), kind=kOutput, calls=%fused_computation.22 | convolution fusion | flops 756449280 | bytes 4128769 | tf_op jit(solution)/shard_map/ab,bn->an/dot_general | solution.py:149
  182.3 3.3 %convolution_convert_fusion.8 = bf16[384,768]{1,0:T(8,128)(2,1)} fusion(bf16[4,128,384]{1,2,0:T(8,128)(2,1)S(1)} %get-tuple-element.61, bf16[1,1,768,768]{3,2,1,0:T(8,128)(2,1)S(1)} %copy-done, bf16[768,384]{1,0:T(8,128)(2,1)} %fusion.7, bf16[1,1,4,768,128]{4,3,2,1,0:T(8,128)(2,1)S(1)} %copy-done.11), kind=kOutput, calls=%fused_computation.14 | convolution fusion | flops 756154368 | bytes 3538944 | tf_op jit(solution)/shard_map/ba,bn->an/dot_general | solution.py:149
  185.6 1.7 fusion.5
  (191 shorter events, 49.6 us)
Async XLA Ops:
  15.2 37.3 %copy-start.2 = (bf16[512,96]{0,1:T(8,128)(2,1)}, bf16[512,96]{0,1:T(8,128)(2,1)S(1)}, u32[]{:S(2)}) copy-start(bf16[512,96]{0,1:T(8,128)(2,1)S(1)} %get-tuple-element.70) | copy-start | bytes 294916
  15.2 8.4 %collective-permute-start = (bf16[512,96]{0,1:T(8,128)(2,1)S(1)}, bf16[512,96]{0,1:T(8,128)(2,1)S(1)}, u32[]{:S(2)}, u32[]{:S(2)}) collective-permute-start(bf16[512,96]{0,1:T(8,128)(2,1)S(1)} %get-tuple-element.67), channel_id=1, source_target_pairs={{0,3},{1,0},{2,1},{3,2},{4,7},{5,4},{6,5},{7,6},{8,11},{9,8},{10,9... | collective-permute-start | bytes 294920 | tf_op jit(solution)/shard_map/ppermute | solution.py:57
  18.5 6.1 %collective-permute-start.1 = (bf16[512,96]{0,1:T(8,128)(2,1)S(1)}, bf16[512,96]{0,1:T(8,128)(2,1)S(1)}, u32[]{:S(2)}, u32[]{:S(2)}) collective-permute-start(bf16[512,96]{0,1:T(8,128)(2,1)S(1)} %get-tuple-element.68), channel_id=1, source_target_pairs={{0,2},{1,3},{2,0},{3,1},{4,6},{5,7},{6,4},{7,5},{8,10},{9,11},{10,... | collective-permute-start | bytes 294920 | tf_op jit(solution)/shard_map/ppermute | solution.py:57
  19.1 7.1 %collective-permute-start.2 = (bf16[512,96]{0,1:T(8,128)(2,1)S(1)}, bf16[512,96]{0,1:T(8,128)(2,1)S(1)}, u32[]{:S(2)}, u32[]{:S(2)}) collective-permute-start(bf16[512,96]{0,1:T(8,128)(2,1)S(1)} %get-tuple-element.69), channel_id=1, source_target_pairs={{0,1},{1,2},{2,3},{3,0},{4,5},{5,6},{6,7},{7,4},{8,9},{9,10},{10,1... | collective-permute-start | bytes 294920 | tf_op jit(solution)/shard_map/ppermute | solution.py:57
  20.3 18.0 %collective-permute-start.3 = (bf16[512,512]{0,1:T(8,128)(2,1)S(1)}, bf16[512,512]{0,1:T(8,128)(2,1)S(1)}, u32[]{:S(2)}, u32[]{:S(2)}) collective-permute-start(bf16[512,512]{0,1:T(8,128)(2,1)S(1)} %fusion.8), channel_id=1, source_target_pairs={{0,1},{1,2},{2,3},{3,0},{4,5},{5,6},{6,7},{7,4},{8,9},{9,10},{10,1... | collective-permute-start | bytes 1572872 | tf_op jit(solution)/shard_map/ppermute | solution.py:57
  21.9 26.2 %collective-permute-start.4 = (bf16[512,512]{0,1:T(8,128)(2,1)S(1)}, bf16[512,512]{0,1:T(8,128)(2,1)}, u32[]{:S(2)}, u32[]{:S(2)}) collective-permute-start(bf16[512,512]{0,1:T(8,128)(2,1)S(1)} %fusion.8), channel_id=1, source_target_pairs={{0,2},{1,3},{2,0},{3,1},{4,6},{5,7},{6,4},{7,5},{8,10},{9,11},{10,... | collective-permute-start | bytes 1572872 | tf_op jit(solution)/shard_map/ppermute | solution.py:57
  23.6 28.9 %copy-start.7 = (bf16[512,96]{0,1:T(8,128)(2,1)}, bf16[512,96]{0,1:T(8,128)(2,1)S(1)}, u32[]{:S(2)}) copy-start(bf16[512,96]{0,1:T(8,128)(2,1)S(1)} %collective-permute-done) | copy-start | bytes 294916
  23.6 24.5 %collective-permute-start.5 = (bf16[512,512]{0,1:T(8,128)(2,1)S(1)}, bf16[512,512]{0,1:T(8,128)(2,1)}, u32[]{:S(2)}, u32[]{:S(2)}) collective-permute-start(bf16[512,512]{0,1:T(8,128)(2,1)S(1)} %fusion.8), channel_id=1, source_target_pairs={{0,3},{1,0},{2,1},{3,2},{4,7},{5,4},{6,5},{7,6},{8,11},{9,8},{10,9... | collective-permute-start | bytes 1572872 | tf_op jit(solution)/shard_map/ppermute | solution.py:57
  24.7 27.9 %copy-start.8 = (bf16[512,96]{0,1:T(8,128)(2,1)}, bf16[512,96]{0,1:T(8,128)(2,1)S(1)}, u32[]{:S(2)}) copy-start(bf16[512,96]{0,1:T(8,128)(2,1)S(1)} %collective-permute-done.1) | copy-start | bytes 294916
  28.0 24.2 %all-to-all-start = ((bf16[32,128,96]{1,2,0:T(8,128)(2,1)}), bf16[32,128,96]{1,2,0:T(8,128)(2,1)S(1)}, u32[]{:S(2)}, u32[]{:S(2)}) async-start(bf16[32,128,96]{1,2,0:T(8,128)(2,1)} %copy.79), calls=%async_computation | async-start | bytes 1572864 | tf_op jit(solution)/shard_map/all_to_all | solution.py:109
  55.1 21.7 %all-to-all-start.1 = ((bf16[32,128,96]{1,2,0:T(8,128)(2,1)}), bf16[32,128,96]{1,2,0:T(8,128)(2,1)S(1)}, u32[]{:S(2)}, u32[]{:S(2)}) async-start(bf16[32,128,96]{1,2,0:T(8,128)(2,1)} %copy.81), calls=%async_computation.1 | async-start | bytes 1572864 | tf_op jit(solution)/shard_map/all_to_all | solution.py:109
  66.1 19.2 %collective-permute-start.11 = (bf16[512,608]{0,1:T(8,128)(2,1)}, bf16[512,608]{0,1:T(8,128)(2,1)}, u32[]{:S(2)}, u32[]{:S(2)}) collective-permute-start(bf16[512,608]{0,1:T(8,128)(2,1)} %get-tuple-element.7), channel_id=1, source_target_pairs={{0,3},{1,0},{2,1},{3,2},{4,7},{5,4},{6,5},{7,6},{8,11},{9,8},{10,9... | collective-permute-start | bytes 1867784 | tf_op jit(solution)/shard_map/ppermute | solution.py:57
  66.4 19.0 %collective-permute-start.10 = (bf16[512,608]{0,1:T(8,128)(2,1)}, bf16[512,608]{0,1:T(8,128)(2,1)}, u32[]{:S(2)}, u32[]{:S(2)}) collective-permute-start(bf16[512,608]{0,1:T(8,128)(2,1)} %get-tuple-element.6), channel_id=1, source_target_pairs={{0,2},{1,3},{2,0},{3,1},{4,6},{5,7},{6,4},{7,5},{8,10},{9,11},{10,... | collective-permute-start | bytes 1867784 | tf_op jit(solution)/shard_map/ppermute | solution.py:57
  67.1 30.4 %collective-permute-start.9 = (bf16[512,608]{0,1:T(8,128)(2,1)}, bf16[512,608]{0,1:T(8,128)(2,1)}, u32[]{:S(2)}, u32[]{:S(2)}) collective-permute-start(bf16[512,608]{0,1:T(8,128)(2,1)} %get-tuple-element.5), channel_id=1, source_target_pairs={{0,1},{1,2},{2,3},{3,0},{4,5},{5,6},{6,7},{7,4},{8,9},{9,10},{10,1... | collective-permute-start | bytes 1867784 | tf_op jit(solution)/shard_map/ppermute | solution.py:57
  80.8 20.0 %all-to-all-start.2 = ((bf16[32,128,96]{1,2,0:T(8,128)(2,1)}), bf16[32,128,96]{1,2,0:T(8,128)(2,1)}, u32[]{:S(2)}, u32[]{:S(2)}) async-start(bf16[32,128,96]{1,2,0:T(8,128)(2,1)} %copy.83), calls=%async_computation.2 | async-start | bytes 1572864 | tf_op jit(solution)/shard_map/all_to_all | solution.py:109
  105.2 21.7 %all-to-all-start.3 = ((bf16[32,128,96]{1,2,0:T(8,128)(2,1)}), bf16[32,128,96]{1,2,0:T(8,128)(2,1)S(1)}, u32[]{:S(2)}, u32[]{:S(2)}) async-start(bf16[32,128,96]{1,2,0:T(8,128)(2,1)} %copy.92), calls=%async_computation.3 | async-start | bytes 1572864 | tf_op jit(solution)/shard_map/all_to_all | solution.py:109
  130.2 18.2 %all-to-all-start.4 = ((bf16[32,128,96]{1,2,0:T(8,128)(2,1)}), bf16[32,128,96]{1,2,0:T(8,128)(2,1)S(1)}, u32[]{:S(2)}, u32[]{:S(2)}) async-start(bf16[32,128,96]{1,2,0:T(8,128)(2,1)} %copy.94), calls=%async_computation.4 | async-start | bytes 1572864 | tf_op jit(solution)/shard_map/all_to_all | solution.py:109
  150.8 18.2 %all-to-all-start.5 = ((bf16[32,128,96]{1,2,0:T(8,128)(2,1)}), bf16[32,128,96]{1,2,0:T(8,128)(2,1)S(1)}, u32[]{:S(2)}, u32[]{:S(2)}) async-start(bf16[32,128,96]{1,2,0:T(8,128)(2,1)} %copy.96), calls=%async_computation.5 | async-start | bytes 1572864 | tf_op jit(solution)/shard_map/all_to_all | solution.py:109
  154.8 17.0 %collective-permute-start.6 = (bf16[4,128,96]{1,0,2:T(4,128)(2,1)S(1)}, bf16[4,128,96]{1,0,2:T(4,128)(2,1)S(1)}, u32[]{:S(2)}, u32[]{:S(2)}) collective-permute-start(bf16[4,128,96]{1,0,2:T(4,128)(2,1)S(1)} %copy-done.38), channel_id=1, source_target_pairs={{0,1},{1,2},{2,3},{3,0},{4,5},{5,6},{6,7},{7,4},{8,9},{9,10},{10,1... | collective-permute-start | bytes 294920 | tf_op jit(solution)/shard_map/ppermute | solution.py:57
  154.9 18.2 %collective-permute-start.7 = (bf16[4,128,96]{1,0,2:T(4,128)(2,1)S(1)}, bf16[4,128,96]{1,0,2:T(4,128)(2,1)S(1)}, u32[]{:S(2)}, u32[]{:S(2)}) collective-permute-start(bf16[4,128,96]{1,0,2:T(4,128)(2,1)S(1)} %copy-done.37), channel_id=1, source_target_pairs={{0,2},{1,3},{2,0},{3,1},{4,6},{5,7},{6,4},{7,5},{8,10},{9,11},{10,... | collective-permute-start | bytes 294920 | tf_op jit(solution)/shard_map/ppermute | solution.py:57
  156.7 16.4 %collective-permute-start.8 = (bf16[4,128,96]{1,0,2:T(4,128)(2,1)S(1)}, bf16[4,128,96]{1,0,2:T(4,128)(2,1)S(1)}, u32[]{:S(2)}, u32[]{:S(2)}) collective-permute-start(bf16[4,128,96]{1,0,2:T(4,128)(2,1)S(1)} %copy-done.36), channel_id=1, source_target_pairs={{0,3},{1,0},{2,1},{3,2},{4,7},{5,4},{6,5},{7,6},{8,11},{9,8},{10,9... | collective-permute-start | bytes 294920 | tf_op jit(solution)/shard_map/ppermute | solution.py:57
  170.2 6.2 %collective-permute-start.13 = (bf16[4,128,96]{1,0,2:T(4,128)(2,1)}, bf16[4,128,96]{1,0,2:T(4,128)(2,1)S(1)}, u32[]{:S(2)}, u32[]{:S(2)}) collective-permute-start(bf16[4,128,96]{1,0,2:T(4,128)(2,1)} %get-tuple-element.49), channel_id=1, source_target_pairs={{0,2},{1,3},{2,0},{3,1},{4,6},{5,7},{6,4},{7,5},{8,10},{9,11},{10,... | collective-permute-start | bytes 294920 | tf_op jit(solution)/shard_map/ppermute | solution.py:57
  170.9 5.8 %collective-permute-start.14 = (bf16[4,128,96]{1,0,2:T(4,128)(2,1)}, bf16[4,128,96]{1,0,2:T(4,128)(2,1)S(1)}, u32[]{:S(2)}, u32[]{:S(2)}) collective-permute-start(bf16[4,128,96]{1,0,2:T(4,128)(2,1)} %get-tuple-element.48), channel_id=1, source_target_pairs={{0,3},{1,0},{2,1},{3,2},{4,7},{5,4},{6,5},{7,6},{8,11},{9,8},{10,9... | collective-permute-start | bytes 294920 | tf_op jit(solution)/shard_map/ppermute | solution.py:57
  171.8 6.7 %collective-permute-start.12 = (bf16[4,128,96]{1,0,2:T(4,128)(2,1)}, bf16[4,128,96]{1,0,2:T(4,128)(2,1)S(1)}, u32[]{:S(2)}, u32[]{:S(2)}) collective-permute-start(bf16[4,128,96]{1,0,2:T(4,128)(2,1)} %get-tuple-element.50), channel_id=1, source_target_pairs={{0,1},{1,2},{2,3},{3,0},{4,5},{5,6},{6,7},{7,4},{8,9},{9,10},{10,1... | collective-permute-start | bytes 294920 | tf_op jit(solution)/shard_map/ppermute | solution.py:57
  (40 other events, 261.1 us)

commit v12 on v11

--- a/solution.py
+++ b/solution.py
@@ -200,7 +200,7 @@
             [gram, take_block(turn, lax.rem(my_row + d, row_count), row_count)], axis=1
         )
         if d:
-            part, _ = lax.optimization_barrier((part, chain[1]))
+            part, _ = lax.optimization_barrier((part, couple_at[1]))
             part = shift(part, d, row_count)
         grams.append(part)
     gram_at = [None] + [from_row(grams, t) for t in range(1, level_count)]

time: 190 us -> 188 us (0.989)
  starting transfers between devices: 52.9 us -> 55.3 us
  transfers between devices with their start and end apart: 21 -> 21, of which waited for: 12 -> 13; matrix products, arithmetic and copies ran while one was open for 9% -> 9% of each run, Pallas kernels for 0% -> 0%
where the time goes in v12:
time: 188 us; the launch traced here: 187 us
  waiting for transfers between devices  78.4 us (42%)
  starting transfers between devices  55.3 us (29%)
  matrix products  28.1 us (15%)
  local copies, waits for them, and re-layouts  13.4 us (7%)
  other arithmetic  10.4 us (6%)
    all_to_all x6, waiting for transfers between devices, route(): lax.all_to_all(holder, 'blk', split_axis=0, concat_axis=0, tiled=True)  48.8 us
    all_to_all x6, starting transfers between devices, route(): lax.all_to_all(holder, 'blk', split_axis=0, concat_axis=0, tiled=True)  38.3 us
    ppermute x15, waiting for transfers between devices, shift(): lax.ppermute(array, 'lvl', [(i, (i + by) % row_count) for i in range(row_...  29.6 us
    dot_general x16, matrix products, dot(): return jnp.einsum(spec, a, b, preferred_element_type=jnp.float32)  20.2 us
    ppermute x15, starting transfers between devices, shift(): lax.ppermute(array, 'lvl', [(i, (i + by) % row_count) for i in range(row_...  17 us
    convert_element_type x6, local copies, waits for them, and re-layouts, route(): holder = holder.astype(piece.dtype)  7.25 us
    unnamed x89, local copies, waits for them, and re-layouts  5.18 us
    select_n x2, other arithmetic, from_row(): chosen = jnp.where(pick == d, parts[d], chosen)  4.9 us
  transfers between devices with their start and end apart: 21, of which 13 were waited for; matrix products, arithmetic and copies ran while one was open for 9% of the time, Pallas kernels for 0%

profile of v12, /device:TPU:1, one launch (start us, length us, event | category | flops | bytes accessed | tf_op | source)
XLA Modules:
  0.0 187.1 jit_solution(15248698063151022722)
XLA Ops:
  12.2 3.3 %collective-permute-start = (bf16[512,96]{0,1:T(8,128)(2,1)S(1)}, bf16[512,96]{0,1:T(8,128)(2,1)S(1)}, u32[]{:S(2)}, u32[]{:S(2)}) collective-permute-start(bf16[512,96]{0,1:T(8,128)(2,1)S(1)} %get-tuple-element.67), channel_id=1, source_target_pairs={{0,3},{1,0},{2,1},{3,2},{4,7},{5,4},{6,5},{7,6},{8,11},{9,8},{10,9... | collective-permute-start | bytes 294920 | tf_op jit(solution)/shard_map/ppermute | solution.py:57
  24.9 10.0 %all-to-all-start = ((bf16[32,128,96]{1,2,0:T(8,128)(2,1)}), bf16[32,128,96]{1,2,0:T(8,128)(2,1)S(1)}, u32[]{:S(2)}, u32[]{:S(2)}) async-start(bf16[32,128,96]{1,2,0:T(8,128)(2,1)} %copy.79), calls=%async_computation | async-start | bytes 1572864 | tf_op jit(solution)/shard_map/all_to_all | solution.py:109
  35.2 9.8 %collective-permute-done.4 = bf16[512,512]{0,1:T(8,128)(2,1)} collective-permute-done((bf16[512,512]{0,1:T(8,128)(2,1)S(1)}, bf16[512,512]{0,1:T(8,128)(2,1)}, u32[]{:S(2)}, u32[]{:S(2)}) %collective-permute-start.4) | collective-permute-done | bytes 524320 | tf_op jit(solution)/shard_map/ppermute | solution.py:57
  46.7 2.5 %all-to-all-done = bf16[32,128,96]{1,2,0:T(8,128)(2,1)S(1)} async-done(((bf16[32,128,96]{1,2,0:T(8,128)(2,1)}), bf16[32,128,96]{1,2,0:T(8,128)(2,1)S(1)}, u32[]{:S(2)}, u32[]{:S(2)}) %all-to-all-start) | async-done | bytes 786464 | tf_op jit(solution)/shard_map/all_to_all | solution.py:109
  52.1 7.5 %all-to-all-start.1 = ((bf16[32,128,96]{1,2,0:T(8,128)(2,1)}), bf16[32,128,96]{1,2,0:T(8,128)(2,1)S(1)}, u32[]{:S(2)}, u32[]{:S(2)}) async-start(bf16[32,128,96]{1,2,0:T(8,128)(2,1)} %copy.81), calls=%async_computation.1 | async-start | bytes 1572864 | tf_op jit(solution)/shard_map/all_to_all | solution.py:109
  59.6 2.0 %convolution_convert_fusion.11 = bf16[512,512]{0,1:T(8,128)(2,1)S(1)} fusion(bf16[512,768]{1,0:T(8,128)(2,1)} %convolution_convert_fusion), kind=kOutput, calls=%fused_computation.17 | convolution fusion | flops 402915328 | bytes 1310720 | tf_op jit(solution)/shard_map/bq,bm->qm/dot_general | solution.py:149
  65.7 8.1 %all-to-all-done.1 = bf16[32,128,96]{1,2,0:T(8,128)(2,1)S(1)} async-done(((bf16[32,128,96]{1,2,0:T(8,128)(2,1)}), bf16[32,128,96]{1,2,0:T(8,128)(2,1)S(1)}, u32[]{:S(2)}, u32[]{:S(2)}) %all-to-all-start.1) | async-done | bytes 786464 | tf_op jit(solution)/shard_map/all_to_all | solution.py:109
  77.7 4.5 %all-to-all-start.2 = ((bf16[32,128,96]{1,2,0:T(8,128)(2,1)}), bf16[32,128,96]{1,2,0:T(8,128)(2,1)}, u32[]{:S(2)}, u32[]{:S(2)}) async-start(bf16[32,128,96]{1,2,0:T(8,128)(2,1)} %copy.83), calls=%async_computation.2 | async-start | bytes 1572864 | tf_op jit(solution)/shard_map/all_to_all | solution.py:109
  82.3 11.0 %collective-permute-done.9 = bf16[512,608]{0,1:T(8,128)(2,1)} collective-permute-done((bf16[512,608]{0,1:T(8,128)(2,1)}, bf16[512,608]{0,1:T(8,128)(2,1)}, u32[]{:S(2)}, u32[]{:S(2)}) %collective-permute-start.9) | collective-permute-done | bytes 622624 | tf_op jit(solution)/shard_map/ppermute | solution.py:57
  93.6 3.3 %select_select_fusion = (bf16[512,608]{0,1:T(8,128)(2,1)}, bf16[512,608]{0,1:T(8,128)(2,1)}, bf16[512,608]{0,1:T(8,128)(2,1)}) fusion(bf16[512,608]{0,1:T(8,128)(2,1)} %collective-permute-done.9, bf16[512,608]{0,1:T(8,128)(2,1)} %collective-permute-done.10, bf16[512,608]{0,1:T(8,128)(2,1)} %collective-permute-done.11, pred[]{:T(512)S(6)} %eq.515, ...), kind=kLoop, calls=%fused_computation.52 | loop fusion | flops 4046848 | bytes 4358153 | tf_op jit(solution)/shard_map/jit(_where)/select_n | solution.py:167
  96.9 2.4 %select_select_fusion.12 = (bf16[4,128,96]{1,0,2:T(4,128)(2,1)}, bf16[4,128,96]{1,0,2:T(4,128)(2,1)}, bf16[4,128,96]{1,0,2:T(4,128)(2,1)}, bf16[4,128,96]{1,0,2:T(4,128)(2,1)}, bf16[4,128,96]{1,0,2:T(4,128)(2,1)S(1)}) fusion(bf16[4,128,96]{1,0,2:T(4,128)(2,1)S(1)} %copy-done.6, bf16[4,128,96]{1,0,2:T(4,128)(2,1)S(1)} %copy-done.4, pred[]{:T(512)S(6)} %eq.223, ...), kind=kOutput, calls=%fused_computation.113 | convolution fusion | flops 3784832 | bytes 1474588 | tf_op jit(solution)/shard_map/kj,jrn->krn/dot_general | solution.py:111
  101.3 8.4 %all-to-all-start.3 = ((bf16[32,128,96]{1,2,0:T(8,128)(2,1)}), bf16[32,128,96]{1,2,0:T(8,128)(2,1)S(1)}, u32[]{:S(2)}, u32[]{:S(2)}) async-start(bf16[32,128,96]{1,2,0:T(8,128)(2,1)} %copy.92), calls=%async_computation.3 | async-start | bytes 1572864 | tf_op jit(solution)/shard_map/all_to_all | solution.py:109
  110.9 13.0 %all-to-all-done.3 = bf16[32,128,96]{1,2,0:T(8,128)(2,1)S(1)} async-done(((bf16[32,128,96]{1,2,0:T(8,128)(2,1)}), bf16[32,128,96]{1,2,0:T(8,128)(2,1)S(1)}, u32[]{:S(2)}, u32[]{:S(2)}) %all-to-all-start.3) | async-done | bytes 786464 | tf_op jit(solution)/shard_map/all_to_all | solution.py:109
  127.2 4.0 %all-to-all-start.4 = ((bf16[32,128,96]{1,2,0:T(8,128)(2,1)}), bf16[32,128,96]{1,2,0:T(8,128)(2,1)S(1)}, u32[]{:S(2)}, u32[]{:S(2)}) async-start(bf16[32,128,96]{1,2,0:T(8,128)(2,1)} %copy.94), calls=%async_computation.4 | async-start | bytes 1572864 | tf_op jit(solution)/shard_map/all_to_all | solution.py:109
  131.4 14.0 %all-to-all-done.4 = bf16[32,128,96]{1,2,0:T(8,128)(2,1)S(1)} async-done(((bf16[32,128,96]{1,2,0:T(8,128)(2,1)}), bf16[32,128,96]{1,2,0:T(8,128)(2,1)S(1)}, u32[]{:S(2)}, u32[]{:S(2)}) %all-to-all-start.4) | async-done | bytes 786464 | tf_op jit(solution)/shard_map/all_to_all | solution.py:109
  147.8 4.0 %all-to-all-start.5 = ((bf16[32,128,96]{1,2,0:T(8,128)(2,1)}), bf16[32,128,96]{1,2,0:T(8,128)(2,1)S(1)}, u32[]{:S(2)}, u32[]{:S(2)}) async-start(bf16[32,128,96]{1,2,0:T(8,128)(2,1)} %copy.96), calls=%async_computation.5 | async-start | bytes 1572864 | tf_op jit(solution)/shard_map/all_to_all | solution.py:109
  151.8 2.1 %collective-permute-start.8 = (bf16[4,128,96]{1,0,2:T(4,128)(2,1)S(1)}, bf16[4,128,96]{1,0,2:T(4,128)(2,1)S(1)}, u32[]{:S(2)}, u32[]{:S(2)}) collective-permute-start(bf16[4,128,96]{1,0,2:T(4,128)(2,1)S(1)} %copy-done.39), channel_id=1, source_target_pairs={{0,3},{1,0},{2,1},{3,2},{4,7},{5,4},{6,5},{7,6},{8,11},{9,8},{10,9... | collective-permute-start | bytes 294920 | tf_op jit(solution)/shard_map/ppermute | solution.py:57
  154.7 11.3 %all-to-all-done.5 = bf16[32,128,96]{1,2,0:T(8,128)(2,1)S(1)} async-done(((bf16[32,128,96]{1,2,0:T(8,128)(2,1)}), bf16[32,128,96]{1,2,0:T(8,128)(2,1)S(1)}, u32[]{:S(2)}, u32[]{:S(2)}) %all-to-all-start.5) | async-done | bytes 786464 | tf_op jit(solution)/shard_map/all_to_all | solution.py:109
  167.1 2.1 %collective-permute-start.14 = (bf16[4,128,96]{1,0,2:T(4,128)(2,1)}, bf16[4,128,96]{1,0,2:T(4,128)(2,1)S(1)}, u32[]{:S(2)}, u32[]{:S(2)}) collective-permute-start(bf16[4,128,96]{1,0,2:T(4,128)(2,1)} %get-tuple-element.48), channel_id=1, source_target_pairs={{0,3},{1,0},{2,1},{3,2},{4,7},{5,4},{6,5},{7,6},{8,11},{9,8},{10,9... | collective-permute-start | bytes 294920 | tf_op jit(solution)/shard_map/ppermute | solution.py:57
  170.6 3.2 %collective-permute-done.14 = bf16[4,128,96]{1,0,2:T(4,128)(2,1)S(1)} collective-permute-done((bf16[4,128,96]{1,0,2:T(4,128)(2,1)}, bf16[4,128,96]{1,0,2:T(4,128)(2,1)S(1)}, u32[]{:S(2)}, u32[]{:S(2)}) %collective-permute-start.14) | collective-permute-done | bytes 98336 | tf_op jit(solution)/shard_map/ppermute | solution.py:57
  175.2 2.0 %collective-permute-done.12 = bf16[4,128,96]{1,0,2:T(4,128)(2,1)S(1)} collective-permute-done((bf16[4,128,96]{1,0,2:T(4,128)(2,1)}, bf16[4,128,96]{1,0,2:T(4,128)(2,1)S(1)}, u32[]{:S(2)}, u32[]{:S(2)}) %collective-permute-start.12) | collective-permute-done | bytes 98336 | tf_op jit(solution)/shard_map/ppermute | solution.py:57
  177.6 3.4 %fusion.7 = bf16[768,384]{1,0:T(8,128)(2,1)} fusion(bf16[768,384]{1,0:T(8,128)(2,1)} %copy-done.42, bf16[4,128,384]{1,2,0:T(8,128)(2,1)S(1)} %get-tuple-element.62, bf16[1,1,768,768]{3,2,1,0:T(8,128)(2,1)S(1)} %copy-done, bf16[4,768,128]{1,2,0:T(8,128)(2,1)S(1)} %copy-done.13, bf16[1,1,768,384]{3,2,1,0:T(8,128)(2,1)} %param.7, pred[]{:T(512)S(6)} %eq.210), kind=kOutput, calls=%fused_computation.22 | convolution fusion | flops 756449280 | bytes 4128769 | tf_op jit(solution)/shard_map/ab,bn->an/dot_general | solution.py:149
  180.9 3.3 %convolution_convert_fusion.8 = bf16[384,768]{1,0:T(8,128)(2,1)} fusion(bf16[4,128,384]{1,2,0:T(8,128)(2,1)S(1)} %get-tuple-element.61, bf16[1,1,768,768]{3,2,1,0:T(8,128)(2,1)S(1)} %copy-done, bf16[768,384]{1,0:T(8,128)(2,1)} %fusion.7, bf16[1,1,4,768,128]{4,3,2,1,0:T(8,128)(2,1)S(1)} %copy-done.11), kind=kOutput, calls=%fused_computation.14 | convolution fusion | flops 756154368 | bytes 3538944 | tf_op jit(solution)/shard_map/ba,bn->an/dot_general | solution.py:149
  184.3 1.7 fusion.5
  (191 shorter events, 48.8 us)
Async XLA Ops:
  12.2 37.3 %copy-start.2 = (bf16[512,96]{0,1:T(8,128)(2,1)}, bf16[512,96]{0,1:T(8,128)(2,1)S(1)}, u32[]{:S(2)}) copy-start(bf16[512,96]{0,1:T(8,128)(2,1)S(1)} %get-tuple-element.70) | copy-start | bytes 294916
  12.2 8.4 %collective-permute-start = (bf16[512,96]{0,1:T(8,128)(2,1)S(1)}, bf16[512,96]{0,1:T(8,128)(2,1)S(1)}, u32[]{:S(2)}, u32[]{:S(2)}) collective-permute-start(bf16[512,96]{0,1:T(8,128)(2,1)S(1)} %get-tuple-element.67), channel_id=1, source_target_pairs={{0,3},{1,0},{2,1},{3,2},{4,7},{5,4},{6,5},{7,6},{8,11},{9,8},{10,9... | collective-permute-start | bytes 294920 | tf_op jit(solution)/shard_map/ppermute | solution.py:57
  15.5 6.1 %collective-permute-start.1 = (bf16[512,96]{0,1:T(8,128)(2,1)S(1)}, bf16[512,96]{0,1:T(8,128)(2,1)S(1)}, u32[]{:S(2)}, u32[]{:S(2)}) collective-permute-start(bf16[512,96]{0,1:T(8,128)(2,1)S(1)} %get-tuple-element.68), channel_id=1, source_target_pairs={{0,2},{1,3},{2,0},{3,1},{4,6},{5,7},{6,4},{7,5},{8,10},{9,11},{10,... | collective-permute-start | bytes 294920 | tf_op jit(solution)/shard_map/ppermute | solution.py:57
  16.0 7.1 %collective-permute-start.2 = (bf16[512,96]{0,1:T(8,128)(2,1)S(1)}, bf16[512,96]{0,1:T(8,128)(2,1)S(1)}, u32[]{:S(2)}, u32[]{:S(2)}) collective-permute-start(bf16[512,96]{0,1:T(8,128)(2,1)S(1)} %get-tuple-element.69), channel_id=1, source_target_pairs={{0,1},{1,2},{2,3},{3,0},{4,5},{5,6},{6,7},{7,4},{8,9},{9,10},{10,1... | collective-permute-start | bytes 294920 | tf_op jit(solution)/shard_map/ppermute | solution.py:57
  17.3 17.9 %collective-permute-start.3 = (bf16[512,512]{0,1:T(8,128)(2,1)S(1)}, bf16[512,512]{0,1:T(8,128)(2,1)S(1)}, u32[]{:S(2)}, u32[]{:S(2)}) collective-permute-start(bf16[512,512]{0,1:T(8,128)(2,1)S(1)} %fusion.8), channel_id=1, source_target_pairs={{0,1},{1,2},{2,3},{3,0},{4,5},{5,6},{6,7},{7,4},{8,9},{9,10},{10,1... | collective-permute-start | bytes 1572872 | tf_op jit(solution)/shard_map/ppermute | solution.py:57
  18.9 26.2 %collective-permute-start.4 = (bf16[512,512]{0,1:T(8,128)(2,1)S(1)}, bf16[512,512]{0,1:T(8,128)(2,1)}, u32[]{:S(2)}, u32[]{:S(2)}) collective-permute-start(bf16[512,512]{0,1:T(8,128)(2,1)S(1)} %fusion.8), channel_id=1, source_target_pairs={{0,2},{1,3},{2,0},{3,1},{4,6},{5,7},{6,4},{7,5},{8,10},{9,11},{10,... | collective-permute-start | bytes 1572872 | tf_op jit(solution)/shard_map/ppermute | solution.py:57
  20.6 28.9 %copy-start.7 = (bf16[512,96]{0,1:T(8,128)(2,1)}, bf16[512,96]{0,1:T(8,128)(2,1)S(1)}, u32[]{:S(2)}) copy-start(bf16[512,96]{0,1:T(8,128)(2,1)S(1)} %collective-permute-done) | copy-start | bytes 294916
  20.6 24.4 %collective-permute-start.5 = (bf16[512,512]{0,1:T(8,128)(2,1)S(1)}, bf16[512,512]{0,1:T(8,128)(2,1)}, u32[]{:S(2)}, u32[]{:S(2)}) collective-permute-start(bf16[512,512]{0,1:T(8,128)(2,1)S(1)} %fusion.8), channel_id=1, source_target_pairs={{0,3},{1,0},{2,1},{3,2},{4,7},{5,4},{6,5},{7,6},{8,11},{9,8},{10,9... | collective-permute-start | bytes 1572872 | tf_op jit(solution)/shard_map/ppermute | solution.py:57
  21.6 27.9 %copy-start.8 = (bf16[512,96]{0,1:T(8,128)(2,1)}, bf16[512,96]{0,1:T(8,128)(2,1)S(1)}, u32[]{:S(2)}) copy-start(bf16[512,96]{0,1:T(8,128)(2,1)S(1)} %collective-permute-done.1) | copy-start | bytes 294916
  24.9 24.2 %all-to-all-start = ((bf16[32,128,96]{1,2,0:T(8,128)(2,1)}), bf16[32,128,96]{1,2,0:T(8,128)(2,1)S(1)}, u32[]{:S(2)}, u32[]{:S(2)}) async-start(bf16[32,128,96]{1,2,0:T(8,128)(2,1)} %copy.79), calls=%async_computation | async-start | bytes 1572864 | tf_op jit(solution)/shard_map/all_to_all | solution.py:109
  52.1 21.7 %all-to-all-start.1 = ((bf16[32,128,96]{1,2,0:T(8,128)(2,1)}), bf16[32,128,96]{1,2,0:T(8,128)(2,1)S(1)}, u32[]{:S(2)}, u32[]{:S(2)}) async-start(bf16[32,128,96]{1,2,0:T(8,128)(2,1)} %copy.81), calls=%async_computation.1 | async-start | bytes 1572864 | tf_op jit(solution)/shard_map/all_to_all | solution.py:109
  63.0 30.3 %collective-permute-start.9 = (bf16[512,608]{0,1:T(8,128)(2,1)}, bf16[512,608]{0,1:T(8,128)(2,1)}, u32[]{:S(2)}, u32[]{:S(2)}) collective-permute-start(bf16[512,608]{0,1:T(8,128)(2,1)} %get-tuple-element.5), channel_id=1, source_target_pairs={{0,1},{1,2},{2,3},{3,0},{4,5},{5,6},{6,7},{7,4},{8,9},{9,10},{10,1... | collective-permute-start | bytes 1867784 | tf_op jit(solution)/shard_map/ppermute | solution.py:57
  63.0 30.3 %collective-permute-start.10 = (bf16[512,608]{0,1:T(8,128)(2,1)}, bf16[512,608]{0,1:T(8,128)(2,1)}, u32[]{:S(2)}, u32[]{:S(2)}) collective-permute-start(bf16[512,608]{0,1:T(8,128)(2,1)} %get-tuple-element.6), channel_id=1, source_target_pairs={{0,2},{1,3},{2,0},{3,1},{4,6},{5,7},{6,4},{7,5},{8,10},{9,11},{10,... | collective-permute-start | bytes 1867784 | tf_op jit(solution)/shard_map/ppermute | solution.py:57
  64.5 29.1 %collective-permute-start.11 = (bf16[512,608]{0,1:T(8,128)(2,1)}, bf16[512,608]{0,1:T(8,128)(2,1)}, u32[]{:S(2)}, u32[]{:S(2)}) collective-permute-start(bf16[512,608]{0,1:T(8,128)(2,1)} %get-tuple-element.7), channel_id=1, source_target_pairs={{0,3},{1,0},{2,1},{3,2},{4,7},{5,4},{6,5},{7,6},{8,11},{9,8},{10,9... | collective-permute-start | bytes 1867784 | tf_op jit(solution)/shard_map/ppermute | solution.py:57
  77.7 19.2 %all-to-all-start.2 = ((bf16[32,128,96]{1,2,0:T(8,128)(2,1)}), bf16[32,128,96]{1,2,0:T(8,128)(2,1)}, u32[]{:S(2)}, u32[]{:S(2)}) async-start(bf16[32,128,96]{1,2,0:T(8,128)(2,1)} %copy.83), calls=%async_computation.2 | async-start | bytes 1572864 | tf_op jit(solution)/shard_map/all_to_all | solution.py:109
  101.3 22.6 %all-to-all-start.3 = ((bf16[32,128,96]{1,2,0:T(8,128)(2,1)}), bf16[32,128,96]{1,2,0:T(8,128)(2,1)S(1)}, u32[]{:S(2)}, u32[]{:S(2)}) async-start(bf16[32,128,96]{1,2,0:T(8,128)(2,1)} %copy.92), calls=%async_computation.3 | async-start | bytes 1572864 | tf_op jit(solution)/shard_map/all_to_all | solution.py:109
  127.2 18.2 %all-to-all-start.4 = ((bf16[32,128,96]{1,2,0:T(8,128)(2,1)}), bf16[32,128,96]{1,2,0:T(8,128)(2,1)S(1)}, u32[]{:S(2)}, u32[]{:S(2)}) async-start(bf16[32,128,96]{1,2,0:T(8,128)(2,1)} %copy.94), calls=%async_computation.4 | async-start | bytes 1572864 | tf_op jit(solution)/shard_map/all_to_all | solution.py:109
  147.8 18.2 %all-to-all-start.5 = ((bf16[32,128,96]{1,2,0:T(8,128)(2,1)}), bf16[32,128,96]{1,2,0:T(8,128)(2,1)S(1)}, u32[]{:S(2)}, u32[]{:S(2)}) async-start(bf16[32,128,96]{1,2,0:T(8,128)(2,1)} %copy.96), calls=%async_computation.5 | async-start | bytes 1572864 | tf_op jit(solution)/shard_map/all_to_all | solution.py:109
  151.8 17.4 %collective-permute-start.8 = (bf16[4,128,96]{1,0,2:T(4,128)(2,1)S(1)}, bf16[4,128,96]{1,0,2:T(4,128)(2,1)S(1)}, u32[]{:S(2)}, u32[]{:S(2)}) collective-permute-start(bf16[4,128,96]{1,0,2:T(4,128)(2,1)S(1)} %copy-done.39), channel_id=1, source_target_pairs={{0,3},{1,0},{2,1},{3,2},{4,7},{5,4},{6,5},{7,6},{8,11},{9,8},{10,9... | collective-permute-start | bytes 294920 | tf_op jit(solution)/shard_map/ppermute | solution.py:57
  153.9 16.6 %collective-permute-start.7 = (bf16[4,128,96]{1,0,2:T(4,128)(2,1)S(1)}, bf16[4,128,96]{1,0,2:T(4,128)(2,1)S(1)}, u32[]{:S(2)}, u32[]{:S(2)}) collective-permute-start(bf16[4,128,96]{1,0,2:T(4,128)(2,1)S(1)} %copy-done.38), channel_id=1, source_target_pairs={{0,2},{1,3},{2,0},{3,1},{4,6},{5,7},{6,4},{7,5},{8,10},{9,11},{10,... | collective-permute-start | bytes 294920 | tf_op jit(solution)/shard_map/ppermute | solution.py:57
  154.0 16.6 %collective-permute-start.6 = (bf16[4,128,96]{1,0,2:T(4,128)(2,1)S(1)}, bf16[4,128,96]{1,0,2:T(4,128)(2,1)S(1)}, u32[]{:S(2)}, u32[]{:S(2)}) collective-permute-start(bf16[4,128,96]{1,0,2:T(4,128)(2,1)S(1)} %copy-done.37), channel_id=1, source_target_pairs={{0,1},{1,2},{2,3},{3,0},{4,5},{5,6},{6,7},{7,4},{8,9},{9,10},{10,1... | collective-permute-start | bytes 294920 | tf_op jit(solution)/shard_map/ppermute | solution.py:57
  167.1 6.6 %collective-permute-start.14 = (bf16[4,128,96]{1,0,2:T(4,128)(2,1)}, bf16[4,128,96]{1,0,2:T(4,128)(2,1)S(1)}, u32[]{:S(2)}, u32[]{:S(2)}) collective-permute-start(bf16[4,128,96]{1,0,2:T(4,128)(2,1)} %get-tuple-element.48), channel_id=1, source_target_pairs={{0,3},{1,0},{2,1},{3,2},{4,7},{5,4},{6,5},{7,6},{8,11},{9,8},{10,9... | collective-permute-start | bytes 294920 | tf_op jit(solution)/shard_map/ppermute | solution.py:57
  169.2 6.0 %collective-permute-start.13 = (bf16[4,128,96]{1,0,2:T(4,128)(2,1)}, bf16[4,128,96]{1,0,2:T(4,128)(2,1)S(1)}, u32[]{:S(2)}, u32[]{:S(2)}) collective-permute-start(bf16[4,128,96]{1,0,2:T(4,128)(2,1)} %get-tuple-element.49), channel_id=1, source_target_pairs={{0,2},{1,3},{2,0},{3,1},{4,6},{5,7},{6,4},{7,5},{8,10},{9,11},{10,... | collective-permute-start | bytes 294920 | tf_op jit(solution)/shard_map/ppermute | solution.py:57
  169.2 8.0 %collective-permute-start.12 = (bf16[4,128,96]{1,0,2:T(4,128)(2,1)}, bf16[4,128,96]{1,0,2:T(4,128)(2,1)S(1)}, u32[]{:S(2)}, u32[]{:S(2)}) collective-permute-start(bf16[4,128,96]{1,0,2:T(4,128)(2,1)} %get-tuple-element.50), channel_id=1, source_target_pairs={{0,1},{1,2},{2,3},{3,0},{4,5},{5,6},{6,7},{7,4},{8,9},{9,10},{10,1... | collective-permute-start | bytes 294920 | tf_op jit(solution)/shard_map/ppermute | solution.py:57
  (40 other events, 275.3 us)

commit v13 on v12

--- a/solution.py
+++ b/solution.py
@@ -154,6 +154,8 @@
     free = dot(right_flat, inv_rhs, "bq,bn->qn").astype(jnp.bfloat16)
     gram = dot(inv_left, inv_left, "bq,bm->qm").astype(jnp.bfloat16)
     turn = dot(inv_left, inv_rhs, "bq,bn->qn").astype(jnp.bfloat16)
+    couple = jnp.where(my_row == last, gram, couple)
+    free = jnp.where(my_row == last, turn, free)
     couples = [couple] + [shift(couple, d, row_count) for d in range(1, row_count)]
     free_blocks = free.reshape(flat, row_count, width)
     frees = [pick_block(free_blocks, my_row, row_count)]
@@ -203,7 +205,7 @@
             part, _ = lax.optimization_barrier((part, couple_at[1]))
             part = shift(part, d, row_count)
         grams.append(part)
-    gram_at = [None] + [from_row(grams, t) for t in range(1, level_count)]
+    gram_at = [None] + [from_row(grams, t) for t in range(1, last)]
 
     def back_free(t):
         return gram_at[t][:, flat:].astype(jnp.float32) - dot(
@@ -221,7 +223,10 @@
     top = dot(inverse_here, solved, "ba,bn->an").astype(jnp.bfloat16)
 
     back = [zero_block] * level_count
-    back[last - 1] = route(back_free(last).astype(jnp.bfloat16).reshape(lane_shape), mine_src[last], mine_target[last], block_count)
+    turned = frees_at(frees, my_row, last, row_count).astype(jnp.float32) - dot(
+        couple_at[last], chain[last].reshape(flat, width), "qm,mn->qn"
+    )
+    back[last - 1] = route(turned.astype(jnp.bfloat16).reshape(lane_shape), mine_src[last], mine_target[last], block_count)
     for t in reversed(range(1, last)):
         step = back_free(t) - dot(
             couple_at[t], back[t - 0].reshape(flat, width), "mq,mn->qn"

time: 188 us -> 190 us (1.011)
  matrix products: 28.1 us -> 30.7 us
    ppermute x15, waiting for transfers between devices: 29.6 us -> 25.8 us  [shift(): lax.ppermute(array, 'lvl', [(i, (i + by) % row_count) for i in range(row_...]
    all_to_all x6, waiting for transfers between devices: 48.8 us -> 52.3 us  [route(): lax.all_to_all(holder, 'blk', split_axis=0, concat_axis=0, tiled=True)]
    dot_general x16, matrix products: 20.2 us -> 22.7 us  [dot(): return jnp.einsum(spec, a, b, preferred_element_type=jnp.float32)]
    all_to_all x6, starting transfers between devices: 38.3 us -> 36.4 us  [route(): lax.all_to_all(holder, 'blk', split_axis=0, concat_axis=0, tiled=True)]
    unnamed x89 -> x97, local copies, waits for them, and re-layouts: 5.18 us -> 6.04 us
  transfers between devices with their start and end apart: 21 -> 21, of which waited for: 13 -> 12; matrix products, arithmetic and copies ran while one was open for 9% -> 9% of each run, Pallas kernels for 0% -> 0%
where the time goes in v13:
time: 190 us; the launch traced here: 189 us
  waiting for transfers between devices  78 us (41%)
  starting transfers between devices  54.5 us (29%)
  matrix products  30.7 us (16%)
  local copies, waits for them, and re-layouts  14.2 us (7%)
  other arithmetic  9.97 us (5%)
    all_to_all x6, waiting for transfers between devices, route(): lax.all_to_all(holder, 'blk', split_axis=0, concat_axis=0, tiled=True)  52.3 us
    all_to_all x6, starting transfers between devices, route(): lax.all_to_all(holder, 'blk', split_axis=0, concat_axis=0, tiled=True)  36.4 us
    ppermute x15, waiting for transfers between devices, shift(): lax.ppermute(array, 'lvl', [(i, (i + by) % row_count) for i in range(row_...  25.8 us
    dot_general x16, matrix products, dot(): return jnp.einsum(spec, a, b, preferred_element_type=jnp.float32)  22.7 us
    ppermute x15, starting transfers between devices, shift(): lax.ppermute(array, 'lvl', [(i, (i + by) % row_count) for i in range(row_...  18.2 us
    convert_element_type x6, local copies, waits for them, and re-layouts, route(): holder = holder.astype(piece.dtype)  7.23 us
    unnamed x97, local copies, waits for them, and re-layouts  6.04 us
    dot_general x6, matrix products, route(): jnp.einsum('kj,jrn->krn', take, arrived, preferred_element_type=jnp.float32)  4.96 us
  transfers between devices with their start and end apart: 21, of which 12 were waited for; matrix products, arithmetic and copies ran while one was open for 9% of the time, Pallas kernels for 0%

profile of v13, /device:TPU:1, one launch (start us, length us, event | category | flops | bytes accessed | tf_op | source)
XLA Modules:
  0.0 188.9 jit_solution(6454091960396225104)
XLA Ops:
  9.3 1.8 convolution_convert_fusion.14
  14.2 3.3 %collective-permute-start = (bf16[512,96]{0,1:T(8,128)(2,1)}, bf16[512,96]{0,1:T(8,128)(2,1)S(1)}, u32[]{:S(2)}, u32[]{:S(2)}) collective-permute-start(bf16[512,96]{0,1:T(8,128)(2,1)} %get-tuple-element.66), channel_id=1, source_target_pairs={{0,3},{1,0},{2,1},{3,2},{4,7},{5,4},{6,5},{7,6},{8,11},{9,8},{10,9... | collective-permute-start | bytes 294920 | tf_op jit(solution)/shard_map/ppermute | solution.py:57
  27.0 9.9 %all-to-all-start = ((bf16[32,128,96]{1,2,0:T(8,128)(2,1)}), bf16[32,128,96]{1,2,0:T(8,128)(2,1)S(1)}, u32[]{:S(2)}, u32[]{:S(2)}) async-start(bf16[32,128,96]{1,2,0:T(8,128)(2,1)} %copy.79), calls=%async_computation | async-start | bytes 1572864 | tf_op jit(solution)/shard_map/all_to_all | solution.py:109
  37.0 10.1 %collective-permute-done.4 = bf16[512,512]{0,1:T(8,128)(2,1)} collective-permute-done((bf16[512,512]{0,1:T(8,128)(2,1)}, bf16[512,512]{0,1:T(8,128)(2,1)}, u32[]{:S(2)}, u32[]{:S(2)}) %collective-permute-start.4) | collective-permute-done | bytes 524320 | tf_op jit(solution)/shard_map/ppermute | solution.py:57
  48.7 2.5 %all-to-all-done = bf16[32,128,96]{1,2,0:T(8,128)(2,1)S(1)} async-done(((bf16[32,128,96]{1,2,0:T(8,128)(2,1)}), bf16[32,128,96]{1,2,0:T(8,128)(2,1)S(1)}, u32[]{:S(2)}, u32[]{:S(2)}) %all-to-all-start) | async-done | bytes 786464 | tf_op jit(solution)/shard_map/all_to_all | solution.py:109
  55.1 7.5 %all-to-all-start.1 = ((bf16[32,128,96]{1,2,0:T(8,128)(2,1)}), bf16[32,128,96]{1,2,0:T(8,128)(2,1)S(1)}, u32[]{:S(2)}, u32[]{:S(2)}) async-start(bf16[32,128,96]{1,2,0:T(8,128)(2,1)} %copy.81), calls=%async_computation.1 | async-start | bytes 1572864 | tf_op jit(solution)/shard_map/all_to_all | solution.py:109
  62.6 14.2 %all-to-all-done.1 = bf16[32,128,96]{1,2,0:T(8,128)(2,1)S(1)} async-done(((bf16[32,128,96]{1,2,0:T(8,128)(2,1)}), bf16[32,128,96]{1,2,0:T(8,128)(2,1)S(1)}, u32[]{:S(2)}, u32[]{:S(2)}) %all-to-all-start.1) | async-done | bytes 786464 | tf_op jit(solution)/shard_map/all_to_all | solution.py:109
  80.7 4.7 %all-to-all-start.2 = ((bf16[32,128,96]{1,2,0:T(8,128)(2,1)}), bf16[32,128,96]{1,2,0:T(8,128)(2,1)}, u32[]{:S(2)}, u32[]{:S(2)}) async-start(bf16[32,128,96]{1,2,0:T(8,128)(2,1)} %copy.83), calls=%async_computation.2 | async-start | bytes 1572864 | tf_op jit(solution)/shard_map/all_to_all | solution.py:109
  87.5 2.3 %collective-permute-start.10 = (bf16[512,608]{0,1:T(8,128)(2,1)}, bf16[512,608]{0,1:T(8,128)(2,1)}, u32[]{:S(2)}, u32[]{:S(2)}) collective-permute-start(bf16[512,608]{0,1:T(8,128)(2,1)} %get-tuple-element.6), channel_id=1, source_target_pairs={{0,2},{1,3},{2,0},{3,1},{4,6},{5,7},{6,4},{7,5},{8,10},{9,11},{10,... | collective-permute-start | bytes 1867784 | tf_op jit(solution)/shard_map/ppermute | solution.py:57
  90.2 9.1 %all-to-all-done.2 = bf16[32,128,96]{1,2,0:T(8,128)(2,1)} async-done(((bf16[32,128,96]{1,2,0:T(8,128)(2,1)}), bf16[32,128,96]{1,2,0:T(8,128)(2,1)}, u32[]{:S(2)}, u32[]{:S(2)}) %all-to-all-start.2) | async-done | bytes 786464 | tf_op jit(solution)/shard_map/all_to_all | solution.py:109
  99.4 2.5 %select_select_fusion.11 = (bf16[4,128,96]{1,0,2:T(4,128)(2,1)}, bf16[4,128,96]{1,0,2:T(4,128)(2,1)}, bf16[4,128,96]{1,0,2:T(4,128)(2,1)}, bf16[4,128,96]{1,0,2:T(4,128)(2,1)}, bf16[4,128,96]{1,0,2:T(4,128)(2,1)S(1)}) fusion(bf16[4,128,96]{1,0,2:T(4,128)(2,1)S(1)} %copy-done.9, bf16[4,128,96]{1,0,2:T(4,128)(2,1)S(1)} %copy-done.6, pred[]{:T(512)S(6)} %eq.223, ...), kind=kOutput, calls=%fused_computation.120 | convolution fusion | flops 3784832 | bytes 1474588 | tf_op jit(solution)/shard_map/kj,jrn->krn/dot_general | solution.py:111
  104.9 3.8 %all-to-all-start.3 = ((bf16[32,128,96]{1,2,0:T(8,128)(2,1)}), bf16[32,128,96]{1,2,0:T(8,128)(2,1)S(1)}, u32[]{:S(2)}, u32[]{:S(2)}) async-start(bf16[32,128,96]{1,2,0:T(8,128)(2,1)} %copy.92), calls=%async_computation.3 | async-start | bytes 1572864 | tf_op jit(solution)/shard_map/all_to_all | solution.py:109
  108.7 8.9 %collective-permute-done.10 = bf16[512,608]{0,1:T(8,128)(2,1)} collective-permute-done((bf16[512,608]{0,1:T(8,128)(2,1)}, bf16[512,608]{0,1:T(8,128)(2,1)}, u32[]{:S(2)}, u32[]{:S(2)}) %collective-permute-start.10) | collective-permute-done | bytes 622624 | tf_op jit(solution)/shard_map/ppermute | solution.py:57
  117.7 2.8 %select_select_fusion = (bf16[512,608]{0,1:T(8,128)(2,1)}, bf16[512,608]{0,1:T(8,128)(2,1)S(1)}) fusion(bf16[512,608]{0,1:T(8,128)(2,1)} %collective-permute-done.9, bf16[512,608]{0,1:T(8,128)(2,1)} %collective-permute-done.10, bf16[512,608]{0,1:T(8,128)(2,1)} %collective-permute-done.11, pred[]{:T(512)S(6)} %eq.520, pred[]{:T(512)S(6)} %eq.521, ...), kind=kLoop, calls=%fused_computation.55 | loop fusion | flops 3112960 | bytes 3735558 | tf_op jit(solution)/shard_map/jit(_where)/select_n | solution.py:169
  126.2 6.5 %all-to-all-start.4 = ((bf16[32,128,96]{1,2,0:T(8,128)(2,1)}), bf16[32,128,96]{1,2,0:T(8,128)(2,1)S(1)}, u32[]{:S(2)}, u32[]{:S(2)}) async-start(bf16[32,128,96]{1,2,0:T(8,128)(2,1)} %copy.94), calls=%async_computation.4 | async-start | bytes 1572864 | tf_op jit(solution)/shard_map/all_to_all | solution.py:109
  133.0 14.0 %all-to-all-done.4 = bf16[32,128,96]{1,2,0:T(8,128)(2,1)S(1)} async-done(((bf16[32,128,96]{1,2,0:T(8,128)(2,1)}), bf16[32,128,96]{1,2,0:T(8,128)(2,1)S(1)}, u32[]{:S(2)}, u32[]{:S(2)}) %all-to-all-start.4) | async-done | bytes 786464 | tf_op jit(solution)/shard_map/all_to_all | solution.py:109
  149.4 4.0 %all-to-all-start.5 = ((bf16[32,128,96]{1,2,0:T(8,128)(2,1)}), bf16[32,128,96]{1,2,0:T(8,128)(2,1)S(1)}, u32[]{:S(2)}, u32[]{:S(2)}) async-start(bf16[32,128,96]{1,2,0:T(8,128)(2,1)} %copy.96), calls=%async_computation.5 | async-start | bytes 1572864 | tf_op jit(solution)/shard_map/all_to_all | solution.py:109
  153.4 2.4 %collective-permute-start.8 = (bf16[4,128,96]{1,0,2:T(4,128)(2,1)S(1)}, bf16[4,128,96]{1,0,2:T(4,128)(2,1)S(1)}, u32[]{:S(2)}, u32[]{:S(2)}) collective-permute-start(bf16[4,128,96]{1,0,2:T(4,128)(2,1)S(1)} %copy-done.44), channel_id=1, source_target_pairs={{0,3},{1,0},{2,1},{3,2},{4,7},{5,4},{6,5},{7,6},{8,11},{9,8},{10,9... | collective-permute-start | bytes 294920 | tf_op jit(solution)/shard_map/ppermute | solution.py:57
  156.6 11.0 %all-to-all-done.5 = bf16[32,128,96]{1,2,0:T(8,128)(2,1)S(1)} async-done(((bf16[32,128,96]{1,2,0:T(8,128)(2,1)}), bf16[32,128,96]{1,2,0:T(8,128)(2,1)S(1)}, u32[]{:S(2)}, u32[]{:S(2)}) %all-to-all-start.5) | async-done | bytes 786464 | tf_op jit(solution)/shard_map/all_to_all | solution.py:109
  168.7 2.3 %collective-permute-start.14 = (bf16[4,128,96]{1,0,2:T(4,128)(2,1)}, bf16[4,128,96]{1,0,2:T(4,128)(2,1)S(1)}, u32[]{:S(2)}, u32[]{:S(2)}) collective-permute-start(bf16[4,128,96]{1,0,2:T(4,128)(2,1)} %get-tuple-element.47), channel_id=1, source_target_pairs={{0,3},{1,0},{2,1},{3,2},{4,7},{5,4},{6,5},{7,6},{8,11},{9,8},{10,9... | collective-permute-start | bytes 294920 | tf_op jit(solution)/shard_map/ppermute | solution.py:57
  172.5 3.2 %collective-permute-done.14 = bf16[4,128,96]{1,0,2:T(4,128)(2,1)S(1)} collective-permute-done((bf16[4,128,96]{1,0,2:T(4,128)(2,1)}, bf16[4,128,96]{1,0,2:T(4,128)(2,1)S(1)}, u32[]{:S(2)}, u32[]{:S(2)}) %collective-permute-start.14) | collective-permute-done | bytes 98336 | tf_op jit(solution)/shard_map/ppermute | solution.py:57
  177.1 1.9 %collective-permute-done.12 = bf16[4,128,96]{1,0,2:T(4,128)(2,1)S(1)} collective-permute-done((bf16[4,128,96]{1,0,2:T(4,128)(2,1)}, bf16[4,128,96]{1,0,2:T(4,128)(2,1)S(1)}, u32[]{:S(2)}, u32[]{:S(2)}) %collective-permute-start.12) | collective-permute-done | bytes 98336 | tf_op jit(solution)/shard_map/ppermute | solution.py:57
  179.4 3.4 %fusion.7 = bf16[768,384]{1,0:T(8,128)(2,1)} fusion(bf16[768,384]{1,0:T(8,128)(2,1)} %convolution_convert_fusion.10, bf16[4,128,384]{1,2,0:T(8,128)(2,1)S(1)} %get-tuple-element.61, bf16[1,1,768,768]{3,2,1,0:T(8,128)(2,1)S(1)} %copy-done, bf16[4,768,128]{1,2,0:T(8,128)(2,1)S(1)} %copy-done.20, bf16[1,1,768,384]{3,2,1,0:T(8,128)(2,1)} %param.7, pred[]{:T(512)S(6)} %eq.210), kind=kOutput, calls=%fused_computation.22 | convolution fusion | flops 756449280 | bytes 4128769 | tf_op jit(solution)/shard_map/ab,bn->an/dot_general | solution.py:149
  182.8 3.3 %convolution_convert_fusion.8 = bf16[384,768]{1,0:T(8,128)(2,1)} fusion(bf16[4,128,384]{1,2,0:T(8,128)(2,1)S(1)} %get-tuple-element.60, bf16[1,1,768,768]{3,2,1,0:T(8,128)(2,1)S(1)} %copy-done, bf16[768,384]{1,0:T(8,128)(2,1)} %fusion.7, bf16[1,1,4,768,128]{4,3,2,1,0:T(8,128)(2,1)S(1)} %copy-done.18), kind=kOutput, calls=%fused_computation.14 | convolution fusion | flops 756154368 | bytes 3538944 | tf_op jit(solution)/shard_map/ba,bn->an/dot_general | solution.py:149
  (199 shorter events, 52.0 us)
Async XLA Ops:
  4.6 20.7 %copy-start.29 = (s32[4]{0:T(128)}, s32[4]{0:T(128)S(1)}, u32[]{:S(2)}) copy-start(s32[4]{0:T(128)S(1)} %get-tuple-element.37) | copy-start | bytes 52
  14.2 9.7 %collective-permute-start = (bf16[512,96]{0,1:T(8,128)(2,1)}, bf16[512,96]{0,1:T(8,128)(2,1)S(1)}, u32[]{:S(2)}, u32[]{:S(2)}) collective-permute-start(bf16[512,96]{0,1:T(8,128)(2,1)} %get-tuple-element.66), channel_id=1, source_target_pairs={{0,3},{1,0},{2,1},{3,2},{4,7},{5,4},{6,5},{7,6},{8,11},{9,8},{10,9... | collective-permute-start | bytes 294920 | tf_op jit(solution)/shard_map/ppermute | solution.py:57
  17.5 7.5 %collective-permute-start.1 = (bf16[512,96]{0,1:T(8,128)(2,1)S(1)}, bf16[512,96]{0,1:T(8,128)(2,1)S(1)}, u32[]{:S(2)}, u32[]{:S(2)}) collective-permute-start(bf16[512,96]{0,1:T(8,128)(2,1)S(1)} %get-tuple-element.67), channel_id=1, source_target_pairs={{0,2},{1,3},{2,0},{3,1},{4,6},{5,7},{6,4},{7,5},{8,10},{9,11},{10,... | collective-permute-start | bytes 294920 | tf_op jit(solution)/shard_map/ppermute | solution.py:57
  18.0 7.2 %collective-permute-start.2 = (bf16[512,96]{0,1:T(8,128)(2,1)S(1)}, bf16[512,96]{0,1:T(8,128)(2,1)S(1)}, u32[]{:S(2)}, u32[]{:S(2)}) collective-permute-start(bf16[512,96]{0,1:T(8,128)(2,1)S(1)} %get-tuple-element.68), channel_id=1, source_target_pairs={{0,1},{1,2},{2,3},{3,0},{4,5},{5,6},{6,7},{7,4},{8,9},{9,10},{10,1... | collective-permute-start | bytes 294920 | tf_op jit(solution)/shard_map/ppermute | solution.py:57
  20.7 16.3 %collective-permute-start.3 = (bf16[512,512]{0,1:T(8,128)(2,1)}, bf16[512,512]{0,1:T(8,128)(2,1)S(1)}, u32[]{:S(2)}, u32[]{:S(2)}) collective-permute-start(bf16[512,512]{0,1:T(8,128)(2,1)} %fusion.9), channel_id=1, source_target_pairs={{0,1},{1,2},{2,3},{3,0},{4,5},{5,6},{6,7},{7,4},{8,9},{9,10},{10,1... | collective-permute-start | bytes 1572872 | tf_op jit(solution)/shard_map/ppermute | solution.py:57
  22.2 24.9 %collective-permute-start.4 = (bf16[512,512]{0,1:T(8,128)(2,1)}, bf16[512,512]{0,1:T(8,128)(2,1)}, u32[]{:S(2)}, u32[]{:S(2)}) collective-permute-start(bf16[512,512]{0,1:T(8,128)(2,1)} %fusion.9), channel_id=1, source_target_pairs={{0,2},{1,3},{2,0},{3,1},{4,6},{5,7},{6,4},{7,5},{8,10},{9,11},{10,... | collective-permute-start | bytes 1572872 | tf_op jit(solution)/shard_map/ppermute | solution.py:57
  23.9 23.2 %collective-permute-start.5 = (bf16[512,512]{0,1:T(8,128)(2,1)}, bf16[512,512]{0,1:T(8,128)(2,1)}, u32[]{:S(2)}, u32[]{:S(2)}) collective-permute-start(bf16[512,512]{0,1:T(8,128)(2,1)} %fusion.9), channel_id=1, source_target_pairs={{0,3},{1,0},{2,1},{3,2},{4,7},{5,4},{6,5},{7,6},{8,11},{9,8},{10,9... | collective-permute-start | bytes 1572872 | tf_op jit(solution)/shard_map/ppermute | solution.py:57
  27.0 24.1 %all-to-all-start = ((bf16[32,128,96]{1,2,0:T(8,128)(2,1)}), bf16[32,128,96]{1,2,0:T(8,128)(2,1)S(1)}, u32[]{:S(2)}, u32[]{:S(2)}) async-start(bf16[32,128,96]{1,2,0:T(8,128)(2,1)} %copy.79), calls=%async_computation | async-start | bytes 1572864 | tf_op jit(solution)/shard_map/all_to_all | solution.py:109
  55.1 21.7 %all-to-all-start.1 = ((bf16[32,128,96]{1,2,0:T(8,128)(2,1)}), bf16[32,128,96]{1,2,0:T(8,128)(2,1)S(1)}, u32[]{:S(2)}, u32[]{:S(2)}) async-start(bf16[32,128,96]{1,2,0:T(8,128)(2,1)} %copy.81), calls=%async_computation.1 | async-start | bytes 1572864 | tf_op jit(solution)/shard_map/all_to_all | solution.py:109
  80.7 18.6 %all-to-all-start.2 = ((bf16[32,128,96]{1,2,0:T(8,128)(2,1)}), bf16[32,128,96]{1,2,0:T(8,128)(2,1)}, u32[]{:S(2)}, u32[]{:S(2)}) async-start(bf16[32,128,96]{1,2,0:T(8,128)(2,1)} %copy.83), calls=%async_computation.2 | async-start | bytes 1572864 | tf_op jit(solution)/shard_map/all_to_all | solution.py:109
  86.9 21.8 %collective-permute-start.9 = (bf16[512,608]{0,1:T(8,128)(2,1)}, bf16[512,608]{0,1:T(8,128)(2,1)}, u32[]{:S(2)}, u32[]{:S(2)}) collective-permute-start(bf16[512,608]{0,1:T(8,128)(2,1)} %get-tuple-element.5), channel_id=1, source_target_pairs={{0,1},{1,2},{2,3},{3,0},{4,5},{5,6},{6,7},{7,4},{8,9},{9,10},{10,1... | collective-permute-start | bytes 1867784 | tf_op jit(solution)/shard_map/ppermute | solution.py:57
  87.5 30.1 %collective-permute-start.10 = (bf16[512,608]{0,1:T(8,128)(2,1)}, bf16[512,608]{0,1:T(8,128)(2,1)}, u32[]{:S(2)}, u32[]{:S(2)}) collective-permute-start(bf16[512,608]{0,1:T(8,128)(2,1)} %get-tuple-element.6), channel_id=1, source_target_pairs={{0,2},{1,3},{2,0},{3,1},{4,6},{5,7},{6,4},{7,5},{8,10},{9,11},{10,... | collective-permute-start | bytes 1867784 | tf_op jit(solution)/shard_map/ppermute | solution.py:57
  89.9 27.8 %collective-permute-start.11 = (bf16[512,608]{0,1:T(8,128)(2,1)}, bf16[512,608]{0,1:T(8,128)(2,1)}, u32[]{:S(2)}, u32[]{:S(2)}) collective-permute-start(bf16[512,608]{0,1:T(8,128)(2,1)} %get-tuple-element.7), channel_id=1, source_target_pairs={{0,3},{1,0},{2,1},{3,2},{4,7},{5,4},{6,5},{7,6},{8,11},{9,8},{10,9... | collective-permute-start | bytes 1867784 | tf_op jit(solution)/shard_map/ppermute | solution.py:57
  104.9 18.0 %all-to-all-start.3 = ((bf16[32,128,96]{1,2,0:T(8,128)(2,1)}), bf16[32,128,96]{1,2,0:T(8,128)(2,1)S(1)}, u32[]{:S(2)}, u32[]{:S(2)}) async-start(bf16[32,128,96]{1,2,0:T(8,128)(2,1)} %copy.92), calls=%async_computation.3 | async-start | bytes 1572864 | tf_op jit(solution)/shard_map/all_to_all | solution.py:109
  126.2 20.7 %all-to-all-start.4 = ((bf16[32,128,96]{1,2,0:T(8,128)(2,1)}), bf16[32,128,96]{1,2,0:T(8,128)(2,1)S(1)}, u32[]{:S(2)}, u32[]{:S(2)}) async-start(bf16[32,128,96]{1,2,0:T(8,128)(2,1)} %copy.94), calls=%async_computation.4 | async-start | bytes 1572864 | tf_op jit(solution)/shard_map/all_to_all | solution.py:109
  149.4 18.2 %copy-start.30 = (s32[4]{0:T(128)S(1)}, s32[4]{0:T(128)}, u32[]{:S(2)}) copy-start(s32[4]{0:T(128)} %copy-done.29) | copy-start | bytes 52
  149.4 18.2 %all-to-all-start.5 = ((bf16[32,128,96]{1,2,0:T(8,128)(2,1)}), bf16[32,128,96]{1,2,0:T(8,128)(2,1)S(1)}, u32[]{:S(2)}, u32[]{:S(2)}) async-start(bf16[32,128,96]{1,2,0:T(8,128)(2,1)} %copy.96), calls=%async_computation.5 | async-start | bytes 1572864 | tf_op jit(solution)/shard_map/all_to_all | solution.py:109
  153.4 17.7 %collective-permute-start.8 = (bf16[4,128,96]{1,0,2:T(4,128)(2,1)S(1)}, bf16[4,128,96]{1,0,2:T(4,128)(2,1)S(1)}, u32[]{:S(2)}, u32[]{:S(2)}) collective-permute-start(bf16[4,128,96]{1,0,2:T(4,128)(2,1)S(1)} %copy-done.44), channel_id=1, source_target_pairs={{0,3},{1,0},{2,1},{3,2},{4,7},{5,4},{6,5},{7,6},{8,11},{9,8},{10,9... | collective-permute-start | bytes 294920 | tf_op jit(solution)/shard_map/ppermute | solution.py:57
  155.8 16.6 %collective-permute-start.7 = (bf16[4,128,96]{1,0,2:T(4,128)(2,1)S(1)}, bf16[4,128,96]{1,0,2:T(4,128)(2,1)S(1)}, u32[]{:S(2)}, u32[]{:S(2)}) collective-permute-start(bf16[4,128,96]{1,0,2:T(4,128)(2,1)S(1)} %copy-done.43), channel_id=1, source_target_pairs={{0,2},{1,3},{2,0},{3,1},{4,6},{5,7},{6,4},{7,5},{8,10},{9,11},{10,... | collective-permute-start | bytes 294920 | tf_op jit(solution)/shard_map/ppermute | solution.py:57
  155.8 16.5 %copy-start.26 = (bf16[4,128,96]{1,0,2:T(4,128)(2,1)S(1)}, bf16[4,128,96]{1,0,2:T(4,128)(2,1)}, u32[]{:S(2)}) copy-start(bf16[4,128,96]{1,0,2:T(4,128)(2,1)} %get-tuple-element.50) | copy-start | bytes 294916
  155.8 16.6 %collective-permute-start.6 = (bf16[4,128,96]{1,0,2:T(4,128)(2,1)S(1)}, bf16[4,128,96]{1,0,2:T(4,128)(2,1)S(1)}, u32[]{:S(2)}, u32[]{:S(2)}) collective-permute-start(bf16[4,128,96]{1,0,2:T(4,128)(2,1)S(1)} %copy-done.42), channel_id=1, source_target_pairs={{0,1},{1,2},{2,3},{3,0},{4,5},{5,6},{6,7},{7,4},{8,9},{9,10},{10,1... | collective-permute-start | bytes 294920 | tf_op jit(solution)/shard_map/ppermute | solution.py:57
  168.7 6.9 %collective-permute-start.14 = (bf16[4,128,96]{1,0,2:T(4,128)(2,1)}, bf16[4,128,96]{1,0,2:T(4,128)(2,1)S(1)}, u32[]{:S(2)}, u32[]{:S(2)}) collective-permute-start(bf16[4,128,96]{1,0,2:T(4,128)(2,1)} %get-tuple-element.47), channel_id=1, source_target_pairs={{0,3},{1,0},{2,1},{3,2},{4,7},{5,4},{6,5},{7,6},{8,11},{9,8},{10,9... | collective-permute-start | bytes 294920 | tf_op jit(solution)/shard_map/ppermute | solution.py:57
  171.1 6.0 %collective-permute-start.13 = (bf16[4,128,96]{1,0,2:T(4,128)(2,1)}, bf16[4,128,96]{1,0,2:T(4,128)(2,1)S(1)}, u32[]{:S(2)}, u32[]{:S(2)}) collective-permute-start(bf16[4,128,96]{1,0,2:T(4,128)(2,1)} %get-tuple-element.48), channel_id=1, source_target_pairs={{0,2},{1,3},{2,0},{3,1},{4,6},{5,7},{6,4},{7,5},{8,10},{9,11},{10,... | collective-permute-start | bytes 294920 | tf_op jit(solution)/shard_map/ppermute | solution.py:57
  171.1 8.0 %collective-permute-start.12 = (bf16[4,128,96]{1,0,2:T(4,128)(2,1)}, bf16[4,128,96]{1,0,2:T(4,128)(2,1)S(1)}, u32[]{:S(2)}, u32[]{:S(2)}) collective-permute-start(bf16[4,128,96]{1,0,2:T(4,128)(2,1)} %get-tuple-element.49), channel_id=1, source_target_pairs={{0,1},{1,2},{2,3},{3,0},{4,5},{5,6},{6,7},{7,4},{8,9},{9,10},{10,1... | collective-permute-start | bytes 294920 | tf_op jit(solution)/shard_map/ppermute | solution.py:57
  (44 other events, 249.1 us)

commit v14 on v9

--- a/solution.py
+++ b/solution.py
@@ -203,10 +203,14 @@
         )
         chain[t + 1] = route(step.astype(jnp.bfloat16).reshape(lane_shape), mine_target[t + 1], mine_src[t + 1], block_count)
 
-    mine_fwd = solve_forward(own_level_blocks(chain))
+    lower_chain = [zero_block] + chain[1:last] + [zero_block]
+    early_fwd = solve_forward(own_level_blocks(lower_chain))
+    inv_t_early = dot(inverse_here, early_fwd, "ba,bn->an").astype(jnp.bfloat16)
+    back_term = dot(left_flat, inv_t_early, "bm,bn->mn").astype(jnp.bfloat16)
+    top_fwd = solve_forward(collect(chain[last], last, row_count))
+    mine_fwd = jnp.where(my_row == last, top_fwd, early_fwd)
     solved = jnp.where(my_row == 0, first, mine_fwd)
     top = dot(inverse_here, solved, "ba,bn->an").astype(jnp.bfloat16)
-    back_term = dot(left_flat, top, "bm,bn->mn").astype(jnp.bfloat16)
     back_parts = [take_block(back_term, my_row, row_count)]
     for d in range(1, row_count):
         back_parts.append(shift(take_block(back_term, lax.rem(my_row + d, row_count), row_count), d, row_count))

time: 187 us -> 184 us (0.984)
  blocking collectives: 40 us -> 22.2 us
  starting transfers between devices: 46.9 us -> 53.3 us
  matrix products: 26.9 us -> 31.5 us
  waiting for transfers between devices: 43.4 us -> 46.3 us
    all_to_all x2 -> x1, blocking collectives: 40 us -> 22.2 us  [route(): lax.all_to_all(holder, 'blk', split_axis=0, concat_axis=0, tiled=True)]
    all_to_all x4 -> x5, waiting for transfers between devices: 24.6 us -> 34.1 us  [route(): lax.all_to_all(holder, 'blk', split_axis=0, concat_axis=0, tiled=True)]
    ppermute x15, waiting for transfers between devices: 18.8 us -> 11.6 us  [shift(): lax.ppermute(array, 'lvl', [(i, (i + by) % row_count) for i in range(row_...]
    all_to_all x4 -> x5, starting transfers between devices: 26.4 us -> 31.9 us  [route(): lax.all_to_all(holder, 'blk', split_axis=0, concat_axis=0, tiled=True)]
    ppermute x0 -> x3, starting transfers between devices: none -> 3.36 us  [collect(): parts.append(lax.ppermute(routed, 'lvl', [(r, dst_row)]))]
    dot_general x15 -> x16, matrix products: 19.2 us -> 22.5 us  [dot(): return jnp.einsum(spec, a, b, preferred_element_type=jnp.float32)]
    ppermute x15, starting transfers between devices: 20.5 us -> 18 us  [shift(): lax.ppermute(array, 'lvl', [(i, (i + by) % row_count) for i in range(row_...]
    dot_general x6, matrix products: 4.04 us -> 6 us  [route(): jnp.einsum('kj,jrn->krn', take, arrived, preferred_element_type=jnp.float32)]
  transfers between devices with their start and end apart: 19 -> 23, of which waited for: 10 -> 10; matrix products, arithmetic and copies ran while one was open for 13% -> 14% of each run, Pallas kernels for 0% -> 0%
where the time goes in v14:
time: 184 us; the launch traced here: 183 us
  starting transfers between devices  53.3 us (29%)
  waiting for transfers between devices  46.3 us (25%)
  matrix products  31.5 us (17%)
  blocking collectives  22.2 us (12%)
  local copies, waits for them, and re-layouts  20.8 us (11%)
  other arithmetic  7.59 us (4%)
    all_to_all x5, waiting for transfers between devices, route(): lax.all_to_all(holder, 'blk', split_axis=0, concat_axis=0, tiled=True)  34.1 us
    all_to_all x5, starting transfers between devices, route(): lax.all_to_all(holder, 'blk', split_axis=0, concat_axis=0, tiled=True)  31.9 us
    dot_general x16, matrix products, dot(): return jnp.einsum(spec, a, b, preferred_element_type=jnp.float32)  22.5 us
    all_to_all x1, blocking collectives, route(): lax.all_to_all(holder, 'blk', split_axis=0, concat_axis=0, tiled=True)  22.2 us
    ppermute x15, starting transfers between devices, shift(): lax.ppermute(array, 'lvl', [(i, (i + by) % row_count) for i in range(row_...  18 us
    ppermute x15, waiting for transfers between devices, shift(): lax.ppermute(array, 'lvl', [(i, (i + by) % row_count) for i in range(row_...  11.6 us
    convert_element_type x6, local copies, waits for them, and re-layouts, route(): holder = holder.astype(piece.dtype)  6.34 us
    dot_general x6, matrix products, route(): jnp.einsum('kj,jrn->krn', take, arrived, preferred_element_type=jnp.float32)  6 us
  transfers between devices with their start and end apart: 23, of which 10 were waited for; matrix products, arithmetic and copies ran while one was open for 14% of the time, Pallas kernels for 0%

profile of v14, /device:TPU:1, one launch (start us, length us, event | category | flops | bytes accessed | tf_op | source)
XLA Modules:
  0.0 183.1 jit_solution(13687579970630438931)
XLA Ops:
  13.5 3.4 %collective-permute-start = (bf16[512,96]{0,1:T(8,128)(2,1)S(1)}, bf16[512,96]{0,1:T(8,128)(2,1)S(1)}, u32[]{:S(2)}, u32[]{:S(2)}) collective-permute-start(bf16[512,96]{0,1:T(8,128)(2,1)S(1)} %get-tuple-element.9), channel_id=1, source_target_pairs={{0,3},{1,0},{2,1},{3,2},{4,7},{5,4},{6,5},{7,6},{8,11},{9,8},{10,9... | collective-permute-start | bytes 294920 | tf_op jit(solution)/shard_map/ppermute | solution.py:57
  18.6 2.0 %fusion.11 = bf16[512,512]{1,0:T(8,128)(2,1)S(1)} fusion(bf16[512,512]{1,0:T(8,128)(2,1)S(1)} %fusion.12, bf16[512,768]{1,0:T(8,128)(2,1)} %copy-done.43, pred[]{:T(512)S(6)} %eq.203), kind=kOutput, calls=%fused_computation.33 | convolution fusion | flops 403177472 | bytes 1835009 | tf_op jit(solution)/shard_map/bq,bm->qm/dot_general | solution.py:149
  22.2 1.7 collective-permute-start.4
  26.5 10.2 %all-to-all-start = ((bf16[32,128,96]{1,2,0:T(8,128)(2,1)}), bf16[32,128,96]{1,2,0:T(8,128)(2,1)S(1)}, u32[]{:S(2)}, u32[]{:S(2)}) async-start(bf16[32,128,96]{1,2,0:T(8,128)(2,1)} %copy.91), calls=%async_computation | async-start | bytes 1572864 | tf_op jit(solution)/shard_map/all_to_all | solution.py:109
  36.8 9.1 %collective-permute-done.4 = bf16[512,512]{1,0:T(8,128)(2,1)S(1)} collective-permute-done((bf16[512,512]{1,0:T(8,128)(2,1)S(1)}, bf16[512,512]{1,0:T(8,128)(2,1)S(1)}, u32[]{:S(2)}, u32[]{:S(2)}) %collective-permute-start.4) | collective-permute-done | bytes 524320 | tf_op jit(solution)/shard_map/ppermute | solution.py:57
  48.1 2.8 %all-to-all-done = bf16[32,128,96]{1,2,0:T(8,128)(2,1)S(1)} async-done(((bf16[32,128,96]{1,2,0:T(8,128)(2,1)}), bf16[32,128,96]{1,2,0:T(8,128)(2,1)S(1)}, u32[]{:S(2)}, u32[]{:S(2)}) %all-to-all-start) | async-done | bytes 786464 | tf_op jit(solution)/shard_map/all_to_all | solution.py:109
  54.9 7.7 %all-to-all-start.1 = ((bf16[32,128,96]{1,2,0:T(8,128)(2,1)}), bf16[32,128,96]{1,2,0:T(8,128)(2,1)S(1)}, u32[]{:S(2)}, u32[]{:S(2)}) async-start(bf16[32,128,96]{1,2,0:T(8,128)(2,1)} %copy.93), calls=%async_computation.1 | async-start | bytes 1572864 | tf_op jit(solution)/shard_map/all_to_all | solution.py:109
  62.7 14.2 %all-to-all-done.1 = bf16[32,128,96]{1,2,0:T(8,128)(2,1)S(1)} async-done(((bf16[32,128,96]{1,2,0:T(8,128)(2,1)}), bf16[32,128,96]{1,2,0:T(8,128)(2,1)S(1)}, u32[]{:S(2)}, u32[]{:S(2)}) %all-to-all-start.1) | async-done | bytes 786464 | tf_op jit(solution)/shard_map/all_to_all | solution.py:109
  76.9 2.2 %select_select_fusion.9 = (bf16[4,128,96]{1,0,2:T(4,128)(2,1)}, bf16[4,128,96]{1,0,2:T(4,128)(2,1)}, bf16[4,128,96]{1,0,2:T(4,128)(2,1)}, bf16[4,128,96]{1,0,2:T(4,128)(2,1)}, bf16[4,128,96]{1,0,2:T(4,128)(2,1)S(1)}) fusion(bf16[4,128,96]{1,0,2:T(4,128)(2,1)} %copy-done.14, pred[]{:T(512)S(6)} %eq.215, pred[]{:T(512)S(6)} %eq.210, pred[]{:T(512)S(6)} %eq.203, ...), kind=kOutput, calls=%fused_computation.123 | convolution fusion | flops 3784832 | bytes 1376284 | tf_op jit(solution)/shard_map/kj,jrn->krn/dot_general | solution.py:111
  81.2 4.0 %all-to-all-start.2 = ((bf16[32,128,96]{1,2,0:T(8,128)(2,1)}), bf16[32,128,96]{1,2,0:T(8,128)(2,1)S(1)}, u32[]{:S(2)}, u32[]{:S(2)}) async-start(bf16[32,128,96]{1,2,0:T(8,128)(2,1)} %copy.95), calls=%async_computation.2 | async-start | bytes 1572864 | tf_op jit(solution)/shard_map/all_to_all | solution.py:109
  85.9 2.3 %collective-permute-start.10 = (bf16[4,128,96]{1,0,2:T(4,128)(2,1)}, bf16[4,128,96]{1,0,2:T(4,128)(2,1)}, u32[]{:S(2)}, u32[]{:S(2)}) collective-permute-start(bf16[4,128,96]{1,0,2:T(4,128)(2,1)} %get-tuple-element.33), channel_id=1, source_target_pairs={{0,2},{1,3},{2,0},{3,1},{4,6},{5,7},{6,4},{7,5},{8,10},{9,11},{10,... | collective-permute-start | bytes 294920 | tf_op jit(solution)/shard_map/ppermute | solution.py:57
  97.0 2.3 %all-to-all-done.2 = bf16[32,128,96]{1,2,0:T(8,128)(2,1)S(1)} async-done(((bf16[32,128,96]{1,2,0:T(8,128)(2,1)}), bf16[32,128,96]{1,2,0:T(8,128)(2,1)S(1)}, u32[]{:S(2)}, u32[]{:S(2)}) %all-to-all-start.2) | async-done | bytes 786464 | tf_op jit(solution)/shard_map/all_to_all | solution.py:109
  104.3 6.0 %all-to-all-start.3 = ((bf16[32,128,96]{1,2,0:T(8,128)(2,1)}), bf16[32,128,96]{1,2,0:T(8,128)(2,1)S(1)}, u32[]{:S(2)}, u32[]{:S(2)}) async-start(bf16[32,128,96]{1,2,0:T(8,128)(2,1)} %copy.108), calls=%async_computation.3 | async-start | bytes 1572864 | tf_op jit(solution)/shard_map/all_to_all | solution.py:109
  110.4 3.3 %convolution_convert_fusion.7 = bf16[384,768]{0,1:T(8,128)(2,1)} fusion(bf16[4,128,384]{1,2,0:T(8,128)(2,1)S(1)} %copy-done.11, bf16[1,1,768,768]{3,2,1,0:T(8,128)(2,1)S(1)} %copy-done, bf16[4,768,128]{1,2,0:T(8,128)(2,1)} %copy-done.3, bf16[1,1,768,384]{3,2,1,0:T(8,128)(2,1)} %param.7), kind=kOutput, calls=%fused_computation.16 | convolution fusion | flops 756154368 | bytes 3538944 | tf_op jit(solution)/shard_map/ab,bn->an/dot_general | solution.py:149
  113.7 2.3 %fusion.7 = bf16[512,384]{0,1:T(8,128)(2,1)S(1)} fusion(bf16[768,512]{0,1:T(8,128)(2,1)} %bitcast.255, bf16[384,768]{0,1:T(8,128)(2,1)} %convolution_convert_fusion.7, bf16[1,1,768,768]{3,2,1,0:T(8,128)(2,1)S(1)} %copy-done), kind=kOutput, calls=%fused_computation.27 | convolution fusion | flops 755466240 | bytes 2949120 | tf_op jit(solution)/shard_map/bm,bn->mn/dot_general | solution.py:149
  117.8 1.9 %collective-permute-start.13 = (bf16[512,96]{0,1:T(8,128)(2,1)}, bf16[512,96]{0,1:T(8,128)(2,1)S(1)}, u32[]{:S(2)}, u32[]{:S(2)}) collective-permute-start(bf16[512,96]{0,1:T(8,128)(2,1)} %get-tuple-element.4), channel_id=1, source_target_pairs={{0,2},{1,3},{2,0},{3,1},{4,6},{5,7},{6,4},{7,5},{8,10},{9,11},{10,... | collective-permute-start | bytes 294920 | tf_op jit(solution)/shard_map/ppermute | solution.py:57
  119.7 4.8 %all-to-all-done.3 = bf16[32,128,96]{1,2,0:T(8,128)(2,1)S(1)} async-done(((bf16[32,128,96]{1,2,0:T(8,128)(2,1)}), bf16[32,128,96]{1,2,0:T(8,128)(2,1)S(1)}, u32[]{:S(2)}, u32[]{:S(2)}) %all-to-all-start.3) | async-done | bytes 786464 | tf_op jit(solution)/shard_map/all_to_all | solution.py:109
  127.0 22.2 %all_to_all.30 = bf16[32,128,96]{1,2,0:T(8,128)(2,1)S(1)} all-to-all(bf16[32,128,96]{1,2,0:T(8,128)(2,1)S(1)} %copy.110), channel_id=1, replica_groups=mesh['blk'=32,'lvl'=4] {'blk'}, dimensions={0} | all-to-all | bytes 1572864 | tf_op jit(solution)/shard_map/all_to_all | solution.py:109
  151.5 4.0 %all-to-all-start.5 = ((bf16[32,128,96]{1,2,0:T(8,128)(2,1)}), bf16[32,128,96]{1,2,0:T(8,128)(2,1)S(1)}, u32[]{:S(2)}, u32[]{:S(2)}) async-start(bf16[32,128,96]{1,2,0:T(8,128)(2,1)} %copy.112), calls=%async_computation.5 | async-start | bytes 1572864 | tf_op jit(solution)/shard_map/all_to_all | solution.py:109
  155.5 2.0 %collective-permute-start.6 = (bf16[4,128,96]{1,0,2:T(4,128)(2,1)S(1)}, bf16[4,128,96]{1,0,2:T(4,128)(2,1)S(1)}, u32[]{:S(2)}, u32[]{:S(2)}) collective-permute-start(bf16[4,128,96]{1,0,2:T(4,128)(2,1)S(1)} %copy-done.8), channel_id=1, source_target_pairs={{0,3},{4,7},{8,11},{12,15},{16,19},{20,23},{24,27},{28,31},{32,35}... | collective-permute-start | bytes 294920 | tf_op jit(solution)/shard_map/ppermute | solution.py:52
  159.8 9.9 %all-to-all-done.5 = bf16[32,128,96]{1,2,0:T(8,128)(2,1)S(1)} async-done(((bf16[32,128,96]{1,2,0:T(8,128)(2,1)}), bf16[32,128,96]{1,2,0:T(8,128)(2,1)S(1)}, u32[]{:S(2)}, u32[]{:S(2)}) %all-to-all-start.5) | async-done | bytes 786464 | tf_op jit(solution)/shard_map/all_to_all | solution.py:109
  169.7 1.8 select_select_fusion.5
  172.8 2.0 %collective-permute-start.17 = (bf16[4,128,96]{1,0,2:T(4,128)(2,1)}, bf16[4,128,96]{1,0,2:T(4,128)(2,1)S(1)}, u32[]{:S(2)}, u32[]{:S(2)}) collective-permute-start(bf16[4,128,96]{1,0,2:T(4,128)(2,1)} %get-tuple-element.28), channel_id=1, source_target_pairs={{0,3},{1,0},{2,1},{3,2},{4,7},{5,4},{6,5},{7,6},{8,11},{9,8},{10,9... | collective-permute-start | bytes 294920 | tf_op jit(solution)/shard_map/ppermute | solution.py:57
  174.9 3.5 %fusion.10 = bf16[768,384]{1,0:T(8,128)(2,1)} fusion(bf16[768,384]{1,0:T(8,128)(2,1)} %convolution_convert_fusion.12, bf16[384,768]{0,1:T(8,128)(2,1)} %convolution_convert_fusion.7, bf16[1,1,768,768]{3,2,1,0:T(8,128)(2,1)S(1)} %copy-done, bf16[4,768,128]{1,2,0:T(8,128)(2,1)S(1)} %copy-done.4, bf16[1,1,768,384]{3,2,1,0:T(8,128)(2,1)} %param.7, ...), kind=kOutput, calls=%fused_computation.30 | convolution fusion | flops 756744192 | bytes 4718594 | tf_op jit(solution)/shard_map/ab,bn->an/dot_general | solution.py:149
  (200 shorter events, 56.0 us)
Async XLA Ops:
  13.0 75.8 %copy-start.28 = (bf16[4]{0:T(256)(128)(2,1)}, bf16[4]{0:T(256)(128)(2,1)S(1)}, u32[]{:S(2)}) copy-start(bf16[4]{0:T(256)(128)(2,1)S(1)} %get-tuple-element.48) | copy-start | bytes 28
  13.5 10.4 %collective-permute-start = (bf16[512,96]{0,1:T(8,128)(2,1)S(1)}, bf16[512,96]{0,1:T(8,128)(2,1)S(1)}, u32[]{:S(2)}, u32[]{:S(2)}) collective-permute-start(bf16[512,96]{0,1:T(8,128)(2,1)S(1)} %get-tuple-element.9), channel_id=1, source_target_pairs={{0,3},{1,0},{2,1},{3,2},{4,7},{5,4},{6,5},{7,6},{8,11},{9,8},{10,9... | collective-permute-start | bytes 294920 | tf_op jit(solution)/shard_map/ppermute | solution.py:57
  16.9 7.8 %collective-permute-start.1 = (bf16[512,96]{0,1:T(8,128)(2,1)S(1)}, bf16[512,96]{0,1:T(8,128)(2,1)S(1)}, u32[]{:S(2)}, u32[]{:S(2)}) collective-permute-start(bf16[512,96]{0,1:T(8,128)(2,1)S(1)} %get-tuple-element.8), channel_id=1, source_target_pairs={{0,2},{1,3},{2,0},{3,1},{4,6},{5,7},{6,4},{7,5},{8,10},{9,11},{10,... | collective-permute-start | bytes 294920 | tf_op jit(solution)/shard_map/ppermute | solution.py:57
  17.4 7.3 %collective-permute-start.2 = (bf16[512,96]{0,1:T(8,128)(2,1)S(1)}, bf16[512,96]{0,1:T(8,128)(2,1)S(1)}, u32[]{:S(2)}, u32[]{:S(2)}) collective-permute-start(bf16[512,96]{0,1:T(8,128)(2,1)S(1)} %get-tuple-element.7), channel_id=1, source_target_pairs={{0,1},{1,2},{2,3},{3,0},{4,5},{5,6},{6,7},{7,4},{8,9},{9,10},{10,1... | collective-permute-start | bytes 294920 | tf_op jit(solution)/shard_map/ppermute | solution.py:57
  20.6 16.1 %collective-permute-start.3 = (bf16[512,512]{1,0:T(8,128)(2,1)S(1)}, bf16[512,512]{1,0:T(8,128)(2,1)S(1)}, u32[]{:S(2)}, u32[]{:S(2)}) collective-permute-start(bf16[512,512]{1,0:T(8,128)(2,1)S(1)} %fusion.11), channel_id=1, source_target_pairs={{0,1},{1,2},{2,3},{3,0},{4,5},{5,6},{6,7},{7,4},{8,9},{9,10},{10,1... | collective-permute-start | bytes 1572872 | tf_op jit(solution)/shard_map/ppermute | solution.py:57
  22.2 23.6 %collective-permute-start.4 = (bf16[512,512]{1,0:T(8,128)(2,1)S(1)}, bf16[512,512]{1,0:T(8,128)(2,1)S(1)}, u32[]{:S(2)}, u32[]{:S(2)}) collective-permute-start(bf16[512,512]{1,0:T(8,128)(2,1)S(1)} %fusion.11), channel_id=1, source_target_pairs={{0,2},{1,3},{2,0},{3,1},{4,6},{5,7},{6,4},{7,5},{8,10},{9,11},{10,... | collective-permute-start | bytes 1572872 | tf_op jit(solution)/shard_map/ppermute | solution.py:57
  24.0 22.7 %collective-permute-start.5 = (bf16[512,512]{1,0:T(8,128)(2,1)S(1)}, bf16[512,512]{1,0:T(8,128)(2,1)}, u32[]{:S(2)}, u32[]{:S(2)}) collective-permute-start(bf16[512,512]{1,0:T(8,128)(2,1)S(1)} %fusion.11), channel_id=1, source_target_pairs={{0,3},{1,0},{2,1},{3,2},{4,7},{5,4},{6,5},{7,6},{8,11},{9,8},{10,9... | collective-permute-start | bytes 1572872 | tf_op jit(solution)/shard_map/ppermute | solution.py:57
  26.5 24.4 %all-to-all-start = ((bf16[32,128,96]{1,2,0:T(8,128)(2,1)}), bf16[32,128,96]{1,2,0:T(8,128)(2,1)S(1)}, u32[]{:S(2)}, u32[]{:S(2)}) async-start(bf16[32,128,96]{1,2,0:T(8,128)(2,1)} %copy.91), calls=%async_computation | async-start | bytes 1572864 | tf_op jit(solution)/shard_map/all_to_all | solution.py:109
  54.9 22.0 %all-to-all-start.1 = ((bf16[32,128,96]{1,2,0:T(8,128)(2,1)}), bf16[32,128,96]{1,2,0:T(8,128)(2,1)S(1)}, u32[]{:S(2)}, u32[]{:S(2)}) async-start(bf16[32,128,96]{1,2,0:T(8,128)(2,1)} %copy.93), calls=%async_computation.1 | async-start | bytes 1572864 | tf_op jit(solution)/shard_map/all_to_all | solution.py:109
  81.2 18.2 %all-to-all-start.2 = ((bf16[32,128,96]{1,2,0:T(8,128)(2,1)}), bf16[32,128,96]{1,2,0:T(8,128)(2,1)S(1)}, u32[]{:S(2)}, u32[]{:S(2)}) async-start(bf16[32,128,96]{1,2,0:T(8,128)(2,1)} %copy.95), calls=%async_computation.2 | async-start | bytes 1572864 | tf_op jit(solution)/shard_map/all_to_all | solution.py:109
  85.2 8.1 %collective-permute-start.9 = (bf16[4,128,96]{1,0,2:T(4,128)(2,1)}, bf16[4,128,96]{1,0,2:T(4,128)(2,1)}, u32[]{:S(2)}, u32[]{:S(2)}) collective-permute-start(bf16[4,128,96]{1,0,2:T(4,128)(2,1)} %get-tuple-element.34), channel_id=1, source_target_pairs={{0,1},{1,2},{2,3},{3,0},{4,5},{5,6},{6,7},{7,4},{8,9},{9,10},{10,1... | collective-permute-start | bytes 294920 | tf_op jit(solution)/shard_map/ppermute | solution.py:57
  85.9 8.3 %collective-permute-start.10 = (bf16[4,128,96]{1,0,2:T(4,128)(2,1)}, bf16[4,128,96]{1,0,2:T(4,128)(2,1)}, u32[]{:S(2)}, u32[]{:S(2)}) collective-permute-start(bf16[4,128,96]{1,0,2:T(4,128)(2,1)} %get-tuple-element.33), channel_id=1, source_target_pairs={{0,2},{1,3},{2,0},{3,1},{4,6},{5,7},{6,4},{7,5},{8,10},{9,11},{10,... | collective-permute-start | bytes 294920 | tf_op jit(solution)/shard_map/ppermute | solution.py:57
  88.2 6.9 %collective-permute-start.11 = (bf16[4,128,96]{1,0,2:T(4,128)(2,1)}, bf16[4,128,96]{1,0,2:T(4,128)(2,1)}, u32[]{:S(2)}, u32[]{:S(2)}) collective-permute-start(bf16[4,128,96]{1,0,2:T(4,128)(2,1)} %get-tuple-element.32), channel_id=1, source_target_pairs={{0,3},{1,0},{2,1},{3,2},{4,7},{5,4},{6,5},{7,6},{8,11},{9,8},{10,9... | collective-permute-start | bytes 294920 | tf_op jit(solution)/shard_map/ppermute | solution.py:57
  104.3 20.3 %all-to-all-start.3 = ((bf16[32,128,96]{1,2,0:T(8,128)(2,1)}), bf16[32,128,96]{1,2,0:T(8,128)(2,1)S(1)}, u32[]{:S(2)}, u32[]{:S(2)}) async-start(bf16[32,128,96]{1,2,0:T(8,128)(2,1)} %copy.108), calls=%async_computation.3 | async-start | bytes 1572864 | tf_op jit(solution)/shard_map/all_to_all | solution.py:109
  117.0 7.9 %collective-permute-start.12 = (bf16[512,96]{0,1:T(8,128)(2,1)}, bf16[512,96]{0,1:T(8,128)(2,1)S(1)}, u32[]{:S(2)}, u32[]{:S(2)}) collective-permute-start(bf16[512,96]{0,1:T(8,128)(2,1)} %get-tuple-element.5), channel_id=1, source_target_pairs={{0,3},{1,0},{2,1},{3,2},{4,7},{5,4},{6,5},{7,6},{8,11},{9,8},{10,9... | collective-permute-start | bytes 294920 | tf_op jit(solution)/shard_map/ppermute | solution.py:57
  117.8 7.1 %collective-permute-start.13 = (bf16[512,96]{0,1:T(8,128)(2,1)}, bf16[512,96]{0,1:T(8,128)(2,1)S(1)}, u32[]{:S(2)}, u32[]{:S(2)}) collective-permute-start(bf16[512,96]{0,1:T(8,128)(2,1)} %get-tuple-element.4), channel_id=1, source_target_pairs={{0,2},{1,3},{2,0},{3,1},{4,6},{5,7},{6,4},{7,5},{8,10},{9,11},{10,... | collective-permute-start | bytes 294920 | tf_op jit(solution)/shard_map/ppermute | solution.py:57
  119.7 6.2 %collective-permute-start.14 = (bf16[512,96]{0,1:T(8,128)(2,1)}, bf16[512,96]{0,1:T(8,128)(2,1)S(1)}, u32[]{:S(2)}, u32[]{:S(2)}) collective-permute-start(bf16[512,96]{0,1:T(8,128)(2,1)} %get-tuple-element.3), channel_id=1, source_target_pairs={{0,1},{1,2},{2,3},{3,0},{4,5},{5,6},{6,7},{7,4},{8,9},{9,10},{10,1... | collective-permute-start | bytes 294920 | tf_op jit(solution)/shard_map/ppermute | solution.py:57
  151.5 18.2 %all-to-all-start.5 = ((bf16[32,128,96]{1,2,0:T(8,128)(2,1)}), bf16[32,128,96]{1,2,0:T(8,128)(2,1)S(1)}, u32[]{:S(2)}, u32[]{:S(2)}) async-start(bf16[32,128,96]{1,2,0:T(8,128)(2,1)} %copy.112), calls=%async_computation.5 | async-start | bytes 1572864 | tf_op jit(solution)/shard_map/all_to_all | solution.py:109
  155.5 4.0 %collective-permute-start.6 = (bf16[4,128,96]{1,0,2:T(4,128)(2,1)S(1)}, bf16[4,128,96]{1,0,2:T(4,128)(2,1)S(1)}, u32[]{:S(2)}, u32[]{:S(2)}) collective-permute-start(bf16[4,128,96]{1,0,2:T(4,128)(2,1)S(1)} %copy-done.8), channel_id=1, source_target_pairs={{0,3},{4,7},{8,11},{12,15},{16,19},{20,23},{24,27},{28,31},{32,35}... | collective-permute-start | bytes 294920 | tf_op jit(solution)/shard_map/ppermute | solution.py:52
  157.5 1.9 %collective-permute-start.7 = (bf16[4,128,96]{1,0,2:T(4,128)(2,1)S(1)}, bf16[4,128,96]{1,0,2:T(4,128)(2,1)S(1)}, u32[]{:S(2)}, u32[]{:S(2)}) collective-permute-start(bf16[4,128,96]{1,0,2:T(4,128)(2,1)S(1)} %copy-done.8), channel_id=1, source_target_pairs={{1,3},{5,7},{9,11},{13,15},{17,19},{21,23},{25,27},{29,31},{33,35}... | collective-permute-start | bytes 294920 | tf_op jit(solution)/shard_map/ppermute | solution.py:52
  158.2 1.3 collective-permute-start.8
  171.5 8.0 %collective-permute-start.15 = (bf16[4,128,96]{1,0,2:T(4,128)(2,1)}, bf16[4,128,96]{1,0,2:T(4,128)(2,1)S(1)}, u32[]{:S(2)}, u32[]{:S(2)}) collective-permute-start(bf16[4,128,96]{1,0,2:T(4,128)(2,1)} %get-tuple-element.30), channel_id=1, source_target_pairs={{0,1},{1,2},{2,3},{3,0},{4,5},{5,6},{6,7},{7,4},{8,9},{9,10},{10,1... | collective-permute-start | bytes 294920 | tf_op jit(solution)/shard_map/ppermute | solution.py:57
  171.8 7.8 %collective-permute-start.16 = (bf16[4,128,96]{1,0,2:T(4,128)(2,1)}, bf16[4,128,96]{1,0,2:T(4,128)(2,1)S(1)}, u32[]{:S(2)}, u32[]{:S(2)}) collective-permute-start(bf16[4,128,96]{1,0,2:T(4,128)(2,1)} %get-tuple-element.29), channel_id=1, source_target_pairs={{0,2},{1,3},{2,0},{3,1},{4,6},{5,7},{6,4},{7,5},{8,10},{9,11},{10,... | collective-permute-start | bytes 294920 | tf_op jit(solution)/shard_map/ppermute | solution.py:57
  172.8 7.1 %collective-permute-start.17 = (bf16[4,128,96]{1,0,2:T(4,128)(2,1)}, bf16[4,128,96]{1,0,2:T(4,128)(2,1)S(1)}, u32[]{:S(2)}, u32[]{:S(2)}) collective-permute-start(bf16[4,128,96]{1,0,2:T(4,128)(2,1)} %get-tuple-element.28), channel_id=1, source_target_pairs={{0,3},{1,0},{2,1},{3,2},{4,7},{5,4},{6,5},{7,6},{8,11},{9,8},{10,9... | collective-permute-start | bytes 294920 | tf_op jit(solution)/shard_map/ppermute | solution.py:57
  (44 other events, 380.7 us)

commit v15 on v14

--- a/solution.py
+++ b/solution.py
@@ -157,7 +157,6 @@
     turn = dot(inv_left_f, inv_rhs, "bq,bn->qn").astype(jnp.bfloat16)
     couple = jnp.where(my_row == last, gram, couple)
     free = jnp.where(my_row == last, turn, free)
-    couples = [couple] + [shift(couple, d, row_count) for d in range(1, row_count)]
     free_blocks = free.reshape(flat, row_count, width)
     frees = [pick_block(free_blocks, my_row, row_count)]
     for d in range(1, row_count):
@@ -195,7 +194,16 @@
     first = inv_rhs
     chain = [zero_block] * level_count
     start_block = frees_at(frees, my_row, 0, row_count).reshape(lane_shape)
-    chain[1] = route(start_block, mine_target[1], mine_src[1], block_count)
+    send = one_hot(mine_target[1], block_count, start_block.dtype)
+    holder = jnp.einsum("kj,krn->jrn", send, start_block, preferred_element_type=jnp.float32)
+    holder = holder.astype(start_block.dtype)
+    couples_in, holder = lax.optimization_barrier((couple, holder))
+    arrived = lax.all_to_all(holder, "blk", split_axis=0, concat_axis=0, tiled=True)
+    take = one_hot(mine_src[1], block_count, start_block.dtype)
+    chain[1] = jnp.einsum(
+        "kj,jrn->krn", take, arrived, preferred_element_type=jnp.float32
+    ).astype(start_block.dtype)
+    couples = [couples_in] + [shift(couples_in, d, row_count) for d in range(1, row_count)]
     couple_at = [None] + [from_row(couples, t) for t in range(1, level_count)]
     for t in range(1, last):
         step = frees_at(frees, my_row, t, row_count).astype(jnp.float32) - dot(

time: 184 us -> 189 us (1.027)
  waiting for transfers between devices: 46.3 us -> 51.1 us
    all_to_all x0 -> x1, starting transfers between devices: none -> 9.98 us  [local(): lax.all_to_all(holder, 'blk', split_axis=0, concat_axis=0, tiled=True)]
    all_to_all x5 -> x4, starting transfers between devices: 31.9 us -> 23.7 us  [route(): lax.all_to_all(holder, 'blk', split_axis=0, concat_axis=0, tiled=True)]
    ppermute x15, waiting for transfers between devices: 11.6 us -> 18.7 us  [shift(): lax.ppermute(array, 'lvl', [(i, (i + by) % row_count) for i in range(row_...]
    all_to_all x5 -> x4, waiting for transfers between devices: 34.1 us -> 31.6 us  [route(): lax.all_to_all(holder, 'blk', split_axis=0, concat_axis=0, tiled=True)]
    convert_element_type x6 -> x5, local copies, waits for them, and re-layouts: 6.34 us -> 5.11 us  [route(): holder = holder.astype(piece.dtype)]
    dot_general x6 -> x5, matrix products: 6 us -> 5.67 us  [route(): jnp.einsum('kj,jrn->krn', take, arrived, preferred_element_type=jnp.float32)]
  transfers between devices with their start and end apart: 23 -> 23, of which waited for: 10 -> 12; matrix products, arithmetic and copies ran while one was open for 14% -> 12% of each run, Pallas kernels for 0% -> 0%
where the time goes in v15:
time: 189 us; the launch traced here: 188 us
  starting transfers between devices  53.4 us (28%)
  waiting for transfers between devices  51.1 us (27%)
  matrix products  31.2 us (17%)
  blocking collectives  22.2 us (12%)
  local copies, waits for them, and re-layouts  21.8 us (12%)
  other arithmetic  6.98 us (4%)
    all_to_all x4, waiting for transfers between devices, route(): lax.all_to_all(holder, 'blk', split_axis=0, concat_axis=0, tiled=True)  31.6 us
    all_to_all x4, starting transfers between devices, route(): lax.all_to_all(holder, 'blk', split_axis=0, concat_axis=0, tiled=True)  23.7 us
    all_to_all x1, blocking collectives, route(): lax.all_to_all(holder, 'blk', split_axis=0, concat_axis=0, tiled=True)  22.2 us
    dot_general x16, matrix products, dot(): return jnp.einsum(spec, a, b, preferred_element_type=jnp.float32)  22.1 us
    ppermute x15, waiting for transfers between devices, shift(): lax.ppermute(array, 'lvl', [(i, (i + by) % row_count) for i in range(row_...  18.7 us
    ppermute x15, starting transfers between devices, shift(): lax.ppermute(array, 'lvl', [(i, (i + by) % row_count) for i in range(row_...  16.3 us
    all_to_all x1, starting transfers between devices, local(): lax.all_to_all(holder, 'blk', split_axis=0, concat_axis=0, tiled=True)  9.98 us
    dot_general x5, matrix products, route(): jnp.einsum('kj,jrn->krn', take, arrived, preferred_element_type=jnp.float32)  5.67 us
  transfers between devices with their start and end apart: 23, of which 12 were waited for; matrix products, arithmetic and copies ran while one was open for 12% of the time, Pallas kernels for 0%

profile of v15, /device:TPU:1, one launch (start us, length us, event | category | flops | bytes accessed | tf_op | source)
XLA Modules:
  0.0 188.1 jit_solution(16652055981253787746)
XLA Ops:
  11.8 1.7 fusion.13
  14.1 3.3 %collective-permute-start = (bf16[512,96]{0,1:T(8,128)(2,1)S(1)}, bf16[512,96]{0,1:T(8,128)(2,1)S(1)}, u32[]{:S(2)}, u32[]{:S(2)}) collective-permute-start(bf16[512,96]{0,1:T(8,128)(2,1)S(1)} %get-tuple-element.13), channel_id=1, source_target_pairs={{0,3},{1,0},{2,1},{3,2},{4,7},{5,4},{6,5},{7,6},{8,11},{9,8},{10,9... | collective-permute-start | bytes 294920 | tf_op jit(solution)/shard_map/ppermute | solution.py:57
  19.8 2.7 %collective-permute-done.1 = bf16[512,96]{0,1:T(8,128)(2,1)S(1)} collective-permute-done((bf16[512,96]{0,1:T(8,128)(2,1)S(1)}, bf16[512,96]{0,1:T(8,128)(2,1)S(1)}, u32[]{:S(2)}, u32[]{:S(2)}) %collective-permute-start.1) | collective-permute-done | bytes 98336 | tf_op jit(solution)/shard_map/ppermute | solution.py:57
  22.5 2.6 %collective-permute-done.2 = bf16[512,96]{0,1:T(8,128)(2,1)S(1)} collective-permute-done((bf16[512,96]{0,1:T(8,128)(2,1)S(1)}, bf16[512,96]{0,1:T(8,128)(2,1)S(1)}, u32[]{:S(2)}, u32[]{:S(2)}) %collective-permute-start.2) | collective-permute-done | bytes 98336 | tf_op jit(solution)/shard_map/ppermute | solution.py:57
  26.5 2.0 %collective-permute-start.5 = (bf16[512,512]{1,0:T(8,128)(2,1)S(1)}, bf16[512,512]{1,0:T(8,128)(2,1)}, u32[]{:S(2)}, u32[]{:S(2)}) collective-permute-start(bf16[512,512]{1,0:T(8,128)(2,1)S(1)} %fusion.11), channel_id=1, source_target_pairs={{0,3},{1,0},{2,1},{3,2},{4,7},{5,4},{6,5},{7,6},{8,11},{9,8},{10,9... | collective-permute-start | bytes 1572872 | tf_op jit(solution)/shard_map/ppermute | solution.py:57
  29.7 10.0 %all-to-all-start = ((bf16[32,128,96]{1,2,0:T(8,128)(2,1)}), bf16[32,128,96]{1,2,0:T(8,128)(2,1)S(1)}, u32[]{:S(2)}, u32[]{:S(2)}) async-start(bf16[32,128,96]{1,2,0:T(8,128)(2,1)} %copy.91), calls=%async_computation | async-start | bytes 1572864 | tf_op jit(solution)/shard_map/all_to_all | solution.py:201
  39.7 10.9 %collective-permute-done.3 = bf16[512,512]{1,0:T(8,128)(2,1)S(1)} collective-permute-done((bf16[512,512]{1,0:T(8,128)(2,1)S(1)}, bf16[512,512]{1,0:T(8,128)(2,1)S(1)}, u32[]{:S(2)}, u32[]{:S(2)}) %collective-permute-start.3) | collective-permute-done | bytes 524320 | tf_op jit(solution)/shard_map/ppermute | solution.py:57
  57.9 10.0 %all-to-all-start.1 = ((bf16[32,128,96]{1,2,0:T(8,128)(2,1)}), bf16[32,128,96]{1,2,0:T(8,128)(2,1)S(1)}, u32[]{:S(2)}, u32[]{:S(2)}) async-start(bf16[32,128,96]{1,2,0:T(8,128)(2,1)} %copy.93), calls=%async_computation.1 | async-start | bytes 1572864 | tf_op jit(solution)/shard_map/all_to_all | solution.py:109
  67.9 14.2 %all-to-all-done.1 = bf16[32,128,96]{1,2,0:T(8,128)(2,1)S(1)} async-done(((bf16[32,128,96]{1,2,0:T(8,128)(2,1)}), bf16[32,128,96]{1,2,0:T(8,128)(2,1)S(1)}, u32[]{:S(2)}, u32[]{:S(2)}) %all-to-all-start.1) | async-done | bytes 786464 | tf_op jit(solution)/shard_map/all_to_all | solution.py:109
  82.1 2.2 %select_select_fusion.9 = (bf16[4,128,96]{1,0,2:T(4,128)(2,1)}, bf16[4,128,96]{1,0,2:T(4,128)(2,1)}, bf16[4,128,96]{1,0,2:T(4,128)(2,1)}, bf16[4,128,96]{1,0,2:T(4,128)(2,1)}, bf16[4,128,96]{1,0,2:T(4,128)(2,1)S(1)}) fusion(bf16[4,128,96]{1,0,2:T(4,128)(2,1)} %copy-done.14, pred[]{:T(512)S(6)} %eq.215, pred[]{:T(512)S(6)} %eq.210, pred[]{:T(512)S(6)} %eq.203, ...), kind=kOutput, calls=%fused_computation.123 | convolution fusion | flops 3784832 | bytes 1376284 | tf_op jit(solution)/shard_map/kj,jrn->krn/dot_general | solution.py:111
  86.4 4.0 %all-to-all-start.2 = ((bf16[32,128,96]{1,2,0:T(8,128)(2,1)}), bf16[32,128,96]{1,2,0:T(8,128)(2,1)S(1)}, u32[]{:S(2)}, u32[]{:S(2)}) async-start(bf16[32,128,96]{1,2,0:T(8,128)(2,1)} %copy.95), calls=%async_computation.2 | async-start | bytes 1572864 | tf_op jit(solution)/shard_map/all_to_all | solution.py:109
  90.6 2.4 %collective-permute-start.10 = (bf16[4,128,96]{1,0,2:T(4,128)(2,1)}, bf16[4,128,96]{1,0,2:T(4,128)(2,1)}, u32[]{:S(2)}, u32[]{:S(2)}) collective-permute-start(bf16[4,128,96]{1,0,2:T(4,128)(2,1)} %get-tuple-element.37), channel_id=1, source_target_pairs={{0,2},{1,3},{2,0},{3,1},{4,6},{5,7},{6,4},{7,5},{8,10},{9,11},{10,... | collective-permute-start | bytes 294920 | tf_op jit(solution)/shard_map/ppermute | solution.py:57
  101.8 2.8 %all-to-all-done.2 = bf16[32,128,96]{1,2,0:T(8,128)(2,1)S(1)} async-done(((bf16[32,128,96]{1,2,0:T(8,128)(2,1)}), bf16[32,128,96]{1,2,0:T(8,128)(2,1)S(1)}, u32[]{:S(2)}, u32[]{:S(2)}) %all-to-all-start.2) | async-done | bytes 786464 | tf_op jit(solution)/shard_map/all_to_all | solution.py:109
  109.5 5.8 %all-to-all-start.3 = ((bf16[32,128,96]{1,2,0:T(8,128)(2,1)}), bf16[32,128,96]{1,2,0:T(8,128)(2,1)S(1)}, u32[]{:S(2)}, u32[]{:S(2)}) async-start(bf16[32,128,96]{1,2,0:T(8,128)(2,1)} %copy.108), calls=%async_computation.3 | async-start | bytes 1572864 | tf_op jit(solution)/shard_map/all_to_all | solution.py:109
  115.3 3.3 %convolution_convert_fusion.7 = bf16[384,768]{0,1:T(8,128)(2,1)} fusion(bf16[4,128,384]{1,2,0:T(8,128)(2,1)S(1)} %copy-done.11, bf16[1,1,768,768]{3,2,1,0:T(8,128)(2,1)S(1)} %copy-done, bf16[4,768,128]{1,2,0:T(8,128)(2,1)} %copy-done.3, bf16[1,1,768,384]{3,2,1,0:T(8,128)(2,1)} %param.7), kind=kOutput, calls=%fused_computation.16 | convolution fusion | flops 756154368 | bytes 3538944 | tf_op jit(solution)/shard_map/ab,bn->an/dot_general | solution.py:149
  118.7 2.3 %fusion.7 = bf16[512,384]{0,1:T(8,128)(2,1)S(1)} fusion(bf16[768,512]{0,1:T(8,128)(2,1)} %bitcast.255, bf16[384,768]{0,1:T(8,128)(2,1)} %convolution_convert_fusion.7, bf16[1,1,768,768]{3,2,1,0:T(8,128)(2,1)S(1)} %copy-done), kind=kOutput, calls=%fused_computation.27 | convolution fusion | flops 755466240 | bytes 2949120 | tf_op jit(solution)/shard_map/bm,bn->mn/dot_general | solution.py:149
  124.8 4.7 %all-to-all-done.3 = bf16[32,128,96]{1,2,0:T(8,128)(2,1)S(1)} async-done(((bf16[32,128,96]{1,2,0:T(8,128)(2,1)}), bf16[32,128,96]{1,2,0:T(8,128)(2,1)S(1)}, u32[]{:S(2)}, u32[]{:S(2)}) %all-to-all-start.3) | async-done | bytes 786464 | tf_op jit(solution)/shard_map/all_to_all | solution.py:109
  132.1 22.2 %all_to_all.30 = bf16[32,128,96]{1,2,0:T(8,128)(2,1)S(1)} all-to-all(bf16[32,128,96]{1,2,0:T(8,128)(2,1)S(1)} %copy.110), channel_id=1, replica_groups=mesh['blk'=32,'lvl'=4] {'blk'}, dimensions={0} | all-to-all | bytes 1572864 | tf_op jit(solution)/shard_map/all_to_all | solution.py:109
  156.6 4.0 %all-to-all-start.5 = ((bf16[32,128,96]{1,2,0:T(8,128)(2,1)}), bf16[32,128,96]{1,2,0:T(8,128)(2,1)S(1)}, u32[]{:S(2)}, u32[]{:S(2)}) async-start(bf16[32,128,96]{1,2,0:T(8,128)(2,1)} %copy.112), calls=%async_computation.5 | async-start | bytes 1572864 | tf_op jit(solution)/shard_map/all_to_all | solution.py:109
  160.5 2.1 %collective-permute-start.6 = (bf16[4,128,96]{1,0,2:T(4,128)(2,1)S(1)}, bf16[4,128,96]{1,0,2:T(4,128)(2,1)S(1)}, u32[]{:S(2)}, u32[]{:S(2)}) collective-permute-start(bf16[4,128,96]{1,0,2:T(4,128)(2,1)S(1)} %copy-done.8), channel_id=1, source_target_pairs={{0,3},{4,7},{8,11},{12,15},{16,19},{20,23},{24,27},{28,31},{32,35}... | collective-permute-start | bytes 294920 | tf_op jit(solution)/shard_map/ppermute | solution.py:52
  164.9 9.9 %all-to-all-done.5 = bf16[32,128,96]{1,2,0:T(8,128)(2,1)S(1)} async-done(((bf16[32,128,96]{1,2,0:T(8,128)(2,1)}), bf16[32,128,96]{1,2,0:T(8,128)(2,1)S(1)}, u32[]{:S(2)}, u32[]{:S(2)}) %all-to-all-start.5) | async-done | bytes 786464 | tf_op jit(solution)/shard_map/all_to_all | solution.py:109
  174.8 1.8 select_select_fusion.5
  177.9 2.0 %collective-permute-start.17 = (bf16[4,128,96]{1,0,2:T(4,128)(2,1)}, bf16[4,128,96]{1,0,2:T(4,128)(2,1)S(1)}, u32[]{:S(2)}, u32[]{:S(2)}) collective-permute-start(bf16[4,128,96]{1,0,2:T(4,128)(2,1)} %get-tuple-element.32), channel_id=1, source_target_pairs={{0,3},{1,0},{2,1},{3,2},{4,7},{5,4},{6,5},{7,6},{8,11},{9,8},{10,9... | collective-permute-start | bytes 294920 | tf_op jit(solution)/shard_map/ppermute | solution.py:57
  180.0 3.5 %fusion.10 = bf16[768,384]{1,0:T(8,128)(2,1)} fusion(bf16[768,384]{1,0:T(8,128)(2,1)} %convolution_convert_fusion.12, bf16[384,768]{0,1:T(8,128)(2,1)} %convolution_convert_fusion.7, bf16[1,1,768,768]{3,2,1,0:T(8,128)(2,1)S(1)} %copy-done, bf16[4,768,128]{1,2,0:T(8,128)(2,1)S(1)} %copy-done.4, bf16[1,1,768,384]{3,2,1,0:T(8,128)(2,1)} %param.7, ...), kind=kOutput, calls=%fused_computation.30 | convolution fusion | flops 756744192 | bytes 4718594 | tf_op jit(solution)/shard_map/ab,bn->an/dot_general | solution.py:149
  (199 shorter events, 56.5 us)
Async XLA Ops:
  10.5 83.1 %copy-start.28 = (bf16[4]{0:T(256)(128)(2,1)}, bf16[4]{0:T(256)(128)(2,1)S(1)}, u32[]{:S(2)}) copy-start(bf16[4]{0:T(256)(128)(2,1)S(1)} %get-tuple-element.52) | copy-start | bytes 28
  14.1 5.7 %collective-permute-start = (bf16[512,96]{0,1:T(8,128)(2,1)S(1)}, bf16[512,96]{0,1:T(8,128)(2,1)S(1)}, u32[]{:S(2)}, u32[]{:S(2)}) collective-permute-start(bf16[512,96]{0,1:T(8,128)(2,1)S(1)} %get-tuple-element.13), channel_id=1, source_target_pairs={{0,3},{1,0},{2,1},{3,2},{4,7},{5,4},{6,5},{7,6},{8,11},{9,8},{10,9... | collective-permute-start | bytes 294920 | tf_op jit(solution)/shard_map/ppermute | solution.py:57
  17.4 5.1 %collective-permute-start.1 = (bf16[512,96]{0,1:T(8,128)(2,1)S(1)}, bf16[512,96]{0,1:T(8,128)(2,1)S(1)}, u32[]{:S(2)}, u32[]{:S(2)}) collective-permute-start(bf16[512,96]{0,1:T(8,128)(2,1)S(1)} %get-tuple-element.12), channel_id=1, source_target_pairs={{0,2},{1,3},{2,0},{3,1},{4,6},{5,7},{6,4},{7,5},{8,10},{9,11},{10,... | collective-permute-start | bytes 294920 | tf_op jit(solution)/shard_map/ppermute | solution.py:57
  17.9 7.2 %collective-permute-start.2 = (bf16[512,96]{0,1:T(8,128)(2,1)S(1)}, bf16[512,96]{0,1:T(8,128)(2,1)S(1)}, u32[]{:S(2)}, u32[]{:S(2)}) collective-permute-start(bf16[512,96]{0,1:T(8,128)(2,1)S(1)} %get-tuple-element.11), channel_id=1, source_target_pairs={{0,1},{1,2},{2,3},{3,0},{4,5},{5,6},{6,7},{7,4},{8,9},{9,10},{10,1... | collective-permute-start | bytes 294920 | tf_op jit(solution)/shard_map/ppermute | solution.py:57
  25.8 24.8 %collective-permute-start.3 = (bf16[512,512]{1,0:T(8,128)(2,1)S(1)}, bf16[512,512]{1,0:T(8,128)(2,1)S(1)}, u32[]{:S(2)}, u32[]{:S(2)}) collective-permute-start(bf16[512,512]{1,0:T(8,128)(2,1)S(1)} %fusion.11), channel_id=1, source_target_pairs={{0,1},{1,2},{2,3},{3,0},{4,5},{5,6},{6,7},{7,4},{8,9},{9,10},{10,1... | collective-permute-start | bytes 1572872 | tf_op jit(solution)/shard_map/ppermute | solution.py:57
  25.8 24.7 %collective-permute-start.4 = (bf16[512,512]{1,0:T(8,128)(2,1)S(1)}, bf16[512,512]{1,0:T(8,128)(2,1)S(1)}, u32[]{:S(2)}, u32[]{:S(2)}) collective-permute-start(bf16[512,512]{1,0:T(8,128)(2,1)S(1)} %fusion.11), channel_id=1, source_target_pairs={{0,2},{1,3},{2,0},{3,1},{4,6},{5,7},{6,4},{7,5},{8,10},{9,11},{10,... | collective-permute-start | bytes 1572872 | tf_op jit(solution)/shard_map/ppermute | solution.py:57
  26.5 25.6 %collective-permute-start.5 = (bf16[512,512]{1,0:T(8,128)(2,1)S(1)}, bf16[512,512]{1,0:T(8,128)(2,1)}, u32[]{:S(2)}, u32[]{:S(2)}) collective-permute-start(bf16[512,512]{1,0:T(8,128)(2,1)S(1)} %fusion.11), channel_id=1, source_target_pairs={{0,3},{1,0},{2,1},{3,2},{4,7},{5,4},{6,5},{7,6},{8,11},{9,8},{10,9... | collective-permute-start | bytes 1572872 | tf_op jit(solution)/shard_map/ppermute | solution.py:57
  29.7 24.2 %all-to-all-start = ((bf16[32,128,96]{1,2,0:T(8,128)(2,1)}), bf16[32,128,96]{1,2,0:T(8,128)(2,1)S(1)}, u32[]{:S(2)}, u32[]{:S(2)}) async-start(bf16[32,128,96]{1,2,0:T(8,128)(2,1)} %copy.91), calls=%async_computation | async-start | bytes 1572864 | tf_op jit(solution)/shard_map/all_to_all | solution.py:201
  57.9 24.2 %all-to-all-start.1 = ((bf16[32,128,96]{1,2,0:T(8,128)(2,1)}), bf16[32,128,96]{1,2,0:T(8,128)(2,1)S(1)}, u32[]{:S(2)}, u32[]{:S(2)}) async-start(bf16[32,128,96]{1,2,0:T(8,128)(2,1)} %copy.93), calls=%async_computation.1 | async-start | bytes 1572864 | tf_op jit(solution)/shard_map/all_to_all | solution.py:109
  86.4 18.2 %all-to-all-start.2 = ((bf16[32,128,96]{1,2,0:T(8,128)(2,1)}), bf16[32,128,96]{1,2,0:T(8,128)(2,1)S(1)}, u32[]{:S(2)}, u32[]{:S(2)}) async-start(bf16[32,128,96]{1,2,0:T(8,128)(2,1)} %copy.95), calls=%async_computation.2 | async-start | bytes 1572864 | tf_op jit(solution)/shard_map/all_to_all | solution.py:109
  90.3 7.6 %collective-permute-start.9 = (bf16[4,128,96]{1,0,2:T(4,128)(2,1)}, bf16[4,128,96]{1,0,2:T(4,128)(2,1)}, u32[]{:S(2)}, u32[]{:S(2)}) collective-permute-start(bf16[4,128,96]{1,0,2:T(4,128)(2,1)} %get-tuple-element.38), channel_id=1, source_target_pairs={{0,1},{1,2},{2,3},{3,0},{4,5},{5,6},{6,7},{7,4},{8,9},{9,10},{10,1... | collective-permute-start | bytes 294920 | tf_op jit(solution)/shard_map/ppermute | solution.py:57
  90.6 8.3 %collective-permute-start.10 = (bf16[4,128,96]{1,0,2:T(4,128)(2,1)}, bf16[4,128,96]{1,0,2:T(4,128)(2,1)}, u32[]{:S(2)}, u32[]{:S(2)}) collective-permute-start(bf16[4,128,96]{1,0,2:T(4,128)(2,1)} %get-tuple-element.37), channel_id=1, source_target_pairs={{0,2},{1,3},{2,0},{3,1},{4,6},{5,7},{6,4},{7,5},{8,10},{9,11},{10,... | collective-permute-start | bytes 294920 | tf_op jit(solution)/shard_map/ppermute | solution.py:57
  93.0 6.8 %collective-permute-start.11 = (bf16[4,128,96]{1,0,2:T(4,128)(2,1)}, bf16[4,128,96]{1,0,2:T(4,128)(2,1)}, u32[]{:S(2)}, u32[]{:S(2)}) collective-permute-start(bf16[4,128,96]{1,0,2:T(4,128)(2,1)} %get-tuple-element.36), channel_id=1, source_target_pairs={{0,3},{1,0},{2,1},{3,2},{4,7},{5,4},{6,5},{7,6},{8,11},{9,8},{10,9... | collective-permute-start | bytes 294920 | tf_op jit(solution)/shard_map/ppermute | solution.py:57
  109.5 20.0 %all-to-all-start.3 = ((bf16[32,128,96]{1,2,0:T(8,128)(2,1)}), bf16[32,128,96]{1,2,0:T(8,128)(2,1)S(1)}, u32[]{:S(2)}, u32[]{:S(2)}) async-start(bf16[32,128,96]{1,2,0:T(8,128)(2,1)} %copy.108), calls=%async_computation.3 | async-start | bytes 1572864 | tf_op jit(solution)/shard_map/all_to_all | solution.py:109
  122.0 7.9 %collective-permute-start.12 = (bf16[512,96]{0,1:T(8,128)(2,1)}, bf16[512,96]{0,1:T(8,128)(2,1)S(1)}, u32[]{:S(2)}, u32[]{:S(2)}) collective-permute-start(bf16[512,96]{0,1:T(8,128)(2,1)} %get-tuple-element.9), channel_id=1, source_target_pairs={{0,3},{1,0},{2,1},{3,2},{4,7},{5,4},{6,5},{7,6},{8,11},{9,8},{10,9... | collective-permute-start | bytes 294920 | tf_op jit(solution)/shard_map/ppermute | solution.py:57
  122.9 7.0 %collective-permute-start.13 = (bf16[512,96]{0,1:T(8,128)(2,1)}, bf16[512,96]{0,1:T(8,128)(2,1)S(1)}, u32[]{:S(2)}, u32[]{:S(2)}) collective-permute-start(bf16[512,96]{0,1:T(8,128)(2,1)} %get-tuple-element.8), channel_id=1, source_target_pairs={{0,2},{1,3},{2,0},{3,1},{4,6},{5,7},{6,4},{7,5},{8,10},{9,11},{10,... | collective-permute-start | bytes 294920 | tf_op jit(solution)/shard_map/ppermute | solution.py:57
  124.6 6.4 %collective-permute-start.14 = (bf16[512,96]{0,1:T(8,128)(2,1)}, bf16[512,96]{0,1:T(8,128)(2,1)S(1)}, u32[]{:S(2)}, u32[]{:S(2)}) collective-permute-start(bf16[512,96]{0,1:T(8,128)(2,1)} %get-tuple-element.7), channel_id=1, source_target_pairs={{0,1},{1,2},{2,3},{3,0},{4,5},{5,6},{6,7},{7,4},{8,9},{9,10},{10,1... | collective-permute-start | bytes 294920 | tf_op jit(solution)/shard_map/ppermute | solution.py:57
  156.6 18.2 %all-to-all-start.5 = ((bf16[32,128,96]{1,2,0:T(8,128)(2,1)}), bf16[32,128,96]{1,2,0:T(8,128)(2,1)S(1)}, u32[]{:S(2)}, u32[]{:S(2)}) async-start(bf16[32,128,96]{1,2,0:T(8,128)(2,1)} %copy.112), calls=%async_computation.5 | async-start | bytes 1572864 | tf_op jit(solution)/shard_map/all_to_all | solution.py:109
  160.5 4.0 %collective-permute-start.6 = (bf16[4,128,96]{1,0,2:T(4,128)(2,1)S(1)}, bf16[4,128,96]{1,0,2:T(4,128)(2,1)S(1)}, u32[]{:S(2)}, u32[]{:S(2)}) collective-permute-start(bf16[4,128,96]{1,0,2:T(4,128)(2,1)S(1)} %copy-done.8), channel_id=1, source_target_pairs={{0,3},{4,7},{8,11},{12,15},{16,19},{20,23},{24,27},{28,31},{32,35}... | collective-permute-start | bytes 294920 | tf_op jit(solution)/shard_map/ppermute | solution.py:52
  162.6 1.9 %collective-permute-start.7 = (bf16[4,128,96]{1,0,2:T(4,128)(2,1)S(1)}, bf16[4,128,96]{1,0,2:T(4,128)(2,1)S(1)}, u32[]{:S(2)}, u32[]{:S(2)}) collective-permute-start(bf16[4,128,96]{1,0,2:T(4,128)(2,1)S(1)} %copy-done.8), channel_id=1, source_target_pairs={{1,3},{5,7},{9,11},{13,15},{17,19},{21,23},{25,27},{29,31},{33,35}... | collective-permute-start | bytes 294920 | tf_op jit(solution)/shard_map/ppermute | solution.py:52
  163.3 1.3 collective-permute-start.8
  176.6 8.0 %collective-permute-start.15 = (bf16[4,128,96]{1,0,2:T(4,128)(2,1)}, bf16[4,128,96]{1,0,2:T(4,128)(2,1)S(1)}, u32[]{:S(2)}, u32[]{:S(2)}) collective-permute-start(bf16[4,128,96]{1,0,2:T(4,128)(2,1)} %get-tuple-element.34), channel_id=1, source_target_pairs={{0,1},{1,2},{2,3},{3,0},{4,5},{5,6},{6,7},{7,4},{8,9},{9,10},{10,1... | collective-permute-start | bytes 294920 | tf_op jit(solution)/shard_map/ppermute | solution.py:57
  176.7 8.0 %collective-permute-start.16 = (bf16[4,128,96]{1,0,2:T(4,128)(2,1)}, bf16[4,128,96]{1,0,2:T(4,128)(2,1)S(1)}, u32[]{:S(2)}, u32[]{:S(2)}) collective-permute-start(bf16[4,128,96]{1,0,2:T(4,128)(2,1)} %get-tuple-element.33), channel_id=1, source_target_pairs={{0,2},{1,3},{2,0},{3,1},{4,6},{5,7},{6,4},{7,5},{8,10},{9,11},{10,... | collective-permute-start | bytes 294920 | tf_op jit(solution)/shard_map/ppermute | solution.py:57
  177.9 7.0 %collective-permute-start.17 = (bf16[4,128,96]{1,0,2:T(4,128)(2,1)}, bf16[4,128,96]{1,0,2:T(4,128)(2,1)S(1)}, u32[]{:S(2)}, u32[]{:S(2)}) collective-permute-start(bf16[4,128,96]{1,0,2:T(4,128)(2,1)} %get-tuple-element.32), channel_id=1, source_target_pairs={{0,3},{1,0},{2,1},{3,2},{4,7},{5,4},{6,5},{7,6},{8,11},{9,8},{10,9... | collective-permute-start | bytes 294920 | tf_op jit(solution)/shard_map/ppermute | solution.py:57
  (44 other events, 395.3 us)

commit v16 on v14

--- a/solution.py
+++ b/solution.py
@@ -53,8 +53,9 @@
     return jnp.concatenate(parts, axis=-1)
 
 
-def shift(array, by, row_count):
-    return lax.ppermute(array, "lvl", [(i, (i + by) % row_count) for i in range(row_count)])
+def shift(array, by, row_count, senders=None):
+    rows = range(row_count) if senders is None else senders
+    return lax.ppermute(array, "lvl", [(i, (i + by) % row_count) for i in rows])
 
 
 def one_hot_rows(index, count, dtype):
@@ -157,7 +158,7 @@
     turn = dot(inv_left_f, inv_rhs, "bq,bn->qn").astype(jnp.bfloat16)
     couple = jnp.where(my_row == last, gram, couple)
     free = jnp.where(my_row == last, turn, free)
-    couples = [couple] + [shift(couple, d, row_count) for d in range(1, row_count)]
+    couples = [couple] + [shift(couple, d, row_count, range(1, row_count)) for d in range(1, row_count)]
     free_blocks = free.reshape(flat, row_count, width)
     frees = [pick_block(free_blocks, my_row, row_count)]
     for d in range(1, row_count):
@@ -213,7 +214,7 @@
     top = dot(inverse_here, solved, "ba,bn->an").astype(jnp.bfloat16)
     back_parts = [take_block(back_term, my_row, row_count)]
     for d in range(1, row_count):
-        back_parts.append(shift(take_block(back_term, lax.rem(my_row + d, row_count), row_count), d, row_count))
+        back_parts.append(shift(take_block(back_term, lax.rem(my_row + d, row_count), row_count), d, row_count, range(1, last)))
 
     def back_free(t):
         return frees_at(back_parts, my_row, t, row_count)

time: 184 us -> 190 us (1.033)
  starting transfers between devices: 53.3 us -> 61.6 us
  waiting for transfers between devices: 46.3 us -> 42.2 us
    all_to_all x5, waiting for transfers between devices: 34.1 us -> 27.9 us  [route(): lax.all_to_all(holder, 'blk', split_axis=0, concat_axis=0, tiled=True)]
    all_to_all x5, starting transfers between devices: 31.9 us -> 35.1 us  [route(): lax.all_to_all(holder, 'blk', split_axis=0, concat_axis=0, tiled=True)]
    ppermute x15, starting transfers between devices: 18 us -> 21.1 us  [shift(): return lax.ppermute(array, 'lvl', [(i, (i + by) % row_count) for i in rows])]
    ppermute x3, starting transfers between devices: 3.36 us -> 5.46 us  [collect(): parts.append(lax.ppermute(routed, 'lvl', [(r, dst_row)]))]
    ppermute x15, waiting for transfers between devices: 11.6 us -> 13.7 us  [shift(): return lax.ppermute(array, 'lvl', [(i, (i + by) % row_count) for i in rows])]
  transfers between devices with their start and end apart: 23 -> 23, of which waited for: 10 -> 8; matrix products, arithmetic and copies ran while one was open for 14% -> 13% of each run, Pallas kernels for 0% -> 0%
where the time goes in v16:
time: 190 us; the launch traced here: 188 us
  starting transfers between devices  61.6 us (32%)
  waiting for transfers between devices  42.2 us (22%)
  matrix products  31.5 us (17%)
  blocking collectives  22.3 us (12%)
  local copies, waits for them, and re-layouts  21.7 us (11%)
  other arithmetic  7.59 us (4%)
    all_to_all x5, starting transfers between devices, route(): lax.all_to_all(holder, 'blk', split_axis=0, concat_axis=0, tiled=True)  35.1 us
    all_to_all x5, waiting for transfers between devices, route(): lax.all_to_all(holder, 'blk', split_axis=0, concat_axis=0, tiled=True)  27.9 us
    dot_general x16, matrix products, dot(): return jnp.einsum(spec, a, b, preferred_element_type=jnp.float32)  22.5 us
    all_to_all x1, blocking collectives, route(): lax.all_to_all(holder, 'blk', split_axis=0, concat_axis=0, tiled=True)  22.3 us
    ppermute x15, starting transfers between devices, shift(): return lax.ppermute(array, 'lvl', [(i, (i + by) % row_count) for i in rows])  21.1 us
    ppermute x15, waiting for transfers between devices, shift(): return lax.ppermute(array, 'lvl', [(i, (i + by) % row_count) for i in rows])  13.7 us
    convert_element_type x6, local copies, waits for them, and re-layouts, route(): holder = holder.astype(piece.dtype)  6.34 us
    dot_general x6, matrix products, route(): jnp.einsum('kj,jrn->krn', take, arrived, preferred_element_type=jnp.float32)  6 us
  transfers between devices with their start and end apart: 23, of which 8 were waited for; matrix products, arithmetic and copies ran while one was open for 13% of the time, Pallas kernels for 0%

profile of v16, /device:TPU:1, one launch (start us, length us, event | category | flops | bytes accessed | tf_op | source)
XLA Modules:
  0.0 188.4 jit_solution(15465134863926356834)
XLA Ops:
  10.8 1.6 fusion.14
  13.5 3.4 %collective-permute-start = (bf16[512,96]{0,1:T(8,128)(2,1)S(1)}, bf16[512,96]{0,1:T(8,128)(2,1)S(1)}, u32[]{:S(2)}, u32[]{:S(2)}) collective-permute-start(bf16[512,96]{0,1:T(8,128)(2,1)S(1)} %get-tuple-element.9), channel_id=1, source_target_pairs={{0,3},{1,0},{2,1},{3,2},{4,7},{5,4},{6,5},{7,6},{8,11},{9,8},{10,9... | collective-permute-start | bytes 294920 | tf_op jit(solution)/shard_map/ppermute | solution.py:58
  18.6 2.0 %fusion.11 = bf16[512,512]{1,0:T(8,128)(2,1)S(1)} fusion(bf16[512,512]{1,0:T(8,128)(2,1)S(1)} %fusion.12, bf16[512,768]{1,0:T(8,128)(2,1)} %copy-done.43, pred[]{:T(512)S(6)} %eq.203), kind=kOutput, calls=%fused_computation.33 | convolution fusion | flops 403177472 | bytes 1835009 | tf_op jit(solution)/shard_map/bq,bm->qm/dot_general | solution.py:150
  26.4 9.6 %all-to-all-start = ((bf16[32,128,96]{1,2,0:T(8,128)(2,1)}), bf16[32,128,96]{1,2,0:T(8,128)(2,1)S(1)}, u32[]{:S(2)}, u32[]{:S(2)}) async-start(bf16[32,128,96]{1,2,0:T(8,128)(2,1)} %copy.91), calls=%async_computation | async-start | bytes 1572864 | tf_op jit(solution)/shard_map/all_to_all | solution.py:110
  36.1 11.4 %collective-permute-done.4 = bf16[512,512]{1,0:T(8,128)(2,1)S(1)} collective-permute-done((bf16[512,512]{1,0:T(8,128)(2,1)S(1)}, bf16[512,512]{1,0:T(8,128)(2,1)S(1)}, u32[]{:S(2)}, u32[]{:S(2)}) %collective-permute-start.4) | collective-permute-done | bytes 524320 | tf_op jit(solution)/shard_map/ppermute | solution.py:58
  54.7 10.9 %all-to-all-start.1 = ((bf16[32,128,96]{1,2,0:T(8,128)(2,1)}), bf16[32,128,96]{1,2,0:T(8,128)(2,1)S(1)}, u32[]{:S(2)}, u32[]{:S(2)}) async-start(bf16[32,128,96]{1,2,0:T(8,128)(2,1)} %copy.93), calls=%async_computation.1 | async-start | bytes 1572864 | tf_op jit(solution)/shard_map/all_to_all | solution.py:110
  65.6 14.2 %all-to-all-done.1 = bf16[32,128,96]{1,2,0:T(8,128)(2,1)S(1)} async-done(((bf16[32,128,96]{1,2,0:T(8,128)(2,1)}), bf16[32,128,96]{1,2,0:T(8,128)(2,1)S(1)}, u32[]{:S(2)}, u32[]{:S(2)}) %all-to-all-start.1) | async-done | bytes 786464 | tf_op jit(solution)/shard_map/all_to_all | solution.py:110
  79.9 2.2 %select_select_fusion.9 = (bf16[4,128,96]{1,0,2:T(4,128)(2,1)}, bf16[4,128,96]{1,0,2:T(4,128)(2,1)}, bf16[4,128,96]{1,0,2:T(4,128)(2,1)}, bf16[4,128,96]{1,0,2:T(4,128)(2,1)}, bf16[4,128,96]{1,0,2:T(4,128)(2,1)S(1)}) fusion(bf16[4,128,96]{1,0,2:T(4,128)(2,1)} %copy-done.14, pred[]{:T(512)S(6)} %eq.215, pred[]{:T(512)S(6)} %eq.210, pred[]{:T(512)S(6)} %eq.203, ...), kind=kOutput, calls=%fused_computation.123 | convolution fusion | flops 3784832 | bytes 1376284 | tf_op jit(solution)/shard_map/kj,jrn->krn/dot_general | solution.py:112
  84.1 4.0 %all-to-all-start.2 = ((bf16[32,128,96]{1,2,0:T(8,128)(2,1)}), bf16[32,128,96]{1,2,0:T(8,128)(2,1)S(1)}, u32[]{:S(2)}, u32[]{:S(2)}) async-start(bf16[32,128,96]{1,2,0:T(8,128)(2,1)} %copy.95), calls=%async_computation.2 | async-start | bytes 1572864 | tf_op jit(solution)/shard_map/all_to_all | solution.py:110
  90.1 2.0 %collective-permute-start.11 = (bf16[4,128,96]{1,0,2:T(4,128)(2,1)}, bf16[4,128,96]{1,0,2:T(4,128)(2,1)}, u32[]{:S(2)}, u32[]{:S(2)}) collective-permute-start(bf16[4,128,96]{1,0,2:T(4,128)(2,1)} %get-tuple-element.32), channel_id=1, source_target_pairs={{0,3},{1,0},{2,1},{3,2},{4,7},{5,4},{6,5},{7,6},{8,11},{9,8},{10,9... | collective-permute-start | bytes 294920 | tf_op jit(solution)/shard_map/ppermute | solution.py:58
  100.6 1.8 all-to-all-done.2
  107.3 6.6 %all-to-all-start.3 = ((bf16[32,128,96]{1,2,0:T(8,128)(2,1)}), bf16[32,128,96]{1,2,0:T(8,128)(2,1)S(1)}, u32[]{:S(2)}, u32[]{:S(2)}) async-start(bf16[32,128,96]{1,2,0:T(8,128)(2,1)} %copy.108), calls=%async_computation.3 | async-start | bytes 1572864 | tf_op jit(solution)/shard_map/all_to_all | solution.py:110
  113.9 3.3 %convolution_convert_fusion.7 = bf16[384,768]{0,1:T(8,128)(2,1)} fusion(bf16[4,128,384]{1,2,0:T(8,128)(2,1)S(1)} %copy-done.11, bf16[1,1,768,768]{3,2,1,0:T(8,128)(2,1)S(1)} %copy-done, bf16[4,768,128]{1,2,0:T(8,128)(2,1)} %copy-done.3, bf16[1,1,768,384]{3,2,1,0:T(8,128)(2,1)} %param.7), kind=kOutput, calls=%fused_computation.16 | convolution fusion | flops 756154368 | bytes 3538944 | tf_op jit(solution)/shard_map/ab,bn->an/dot_general | solution.py:150
  117.2 2.3 %fusion.7 = bf16[512,384]{0,1:T(8,128)(2,1)S(1)} fusion(bf16[768,512]{0,1:T(8,128)(2,1)} %bitcast.255, bf16[384,768]{0,1:T(8,128)(2,1)} %convolution_convert_fusion.7, bf16[1,1,768,768]{3,2,1,0:T(8,128)(2,1)S(1)} %copy-done), kind=kOutput, calls=%fused_computation.27 | convolution fusion | flops 755466240 | bytes 2949120 | tf_op jit(solution)/shard_map/bm,bn->mn/dot_general | solution.py:150
  123.9 4.1 %all-to-all-done.3 = bf16[32,128,96]{1,2,0:T(8,128)(2,1)S(1)} async-done(((bf16[32,128,96]{1,2,0:T(8,128)(2,1)}), bf16[32,128,96]{1,2,0:T(8,128)(2,1)S(1)}, u32[]{:S(2)}, u32[]{:S(2)}) %all-to-all-start.3) | async-done | bytes 786464 | tf_op jit(solution)/shard_map/all_to_all | solution.py:110
  130.9 22.3 %all_to_all.30 = bf16[32,128,96]{1,2,0:T(8,128)(2,1)S(1)} all-to-all(bf16[32,128,96]{1,2,0:T(8,128)(2,1)S(1)} %copy.110), channel_id=1, replica_groups=mesh['blk'=32,'lvl'=4] {'blk'}, dimensions={0} | all-to-all | bytes 1572864 | tf_op jit(solution)/shard_map/all_to_all | solution.py:110
  155.4 4.0 %all-to-all-start.5 = ((bf16[32,128,96]{1,2,0:T(8,128)(2,1)}), bf16[32,128,96]{1,2,0:T(8,128)(2,1)S(1)}, u32[]{:S(2)}, u32[]{:S(2)}) async-start(bf16[32,128,96]{1,2,0:T(8,128)(2,1)} %copy.112), calls=%async_computation.5 | async-start | bytes 1572864 | tf_op jit(solution)/shard_map/all_to_all | solution.py:110
  159.4 4.1 %collective-permute-start.6 = (bf16[4,128,96]{1,0,2:T(4,128)(2,1)S(1)}, bf16[4,128,96]{1,0,2:T(4,128)(2,1)S(1)}, u32[]{:S(2)}, u32[]{:S(2)}) collective-permute-start(bf16[4,128,96]{1,0,2:T(4,128)(2,1)S(1)} %copy-done.8), channel_id=1, source_target_pairs={{0,3},{4,7},{8,11},{12,15},{16,19},{20,23},{24,27},{28,31},{32,35}... | collective-permute-start | bytes 294920 | tf_op jit(solution)/shard_map/ppermute | solution.py:52
  165.8 7.8 %all-to-all-done.5 = bf16[32,128,96]{1,2,0:T(8,128)(2,1)S(1)} async-done(((bf16[32,128,96]{1,2,0:T(8,128)(2,1)}), bf16[32,128,96]{1,2,0:T(8,128)(2,1)S(1)}, u32[]{:S(2)}, u32[]{:S(2)}) %all-to-all-start.5) | async-done | bytes 786464 | tf_op jit(solution)/shard_map/all_to_all | solution.py:110
  173.6 1.8 select_select_fusion.5
  176.4 2.5 %collective-permute-start.16 = (bf16[4,128,96]{1,0,2:T(4,128)(2,1)}, bf16[4,128,96]{1,0,2:T(4,128)(2,1)S(1)}, u32[]{:S(2)}, u32[]{:S(2)}) collective-permute-start(bf16[4,128,96]{1,0,2:T(4,128)(2,1)} %get-tuple-element.29), channel_id=1, source_target_pairs={{0,2},{1,3},{2,0},{3,1},{4,6},{5,7},{6,4},{7,5},{8,10},{9,11},{10,... | collective-permute-start | bytes 294920 | tf_op jit(solution)/shard_map/ppermute | solution.py:58
  178.9 1.9 %collective-permute-start.17 = (bf16[4,128,96]{1,0,2:T(4,128)(2,1)}, bf16[4,128,96]{1,0,2:T(4,128)(2,1)S(1)}, u32[]{:S(2)}, u32[]{:S(2)}) collective-permute-start(bf16[4,128,96]{1,0,2:T(4,128)(2,1)} %get-tuple-element.28), channel_id=1, source_target_pairs={{0,3},{1,0},{2,1},{3,2},{4,7},{5,4},{6,5},{7,6},{8,11},{9,8},{10,9... | collective-permute-start | bytes 294920 | tf_op jit(solution)/shard_map/ppermute | solution.py:58
  180.8 3.5 %fusion.10 = bf16[768,384]{1,0:T(8,128)(2,1)} fusion(bf16[768,384]{1,0:T(8,128)(2,1)} %convolution_convert_fusion.12, bf16[384,768]{0,1:T(8,128)(2,1)} %convolution_convert_fusion.7, bf16[1,1,768,768]{3,2,1,0:T(8,128)(2,1)S(1)} %copy-done, bf16[4,768,128]{1,2,0:T(8,128)(2,1)S(1)} %copy-done.4, bf16[1,1,768,384]{3,2,1,0:T(8,128)(2,1)} %param.7, ...), kind=kOutput, calls=%fused_computation.30 | convolution fusion | flops 756744192 | bytes 4718594 | tf_op jit(solution)/shard_map/ab,bn->an/dot_general | solution.py:150
  186.8 1.6 fusion.5
  (200 shorter events, 58.0 us)
Async XLA Ops:
  13.0 79.3 %copy-start.28 = (bf16[4]{0:T(256)(128)(2,1)}, bf16[4]{0:T(256)(128)(2,1)S(1)}, u32[]{:S(2)}) copy-start(bf16[4]{0:T(256)(128)(2,1)S(1)} %get-tuple-element.48) | copy-start | bytes 28
  13.5 9.7 %collective-permute-start = (bf16[512,96]{0,1:T(8,128)(2,1)S(1)}, bf16[512,96]{0,1:T(8,128)(2,1)S(1)}, u32[]{:S(2)}, u32[]{:S(2)}) collective-permute-start(bf16[512,96]{0,1:T(8,128)(2,1)S(1)} %get-tuple-element.9), channel_id=1, source_target_pairs={{0,3},{1,0},{2,1},{3,2},{4,7},{5,4},{6,5},{7,6},{8,11},{9,8},{10,9... | collective-permute-start | bytes 294920 | tf_op jit(solution)/shard_map/ppermute | solution.py:58
  16.9 7.7 %collective-permute-start.1 = (bf16[512,96]{0,1:T(8,128)(2,1)S(1)}, bf16[512,96]{0,1:T(8,128)(2,1)S(1)}, u32[]{:S(2)}, u32[]{:S(2)}) collective-permute-start(bf16[512,96]{0,1:T(8,128)(2,1)S(1)} %get-tuple-element.8), channel_id=1, source_target_pairs={{0,2},{1,3},{2,0},{3,1},{4,6},{5,7},{6,4},{7,5},{8,10},{9,11},{10,... | collective-permute-start | bytes 294920 | tf_op jit(solution)/shard_map/ppermute | solution.py:58
  17.4 7.2 %collective-permute-start.2 = (bf16[512,96]{0,1:T(8,128)(2,1)S(1)}, bf16[512,96]{0,1:T(8,128)(2,1)S(1)}, u32[]{:S(2)}, u32[]{:S(2)}) collective-permute-start(bf16[512,96]{0,1:T(8,128)(2,1)S(1)} %get-tuple-element.7), channel_id=1, source_target_pairs={{0,1},{1,2},{2,3},{3,0},{4,5},{5,6},{6,7},{7,4},{8,9},{9,10},{10,1... | collective-permute-start | bytes 294920 | tf_op jit(solution)/shard_map/ppermute | solution.py:58
  20.6 15.4 %collective-permute-start.3 = (bf16[512,512]{1,0:T(8,128)(2,1)S(1)}, bf16[512,512]{1,0:T(8,128)(2,1)S(1)}, u32[]{:S(2)}, u32[]{:S(2)}) collective-permute-start(bf16[512,512]{1,0:T(8,128)(2,1)S(1)} %fusion.11), channel_id=1, source_target_pairs={{1,2},{2,3},{3,0},{5,6},{6,7},{7,4},{9,10},{10,11},{11,8},{13,14},... | collective-permute-start | bytes 1572872 | tf_op jit(solution)/shard_map/ppermute | solution.py:58
  21.9 25.5 %collective-permute-start.4 = (bf16[512,512]{1,0:T(8,128)(2,1)S(1)}, bf16[512,512]{1,0:T(8,128)(2,1)S(1)}, u32[]{:S(2)}, u32[]{:S(2)}) collective-permute-start(bf16[512,512]{1,0:T(8,128)(2,1)S(1)} %fusion.11), channel_id=1, source_target_pairs={{1,3},{2,0},{3,1},{5,7},{6,4},{7,5},{9,11},{10,8},{11,9},{13,15},{... | collective-permute-start | bytes 1572872 | tf_op jit(solution)/shard_map/ppermute | solution.py:58
  23.3 25.9 %collective-permute-start.5 = (bf16[512,512]{1,0:T(8,128)(2,1)S(1)}, bf16[512,512]{1,0:T(8,128)(2,1)}, u32[]{:S(2)}, u32[]{:S(2)}) collective-permute-start(bf16[512,512]{1,0:T(8,128)(2,1)S(1)} %fusion.11), channel_id=1, source_target_pairs={{1,0},{2,1},{3,2},{5,4},{6,5},{7,6},{9,8},{10,9},{11,10},{13,12},{... | collective-permute-start | bytes 1572872 | tf_op jit(solution)/shard_map/ppermute | solution.py:58
  26.4 24.3 %all-to-all-start = ((bf16[32,128,96]{1,2,0:T(8,128)(2,1)}), bf16[32,128,96]{1,2,0:T(8,128)(2,1)S(1)}, u32[]{:S(2)}, u32[]{:S(2)}) async-start(bf16[32,128,96]{1,2,0:T(8,128)(2,1)} %copy.91), calls=%async_computation | async-start | bytes 1572864 | tf_op jit(solution)/shard_map/all_to_all | solution.py:110
  54.7 25.2 %all-to-all-start.1 = ((bf16[32,128,96]{1,2,0:T(8,128)(2,1)}), bf16[32,128,96]{1,2,0:T(8,128)(2,1)S(1)}, u32[]{:S(2)}, u32[]{:S(2)}) async-start(bf16[32,128,96]{1,2,0:T(8,128)(2,1)} %copy.93), calls=%async_computation.1 | async-start | bytes 1572864 | tf_op jit(solution)/shard_map/all_to_all | solution.py:110
  84.1 18.2 %all-to-all-start.2 = ((bf16[32,128,96]{1,2,0:T(8,128)(2,1)}), bf16[32,128,96]{1,2,0:T(8,128)(2,1)S(1)}, u32[]{:S(2)}, u32[]{:S(2)}) async-start(bf16[32,128,96]{1,2,0:T(8,128)(2,1)} %copy.95), calls=%async_computation.2 | async-start | bytes 1572864 | tf_op jit(solution)/shard_map/all_to_all | solution.py:110
  88.1 8.7 %collective-permute-start.9 = (bf16[4,128,96]{1,0,2:T(4,128)(2,1)}, bf16[4,128,96]{1,0,2:T(4,128)(2,1)}, u32[]{:S(2)}, u32[]{:S(2)}) collective-permute-start(bf16[4,128,96]{1,0,2:T(4,128)(2,1)} %get-tuple-element.34), channel_id=1, source_target_pairs={{0,1},{1,2},{2,3},{3,0},{4,5},{5,6},{6,7},{7,4},{8,9},{9,10},{10,1... | collective-permute-start | bytes 294920 | tf_op jit(solution)/shard_map/ppermute | solution.py:58
  89.4 8.3 %collective-permute-start.10 = (bf16[4,128,96]{1,0,2:T(4,128)(2,1)}, bf16[4,128,96]{1,0,2:T(4,128)(2,1)}, u32[]{:S(2)}, u32[]{:S(2)}) collective-permute-start(bf16[4,128,96]{1,0,2:T(4,128)(2,1)} %get-tuple-element.33), channel_id=1, source_target_pairs={{0,2},{1,3},{2,0},{3,1},{4,6},{5,7},{6,4},{7,5},{8,10},{9,11},{10,... | collective-permute-start | bytes 294920 | tf_op jit(solution)/shard_map/ppermute | solution.py:58
  90.1 8.5 %collective-permute-start.11 = (bf16[4,128,96]{1,0,2:T(4,128)(2,1)}, bf16[4,128,96]{1,0,2:T(4,128)(2,1)}, u32[]{:S(2)}, u32[]{:S(2)}) collective-permute-start(bf16[4,128,96]{1,0,2:T(4,128)(2,1)} %get-tuple-element.32), channel_id=1, source_target_pairs={{0,3},{1,0},{2,1},{3,2},{4,7},{5,4},{6,5},{7,6},{8,11},{9,8},{10,9... | collective-permute-start | bytes 294920 | tf_op jit(solution)/shard_map/ppermute | solution.py:58
  107.3 20.8 %all-to-all-start.3 = ((bf16[32,128,96]{1,2,0:T(8,128)(2,1)}), bf16[32,128,96]{1,2,0:T(8,128)(2,1)S(1)}, u32[]{:S(2)}, u32[]{:S(2)}) async-start(bf16[32,128,96]{1,2,0:T(8,128)(2,1)} %copy.108), calls=%async_computation.3 | async-start | bytes 1572864 | tf_op jit(solution)/shard_map/all_to_all | solution.py:110
  120.5 7.9 %collective-permute-start.12 = (bf16[512,96]{0,1:T(8,128)(2,1)}, bf16[512,96]{0,1:T(8,128)(2,1)S(1)}, u32[]{:S(2)}, u32[]{:S(2)}) collective-permute-start(bf16[512,96]{0,1:T(8,128)(2,1)} %get-tuple-element.5), channel_id=1, source_target_pairs={{1,0},{2,1},{5,4},{6,5},{9,8},{10,9},{13,12},{14,13},{17,16},{18,1... | collective-permute-start | bytes 294920 | tf_op jit(solution)/shard_map/ppermute | solution.py:58
  122.0 7.8 %collective-permute-start.13 = (bf16[512,96]{0,1:T(8,128)(2,1)}, bf16[512,96]{0,1:T(8,128)(2,1)S(1)}, u32[]{:S(2)}, u32[]{:S(2)}) collective-permute-start(bf16[512,96]{0,1:T(8,128)(2,1)} %get-tuple-element.4), channel_id=1, source_target_pairs={{1,3},{2,0},{5,7},{6,4},{9,11},{10,8},{13,15},{14,12},{17,19},{18,... | collective-permute-start | bytes 294920 | tf_op jit(solution)/shard_map/ppermute | solution.py:58
  123.3 6.5 %collective-permute-start.14 = (bf16[512,96]{0,1:T(8,128)(2,1)}, bf16[512,96]{0,1:T(8,128)(2,1)S(1)}, u32[]{:S(2)}, u32[]{:S(2)}) collective-permute-start(bf16[512,96]{0,1:T(8,128)(2,1)} %get-tuple-element.3), channel_id=1, source_target_pairs={{1,2},{2,3},{5,6},{6,7},{9,10},{10,11},{13,14},{14,15},{17,18},{18... | collective-permute-start | bytes 294920 | tf_op jit(solution)/shard_map/ppermute | solution.py:58
  155.4 18.2 %all-to-all-start.5 = ((bf16[32,128,96]{1,2,0:T(8,128)(2,1)}), bf16[32,128,96]{1,2,0:T(8,128)(2,1)S(1)}, u32[]{:S(2)}, u32[]{:S(2)}) async-start(bf16[32,128,96]{1,2,0:T(8,128)(2,1)} %copy.112), calls=%async_computation.5 | async-start | bytes 1572864 | tf_op jit(solution)/shard_map/all_to_all | solution.py:110
  159.4 6.1 %collective-permute-start.6 = (bf16[4,128,96]{1,0,2:T(4,128)(2,1)S(1)}, bf16[4,128,96]{1,0,2:T(4,128)(2,1)S(1)}, u32[]{:S(2)}, u32[]{:S(2)}) collective-permute-start(bf16[4,128,96]{1,0,2:T(4,128)(2,1)S(1)} %copy-done.8), channel_id=1, source_target_pairs={{0,3},{4,7},{8,11},{12,15},{16,19},{20,23},{24,27},{28,31},{32,35}... | collective-permute-start | bytes 294920 | tf_op jit(solution)/shard_map/ppermute | solution.py:52
  163.6 1.9 %collective-permute-start.7 = (bf16[4,128,96]{1,0,2:T(4,128)(2,1)S(1)}, bf16[4,128,96]{1,0,2:T(4,128)(2,1)S(1)}, u32[]{:S(2)}, u32[]{:S(2)}) collective-permute-start(bf16[4,128,96]{1,0,2:T(4,128)(2,1)S(1)} %copy-done.8), channel_id=1, source_target_pairs={{1,3},{5,7},{9,11},{13,15},{17,19},{21,23},{25,27},{29,31},{33,35}... | collective-permute-start | bytes 294920 | tf_op jit(solution)/shard_map/ppermute | solution.py:52
  164.2 1.3 collective-permute-start.8
  175.5 8.8 %collective-permute-start.15 = (bf16[4,128,96]{1,0,2:T(4,128)(2,1)}, bf16[4,128,96]{1,0,2:T(4,128)(2,1)S(1)}, u32[]{:S(2)}, u32[]{:S(2)}) collective-permute-start(bf16[4,128,96]{1,0,2:T(4,128)(2,1)} %get-tuple-element.30), channel_id=1, source_target_pairs={{0,1},{1,2},{2,3},{3,0},{4,5},{5,6},{6,7},{7,4},{8,9},{9,10},{10,1... | collective-permute-start | bytes 294920 | tf_op jit(solution)/shard_map/ppermute | solution.py:58
  176.4 7.9 %collective-permute-start.16 = (bf16[4,128,96]{1,0,2:T(4,128)(2,1)}, bf16[4,128,96]{1,0,2:T(4,128)(2,1)S(1)}, u32[]{:S(2)}, u32[]{:S(2)}) collective-permute-start(bf16[4,128,96]{1,0,2:T(4,128)(2,1)} %get-tuple-element.29), channel_id=1, source_target_pairs={{0,2},{1,3},{2,0},{3,1},{4,6},{5,7},{6,4},{7,5},{8,10},{9,11},{10,... | collective-permute-start | bytes 294920 | tf_op jit(solution)/shard_map/ppermute | solution.py:58
  178.9 5.5 %collective-permute-start.17 = (bf16[4,128,96]{1,0,2:T(4,128)(2,1)}, bf16[4,128,96]{1,0,2:T(4,128)(2,1)S(1)}, u32[]{:S(2)}, u32[]{:S(2)}) collective-permute-start(bf16[4,128,96]{1,0,2:T(4,128)(2,1)} %get-tuple-element.28), channel_id=1, source_target_pairs={{0,3},{1,0},{2,1},{3,2},{4,7},{5,4},{6,5},{7,6},{8,11},{9,8},{10,9... | collective-permute-start | bytes 294920 | tf_op jit(solution)/shard_map/ppermute | solution.py:58
  (44 other events, 389.9 us)

commit v17 on v14

--- a/solution.py
+++ b/solution.py
@@ -104,8 +104,7 @@
 
 def route(piece, send_to, take_from, block_count):
     send = one_hot(send_to, block_count, piece.dtype)
-    holder = jnp.einsum("kj,krn->jrn", send, piece, preferred_element_type=jnp.float32)
-    holder = holder.astype(piece.dtype)
+    holder = jnp.sum(send[:, :, None, None] * piece[:, None, :, :], axis=0).astype(piece.dtype)
     arrived = lax.all_to_all(holder, "blk", split_axis=0, concat_axis=0, tiled=True)
     take = one_hot(take_from, block_count, piece.dtype)
     routed = jnp.einsum("kj,jrn->krn", take, arrived, preferred_element_type=jnp.float32)

time: 184 us -> 198 us (1.076)
  waiting for transfers between devices: 46.3 us -> 70.4 us
  blocking collectives: 22.2 us -> 0 us
  other arithmetic: 7.59 us -> 21.1 us
  starting transfers between devices: 53.3 us -> 62.2 us
  local copies, waits for them, and re-layouts: 20.8 us -> 13.2 us
  matrix products: 31.5 us -> 28.3 us
    all_to_all x1 -> x0, blocking collectives: 22.2 us -> none  [route(): lax.all_to_all(holder, 'blk', split_axis=0, concat_axis=0, tiled=True)]
    all_to_all x5 -> x6, waiting for transfers between devices: 34.1 us -> 48 us  [route(): lax.all_to_all(holder, 'blk', split_axis=0, concat_axis=0, tiled=True)]
    reduce_sum x0 -> x6, other arithmetic: none -> 8.59 us  [route(): jnp.sum(send[:, :, None, None] * piece[:, None, :, :], axis=0)]
    ppermute x15, waiting for transfers between devices: 11.6 us -> 18.8 us  [shift(): lax.ppermute(array, 'lvl', [(i, (i + by) % row_count) for i in range(row_...]
    all_to_all x5 -> x6, starting transfers between devices: 31.9 us -> 38.5 us  [route(): lax.all_to_all(holder, 'blk', split_axis=0, concat_axis=0, tiled=True)]
    convert_element_type x6 -> x0, local copies, waits for them, and re-layouts: 6.34 us -> none  [route(): holder = holder.astype(piece.dtype)]
    convert_element_type x0 -> x6, other arithmetic: none -> 4.71 us  [one_hot(): (index[:, None] == jnp.arange(count, dtype=jnp.int32)[None, :]).astype(dt...]
    ppermute x3, waiting for transfers between devices: 0.59 us -> 3.61 us  [collect(): parts.append(lax.ppermute(routed, 'lvl', [(r, dst_row)]))]
  transfers between devices with their start and end apart: 23 -> 24, of which waited for: 10 -> 10; matrix products, arithmetic and copies ran while one was open for 14% -> 17% of each run, Pallas kernels for 0% -> 0%
where the time goes in v17:
time: 198 us; the launch traced here: 197 us
  waiting for transfers between devices  70.4 us (36%)
  starting transfers between devices  62.2 us (31%)
  matrix products  28.3 us (14%)
  other arithmetic  21.1 us (11%)
  local copies, waits for them, and re-layouts  13.2 us (7%)
    all_to_all x6, waiting for transfers between devices, route(): lax.all_to_all(holder, 'blk', split_axis=0, concat_axis=0, tiled=True)  48 us
    all_to_all x6, starting transfers between devices, route(): lax.all_to_all(holder, 'blk', split_axis=0, concat_axis=0, tiled=True)  38.5 us
    dot_general x16, matrix products, dot(): return jnp.einsum(spec, a, b, preferred_element_type=jnp.float32)  22.5 us
    ppermute x15, starting transfers between devices, shift(): lax.ppermute(array, 'lvl', [(i, (i + by) % row_count) for i in range(row_...  18.9 us
    ppermute x15, waiting for transfers between devices, shift(): lax.ppermute(array, 'lvl', [(i, (i + by) % row_count) for i in range(row_...  18.8 us
    reduce_sum x6, other arithmetic, route(): jnp.sum(send[:, :, None, None] * piece[:, None, :, :], axis=0)  8.59 us
    dot_general x6, matrix products, route(): jnp.einsum('kj,jrn->krn', take, arrived, preferred_element_type=jnp.float32)  5.83 us
    mul x8, local copies, waits for them, and re-layouts, put_block(): full = part[..., None, :] * hot[:, None]  5.28 us
  transfers between devices with their start and end apart: 24, of which 10 were waited for; matrix products, arithmetic and copies ran while one was open for 17% of the time, Pallas kernels for 0%

profile of v17, /device:TPU:1, one launch (start us, length us, event | category | flops | bytes accessed | tf_op | source)
XLA Modules:
  0.0 196.6 jit_solution(10556770890587145404)
XLA Ops:
  8.4 2.1 %collective-permute-start.3 = (bf16[512,512]{1,0:T(8,128)(2,1)S(1)}, bf16[512,512]{1,0:T(8,128)(2,1)}, u32[]{:S(2)}, u32[]{:S(2)}) collective-permute-start(bf16[512,512]{1,0:T(8,128)(2,1)S(1)} %fusion.11), channel_id=1, source_target_pairs={{0,1},{1,2},{2,3},{3,0},{4,5},{5,6},{6,7},{7,4},{8,9},{9,10},{10,1... | collective-permute-start | bytes 1572872 | tf_op jit(solution)/shard_map/ppermute | solution.py:57
  10.5 2.5 %collective-permute-start.4 = (bf16[512,512]{1,0:T(8,128)(2,1)S(1)}, bf16[512,512]{1,0:T(8,128)(2,1)}, u32[]{:S(2)}, u32[]{:S(2)}) collective-permute-start(bf16[512,512]{1,0:T(8,128)(2,1)S(1)} %fusion.11), channel_id=1, source_target_pairs={{0,2},{1,3},{2,0},{3,1},{4,6},{5,7},{6,4},{7,5},{8,10},{9,11},{10,... | collective-permute-start | bytes 1572872 | tf_op jit(solution)/shard_map/ppermute | solution.py:57
  19.2 7.5 %collective-permute-done = bf16[512,96]{0,1:T(8,128)(2,1)S(1)} collective-permute-done((bf16[512,96]{0,1:T(8,128)(2,1)S(1)}, bf16[512,96]{0,1:T(8,128)(2,1)S(1)}, u32[]{:S(2)}, u32[]{:S(2)}) %collective-permute-start) | collective-permute-done | bytes 98336 | tf_op jit(solution)/shard_map/ppermute | solution.py:57
  26.7 3.6 %collective-permute-start.5 = (bf16[512,512]{1,0:T(8,128)(2,1)S(1)}, bf16[512,512]{1,0:T(8,128)(2,1)}, u32[]{:S(2)}, u32[]{:S(2)}) collective-permute-start(bf16[512,512]{1,0:T(8,128)(2,1)S(1)} %fusion.11), channel_id=1, source_target_pairs={{0,3},{1,0},{2,1},{3,2},{4,7},{5,4},{6,5},{7,6},{8,11},{9,8},{10,9... | collective-permute-start | bytes 1572872 | tf_op jit(solution)/shard_map/ppermute | solution.py:57
  30.4 7.4 %collective-permute-done.1 = bf16[512,96]{0,1:T(8,128)(2,1)S(1)} collective-permute-done((bf16[512,96]{0,1:T(8,128)(2,1)S(1)}, bf16[512,96]{0,1:T(8,128)(2,1)S(1)}, u32[]{:S(2)}, u32[]{:S(2)}) %collective-permute-start.1) | collective-permute-done | bytes 98336 | tf_op jit(solution)/shard_map/ppermute | solution.py:57
  39.3 10.6 %all-to-all-start = ((bf16[32,128,96]{1,2,0:T(8,128)(2,1)}), bf16[32,128,96]{1,2,0:T(8,128)(2,1)S(1)}, u32[]{:S(2)}, u32[]{:S(2)}) async-start(bf16[32,128,96]{1,2,0:T(8,128)(2,1)} %multiply_reduce_fusion.5), calls=%async_computation | async-start | bytes 1572864 | tf_op jit(solution)/shard_map/all_to_all | solution.py:108
  52.0 12.1 %all-to-all-done = bf16[32,128,96]{1,2,0:T(8,128)(2,1)S(1)} async-done(((bf16[32,128,96]{1,2,0:T(8,128)(2,1)}), bf16[32,128,96]{1,2,0:T(8,128)(2,1)S(1)}, u32[]{:S(2)}, u32[]{:S(2)}) %all-to-all-start) | async-done | bytes 786464 | tf_op jit(solution)/shard_map/all_to_all | solution.py:108
  68.4 3.8 %all-to-all-start.1 = ((bf16[32,128,96]{1,2,0:T(8,128)(2,1)}), bf16[32,128,96]{1,2,0:T(8,128)(2,1)S(1)}, u32[]{:S(2)}, u32[]{:S(2)}) async-start(bf16[32,128,96]{1,2,0:T(8,128)(2,1)} %multiply_reduce_fusion.4), calls=%async_computation.1 | async-start | bytes 1572864 | tf_op jit(solution)/shard_map/all_to_all | solution.py:108
  73.6 12.9 %all-to-all-done.1 = bf16[32,128,96]{1,2,0:T(8,128)(2,1)S(1)} async-done(((bf16[32,128,96]{1,2,0:T(8,128)(2,1)}), bf16[32,128,96]{1,2,0:T(8,128)(2,1)S(1)}, u32[]{:S(2)}, u32[]{:S(2)}) %all-to-all-start.1) | async-done | bytes 786464 | tf_op jit(solution)/shard_map/all_to_all | solution.py:108
  86.5 2.1 %select_select_fusion.9 = (bf16[4,128,96]{1,0,2:T(4,128)(2,1)}, bf16[4,128,96]{1,0,2:T(4,128)(2,1)}, bf16[4,128,96]{1,0,2:T(4,128)(2,1)}, bf16[4,128,96]{1,0,2:T(4,128)(2,1)}, bf16[4,128,96]{1,0,2:T(4,128)(2,1)S(1)}) fusion(bf16[4,128,96]{1,0,2:T(4,128)(2,1)} %copy-done.11, pred[]{:T(512)S(6)} %eq.239, pred[]{:T(512)S(6)} %eq.234, pred[]{:T(512)S(6)} %eq.227, ...), kind=kOutput, calls=%fused_computation.134 | convolution fusion | flops 3784832 | bytes 1376284 | tf_op jit(solution)/shard_map/kj,jrn->krn/dot_general | solution.py:110
  90.8 3.8 %all-to-all-start.2 = ((bf16[32,128,96]{1,2,0:T(8,128)(2,1)}), bf16[32,128,96]{1,2,0:T(8,128)(2,1)S(1)}, u32[]{:S(2)}, u32[]{:S(2)}) async-start(bf16[32,128,96]{1,2,0:T(8,128)(2,1)} %multiply_reduce_fusion.3), calls=%async_computation.2 | async-start | bytes 1572864 | tf_op jit(solution)/shard_map/all_to_all | solution.py:108
  113.6 8.2 %all-to-all-start.3 = ((bf16[32,128,96]{1,2,0:T(8,128)(2,1)}), bf16[32,128,96]{1,2,0:T(8,128)(2,1)S(1)}, u32[]{:S(2)}, u32[]{:S(2)}) async-start(bf16[32,128,96]{1,2,0:T(8,128)(2,1)} %multiply_reduce_fusion.2), calls=%async_computation.3 | async-start | bytes 1572864 | tf_op jit(solution)/shard_map/all_to_all | solution.py:108
  121.9 3.3 %convolution_convert_fusion.1 = bf16[384,768]{0,1:T(8,128)(2,1)} fusion(bf16[4,128,384]{1,2,0:T(8,128)(2,1)S(1)} %copy-done.8, bf16[1,1,768,768]{3,2,1,0:T(8,128)(2,1)S(1)} %copy-done, bf16[4,768,128]{1,2,0:T(8,128)(2,1)} %copy-done.3, bf16[1,1,768,384]{3,2,1,0:T(8,128)(2,1)} %param.7), kind=kOutput, calls=%fused_computation.16 | convolution fusion | flops 756154368 | bytes 3538944 | tf_op jit(solution)/shard_map/ab,bn->an/dot_general | solution.py:148
  125.2 2.3 %fusion.7 = bf16[512,384]{0,1:T(8,128)(2,1)S(1)} fusion(bf16[768,512]{0,1:T(8,128)(2,1)} %bitcast.261, bf16[384,768]{0,1:T(8,128)(2,1)} %convolution_convert_fusion.1, bf16[1,1,768,768]{3,2,1,0:T(8,128)(2,1)S(1)} %copy-done), kind=kOutput, calls=%fused_computation.27 | convolution fusion | flops 755466240 | bytes 2949120 | tf_op jit(solution)/shard_map/bm,bn->mn/dot_general | solution.py:148
  132.0 4.1 %all-to-all-done.3 = bf16[32,128,96]{1,2,0:T(8,128)(2,1)S(1)} async-done(((bf16[32,128,96]{1,2,0:T(8,128)(2,1)}), bf16[32,128,96]{1,2,0:T(8,128)(2,1)S(1)}, u32[]{:S(2)}, u32[]{:S(2)}) %all-to-all-start.3) | async-done | bytes 786464 | tf_op jit(solution)/shard_map/all_to_all | solution.py:108
  136.4 2.1 %collective-permute-done.14 = bf16[512,96]{0,1:T(8,128)(2,1)S(1)} collective-permute-done((bf16[512,96]{0,1:T(8,128)(2,1)}, bf16[512,96]{0,1:T(8,128)(2,1)S(1)}, u32[]{:S(2)}, u32[]{:S(2)}) %collective-permute-start.14) | collective-permute-done | bytes 98336 | tf_op jit(solution)/shard_map/ppermute | solution.py:57
  140.3 8.0 %all-to-all-start.4 = ((bf16[32,128,96]{1,2,0:T(8,128)(2,1)}), bf16[32,128,96]{1,2,0:T(8,128)(2,1)S(1)}, u32[]{:S(2)}, u32[]{:S(2)}) async-start(bf16[32,128,96]{1,2,0:T(8,128)(2,1)} %multiply_reduce_fusion.1), calls=%async_computation.4 | async-start | bytes 1572864 | tf_op jit(solution)/shard_map/all_to_all | solution.py:108
  148.4 14.1 %all-to-all-done.4 = bf16[32,128,96]{1,2,0:T(8,128)(2,1)S(1)} async-done(((bf16[32,128,96]{1,2,0:T(8,128)(2,1)}), bf16[32,128,96]{1,2,0:T(8,128)(2,1)S(1)}, u32[]{:S(2)}, u32[]{:S(2)}) %all-to-all-start.4) | async-done | bytes 786464 | tf_op jit(solution)/shard_map/all_to_all | solution.py:108
  164.6 4.0 %all-to-all-start.5 = ((bf16[32,128,96]{1,2,0:T(8,128)(2,1)}), bf16[32,128,96]{1,2,0:T(8,128)(2,1)S(1)}, u32[]{:S(2)}, u32[]{:S(2)}) async-start(bf16[32,128,96]{1,2,0:T(8,128)(2,1)} %multiply_reduce_fusion), calls=%async_computation.5 | async-start | bytes 1572864 | tf_op jit(solution)/shard_map/all_to_all | solution.py:108
  169.9 3.4 %collective-permute-start.6 = (bf16[4,128,96]{1,0,2:T(4,128)(2,1)S(1)}, bf16[4,128,96]{1,0,2:T(4,128)(2,1)S(1)}, u32[]{:S(2)}, u32[]{:S(2)}) collective-permute-start(bf16[4,128,96]{1,0,2:T(4,128)(2,1)S(1)} %copy-done.6), channel_id=1, source_target_pairs={{0,3},{4,7},{8,11},{12,15},{16,19},{20,23},{24,27},{28,31},{32,35}... | collective-permute-start | bytes 294920 | tf_op jit(solution)/shard_map/ppermute | solution.py:52
  173.4 3.6 %collective-permute-done.6 = bf16[4,128,96]{1,0,2:T(4,128)(2,1)S(1)} collective-permute-done((bf16[4,128,96]{1,0,2:T(4,128)(2,1)S(1)}, bf16[4,128,96]{1,0,2:T(4,128)(2,1)S(1)}, u32[]{:S(2)}, u32[]{:S(2)}) %collective-permute-start.6) | collective-permute-done | bytes 98336 | tf_op jit(solution)/shard_map/ppermute | solution.py:52
  178.0 4.8 %all-to-all-done.5 = bf16[32,128,96]{1,2,0:T(8,128)(2,1)S(1)} async-done(((bf16[32,128,96]{1,2,0:T(8,128)(2,1)}), bf16[32,128,96]{1,2,0:T(8,128)(2,1)S(1)}, u32[]{:S(2)}, u32[]{:S(2)}) %all-to-all-start.5) | async-done | bytes 786464 | tf_op jit(solution)/shard_map/all_to_all | solution.py:108
  186.9 3.6 %fusion.10 = bf16[768,384]{1,0:T(8,128)(2,1)} fusion(bf16[768,384]{1,0:T(8,128)(2,1)} %convolution_convert_fusion.6, bf16[384,768]{0,1:T(8,128)(2,1)} %convolution_convert_fusion.1, bf16[1,1,768,768]{3,2,1,0:T(8,128)(2,1)S(1)} %copy-done, bf16[4,768,128]{1,2,0:T(8,128)(2,1)S(1)} %copy-done.4, bf16[1,1,768,384]{3,2,1,0:T(8,128)(2,1)} %param.7, ...), kind=kOutput, calls=%fused_computation.30 | convolution fusion | flops 756744192 | bytes 4718594 | tf_op jit(solution)/shard_map/ab,bn->an/dot_general | solution.py:148
  192.7 2.3 %convolution_convert_fusion.3 = bf16[384,768]{0,1:T(8,128)(2,1)S(1)} fusion(bf16[4,128,384]{1,2,0:T(8,128)(2,1)S(1)} %fusion.46, bf16[1,1,768,768]{3,2,1,0:T(8,128)(2,1)S(1)} %copy-done, bf16[768,384]{1,0:T(8,128)(2,1)} %fusion.10, bf16[1,1,4,768,128]{4,3,2,1,0:T(8,128)(2,1)S(1)} %copy-done.2), kind=kOutput, calls=%fused_computation.18 | convolution fusion | flops 756154368 | bytes 3538944 | tf_op jit(solution)/shard_map/ba,bn->an/dot_general | solution.py:148
  (196 shorter events, 62.8 us)
Async XLA Ops:
  8.4 42.1 %collective-permute-start.3 = (bf16[512,512]{1,0:T(8,128)(2,1)S(1)}, bf16[512,512]{1,0:T(8,128)(2,1)}, u32[]{:S(2)}, u32[]{:S(2)}) collective-permute-start(bf16[512,512]{1,0:T(8,128)(2,1)S(1)} %fusion.11), channel_id=1, source_target_pairs={{0,1},{1,2},{2,3},{3,0},{4,5},{5,6},{6,7},{7,4},{8,9},{9,10},{10,1... | collective-permute-start | bytes 1572872 | tf_op jit(solution)/shard_map/ppermute | solution.py:57
  10.5 40.0 %collective-permute-start.4 = (bf16[512,512]{1,0:T(8,128)(2,1)S(1)}, bf16[512,512]{1,0:T(8,128)(2,1)}, u32[]{:S(2)}, u32[]{:S(2)}) collective-permute-start(bf16[512,512]{1,0:T(8,128)(2,1)S(1)} %fusion.11), channel_id=1, source_target_pairs={{0,2},{1,3},{2,0},{3,1},{4,6},{5,7},{6,4},{7,5},{8,10},{9,11},{10,... | collective-permute-start | bytes 1572872 | tf_op jit(solution)/shard_map/ppermute | solution.py:57
  17.2 9.5 %collective-permute-start = (bf16[512,96]{0,1:T(8,128)(2,1)S(1)}, bf16[512,96]{0,1:T(8,128)(2,1)S(1)}, u32[]{:S(2)}, u32[]{:S(2)}) collective-permute-start(bf16[512,96]{0,1:T(8,128)(2,1)S(1)} %get-tuple-element.9), channel_id=1, source_target_pairs={{0,3},{1,0},{2,1},{3,2},{4,7},{5,4},{6,5},{7,6},{8,11},{9,8},{10,9... | collective-permute-start | bytes 294920 | tf_op jit(solution)/shard_map/ppermute | solution.py:57
  18.4 19.3 %collective-permute-start.1 = (bf16[512,96]{0,1:T(8,128)(2,1)S(1)}, bf16[512,96]{0,1:T(8,128)(2,1)S(1)}, u32[]{:S(2)}, u32[]{:S(2)}) collective-permute-start(bf16[512,96]{0,1:T(8,128)(2,1)S(1)} %get-tuple-element.8), channel_id=1, source_target_pairs={{0,2},{1,3},{2,0},{3,1},{4,6},{5,7},{6,4},{7,5},{8,10},{9,11},{10,... | collective-permute-start | bytes 294920 | tf_op jit(solution)/shard_map/ppermute | solution.py:57
  18.6 19.2 %collective-permute-start.2 = (bf16[512,96]{0,1:T(8,128)(2,1)S(1)}, bf16[512,96]{0,1:T(8,128)(2,1)S(1)}, u32[]{:S(2)}, u32[]{:S(2)}) collective-permute-start(bf16[512,96]{0,1:T(8,128)(2,1)S(1)} %get-tuple-element.7), channel_id=1, source_target_pairs={{0,1},{1,2},{2,3},{3,0},{4,5},{5,6},{6,7},{7,4},{8,9},{9,10},{10,1... | collective-permute-start | bytes 294920 | tf_op jit(solution)/shard_map/ppermute | solution.py:57
  26.7 23.8 %collective-permute-start.5 = (bf16[512,512]{1,0:T(8,128)(2,1)S(1)}, bf16[512,512]{1,0:T(8,128)(2,1)}, u32[]{:S(2)}, u32[]{:S(2)}) collective-permute-start(bf16[512,512]{1,0:T(8,128)(2,1)S(1)} %fusion.11), channel_id=1, source_target_pairs={{0,3},{1,0},{2,1},{3,2},{4,7},{5,4},{6,5},{7,6},{8,11},{9,8},{10,9... | collective-permute-start | bytes 1572872 | tf_op jit(solution)/shard_map/ppermute | solution.py:57
  39.3 24.9 %all-to-all-start = ((bf16[32,128,96]{1,2,0:T(8,128)(2,1)}), bf16[32,128,96]{1,2,0:T(8,128)(2,1)S(1)}, u32[]{:S(2)}, u32[]{:S(2)}) async-start(bf16[32,128,96]{1,2,0:T(8,128)(2,1)} %multiply_reduce_fusion.5), calls=%async_computation | async-start | bytes 1572864 | tf_op jit(solution)/shard_map/all_to_all | solution.py:108
  68.4 18.1 %all-to-all-start.1 = ((bf16[32,128,96]{1,2,0:T(8,128)(2,1)}), bf16[32,128,96]{1,2,0:T(8,128)(2,1)S(1)}, u32[]{:S(2)}, u32[]{:S(2)}) async-start(bf16[32,128,96]{1,2,0:T(8,128)(2,1)} %multiply_reduce_fusion.4), calls=%async_computation.1 | async-start | bytes 1572864 | tf_op jit(solution)/shard_map/all_to_all | solution.py:108
  90.8 18.8 %all-to-all-start.2 = ((bf16[32,128,96]{1,2,0:T(8,128)(2,1)}), bf16[32,128,96]{1,2,0:T(8,128)(2,1)S(1)}, u32[]{:S(2)}, u32[]{:S(2)}) async-start(bf16[32,128,96]{1,2,0:T(8,128)(2,1)} %multiply_reduce_fusion.3), calls=%async_computation.2 | async-start | bytes 1572864 | tf_op jit(solution)/shard_map/all_to_all | solution.py:108
  95.9 9.9 %collective-permute-start.11 = (bf16[4,128,96]{1,0,2:T(4,128)(2,1)}, bf16[4,128,96]{1,0,2:T(4,128)(2,1)}, u32[]{:S(2)}, u32[]{:S(2)}) collective-permute-start(bf16[4,128,96]{1,0,2:T(4,128)(2,1)} %get-tuple-element.32), channel_id=1, source_target_pairs={{0,3},{1,0},{2,1},{3,2},{4,7},{5,4},{6,5},{7,6},{8,11},{9,8},{10,9... | collective-permute-start | bytes 294920 | tf_op jit(solution)/shard_map/ppermute | solution.py:57
  97.2 9.5 %collective-permute-start.10 = (bf16[4,128,96]{1,0,2:T(4,128)(2,1)}, bf16[4,128,96]{1,0,2:T(4,128)(2,1)}, u32[]{:S(2)}, u32[]{:S(2)}) collective-permute-start(bf16[4,128,96]{1,0,2:T(4,128)(2,1)} %get-tuple-element.33), channel_id=1, source_target_pairs={{0,2},{1,3},{2,0},{3,1},{4,6},{5,7},{6,4},{7,5},{8,10},{9,11},{10,... | collective-permute-start | bytes 294920 | tf_op jit(solution)/shard_map/ppermute | solution.py:57
  97.7 9.9 %collective-permute-start.9 = (bf16[4,128,96]{1,0,2:T(4,128)(2,1)}, bf16[4,128,96]{1,0,2:T(4,128)(2,1)}, u32[]{:S(2)}, u32[]{:S(2)}) collective-permute-start(bf16[4,128,96]{1,0,2:T(4,128)(2,1)} %get-tuple-element.34), channel_id=1, source_target_pairs={{0,1},{1,2},{2,3},{3,0},{4,5},{5,6},{6,7},{7,4},{8,9},{9,10},{10,1... | collective-permute-start | bytes 294920 | tf_op jit(solution)/shard_map/ppermute | solution.py:57
  113.6 22.5 %all-to-all-start.3 = ((bf16[32,128,96]{1,2,0:T(8,128)(2,1)}), bf16[32,128,96]{1,2,0:T(8,128)(2,1)S(1)}, u32[]{:S(2)}, u32[]{:S(2)}) async-start(bf16[32,128,96]{1,2,0:T(8,128)(2,1)} %multiply_reduce_fusion.2), calls=%async_computation.3 | async-start | bytes 1572864 | tf_op jit(solution)/shard_map/all_to_all | solution.py:108
  128.6 7.9 %collective-permute-start.12 = (bf16[512,96]{0,1:T(8,128)(2,1)}, bf16[512,96]{0,1:T(8,128)(2,1)S(1)}, u32[]{:S(2)}, u32[]{:S(2)}) collective-permute-start(bf16[512,96]{0,1:T(8,128)(2,1)} %get-tuple-element.5), channel_id=1, source_target_pairs={{0,3},{1,0},{2,1},{3,2},{4,7},{5,4},{6,5},{7,6},{8,11},{9,8},{10,9... | collective-permute-start | bytes 294920 | tf_op jit(solution)/shard_map/ppermute | solution.py:57
  130.5 5.9 %collective-permute-start.13 = (bf16[512,96]{0,1:T(8,128)(2,1)}, bf16[512,96]{0,1:T(8,128)(2,1)S(1)}, u32[]{:S(2)}, u32[]{:S(2)}) collective-permute-start(bf16[512,96]{0,1:T(8,128)(2,1)} %get-tuple-element.4), channel_id=1, source_target_pairs={{0,2},{1,3},{2,0},{3,1},{4,6},{5,7},{6,4},{7,5},{8,10},{9,11},{10,... | collective-permute-start | bytes 294920 | tf_op jit(solution)/shard_map/ppermute | solution.py:57
  131.8 6.7 %collective-permute-start.14 = (bf16[512,96]{0,1:T(8,128)(2,1)}, bf16[512,96]{0,1:T(8,128)(2,1)S(1)}, u32[]{:S(2)}, u32[]{:S(2)}) collective-permute-start(bf16[512,96]{0,1:T(8,128)(2,1)} %get-tuple-element.3), channel_id=1, source_target_pairs={{0,1},{1,2},{2,3},{3,0},{4,5},{5,6},{6,7},{7,4},{8,9},{9,10},{10,1... | collective-permute-start | bytes 294920 | tf_op jit(solution)/shard_map/ppermute | solution.py:57
  140.3 22.3 %all-to-all-start.4 = ((bf16[32,128,96]{1,2,0:T(8,128)(2,1)}), bf16[32,128,96]{1,2,0:T(8,128)(2,1)S(1)}, u32[]{:S(2)}, u32[]{:S(2)}) async-start(bf16[32,128,96]{1,2,0:T(8,128)(2,1)} %multiply_reduce_fusion.1), calls=%async_computation.4 | async-start | bytes 1572864 | tf_op jit(solution)/shard_map/all_to_all | solution.py:108
  164.6 18.2 %all-to-all-start.5 = ((bf16[32,128,96]{1,2,0:T(8,128)(2,1)}), bf16[32,128,96]{1,2,0:T(8,128)(2,1)S(1)}, u32[]{:S(2)}, u32[]{:S(2)}) async-start(bf16[32,128,96]{1,2,0:T(8,128)(2,1)} %multiply_reduce_fusion), calls=%async_computation.5 | async-start | bytes 1572864 | tf_op jit(solution)/shard_map/all_to_all | solution.py:108
  168.5 4.8 %collective-permute-start.8 = (bf16[4,128,96]{1,0,2:T(4,128)(2,1)S(1)}, bf16[4,128,96]{1,0,2:T(4,128)(2,1)S(1)}, u32[]{:S(2)}, u32[]{:S(2)}) collective-permute-start(bf16[4,128,96]{1,0,2:T(4,128)(2,1)S(1)} %copy-done.6), channel_id=1, source_target_pairs={{2,3},{6,7},{10,11},{14,15},{18,19},{22,23},{26,27},{30,31},{34,35... | collective-permute-start | bytes 294920 | tf_op jit(solution)/shard_map/ppermute | solution.py:52
  169.2 4.1 %collective-permute-start.7 = (bf16[4,128,96]{1,0,2:T(4,128)(2,1)S(1)}, bf16[4,128,96]{1,0,2:T(4,128)(2,1)S(1)}, u32[]{:S(2)}, u32[]{:S(2)}) collective-permute-start(bf16[4,128,96]{1,0,2:T(4,128)(2,1)S(1)} %copy-done.6), channel_id=1, source_target_pairs={{1,3},{5,7},{9,11},{13,15},{17,19},{21,23},{25,27},{29,31},{33,35}... | collective-permute-start | bytes 294920 | tf_op jit(solution)/shard_map/ppermute | solution.py:52
  169.9 7.1 %collective-permute-start.6 = (bf16[4,128,96]{1,0,2:T(4,128)(2,1)S(1)}, bf16[4,128,96]{1,0,2:T(4,128)(2,1)S(1)}, u32[]{:S(2)}, u32[]{:S(2)}) collective-permute-start(bf16[4,128,96]{1,0,2:T(4,128)(2,1)S(1)} %copy-done.6), channel_id=1, source_target_pairs={{0,3},{4,7},{8,11},{12,15},{16,19},{20,23},{24,27},{28,31},{32,35}... | collective-permute-start | bytes 294920 | tf_op jit(solution)/shard_map/ppermute | solution.py:52
  183.8 6.7 %collective-permute-start.17 = (bf16[4,128,96]{1,0,2:T(4,128)(2,1)}, bf16[4,128,96]{1,0,2:T(4,128)(2,1)S(1)}, u32[]{:S(2)}, u32[]{:S(2)}) collective-permute-start(bf16[4,128,96]{1,0,2:T(4,128)(2,1)} %get-tuple-element.28), channel_id=1, source_target_pairs={{0,3},{1,0},{2,1},{3,2},{4,7},{5,4},{6,5},{7,6},{8,11},{9,8},{10,9... | collective-permute-start | bytes 294920 | tf_op jit(solution)/shard_map/ppermute | solution.py:57
  184.1 6.4 %collective-permute-start.16 = (bf16[4,128,96]{1,0,2:T(4,128)(2,1)S(1)}, bf16[4,128,96]{1,0,2:T(4,128)(2,1)S(1)}, u32[]{:S(2)}, u32[]{:S(2)}) collective-permute-start(bf16[4,128,96]{1,0,2:T(4,128)(2,1)S(1)} %get-tuple-element.29), channel_id=1, source_target_pairs={{0,2},{1,3},{2,0},{3,1},{4,6},{5,7},{6,4},{7,5},{8,10},{9,11},{10,... | collective-permute-start | bytes 294920 | tf_op jit(solution)/shard_map/ppermute | solution.py:57
  186.1 6.3 %collective-permute-start.15 = (bf16[4,128,96]{1,0,2:T(4,128)(2,1)S(1)}, bf16[4,128,96]{1,0,2:T(4,128)(2,1)S(1)}, u32[]{:S(2)}, u32[]{:S(2)}) collective-permute-start(bf16[4,128,96]{1,0,2:T(4,128)(2,1)S(1)} %get-tuple-element.30), channel_id=1, source_target_pairs={{0,1},{1,2},{2,3},{3,0},{4,5},{5,6},{6,7},{7,4},{8,9},{9,10},{10,1... | collective-permute-start | bytes 294920 | tf_op jit(solution)/shard_map/ppermute | solution.py:57
  (43 other events, 572.8 us)
